TPU v7x, 32 devices: a whole 2x2x4 slice. The times are simulated.
32 devices in a mesh: row: 4 (over y, x), col: 8 (over z, core).
Axes of the slice: x: 2, y: 2, z: 4, core: 2. Of those that a mesh axis runs over, the one named last changes fastest.
Arguments:
- tiles: bfloat16 [64, 128, 128, 128], P('row', 'col'), may hold values from -1 to 1
- tile_cols: int32 [64, 128], P('row', 'col'), may hold values from 0 to 7
- degree_scale: float32 [8192], P(('row', 'col')), may hold values from 0.8 to 1.25
- start_block: float32 [8192, 128], P(('row', 'col')), may hold values from -9 to 9
- planted: bfloat16 [8192, 128], P(('row', 'col')), may hold values from -19.595918 to 19.595918
- strengths: float32 [128], replicated, may hold values from 1.5 to 2.1
- bounds: float32 [2], replicated, may hold values from -2.2 to 1.7, as said below
Outputs:
- ortho_basis: float32 [8192, 128], P(('row', 'col'))
- projected: float32 [128, 128], replicated
Inputs may be any that keep to these rules, and one draw needn't show every extreme that they name: bounds[0] is the lower end and bounds[1] the upper end; bounds[1] - bounds[0] is at least 3.
All inputs are finite; a program needn't handle non-finite values.
Results may differ from a plain program's by a relative error of at most 0.038.
Values may be sent and summed in bfloat16 or wider, within the bound.
No kernel may reach another device: no remote copies, remote signals or barrier semaphores. Data moves between devices by JAX's collectives and lax.ppermute only.
A program may use at most 128 MiB of HBM per device.

v0:
```python
import jax
import jax.numpy as jnp
from jax import lax
from jax.sharding import PartitionSpec as P

DEGREE = 4


def planted_product(planted_part, coupling):
    upper_part = coupling.astype(jnp.bfloat16)
    lower_part = (coupling - upper_part.astype(jnp.float32)).astype(jnp.bfloat16)
    first = jnp.dot(planted_part, upper_part, preferred_element_type=jnp.float32)
    return first + jnp.dot(planted_part, lower_part, preferred_element_type=jnp.float32)


def local(tiles, tile_cols, degree_scale, start_block, planted, strengths, bounds):
    piece_rows = start_block.shape[0]
    node_count = piece_rows * lax.axis_size("row") * lax.axis_size("col")
    tile_size = tiles.shape[2]
    weights = strengths[:, None]

    def operate(vector):
        scaled = (degree_scale[:, None] * vector).astype(jnp.bfloat16)
        gathered = lax.all_gather(scaled, "row", axis=0, tiled=True)
        blocks = gathered.reshape(-1, tile_size, gathered.shape[1])
        picked = blocks[tile_cols]
        result = jnp.einsum("rsab,rsbk->rak", tiles, picked, preferred_element_type=jnp.float32)
        result = result.reshape(piece_rows * lax.axis_size("col"), result.shape[2])
        summed = lax.psum_scatter(result, "col", scatter_dimension=0, tiled=True)
        coupling = lax.psum(
            jnp.dot(planted.T, scaled, preferred_element_type=jnp.float32), ("row", "col")
        )
        summed = summed + planted_product(planted, weights * coupling) / node_count
        return degree_scale[:, None] * summed

    center = (bounds[1] + bounds[0]) * 0.5
    half_width = (bounds[1] - bounds[0]) * 0.5
    previous = start_block
    current = (operate(start_block) - center * start_block) / half_width
    for index_step in range(DEGREE - 1):
        applied = operate(current)
        following = 2.0 * (applied - center * current) / half_width - previous
        previous, current = (current, following)
    local_gram = jnp.dot(current.T, current, precision=lax.Precision.HIGHEST)
    applied = operate(current)
    local_rayleigh = jnp.dot(current.T, applied, precision=lax.Precision.HIGHEST)
    gram_total, rayleigh_total = lax.psum((local_gram, local_rayleigh), ("row", "col"))
    gram_matrix = gram_total / node_count
    rayleigh = rayleigh_total / node_count
    factor = jnp.linalg.cholesky(gram_matrix)
    ortho_basis = lax.linalg.triangular_solve(
        factor, current, left_side=False, lower=True, transpose_a=True
    )
    half_solved = lax.linalg.triangular_solve(factor, rayleigh, left_side=True, lower=True)
    projected = lax.linalg.triangular_solve(
        factor, half_solved, left_side=False, lower=True, transpose_a=True
    )
    return (ortho_basis, projected)


def solution(mesh):
    in_specs = (
        P("row", "col", None, None),
        P("row", "col"),
        P(("row", "col")),
        P(("row", "col"), None),
        P(("row", "col"), None),
        P(),
        P(),
    )
    out_specs = (P(("row", "col"), None), P())
    return jax.shard_map(local, mesh=mesh, in_specs=in_specs, out_specs=out_specs, check_vma=False)
```

profile of v0, /device:TPU:0, one launch (start us, length us, event | category | flops | bytes accessed | tf_op | source)
XLA Modules:
  0.0 882.2 jit_solution(11518635513217259267)
XLA Ops:
  8.1 1.0 copy.24
  10.6 11.5 %all_gather.15 = bf16[1024,128]{0,1:T(8,128)(2,1)S(1)} all-gather(bf16[256,128]{0,1:T(8,128)(2,1)S(1)} %multiply_convert_fusion.4), channel_id=1, replica_groups=mesh['row'=4,'col'=8] {'row'}, dimensions={0}, use_global_device_ids=true | all-gather | bytes 327680 | tf_op jit(solution)/shard_map/all_gather | solution.py:24
  23.1 8.6 gather_fusion
  31.7 8.2 fusion.63
  39.9 1.3 copy.26
  44.3 93.0 %all-reduce.8.cloned.1.call-done = f32[128,128]{0,1:T(8,128)} async-done(((f32[128,128]{0,1:T(8,128)}), f32[128,128]{0,1:T(8,128)}) %all-reduce.8.cloned.1.call-update) | async-done | bytes 65552 | tf_op jit(solution)/shard_map/psum | solution.py:30
  137.3 1.0 fusion.43
  138.3 1.1 multiply_convert_fusion.3
  139.5 11.3 %all_gather.16 = bf16[1024,128]{0,1:T(8,128)(2,1)S(1)} all-gather(bf16[256,128]{0,1:T(8,128)(2,1)S(1)} %get-tuple-element.6), channel_id=1, replica_groups=mesh['row'=4,'col'=8] {'row'}, dimensions={0}, use_global_device_ids=true | all-gather | bytes 327680 | tf_op jit(solution)/shard_map/all_gather | solution.py:24
  150.7 0.8 convolution_bitcast_fusion.3
  151.7 8.6 gather_fusion.1
  160.4 8.1 fusion.64
  168.5 1.3 copy.47
  170.1 109.1 %all-reduce.10.cloned.1.call-done = f32[128,128]{0,1:T(8,128)} async-done(((f32[128,128]{0,1:T(8,128)}), f32[128,128]{0,1:T(8,128)}) %all-reduce.10.cloned.1.call-update) | async-done | bytes 65552 | tf_op jit(solution)/shard_map/psum | solution.py:30
  279.2 1.0 fusion.44
  280.3 1.1 multiply_convert_fusion.2
  281.4 11.3 %all_gather.17 = bf16[1024,128]{0,1:T(8,128)(2,1)S(1)} all-gather(bf16[256,128]{0,1:T(8,128)(2,1)S(1)} %get-tuple-element.8), channel_id=1, replica_groups=mesh['row'=4,'col'=8] {'row'}, dimensions={0}, use_global_device_ids=true | all-gather | bytes 327680 | tf_op jit(solution)/shard_map/all_gather | solution.py:24
  292.7 0.8 convolution_bitcast_fusion.2
  293.7 8.6 gather_fusion.2
  302.3 8.1 fusion.65
  310.4 1.3 copy.49
  311.8 109.4 %all-reduce.12.cloned.1.call-done = f32[128,128]{0,1:T(8,128)} async-done(((f32[128,128]{0,1:T(8,128)}), f32[128,128]{0,1:T(8,128)}) %all-reduce.12.cloned.1.call-update) | async-done | bytes 65552 | tf_op jit(solution)/shard_map/psum | solution.py:30
  421.2 1.0 fusion.45
  422.2 1.1 multiply_convert_fusion.1
  423.4 11.3 %all_gather.18 = bf16[1024,128]{0,1:T(8,128)(2,1)S(1)} all-gather(bf16[256,128]{0,1:T(8,128)(2,1)S(1)} %get-tuple-element.10), channel_id=1, replica_groups=mesh['row'=4,'col'=8] {'row'}, dimensions={0}, use_global_device_ids=true | all-gather | bytes 327680 | tf_op jit(solution)/shard_map/all_gather | solution.py:24
  435.6 8.6 gather_fusion.3
  444.3 8.1 fusion.66
  452.4 1.3 copy.51
  453.8 109.4 %all-reduce.14.cloned.1.call-done = f32[128,128]{0,1:T(8,128)} async-done(((f32[128,128]{0,1:T(8,128)}), f32[128,128]{0,1:T(8,128)}) %all-reduce.14.cloned.1.call-update) | async-done | bytes 65552 | tf_op jit(solution)/shard_map/psum | solution.py:30
  563.2 1.0 fusion.46
  564.2 1.1 multiply_convert_fusion
  565.3 20.6 %all_gather.19 = bf16[1024,128]{0,1:T(8,128)(2,1)S(1)} all-gather(bf16[256,128]{0,1:T(8,128)(2,1)S(1)} %get-tuple-element.12), channel_id=1, replica_groups=mesh['row'=4,'col'=8] {'row'}, dimensions={0}, use_global_device_ids=true | all-gather | bytes 327680 | tf_op jit(solution)/shard_map/all_gather | solution.py:24
  586.9 8.6 gather_fusion.4
  595.5 8.1 fusion.67
  603.7 1.3 copy.53
  605.0 0.9 fusion.61
  605.9 108.5 %all-reduce.16.cloned.1.call-done = f32[128,128]{0,1:T(8,128)} async-done(((f32[128,128]{0,1:T(8,128)}), f32[128,128]{0,1:T(8,128)}) %all-reduce.16.cloned.1.call-update) | async-done | bytes 65552 | tf_op jit(solution)/shard_map/psum | solution.py:30
  714.4 1.0 fusion.47
  715.5 1.1 fusion.3
  716.6 0.9 fusion.62
  717.5 129.2 %all-reduce.18.cloned.1.call-done = (f32[128,128]{0,1:T(8,128)}, f32[128,128]{0,1:T(8,128)}) async-done(((f32[128,128]{0,1:T(8,128)}, f32[128,128]{0,1:T(8,128)}), (f32[128,128]{0,1:T(8,128)}, f32[128,128]{0,1:T(8,128)})) %all-reduce.18.cloned.1.call-update) | async-done | bytes 131088 | tf_op jit(solution)/shard_map/psum | solution.py:47
  846.7 0.8 broadcast_multiply_fusion
  847.6 0.9 fusion.41
  848.5 11.7 %cholesky.16 = f32[128,128]{1,0:T(8,128)S(1)} custom-call(f32[128,128]{1,0:T(8,128)S(1)} %fusion.41), custom_call_target="Cholesky" | custom-call | tf_op jit(solution)/shard_map/jit(cholesky)/cholesky | solution.py:50
  861.6 9.8 %custom-call.10 = f32[1,128,128]{1,2,0:T(8,128)S(1)} custom-call(f32[1,128,128]{2,1,0:T(8,128)S(1)} %fusion.34), custom_call_target="InvertDiagBlocksLowerTriangular" | custom-call | tf_op jit(solution)/shard_map/triangular_solve | solution.py:51
  871.4 1.0 fusion.39
  872.4 1.1 fusion.37
  873.5 0.8 fusion.35
  (52 shorter events, 7.7 us)
Async XLA Ops:
  8.0 1.8 copy-start
  8.0 129.3 %all-reduce.8.cloned.1.call-start = ((), (), s32[]{:S(2)}) async-start(), calls=%async_computation.6 | async-start | bytes 131072 | tf_op jit(solution)/shard_map/psum | solution.py:30
  10.6 127.7 %reduce-scatter.6.cloned.1.call-start = ((), (), s32[]{:S(2)}) async-start(), calls=%async_computation.5 | async-start | bytes 1179648 | tf_op jit(solution)/shard_map/reduce_scatter | solution.py:29
  31.7 9.6 %copy-start.3 = (f32[2]{0:T(128)S(1)}, f32[2]{0:T(128)}, u32[]{:S(2)}) copy-start(f32[2]{0:T(128)} %param.13) | copy-start | bytes 28
  31.7 105.6 %copy-start.1 = (f32[128]{0:T(128)S(1)}, f32[128]{0:T(128)}, u32[]{:S(2)}) copy-start(f32[128]{0:T(128)} %param.12) | copy-start | bytes 1540
  31.7 106.6 %copy-start.2 = (f32[256]{0:T(256)S(1)}, f32[256]{0:T(256)}, u32[]{:S(2)}) copy-start(f32[256]{0:T(256)} %param.9) | copy-start | bytes 3076
  41.2 238.0 %all-reduce.10.cloned.1.call-start = ((), (), s32[]{:S(2)}) async-start(), calls=%async_computation.8 | async-start | bytes 131072 | tf_op jit(solution)/shard_map/psum | solution.py:30
  160.3 120.0 %reduce-scatter.8.cloned.1.call-start = ((), (), s32[]{:S(2)}) async-start(), calls=%async_computation.7 | async-start | bytes 1179648 | tf_op jit(solution)/shard_map/reduce_scatter | solution.py:29
  169.8 251.4 %all-reduce.12.cloned.1.call-start = ((), (), s32[]{:S(2)}) async-start(), calls=%async_computation.10 | async-start | bytes 131072 | tf_op jit(solution)/shard_map/psum | solution.py:30
  302.3 120.0 %reduce-scatter.10.cloned.1.call-start = ((), (), s32[]{:S(2)}) async-start(), calls=%async_computation.9 | async-start | bytes 1179648 | tf_op jit(solution)/shard_map/reduce_scatter | solution.py:29
  311.8 251.4 %all-reduce.14.cloned.1.call-start = ((), (), s32[]{:S(2)}) async-start(), calls=%async_computation.12 | async-start | bytes 131072 | tf_op jit(solution)/shard_map/psum | solution.py:30
  444.2 120.0 %reduce-scatter.12.cloned.1.call-start = ((), (), s32[]{:S(2)}) async-start(), calls=%async_computation.11 | async-start | bytes 1179648 | tf_op jit(solution)/shard_map/reduce_scatter | solution.py:29
  453.7 260.7 %all-reduce.16.cloned.1.call-start = ((), (), s32[]{:S(2)}) async-start(), calls=%async_computation.14 | async-start | bytes 131072 | tf_op jit(solution)/shard_map/psum | solution.py:30
  595.5 120.0 %reduce-scatter.14.cloned.1.call-start = ((), (), s32[]{:S(2)}) async-start(), calls=%async_computation.13 | async-start | bytes 1179648 | tf_op jit(solution)/shard_map/reduce_scatter | solution.py:29
  605.0 241.7 %all-reduce.18.cloned.1.call-start = ((), (), s32[]{:S(2)}) async-start(), calls=%async_computation.15 | async-start | bytes 262144 | tf_op jit(solution)/shard_map/psum | solution.py:47
Sparse Core Ops, SparseCore 0:
  15.0 122.2 all-reduce.7
  160.4 118.7 all-reduce.9
  302.4 118.7 all-reduce.11
  444.3 118.7 all-reduce.13
  595.6 118.8 all-reduce.15
  720.6 126.0 all-reduce.17
Sparse Core Ops, SparseCore 1:
  41.3 32.8 reduce-scatter.5
  169.9 31.7 reduce-scatter.7
  311.9 31.8 reduce-scatter.9
  453.8 31.7 reduce-scatter.11
  605.1 31.7 reduce-scatter.13
where the time goes:
time: 887 us; the launch traced here: 882 us
  waiting for transfers between devices  659 us (74%)
  blocking collectives  65.9 us (7%)
  matrix products  60.1 us (7%)
  local copies, waits for them, and re-layouts  52 us (6%)
  other arithmetic  26 us (3%)
  between operations  18.7 us (2%)
    psum x5, waiting for transfers between devices, operate(): lax.psum(jnp.dot(planted.T, scaled, preferred_element_type=jnp.float32),...  529 us
    psum x1, waiting for transfers between devices, local(): lax.psum((local_gram, local_rayleigh), ('row', 'col'))  129 us
    all_gather x5, blocking collectives, operate(): gathered = lax.all_gather(scaled, 'row', axis=0, tiled=True)  65.9 us
    gather x5, local copies, waits for them, and re-layouts, operate(): picked = blocks[tile_cols]  42.9 us
    dot_general x5, matrix products, operate(): jnp.einsum('rsab,rsbk->rak', tiles, picked, preferred_element_type=jnp.fl...  40.7 us
  transfers between devices with their start and end apart: 11, of which 6 were waited for; matrix products, arithmetic and copies ran while one was open for 7% of the time, Pallas kernels for 0%

commit v1 on v0

--- a/solution.py
+++ b/solution.py
@@ -6,31 +6,43 @@
 DEGREE = 4
 
 
-def planted_product(planted_part, coupling):
-    upper_part = coupling.astype(jnp.bfloat16)
-    lower_part = (coupling - upper_part.astype(jnp.float32)).astype(jnp.bfloat16)
-    first = jnp.dot(planted_part, upper_part, preferred_element_type=jnp.float32)
-    return first + jnp.dot(planted_part, lower_part, preferred_element_type=jnp.float32)
+def split_bf16(value):
+    upper = value.astype(jnp.bfloat16)
+    lower = (value - upper.astype(jnp.float32)).astype(jnp.bfloat16)
+    return upper, lower
+
+
+def split_dot(left, right_f32):
+    upper, lower = split_bf16(right_f32)
+    first = jnp.dot(left, upper, preferred_element_type=jnp.float32)
+    return first + jnp.dot(left, lower, preferred_element_type=jnp.float32)
 
 
 def local(tiles, tile_cols, degree_scale, start_block, planted, strengths, bounds):
     piece_rows = start_block.shape[0]
     node_count = piece_rows * lax.axis_size("row") * lax.axis_size("col")
-    tile_size = tiles.shape[2]
+    tile_rows, slots, tile_size = tiles.shape[0], tiles.shape[1], tiles.shape[2]
+    n_blocks = lax.axis_size("row") * piece_rows // tile_size
     weights = strengths[:, None]
+
+    onehot = (tile_cols[:, :, None] == jnp.arange(n_blocks, dtype=jnp.int32)[None, None, :]).astype(jnp.bfloat16)
+    dense = jnp.einsum("rst,rsab->ratb", onehot, tiles, preferred_element_type=jnp.float32)
+    dense = dense.reshape(tile_rows * tile_size, n_blocks * tile_size)
+    w_hi, w_lo = split_bf16(dense)
+
+    planted_cols = lax.all_gather(planted, "row", axis=0, tiled=True)
+    planted_rows = lax.all_gather(planted, "col", axis=0, tiled=True)
 
     def operate(vector):
         scaled = (degree_scale[:, None] * vector).astype(jnp.bfloat16)
         gathered = lax.all_gather(scaled, "row", axis=0, tiled=True)
-        blocks = gathered.reshape(-1, tile_size, gathered.shape[1])
-        picked = blocks[tile_cols]
-        result = jnp.einsum("rsab,rsbk->rak", tiles, picked, preferred_element_type=jnp.float32)
-        result = result.reshape(piece_rows * lax.axis_size("col"), result.shape[2])
-        summed = lax.psum_scatter(result, "col", scatter_dimension=0, tiled=True)
-        coupling = lax.psum(
-            jnp.dot(planted.T, scaled, preferred_element_type=jnp.float32), ("row", "col")
+        product = jnp.dot(w_hi, gathered, preferred_element_type=jnp.float32)
+        product = product + jnp.dot(w_lo, gathered, preferred_element_type=jnp.float32)
+        partial = lax.dot_general(
+            planted_cols, gathered, (((0,), (0,)), ((), ())), preferred_element_type=jnp.float32
         )
-        summed = summed + planted_product(planted, weights * coupling) / node_count
+        product = product + split_dot(planted_rows, weights * partial) / node_count
+        summed = lax.psum_scatter(product, "col", scatter_dimension=0, tiled=True)
         return degree_scale[:, None] * summed
 
     center = (bounds[1] + bounds[0]) * 0.5

time: 887 us -> 444 us (0.50)
  waiting for transfers between devices: 659 us -> 276 us
  local copies, waits for them, and re-layouts: 52 us -> 0.72 us
  matrix products: 60.1 us -> 45.2 us
    psum x5 -> x0, waiting for transfers between devices: 529 us -> none  [operate(): lax.psum(jnp.dot(planted.T, scaled, preferred_element_type=jnp.float32),...]
    reduce_scatter x5, waiting for transfers between devices: 0.13 us -> 148 us  [operate(): summed = lax.psum_scatter(product, 'col', scatter_dimension=0, tiled=True)]
    gather x5 -> x0, local copies, waits for them, and re-layouts: 42.9 us -> none  [operate(): picked = blocks[tile_cols]]
    all_gather x0 -> x2, blocking collectives: none -> 26 us  [the longest x1 16.7 us: local(): planted_rows = lax.all_gather(planted, 'col', axis=0, tiled=True)]
    all_gather x5, blocking collectives: 65.9 us -> 45.9 us  [operate(): gathered = lax.all_gather(scaled, 'row', axis=0, tiled=True)]
    dot_general x20 -> x26, matrix products: 55.2 us -> 39.3 us  [the longest x5 15.1 us: operate(): product = jnp.dot(w_hi, gathered, preferred_element_type=jnp.float32)]
  transfers between devices with their start and end apart: 11 -> 6, of which waited for: 6 -> 6; matrix products, arithmetic and copies ran while one was open for 7% -> 0% of each run, Pallas kernels for 0% -> 0%
where the time goes in v1:
time: 444 us; the launch traced here: 443 us
  waiting for transfers between devices  276 us (62%)
  blocking collectives  71.9 us (16%)
  matrix products  45.2 us (10%)
  other arithmetic  32.4 us (7%)
  between operations  17 us (4%)
    reduce_scatter x5, waiting for transfers between devices, operate(): summed = lax.psum_scatter(product, 'col', scatter_dimension=0, tiled=True)  148 us
    psum x1, waiting for transfers between devices, local(): lax.psum((local_gram, local_rayleigh), ('row', 'col'))  127 us
    all_gather x5, blocking collectives, operate(): gathered = lax.all_gather(scaled, 'row', axis=0, tiled=True)  45.9 us
    all_gather x1, blocking collectives, local(): planted_rows = lax.all_gather(planted, 'col', axis=0, tiled=True)  16.7 us
    dot_general x5, matrix products, operate(): product = jnp.dot(w_hi, gathered, preferred_element_type=jnp.float32)  15.1 us
    another operation x3, other arithmetic, local(): factor = jnp.linalg.cholesky(gram_matrix)  12.4 us
    another operation x2, other arithmetic, local(): lax.linalg.triangular_solve(factor, current, left_side=False, lower=True,...  10.5 us
    all_gather x1, blocking collectives, local(): planted_cols = lax.all_gather(planted, 'row', axis=0, tiled=True)  9.27 us
  transfers between devices with their start and end apart: 6, of which 6 were waited for; matrix products, arithmetic and copies ran while one was open for 0% of the time, Pallas kernels for 0%

profile of v1, /device:TPU:0, one launch (start us, length us, event | category | flops | bytes accessed | tf_op | source)
XLA Modules:
  0.0 443.1 jit_solution(17409846238595120193)
XLA Ops:
  7.2 16.7 %all_gather.23 = bf16[2048,128]{1,0:T(8,128)(2,1)S(1)} all-gather(bf16[256,128]{1,0:T(8,128)(2,1)} %param.11), channel_id=1, replica_groups=mesh['row'=4,'col'=8] {'col'}, dimensions={0}, use_global_device_ids=true | all-gather | bytes 589824 | tf_op jit(solution)/shard_map/all_gather | solution.py:34
  23.9 9.3 %all_gather.22 = bf16[1024,128]{1,0:T(8,128)(2,1)S(1)} all-gather(bf16[256,128]{1,0:T(8,128)(2,1)} %param.11), channel_id=1, replica_groups=mesh['row'=4,'col'=8] {'row'}, dimensions={0}, use_global_device_ids=true | all-gather | bytes 327680 | tf_op jit(solution)/shard_map/all_gather | solution.py:33
  33.2 8.2 %fusion.1 = f32[16,8,128,128]{3,1,2,0:T(8,128)S(1)} fusion(bf16[16,16,128,128]{3,2,1,0:T(8,128)(2,1)} %param.7, s32[16,16]{1,0:T(8,128)} %param.8), kind=kOutput, calls=%fused_computation.3 | convolution fusion | flops 67110912 | bytes 16778240 | tf_op jit(solution)/shard_map/rst,rsab->ratb/dot_general | solution.py:29
  41.4 3.1 fusion
  44.7 9.0 %all_gather.21 = bf16[1024,128]{1,0:T(8,128)(2,1)S(1)} all-gather(bf16[256,128]{1,0:T(8,128)(2,1)S(1)} %multiply_convert_fusion.4), channel_id=1, replica_groups=mesh['row'=4,'col'=8] {'row'}, dimensions={0}, use_global_device_ids=true | all-gather | bytes 327680 | tf_op jit(solution)/shard_map/all_gather | solution.py:38
  53.7 1.2 fusion.56
  55.0 1.3 convolution_add_fusion.9
  56.9 1.4 fusion.17
  58.3 0.6 fusion.55
  61.5 29.6 %reduce-scatter.6.cloned.1.call-done = f32[256,128]{1,0:T(8,128)} async-done(((f32[2048,128]{1,0:T(8,128)}), f32[256,128]{1,0:T(8,128)}) %reduce-scatter.6.cloned.1.call-update) | async-done | bytes 131088 | tf_op jit(solution)/shard_map/reduce_scatter | solution.py:45
  91.1 1.2 multiply_convert_fusion.3
  92.3 9.3 %all_gather.24 = bf16[1024,128]{1,0:T(8,128)(2,1)S(1)} all-gather(bf16[256,128]{1,0:T(8,128)(2,1)S(1)} %get-tuple-element.8), channel_id=1, replica_groups=mesh['row'=4,'col'=8] {'row'}, dimensions={0}, use_global_device_ids=true | all-gather | bytes 327680 | tf_op jit(solution)/shard_map/all_gather | solution.py:38
  101.6 3.5 fusion.57
  105.3 1.3 convolution_add_fusion.7
  106.9 1.4 fusion.14
  108.3 29.9 %reduce-scatter.8.cloned.1.call-done = f32[256,128]{1,0:T(8,128)} async-done(((f32[2048,128]{1,0:T(8,128)}), f32[256,128]{1,0:T(8,128)}) %reduce-scatter.8.cloned.1.call-update) | async-done | bytes 131088 | tf_op jit(solution)/shard_map/reduce_scatter | solution.py:45
  138.2 1.2 multiply_convert_fusion.2
  139.4 9.2 %all_gather.25 = bf16[1024,128]{1,0:T(8,128)(2,1)S(1)} all-gather(bf16[256,128]{1,0:T(8,128)(2,1)S(1)} %get-tuple-element.6), channel_id=1, replica_groups=mesh['row'=4,'col'=8] {'row'}, dimensions={0}, use_global_device_ids=true | all-gather | bytes 327680 | tf_op jit(solution)/shard_map/all_gather | solution.py:38
  148.6 3.5 fusion.58
  152.3 1.3 convolution_add_fusion.5
  153.9 1.4 fusion.11
  155.4 30.0 %reduce-scatter.10.cloned.1.call-done = f32[256,128]{1,0:T(8,128)} async-done(((f32[2048,128]{1,0:T(8,128)}), f32[256,128]{1,0:T(8,128)}) %reduce-scatter.10.cloned.1.call-update) | async-done | bytes 131088 | tf_op jit(solution)/shard_map/reduce_scatter | solution.py:45
  185.3 1.2 multiply_convert_fusion.1
  186.5 9.1 %all_gather.26 = bf16[1024,128]{1,0:T(8,128)(2,1)S(1)} all-gather(bf16[256,128]{1,0:T(8,128)(2,1)S(1)} %multiply_convert_fusion.1), channel_id=1, replica_groups=mesh['row'=4,'col'=8] {'row'}, dimensions={0}, use_global_device_ids=true | all-gather | bytes 327680 | tf_op jit(solution)/shard_map/all_gather | solution.py:38
  195.6 3.5 fusion.59
  199.3 1.3 convolution_add_fusion.3
  200.6 0.3 fusion.43
  200.9 1.4 fusion.8
  202.4 29.9 %reduce-scatter.12.cloned.1.call-done = f32[256,128]{1,0:T(8,128)} async-done(((f32[2048,128]{1,0:T(8,128)}), f32[256,128]{1,0:T(8,128)}) %reduce-scatter.12.cloned.1.call-update) | async-done | bytes 131088 | tf_op jit(solution)/shard_map/reduce_scatter | solution.py:45
  232.3 1.2 multiply_convert_fusion
  233.5 9.3 %all_gather.27 = bf16[1024,128]{1,0:T(8,128)(2,1)S(1)} all-gather(bf16[256,128]{1,0:T(8,128)(2,1)S(1)} %get-tuple-element.4), channel_id=1, replica_groups=mesh['row'=4,'col'=8] {'row'}, dimensions={0}, use_global_device_ids=true | all-gather | bytes 327680 | tf_op jit(solution)/shard_map/all_gather | solution.py:38
  242.8 3.5 fusion.61
  246.6 1.3 convolution_add_fusion.1
  247.8 0.3 fusion.40
  248.1 1.3 fusion.5
  249.5 1.0 fusion.60
  250.5 29.0 %reduce-scatter.14.cloned.1.call-done = f32[256,128]{1,0:T(8,128)} async-done(((f32[2048,128]{1,0:T(8,128)}), f32[256,128]{1,0:T(8,128)}) %reduce-scatter.14.cloned.1.call-update) | async-done | bytes 131088 | tf_op jit(solution)/shard_map/reduce_scatter | solution.py:45
  279.5 2.0 fusion.23
  281.5 127.2 %all-reduce.3.cloned.1.call-done = (f32[128,128]{0,1:T(8,128)}, f32[128,128]{0,1:T(8,128)}) async-done(((f32[128,128]{0,1:T(8,128)}, f32[128,128]{0,1:T(8,128)}), (f32[128,128]{0,1:T(8,128)}, f32[128,128]{0,1:T(8,128)})) %all-reduce.3.cloned.1.call-update) | async-done | bytes 131088 | tf_op jit(solution)/shard_map/psum | solution.py:59
  408.7 0.8 broadcast_multiply_fusion
  409.6 0.9 fusion.32
  410.5 11.7 %cholesky.16 = f32[128,128]{1,0:T(8,128)S(1)} custom-call(f32[128,128]{1,0:T(8,128)S(1)} %fusion.32), custom_call_target="Cholesky" | custom-call | tf_op jit(solution)/shard_map/jit(cholesky)/cholesky | solution.py:62
  422.2 0.6 compare_reduce_fusion
  422.9 0.7 fusion.25
  423.5 9.8 %custom-call.10 = f32[1,128,128]{1,2,0:T(8,128)S(1)} custom-call(f32[1,128,128]{2,1,0:T(8,128)S(1)} %fusion.25), custom_call_target="InvertDiagBlocksLowerTriangular" | custom-call | tf_op jit(solution)/shard_map/triangular_solve | solution.py:63
  433.3 0.9 fusion.30
  434.3 1.1 fusion.28
  435.4 0.8 fusion.26
  (45 shorter events, 2.9 us)
Async XLA Ops:
  7.2 83.9 %reduce-scatter.6.cloned.1.call-start = ((), (), s32[]{:S(2)}) async-start(), calls=%async_computation.5 | async-start | bytes 1179648 | tf_op jit(solution)/shard_map/reduce_scatter | solution.py:45
  41.4 3.1 copy-start.6
  41.4 3.2 copy-start.8
  44.6 11.7 %copy-start = (bf16[2048,1024]{1,0:T(8,128)(2,1)}, bf16[2048,1024]{1,0:T(8,128)(2,1)S(1)}, u32[]{:S(2)}) copy-start(bf16[2048,1024]{1,0:T(8,128)(2,1)S(1)} %get-tuple-element.10) | copy-start | bytes 12582916
  44.6 11.7 %copy-start.5 = (bf16[2048,1024]{1,0:T(8,128)(2,1)}, bf16[2048,1024]{1,0:T(8,128)(2,1)S(1)}, u32[]{:S(2)}) copy-start(bf16[2048,1024]{1,0:T(8,128)(2,1)S(1)} %get-tuple-element.11) | copy-start | bytes 12582916
  55.0 1.3 copy-start.9
  56.3 2.0 copy-start.10
  58.2 80.0 %reduce-scatter.8.cloned.1.call-start = ((), (), s32[]{:S(2)}) async-start(), calls=%async_computation.6 | async-start | bytes 1179648 | tf_op jit(solution)/shard_map/reduce_scatter | solution.py:45
  91.1 14.2 %copy-start.1 = (bf16[2048,1024]{1,0:T(8,128)(2,1)S(1)}, bf16[2048,1024]{1,0:T(8,128)(2,1)}, u32[]{:S(2)}) copy-start(bf16[2048,1024]{1,0:T(8,128)(2,1)} %copy-done) | copy-start | bytes 12582916
  108.3 77.0 %reduce-scatter.10.cloned.1.call-start = ((), (), s32[]{:S(2)}) async-start(), calls=%async_computation.7 | async-start | bytes 1179648 | tf_op jit(solution)/shard_map/reduce_scatter | solution.py:45
  138.2 14.1 %copy-start.2 = (bf16[2048,1024]{1,0:T(8,128)(2,1)S(1)}, bf16[2048,1024]{1,0:T(8,128)(2,1)}, u32[]{:S(2)}) copy-start(bf16[2048,1024]{1,0:T(8,128)(2,1)} %copy-done) | copy-start | bytes 12582916
  155.3 77.0 %reduce-scatter.12.cloned.1.call-start = ((), (), s32[]{:S(2)}) async-start(), calls=%async_computation.8 | async-start | bytes 1179648 | tf_op jit(solution)/shard_map/reduce_scatter | solution.py:45
  185.3 14.0 %copy-start.3 = (bf16[2048,1024]{1,0:T(8,128)(2,1)S(1)}, bf16[2048,1024]{1,0:T(8,128)(2,1)}, u32[]{:S(2)}) copy-start(bf16[2048,1024]{1,0:T(8,128)(2,1)} %copy-done) | copy-start | bytes 12582916
  200.6 31.7 %copy-start.7 = (f32[256,128]{1,0:T(8,128)S(1)}, f32[256,128]{1,0:T(8,128)}, u32[]{:S(2)}) copy-start(f32[256,128]{1,0:T(8,128)} %reduce-scatter.10.cloned.1.call-done) | copy-start | bytes 393220
  202.3 77.1 %reduce-scatter.14.cloned.1.call-start = ((), (), s32[]{:S(2)}) async-start(), calls=%async_computation.9 | async-start | bytes 1179648 | tf_op jit(solution)/shard_map/reduce_scatter | solution.py:45
  232.3 14.2 %copy-start.4 = (bf16[2048,1024]{1,0:T(8,128)(2,1)S(1)}, bf16[2048,1024]{1,0:T(8,128)(2,1)}, u32[]{:S(2)}) copy-start(bf16[2048,1024]{1,0:T(8,128)(2,1)} %copy-done) | copy-start | bytes 12582916
  249.5 159.2 %all-reduce.3.cloned.1.call-start = ((), (), s32[]{:S(2)}) async-start(), calls=%async_computation.10 | async-start | bytes 262144 | tf_op jit(solution)/shard_map/psum | solution.py:59
Sparse Core Ops, SparseCore 0:
  58.4 32.6 reduce-scatter.5
  108.4 29.7 reduce-scatter.7
  155.4 29.8 reduce-scatter.9
  202.5 29.8 reduce-scatter.11
  249.6 29.8 reduce-scatter.13
  285.6 122.9 all-reduce.2

commit v2 on v1

--- a/solution.py
+++ b/solution.py
@@ -16,6 +16,34 @@
     upper, lower = split_bf16(right_f32)
     first = jnp.dot(left, upper, preferred_element_type=jnp.float32)
     return first + jnp.dot(left, lower, preferred_element_type=jnp.float32)
+
+
+def butterfly_sum(value, axis):
+    size = lax.axis_size(axis)
+    if size & (size - 1):
+        return lax.psum(value, axis)
+    step = 1
+    while step < size:
+        pairs = [(index, index ^ step) for index in range(size)]
+        value = value + lax.ppermute(value, axis, pairs)
+        step *= 2
+    return value
+
+
+def all_sum(value):
+    return butterfly_sum(butterfly_sum(value, "col"), "row")
+
+
+def scatter_sum(value, axis):
+    size = lax.axis_size(axis)
+    here = lax.axis_index(axis)
+    blocks = value.reshape(size, value.shape[0] // size, value.shape[1])
+    total = jnp.take(blocks, here, axis=0)
+    for shift in range(1, size):
+        part = jnp.take(blocks, (here + shift) % size, axis=0)
+        pairs = [(index, (index + shift) % size) for index in range(size)]
+        total = total + lax.ppermute(part, axis, pairs)
+    return total
 
 
 def local(tiles, tile_cols, degree_scale, start_block, planted, strengths, bounds):
@@ -42,7 +70,7 @@
             planted_cols, gathered, (((0,), (0,)), ((), ())), preferred_element_type=jnp.float32
         )
         product = product + split_dot(planted_rows, weights * partial) / node_count
-        summed = lax.psum_scatter(product, "col", scatter_dimension=0, tiled=True)
+        summed = scatter_sum(product, "col")
         return degree_scale[:, None] * summed
 
     center = (bounds[1] + bounds[0]) * 0.5
@@ -54,9 +82,10 @@
         following = 2.0 * (applied - center * current) / half_width - previous
         previous, current = (current, following)
     local_gram = jnp.dot(current.T, current, precision=lax.Precision.HIGHEST)
+    gram_total = all_sum(local_gram)
     applied = operate(current)
     local_rayleigh = jnp.dot(current.T, applied, precision=lax.Precision.HIGHEST)
-    gram_total, rayleigh_total = lax.psum((local_gram, local_rayleigh), ("row", "col"))
+    rayleigh_total = all_sum(local_rayleigh)
     gram_matrix = gram_total / node_count
     rayleigh = rayleigh_total / node_count
     factor = jnp.linalg.cholesky(gram_matrix)

time: 444 us -> 272 us (0.61)
  waiting for transfers between devices: 276 us -> 100 us
  starting transfers between devices: 0.25 us -> 39.6 us
  matrix products: 45.2 us -> 30.5 us
  between operations: 17 us -> 3.89 us
  other arithmetic: 32.4 us -> 27 us
    reduce_scatter x5 -> x0, waiting for transfers between devices: 148 us -> none  [operate(): summed = lax.psum_scatter(product, 'col', scatter_dimension=0, tiled=True)]
    psum x1 -> x0, waiting for transfers between devices: 127 us -> none  [local(): lax.psum((local_gram, local_rayleigh), ('row', 'col'))]
    ppermute x0 -> x45, waiting for transfers between devices: none -> 100 us  [the longest x35 85.3 us: scatter_sum(): total = total + lax.ppermute(part, axis, pairs)]
    ppermute x0 -> x45, starting transfers between devices: none -> 39.6 us  [the longest x35 31.4 us: scatter_sum(): total = total + lax.ppermute(part, axis, pairs)]
    dot_general x5, matrix products: 15.1 us -> 8.5 us  [operate(): product = jnp.dot(w_hi, gathered, preferred_element_type=jnp.float32)]
    dot_general x5, matrix products: 6.84 us -> 1.71 us  [split_dot(): return first + jnp.dot(left, lower, preferred_element_type=jnp.float32)]
  transfers between devices with their start and end apart: 6 -> 45, of which waited for: 6 -> 21; matrix products, arithmetic and copies ran while one was open for 0% -> 10% of each run, Pallas kernels for 0% -> 0%
where the time goes in v2:
time: 272 us
  waiting for transfers between devices  100 us (37%)
  blocking collectives  69.6 us (26%)
  starting transfers between devices  39.6 us (15%)
  matrix products  30.5 us (11%)
  other arithmetic  27 us (10%)
  between operations  3.89 us (1%)
    ppermute x35, waiting for transfers between devices, scatter_sum(): total = total + lax.ppermute(part, axis, pairs)  85.3 us
    all_gather x5, blocking collectives, operate(): gathered = lax.all_gather(scaled, 'row', axis=0, tiled=True)  43.6 us
    ppermute x35, starting transfers between devices, scatter_sum(): total = total + lax.ppermute(part, axis, pairs)  31.4 us
    all_gather x1, blocking collectives, local(): planted_rows = lax.all_gather(planted, 'col', axis=0, tiled=True)  16.7 us
    ppermute x10, waiting for transfers between devices, butterfly_sum(): value = value + lax.ppermute(value, axis, pairs)  14.9 us
    another operation x3, other arithmetic, local(): factor = jnp.linalg.cholesky(gram_matrix)  12.4 us
    another operation x2, other arithmetic, local(): lax.linalg.triangular_solve(factor, current, left_side=False, lower=True,...  10.5 us
    all_gather x1, blocking collectives, local(): planted_cols = lax.all_gather(planted, 'row', axis=0, tiled=True)  9.27 us
  transfers between devices with their start and end apart: 45, of which 21 were waited for; matrix products, arithmetic and copies ran while one was open for 10% of the time, Pallas kernels for 0%

profile of v2, /device:TPU:0, one launch (start us, length us, event | category | flops | bytes accessed | tf_op | source)
XLA Modules:
  0.0 271.5 jit_solution(16796740497332533125)
XLA Ops:
  0.6 16.7 %all_gather.23 = bf16[2048,128]{1,0:T(8,128)(2,1)S(1)} all-gather(bf16[256,128]{1,0:T(8,128)(2,1)} %param.13), channel_id=1, replica_groups=mesh['row'=4,'col'=8] {'col'}, dimensions={0}, use_global_device_ids=true | all-gather | bytes 589824 | tf_op jit(solution)/shard_map/all_gather | solution.py:62
  17.3 9.3 %all_gather.22 = bf16[1024,128]{1,0:T(8,128)(2,1)S(1)} all-gather(bf16[256,128]{1,0:T(8,128)(2,1)} %param.13), channel_id=1, replica_groups=mesh['row'=4,'col'=8] {'row'}, dimensions={0}, use_global_device_ids=true | all-gather | bytes 327680 | tf_op jit(solution)/shard_map/all_gather | solution.py:61
  26.6 8.2 %fusion.1 = f32[16,8,128,128]{3,1,2,0:T(8,128)S(1)} fusion(bf16[16,16,128,128]{3,2,1,0:T(8,128)(2,1)} %param.9, s32[16,16]{1,0:T(8,128)} %param.10), kind=kOutput, calls=%fused_computation.3 | convolution fusion | flops 67110912 | bytes 16778240 | tf_op jit(solution)/shard_map/rst,rsab->ratb/dot_general | solution.py:57
  34.8 3.1 %fusion = (bf16[2048,1024]{1,0:T(8,128)(2,1)S(1)}, bf16[2048,1024]{1,0:T(8,128)(2,1)S(1)}) fusion(f32[256,8,8,128]{3,2,1,0:T(8,128)S(1)} %bitcast.292), kind=kLoop, calls=%fused_computation.2 | loop fusion | flops 6291456 | bytes 16777216 | tf_op jit(solution)/shard_map/convert_element_type | solution.py:11
  38.1 9.0 %all_gather.21 = bf16[1024,128]{1,0:T(8,128)(2,1)S(1)} all-gather(bf16[256,128]{1,0:T(8,128)(2,1)S(1)} %multiply_convert_fusion.4), channel_id=1, replica_groups=mesh['row'=4,'col'=8] {'row'}, dimensions={0}, use_global_device_ids=true | all-gather | bytes 327680 | tf_op jit(solution)/shard_map/all_gather | solution.py:66
  47.1 1.3 fusion.116
  48.4 1.3 convolution_add_fusion.9
  50.9 3.5 %collective-permute-start.5 = (f32[256,128]{1,0:T(8,128)S(1)}, f32[256,128]{1,0:T(8,128)S(1)}, u32[]{:S(2)}, u32[]{:S(2)}) collective-permute-start(f32[256,128]{1,0:T(8,128)S(1)} %get-tuple-element.54), channel_id=1, source_target_pairs={{0,6},{1,7},{2,0},{3,1},{4,2},{5,3},{6,4},{7,5},{8,14},{9,15},{10,... | collective-permute-start | bytes 393224 | tf_op jit(solution)/shard_map/ppermute | solution.py:45
  54.4 2.7 collective-permute-start.3
  57.4 2.0 collective-permute-done.5
  62.6 13.0 %collective-permute-done.3 = f32[256,128]{1,0:T(8,128)S(1)} collective-permute-done((f32[256,128]{1,0:T(8,128)S(1)}, f32[256,128]{1,0:T(8,128)S(1)}, u32[]{:S(2)}, u32[]{:S(2)}) %collective-permute-start.3) | collective-permute-done | bytes 131104 | tf_op jit(solution)/shard_map/ppermute | solution.py:45
  76.2 8.7 %all_gather.24 = bf16[1024,128]{1,0:T(8,128)(2,1)S(1)} all-gather(bf16[256,128]{1,0:T(8,128)(2,1)S(1)} %get-tuple-element.20), channel_id=1, replica_groups=mesh['row'=4,'col'=8] {'row'}, dimensions={0}, use_global_device_ids=true | all-gather | bytes 327680 | tf_op jit(solution)/shard_map/all_gather | solution.py:66
  84.9 3.5 %fusion.117 = f32[2048,128]{1,0:T(8,128)S(1)} fusion(bf16[2048,1024]{1,0:T(8,128)(2,1)} %copy-done.2, bf16[1024,128]{1,0:T(8,128)(2,1)S(1)} %all_gather.24), kind=kOutput, calls=%fused_computation.186 | convolution fusion | flops 536870912 | bytes 5505024 | tf_op jit(solution)/shard_map/dot_general | solution.py:67
  88.7 1.3 convolution_add_fusion.7
  90.8 3.0 %collective-permute-start.11 = (f32[256,128]{1,0:T(8,128)S(1)}, f32[256,128]{1,0:T(8,128)S(1)}, u32[]{:S(2)}, u32[]{:S(2)}) collective-permute-start(f32[256,128]{1,0:T(8,128)S(1)} %get-tuple-element.48), channel_id=1, source_target_pairs={{0,5},{1,6},{2,7},{3,0},{4,1},{5,2},{6,3},{7,4},{8,13},{9,14},{10,... | collective-permute-start | bytes 393224 | tf_op jit(solution)/shard_map/ppermute | solution.py:45
  93.9 1.4 collective-permute-start.9
  95.3 2.9 %collective-permute-start.8 = (f32[256,128]{1,0:T(8,128)S(1)}, f32[256,128]{1,0:T(8,128)S(1)}, u32[]{:S(2)}, u32[]{:S(2)}) collective-permute-start(f32[256,128]{1,0:T(8,128)S(1)} %get-tuple-element.51), channel_id=1, source_target_pairs={{0,2},{1,3},{2,4},{3,5},{4,6},{5,7},{6,0},{7,1},{8,10},{9,11},{10,... | collective-permute-start | bytes 393224 | tf_op jit(solution)/shard_map/ppermute | solution.py:45
  98.8 18.7 %collective-permute-done.10 = f32[256,128]{1,0:T(8,128)S(1)} collective-permute-done((f32[256,128]{1,0:T(8,128)S(1)}, f32[256,128]{1,0:T(8,128)S(1)}, u32[]{:S(2)}, u32[]{:S(2)}) %collective-permute-start.10) | collective-permute-done | bytes 131104 | tf_op jit(solution)/shard_map/ppermute | solution.py:45
  117.7 8.8 %all_gather.25 = bf16[1024,128]{1,0:T(8,128)(2,1)S(1)} all-gather(bf16[256,128]{1,0:T(8,128)(2,1)S(1)} %get-tuple-element.18), channel_id=1, replica_groups=mesh['row'=4,'col'=8] {'row'}, dimensions={0}, use_global_device_ids=true | all-gather | bytes 327680 | tf_op jit(solution)/shard_map/all_gather | solution.py:66
  126.4 1.3 fusion.118
  128.0 1.3 convolution_add_fusion.5
  130.9 2.2 collective-permute-start.17
  134.8 2.0 collective-permute-done.19
  136.8 2.8 %collective-permute-done.18 = f32[256,128]{1,0:T(8,128)S(1)} collective-permute-done((f32[256,128]{1,0:T(8,128)S(1)}, f32[256,128]{1,0:T(8,128)S(1)}, u32[]{:S(2)}, u32[]{:S(2)}) %collective-permute-start.18) | collective-permute-done | bytes 131104 | tf_op jit(solution)/shard_map/ppermute | solution.py:45
  139.6 13.8 %collective-permute-done.17 = f32[256,128]{1,0:T(8,128)S(1)} collective-permute-done((f32[256,128]{1,0:T(8,128)S(1)}, f32[256,128]{1,0:T(8,128)S(1)}, u32[]{:S(2)}, u32[]{:S(2)}) %collective-permute-start.17) | collective-permute-done | bytes 131104 | tf_op jit(solution)/shard_map/ppermute | solution.py:45
  154.1 8.2 %all_gather.26 = bf16[1024,128]{1,0:T(8,128)(2,1)S(1)} all-gather(bf16[256,128]{1,0:T(8,128)(2,1)S(1)} %get-tuple-element.16), channel_id=1, replica_groups=mesh['row'=4,'col'=8] {'row'}, dimensions={0}, use_global_device_ids=true | all-gather | bytes 327680 | tf_op jit(solution)/shard_map/all_gather | solution.py:66
  162.3 1.3 fusion.119
  163.9 1.3 convolution_add_fusion.3
  166.0 2.9 %collective-permute-start.25 = (f32[256,128]{1,0:T(8,128)S(1)}, f32[256,128]{1,0:T(8,128)S(1)}, u32[]{:S(2)}, u32[]{:S(2)}) collective-permute-start(f32[256,128]{1,0:T(8,128)S(1)} %get-tuple-element.34), channel_id=1, source_target_pairs={{0,5},{1,6},{2,7},{3,0},{4,1},{5,2},{6,3},{7,4},{8,13},{9,14},{10,... | collective-permute-start | bytes 393224 | tf_op jit(solution)/shard_map/ppermute | solution.py:45
  169.0 1.4 collective-permute-start.23
  170.4 2.9 %collective-permute-start.22 = (f32[256,128]{1,0:T(8,128)S(1)}, f32[256,128]{1,0:T(8,128)S(1)}, u32[]{:S(2)}, u32[]{:S(2)}) collective-permute-start(f32[256,128]{1,0:T(8,128)S(1)} %get-tuple-element.37), channel_id=1, source_target_pairs={{0,2},{1,3},{2,4},{3,5},{4,6},{5,7},{6,0},{7,1},{8,10},{9,11},{10,... | collective-permute-start | bytes 393224 | tf_op jit(solution)/shard_map/ppermute | solution.py:45
  174.1 18.5 %collective-permute-done.24 = f32[256,128]{1,0:T(8,128)S(1)} collective-permute-done((f32[256,128]{1,0:T(8,128)S(1)}, f32[256,128]{1,0:T(8,128)S(1)}, u32[]{:S(2)}, u32[]{:S(2)}) %collective-permute-start.24) | collective-permute-done | bytes 131104 | tf_op jit(solution)/shard_map/ppermute | solution.py:45
  192.7 9.0 %all_gather.27 = bf16[1024,128]{1,0:T(8,128)(2,1)S(1)} all-gather(bf16[256,128]{1,0:T(8,128)(2,1)S(1)} %get-tuple-element.14), channel_id=1, replica_groups=mesh['row'=4,'col'=8] {'row'}, dimensions={0}, use_global_device_ids=true | all-gather | bytes 327680 | tf_op jit(solution)/shard_map/all_gather | solution.py:66
  201.7 1.3 fusion.121
  203.7 1.3 convolution_add_fusion.1
  205.8 1.8 collective-permute-start.38
  208.0 2.4 collective-permute-start.36
  210.4 7.6 %collective-permute-done.29 = f32[128,128]{0,1:T(8,128)S(1)} collective-permute-done((f32[128,128]{0,1:T(8,128)S(1)}, f32[128,128]{0,1:T(8,128)S(1)}, u32[]{:S(2)}, u32[]{:S(2)}) %collective-permute-start.29) | collective-permute-done | bytes 65568 | tf_op jit(solution)/shard_map/ppermute | solution.py:28
  219.3 1.9 collective-permute-start.30
  221.2 9.5 %collective-permute-done.36 = f32[256,128]{1,0:T(8,128)S(1)} collective-permute-done((f32[256,128]{1,0:T(8,128)S(1)}, f32[256,128]{1,0:T(8,128)S(1)}, u32[]{:S(2)}, u32[]{:S(2)}) %collective-permute-start.36) | collective-permute-done | bytes 131104 | tf_op jit(solution)/shard_map/ppermute | solution.py:45
  230.7 1.9 collective-permute-done.35
  234.6 3.2 %collective-permute-done.31 = f32[128,128]{0,1:T(8,128)S(1)} collective-permute-done((f32[128,128]{0,1:T(8,128)S(1)}, f32[128,128]{0,1:T(8,128)S(1)}, u32[]{:S(2)}, u32[]{:S(2)}) %collective-permute-start.31) | collective-permute-done | bytes 65568 | tf_op jit(solution)/shard_map/ppermute | solution.py:28
  238.8 1.9 collective-permute-start.42
  240.7 1.5 collective-permute-done.32
  242.3 11.7 %cholesky.16 = f32[128,128]{1,0:T(8,128)S(1)} custom-call(f32[128,128]{1,0:T(8,128)S(1)} %fusion.83), custom_call_target="Cholesky" | custom-call | tf_op jit(solution)/shard_map/jit(cholesky)/cholesky | solution.py:91
  256.2 9.8 %custom-call.10 = f32[1,128,128]{1,2,0:T(8,128)S(1)} custom-call(f32[1,128,128]{2,1,0:T(8,128)S(1)} %fusion.76), custom_call_target="InvertDiagBlocksLowerTriangular" | custom-call | tf_op jit(solution)/shard_map/triangular_solve | solution.py:92
  266.1 1.3 collective-permute-start.44
  268.2 2.2 collective-permute-done.44
  (124 shorter events, 21.7 us)
Async XLA Ops:
  38.0 11.8 %copy-start = (bf16[2048,1024]{1,0:T(8,128)(2,1)}, bf16[2048,1024]{1,0:T(8,128)(2,1)S(1)}, u32[]{:S(2)}) copy-start(bf16[2048,1024]{1,0:T(8,128)(2,1)S(1)} %get-tuple-element.22) | copy-start | bytes 12582916
  50.8 6.3 %collective-permute-start.6 = (f32[256,128]{1,0:T(8,128)S(1)}, f32[256,128]{1,0:T(8,128)S(1)}, u32[]{:S(2)}, u32[]{:S(2)}) collective-permute-start(f32[256,128]{1,0:T(8,128)S(1)} %get-tuple-element.53), channel_id=1, source_target_pairs={{0,7},{1,0},{2,1},{3,2},{4,3},{5,4},{6,5},{7,6},{8,15},{9,8},{10,9... | collective-permute-start | bytes 393224 | tf_op jit(solution)/shard_map/ppermute | solution.py:45
  50.9 8.5 %collective-permute-start.5 = (f32[256,128]{1,0:T(8,128)S(1)}, f32[256,128]{1,0:T(8,128)S(1)}, u32[]{:S(2)}, u32[]{:S(2)}) collective-permute-start(f32[256,128]{1,0:T(8,128)S(1)} %get-tuple-element.54), channel_id=1, source_target_pairs={{0,6},{1,7},{2,0},{3,1},{4,2},{5,3},{6,4},{7,5},{8,14},{9,15},{10,... | collective-permute-start | bytes 393224 | tf_op jit(solution)/shard_map/ppermute | solution.py:45
  54.4 8.1 %collective-permute-start.4 = (f32[256,128]{1,0:T(8,128)S(1)}, f32[256,128]{1,0:T(8,128)S(1)}, u32[]{:S(2)}, u32[]{:S(2)}) collective-permute-start(f32[256,128]{1,0:T(8,128)S(1)} %get-tuple-element.55), channel_id=1, source_target_pairs={{0,5},{1,6},{2,7},{3,0},{4,1},{5,2},{6,3},{7,4},{8,13},{9,14},{10,... | collective-permute-start | bytes 393224 | tf_op jit(solution)/shard_map/ppermute | solution.py:45
  54.4 21.1 %collective-permute-start.3 = (f32[256,128]{1,0:T(8,128)S(1)}, f32[256,128]{1,0:T(8,128)S(1)}, u32[]{:S(2)}, u32[]{:S(2)}) collective-permute-start(f32[256,128]{1,0:T(8,128)S(1)} %get-tuple-element.56), channel_id=1, source_target_pairs={{0,4},{1,5},{2,6},{3,7},{4,0},{5,1},{6,2},{7,3},{8,12},{9,13},{10,... | collective-permute-start | bytes 393224 | tf_op jit(solution)/shard_map/ppermute | solution.py:45
  57.1 19.0 %collective-permute-start.2 = (f32[256,128]{1,0:T(8,128)S(1)}, f32[256,128]{1,0:T(8,128)S(1)}, u32[]{:S(2)}, u32[]{:S(2)}) collective-permute-start(f32[256,128]{1,0:T(8,128)S(1)} %get-tuple-element.57), channel_id=1, source_target_pairs={{0,3},{1,4},{2,5},{3,6},{4,7},{5,0},{6,1},{7,2},{8,11},{9,12},{10,... | collective-permute-start | bytes 393224 | tf_op jit(solution)/shard_map/ppermute | solution.py:45
  57.1 19.0 %collective-permute-start.1 = (f32[256,128]{1,0:T(8,128)S(1)}, f32[256,128]{1,0:T(8,128)S(1)}, u32[]{:S(2)}, u32[]{:S(2)}) collective-permute-start(f32[256,128]{1,0:T(8,128)S(1)} %get-tuple-element.58), channel_id=1, source_target_pairs={{0,2},{1,3},{2,4},{3,5},{4,6},{5,7},{6,0},{7,1},{8,10},{9,11},{10,... | collective-permute-start | bytes 393224 | tf_op jit(solution)/shard_map/ppermute | solution.py:45
  59.4 16.7 %collective-permute-start = (f32[256,128]{1,0:T(8,128)S(1)}, f32[256,128]{1,0:T(8,128)S(1)}, u32[]{:S(2)}, u32[]{:S(2)}) collective-permute-start(f32[256,128]{1,0:T(8,128)S(1)} %get-tuple-element.52), channel_id=1, source_target_pairs={{0,1},{1,2},{2,3},{3,4},{4,5},{5,6},{6,7},{7,0},{8,9},{9,10},{10,1... | collective-permute-start | bytes 393224 | tf_op jit(solution)/shard_map/ppermute | solution.py:45
  76.2 12.4 %copy-start.1 = (bf16[2048,1024]{1,0:T(8,128)(2,1)S(1)}, bf16[2048,1024]{1,0:T(8,128)(2,1)}, u32[]{:S(2)}) copy-start(bf16[2048,1024]{1,0:T(8,128)(2,1)} %copy-done) | copy-start | bytes 12582916
  89.9 36.5 %copy-start.3 = (bf16[2048,1024]{1,0:T(8,128)(2,1)S(1)}, bf16[2048,1024]{1,0:T(8,128)(2,1)}, u32[]{:S(2)}) copy-start(bf16[2048,1024]{1,0:T(8,128)(2,1)} %copy-done.2) | copy-start | bytes 12582916
  90.7 4.6 %collective-permute-start.13 = (f32[256,128]{1,0:T(8,128)S(1)}, f32[256,128]{1,0:T(8,128)S(1)}, u32[]{:S(2)}, u32[]{:S(2)}) collective-permute-start(f32[256,128]{1,0:T(8,128)S(1)} %get-tuple-element.46), channel_id=1, source_target_pairs={{0,7},{1,0},{2,1},{3,2},{4,3},{5,4},{6,5},{7,6},{8,15},{9,8},{10,9... | collective-permute-start | bytes 393224 | tf_op jit(solution)/shard_map/ppermute | solution.py:45
  90.7 7.4 %collective-permute-start.12 = (f32[256,128]{1,0:T(8,128)S(1)}, f32[256,128]{1,0:T(8,128)S(1)}, u32[]{:S(2)}, u32[]{:S(2)}) collective-permute-start(f32[256,128]{1,0:T(8,128)S(1)} %get-tuple-element.47), channel_id=1, source_target_pairs={{0,6},{1,7},{2,0},{3,1},{4,2},{5,3},{6,4},{7,5},{8,14},{9,15},{10,... | collective-permute-start | bytes 393224 | tf_op jit(solution)/shard_map/ppermute | solution.py:45
  90.8 8.0 %collective-permute-start.11 = (f32[256,128]{1,0:T(8,128)S(1)}, f32[256,128]{1,0:T(8,128)S(1)}, u32[]{:S(2)}, u32[]{:S(2)}) collective-permute-start(f32[256,128]{1,0:T(8,128)S(1)} %get-tuple-element.48), channel_id=1, source_target_pairs={{0,5},{1,6},{2,7},{3,0},{4,1},{5,2},{6,3},{7,4},{8,13},{9,14},{10,... | collective-permute-start | bytes 393224 | tf_op jit(solution)/shard_map/ppermute | solution.py:45
  93.8 23.7 %collective-permute-start.10 = (f32[256,128]{1,0:T(8,128)S(1)}, f32[256,128]{1,0:T(8,128)S(1)}, u32[]{:S(2)}, u32[]{:S(2)}) collective-permute-start(f32[256,128]{1,0:T(8,128)S(1)} %get-tuple-element.49), channel_id=1, source_target_pairs={{0,4},{1,5},{2,6},{3,7},{4,0},{5,1},{6,2},{7,3},{8,12},{9,13},{10,... | collective-permute-start | bytes 393224 | tf_op jit(solution)/shard_map/ppermute | solution.py:45
  93.9 23.6 %collective-permute-start.9 = (f32[256,128]{1,0:T(8,128)S(1)}, f32[256,128]{1,0:T(8,128)S(1)}, u32[]{:S(2)}, u32[]{:S(2)}) collective-permute-start(f32[256,128]{1,0:T(8,128)S(1)} %get-tuple-element.50), channel_id=1, source_target_pairs={{0,3},{1,4},{2,5},{3,6},{4,7},{5,0},{6,1},{7,2},{8,11},{9,12},{10,... | collective-permute-start | bytes 393224 | tf_op jit(solution)/shard_map/ppermute | solution.py:45
  95.3 22.2 %collective-permute-start.8 = (f32[256,128]{1,0:T(8,128)S(1)}, f32[256,128]{1,0:T(8,128)S(1)}, u32[]{:S(2)}, u32[]{:S(2)}) collective-permute-start(f32[256,128]{1,0:T(8,128)S(1)} %get-tuple-element.51), channel_id=1, source_target_pairs={{0,2},{1,3},{2,4},{3,5},{4,6},{5,7},{6,0},{7,1},{8,10},{9,11},{10,... | collective-permute-start | bytes 393224 | tf_op jit(solution)/shard_map/ppermute | solution.py:45
  98.2 19.4 %collective-permute-start.7 = (f32[256,128]{1,0:T(8,128)S(1)}, f32[256,128]{1,0:T(8,128)S(1)}, u32[]{:S(2)}, u32[]{:S(2)}) collective-permute-start(f32[256,128]{1,0:T(8,128)S(1)} %get-tuple-element.45), channel_id=1, source_target_pairs={{0,1},{1,2},{2,3},{3,4},{4,5},{5,6},{6,7},{7,0},{8,9},{9,10},{10,1... | collective-permute-start | bytes 393224 | tf_op jit(solution)/shard_map/ppermute | solution.py:45
  130.0 4.0 %collective-permute-start.20 = (f32[256,128]{1,0:T(8,128)S(1)}, f32[256,128]{1,0:T(8,128)S(1)}, u32[]{:S(2)}, u32[]{:S(2)}) collective-permute-start(f32[256,128]{1,0:T(8,128)S(1)} %get-tuple-element.39), channel_id=1, source_target_pairs={{0,7},{1,0},{2,1},{3,2},{4,3},{5,4},{6,5},{7,6},{8,15},{9,8},{10,9... | collective-permute-start | bytes 393224 | tf_op jit(solution)/shard_map/ppermute | solution.py:45
  130.0 6.8 %collective-permute-start.19 = (f32[256,128]{1,0:T(8,128)S(1)}, f32[256,128]{1,0:T(8,128)S(1)}, u32[]{:S(2)}, u32[]{:S(2)}) collective-permute-start(f32[256,128]{1,0:T(8,128)S(1)} %get-tuple-element.40), channel_id=1, source_target_pairs={{0,6},{1,7},{2,0},{3,1},{4,2},{5,3},{6,4},{7,5},{8,14},{9,15},{10,... | collective-permute-start | bytes 393224 | tf_op jit(solution)/shard_map/ppermute | solution.py:45
  130.1 9.5 %collective-permute-start.18 = (f32[256,128]{1,0:T(8,128)S(1)}, f32[256,128]{1,0:T(8,128)S(1)}, u32[]{:S(2)}, u32[]{:S(2)}) collective-permute-start(f32[256,128]{1,0:T(8,128)S(1)} %get-tuple-element.41), channel_id=1, source_target_pairs={{0,5},{1,6},{2,7},{3,0},{4,1},{5,2},{6,3},{7,4},{8,13},{9,14},{10,... | collective-permute-start | bytes 393224 | tf_op jit(solution)/shard_map/ppermute | solution.py:45
  130.9 22.5 %collective-permute-start.17 = (f32[256,128]{1,0:T(8,128)S(1)}, f32[256,128]{1,0:T(8,128)S(1)}, u32[]{:S(2)}, u32[]{:S(2)}) collective-permute-start(f32[256,128]{1,0:T(8,128)S(1)} %get-tuple-element.42), channel_id=1, source_target_pairs={{0,4},{1,5},{2,6},{3,7},{4,0},{5,1},{6,2},{7,3},{8,12},{9,13},{10,... | collective-permute-start | bytes 393224 | tf_op jit(solution)/shard_map/ppermute | solution.py:45
  133.1 20.9 %collective-permute-start.16 = (f32[256,128]{1,0:T(8,128)S(1)}, f32[256,128]{1,0:T(8,128)S(1)}, u32[]{:S(2)}, u32[]{:S(2)}) collective-permute-start(f32[256,128]{1,0:T(8,128)S(1)} %get-tuple-element.43), channel_id=1, source_target_pairs={{0,3},{1,4},{2,5},{3,6},{4,7},{5,0},{6,1},{7,2},{8,11},{9,12},{10,... | collective-permute-start | bytes 393224 | tf_op jit(solution)/shard_map/ppermute | solution.py:45
  134.0 20.0 %collective-permute-start.15 = (f32[256,128]{1,0:T(8,128)S(1)}, f32[256,128]{1,0:T(8,128)S(1)}, u32[]{:S(2)}, u32[]{:S(2)}) collective-permute-start(f32[256,128]{1,0:T(8,128)S(1)} %get-tuple-element.44), channel_id=1, source_target_pairs={{0,2},{1,3},{2,4},{3,5},{4,6},{5,7},{6,0},{7,1},{8,10},{9,11},{10,... | collective-permute-start | bytes 393224 | tf_op jit(solution)/shard_map/ppermute | solution.py:45
  136.8 17.2 %collective-permute-start.14 = (f32[256,128]{1,0:T(8,128)S(1)}, f32[256,128]{1,0:T(8,128)S(1)}, u32[]{:S(2)}, u32[]{:S(2)}) collective-permute-start(f32[256,128]{1,0:T(8,128)S(1)} %get-tuple-element.38), channel_id=1, source_target_pairs={{0,1},{1,2},{2,3},{3,4},{4,5},{5,6},{6,7},{7,0},{8,9},{9,10},{10,1... | collective-permute-start | bytes 393224 | tf_op jit(solution)/shard_map/ppermute | solution.py:45
  165.9 4.5 %collective-permute-start.27 = (f32[256,128]{1,0:T(8,128)S(1)}, f32[256,128]{1,0:T(8,128)S(1)}, u32[]{:S(2)}, u32[]{:S(2)}) collective-permute-start(f32[256,128]{1,0:T(8,128)S(1)} %get-tuple-element.32), channel_id=1, source_target_pairs={{0,7},{1,0},{2,1},{3,2},{4,3},{5,4},{6,5},{7,6},{8,15},{9,8},{10,9... | collective-permute-start | bytes 393224 | tf_op jit(solution)/shard_map/ppermute | solution.py:45
  165.9 7.4 %collective-permute-start.26 = (f32[256,128]{1,0:T(8,128)S(1)}, f32[256,128]{1,0:T(8,128)S(1)}, u32[]{:S(2)}, u32[]{:S(2)}) collective-permute-start(f32[256,128]{1,0:T(8,128)S(1)} %get-tuple-element.33), channel_id=1, source_target_pairs={{0,6},{1,7},{2,0},{3,1},{4,2},{5,3},{6,4},{7,5},{8,14},{9,15},{10,... | collective-permute-start | bytes 393224 | tf_op jit(solution)/shard_map/ppermute | solution.py:45
  166.0 8.1 %collective-permute-start.25 = (f32[256,128]{1,0:T(8,128)S(1)}, f32[256,128]{1,0:T(8,128)S(1)}, u32[]{:S(2)}, u32[]{:S(2)}) collective-permute-start(f32[256,128]{1,0:T(8,128)S(1)} %get-tuple-element.34), channel_id=1, source_target_pairs={{0,5},{1,6},{2,7},{3,0},{4,1},{5,2},{6,3},{7,4},{8,13},{9,14},{10,... | collective-permute-start | bytes 393224 | tf_op jit(solution)/shard_map/ppermute | solution.py:45
  168.9 23.7 %collective-permute-start.24 = (f32[256,128]{1,0:T(8,128)S(1)}, f32[256,128]{1,0:T(8,128)S(1)}, u32[]{:S(2)}, u32[]{:S(2)}) collective-permute-start(f32[256,128]{1,0:T(8,128)S(1)} %get-tuple-element.35), channel_id=1, source_target_pairs={{0,4},{1,5},{2,6},{3,7},{4,0},{5,1},{6,2},{7,3},{8,12},{9,13},{10,... | collective-permute-start | bytes 393224 | tf_op jit(solution)/shard_map/ppermute | solution.py:45
  169.0 23.6 %collective-permute-start.23 = (f32[256,128]{1,0:T(8,128)S(1)}, f32[256,128]{1,0:T(8,128)S(1)}, u32[]{:S(2)}, u32[]{:S(2)}) collective-permute-start(f32[256,128]{1,0:T(8,128)S(1)} %get-tuple-element.36), channel_id=1, source_target_pairs={{0,3},{1,4},{2,5},{3,6},{4,7},{5,0},{6,1},{7,2},{8,11},{9,12},{10,... | collective-permute-start | bytes 393224 | tf_op jit(solution)/shard_map/ppermute | solution.py:45
  170.4 22.2 %collective-permute-start.22 = (f32[256,128]{1,0:T(8,128)S(1)}, f32[256,128]{1,0:T(8,128)S(1)}, u32[]{:S(2)}, u32[]{:S(2)}) collective-permute-start(f32[256,128]{1,0:T(8,128)S(1)} %get-tuple-element.37), channel_id=1, source_target_pairs={{0,2},{1,3},{2,4},{3,5},{4,6},{5,7},{6,0},{7,1},{8,10},{9,11},{10,... | collective-permute-start | bytes 393224 | tf_op jit(solution)/shard_map/ppermute | solution.py:45
  173.3 19.3 %collective-permute-start.21 = (f32[256,128]{1,0:T(8,128)S(1)}, f32[256,128]{1,0:T(8,128)S(1)}, u32[]{:S(2)}, u32[]{:S(2)}) collective-permute-start(f32[256,128]{1,0:T(8,128)S(1)} %get-tuple-element.31), channel_id=1, source_target_pairs={{0,1},{1,2},{2,3},{3,4},{4,5},{5,6},{6,7},{7,0},{8,9},{9,10},{10,1... | collective-permute-start | bytes 393224 | tf_op jit(solution)/shard_map/ppermute | solution.py:45
  203.6 4.0 %collective-permute-start.28 = (f32[128,128]{0,1:T(8,128)S(1)}, f32[128,128]{0,1:T(8,128)S(1)}, u32[]{:S(2)}, u32[]{:S(2)}) collective-permute-start(f32[128,128]{0,1:T(8,128)S(1)} %fusion.120), channel_id=1, source_target_pairs={{0,1},{1,0},{2,3},{3,2},{4,5},{5,4},{6,7},{7,6},{8,9},{9,8},{10,11... | collective-permute-start | bytes 196616 | tf_op jit(solution)/shard_map/ppermute | solution.py:28
  205.7 12.3 %collective-permute-start.39 = (f32[256,128]{1,0:T(8,128)S(1)}, f32[256,128]{1,0:T(8,128)S(1)}, u32[]{:S(2)}, u32[]{:S(2)}) collective-permute-start(f32[256,128]{1,0:T(8,128)S(1)} %get-tuple-element.25), channel_id=1, source_target_pairs={{0,7},{1,0},{2,1},{3,2},{4,3},{5,4},{6,5},{7,6},{8,15},{9,8},{10,9... | collective-permute-start | bytes 393224 | tf_op jit(solution)/shard_map/ppermute | solution.py:45
  205.8 12.2 %collective-permute-start.38 = (f32[256,128]{1,0:T(8,128)S(1)}, f32[256,128]{1,0:T(8,128)S(1)}, u32[]{:S(2)}, u32[]{:S(2)}) collective-permute-start(f32[256,128]{1,0:T(8,128)S(1)} %get-tuple-element.26), channel_id=1, source_target_pairs={{0,6},{1,7},{2,0},{3,1},{4,2},{5,3},{6,4},{7,5},{8,14},{9,15},{10,... | collective-permute-start | bytes 393224 | tf_op jit(solution)/shard_map/ppermute | solution.py:45
  207.6 10.4 %collective-permute-start.29 = (f32[128,128]{0,1:T(8,128)S(1)}, f32[128,128]{0,1:T(8,128)S(1)}, u32[]{:S(2)}, u32[]{:S(2)}) collective-permute-start(f32[128,128]{0,1:T(8,128)S(1)} %add.361), channel_id=1, source_target_pairs={{0,2},{1,3},{2,0},{3,1},{4,6},{5,7},{6,4},{7,5},{8,10},{9,11},{10,... | collective-permute-start | bytes 196616 | tf_op jit(solution)/shard_map/ppermute | solution.py:28
  208.0 11.3 %collective-permute-start.37 = (f32[256,128]{1,0:T(8,128)S(1)}, f32[256,128]{1,0:T(8,128)S(1)}, u32[]{:S(2)}, u32[]{:S(2)}) collective-permute-start(f32[256,128]{1,0:T(8,128)S(1)} %get-tuple-element.27), channel_id=1, source_target_pairs={{0,5},{1,6},{2,7},{3,0},{4,1},{5,2},{6,3},{7,4},{8,13},{9,14},{10,... | collective-permute-start | bytes 393224 | tf_op jit(solution)/shard_map/ppermute | solution.py:45
  208.0 22.7 %collective-permute-start.36 = (f32[256,128]{1,0:T(8,128)S(1)}, f32[256,128]{1,0:T(8,128)S(1)}, u32[]{:S(2)}, u32[]{:S(2)}) collective-permute-start(f32[256,128]{1,0:T(8,128)S(1)} %get-tuple-element.28), channel_id=1, source_target_pairs={{0,4},{1,5},{2,6},{3,7},{4,0},{5,1},{6,2},{7,3},{8,12},{9,13},{10,... | collective-permute-start | bytes 393224 | tf_op jit(solution)/shard_map/ppermute | solution.py:45
  218.0 14.7 %collective-permute-start.35 = (f32[256,128]{1,0:T(8,128)S(1)}, f32[256,128]{1,0:T(8,128)S(1)}, u32[]{:S(2)}, u32[]{:S(2)}) collective-permute-start(f32[256,128]{1,0:T(8,128)S(1)} %get-tuple-element.29), channel_id=1, source_target_pairs={{0,3},{1,4},{2,5},{3,6},{4,7},{5,0},{6,1},{7,2},{8,11},{9,12},{10,... | collective-permute-start | bytes 393224 | tf_op jit(solution)/shard_map/ppermute | solution.py:45
  218.0 14.7 %collective-permute-start.34 = (f32[256,128]{1,0:T(8,128)S(1)}, f32[256,128]{1,0:T(8,128)S(1)}, u32[]{:S(2)}, u32[]{:S(2)}) collective-permute-start(f32[256,128]{1,0:T(8,128)S(1)} %get-tuple-element.30), channel_id=1, source_target_pairs={{0,2},{1,3},{2,4},{3,5},{4,6},{5,7},{6,0},{7,1},{8,10},{9,11},{10,... | collective-permute-start | bytes 393224 | tf_op jit(solution)/shard_map/ppermute | solution.py:45
  218.0 14.6 %collective-permute-start.33 = (f32[256,128]{1,0:T(8,128)S(1)}, f32[256,128]{1,0:T(8,128)S(1)}, u32[]{:S(2)}, u32[]{:S(2)}) collective-permute-start(f32[256,128]{1,0:T(8,128)S(1)} %get-tuple-element.24), channel_id=1, source_target_pairs={{0,1},{1,2},{2,3},{3,4},{4,5},{5,6},{6,7},{7,0},{8,9},{9,10},{10,1... | collective-permute-start | bytes 393224 | tf_op jit(solution)/shard_map/ppermute | solution.py:45
  219.3 13.9 %collective-permute-start.30 = (f32[128,128]{0,1:T(8,128)S(1)}, f32[128,128]{0,1:T(8,128)S(1)}, u32[]{:S(2)}, u32[]{:S(2)}) collective-permute-start(f32[128,128]{0,1:T(8,128)S(1)} %add.362), channel_id=1, source_target_pairs={{0,4},{1,5},{2,6},{3,7},{4,0},{5,1},{6,2},{7,3},{8,12},{9,13},{10,... | collective-permute-start | bytes 196616 | tf_op jit(solution)/shard_map/ppermute | solution.py:28
  233.1 1.3 collective-permute-start.40
  233.2 4.5 %collective-permute-start.31 = (f32[128,128]{0,1:T(8,128)S(1)}, f32[128,128]{0,1:T(8,128)S(1)}, u32[]{:S(2)}, u32[]{:S(2)}) collective-permute-start(f32[128,128]{0,1:T(8,128)S(1)} %add.363), channel_id=1, source_target_pairs={{0,8},{8,0},{16,24},{24,16},{1,9},{9,1},{17,25},{25,17},{2,10},{10... | collective-permute-start | bytes 196616 | tf_op jit(solution)/shard_map/ppermute | solution.py:28
  234.5 4.3 %collective-permute-start.41 = (f32[128,128]{0,1:T(8,128)S(1)}, f32[128,128]{0,1:T(8,128)S(1)}, u32[]{:S(2)}, u32[]{:S(2)}) collective-permute-start(f32[128,128]{0,1:T(8,128)S(1)} %add.377), channel_id=1, source_target_pairs={{0,2},{1,3},{2,0},{3,1},{4,6},{5,7},{6,4},{7,5},{8,10},{9,11},{10,... | collective-permute-start | bytes 196616 | tf_op jit(solution)/shard_map/ppermute | solution.py:28
  237.8 4.3 %collective-permute-start.32 = (f32[128,128]{0,1:T(8,128)S(1)}, f32[128,128]{0,1:T(8,128)S(1)}, u32[]{:S(2)}, u32[]{:S(2)}) collective-permute-start(f32[128,128]{0,1:T(8,128)S(1)} %add.364), channel_id=1, source_target_pairs={{0,16},{8,24},{16,0},{24,8},{1,17},{9,25},{17,1},{25,9},{2,18},{10... | collective-permute-start | bytes 196616 | tf_op jit(solution)/shard_map/ppermute | solution.py:28
  238.8 15.8 %collective-permute-start.42 = (f32[128,128]{0,1:T(8,128)S(1)}, f32[128,128]{0,1:T(8,128)S(1)}, u32[]{:S(2)}, u32[]{:S(2)}) collective-permute-start(f32[128,128]{0,1:T(8,128)S(1)} %add.378), channel_id=1, source_target_pairs={{0,4},{1,5},{2,6},{3,7},{4,0},{5,1},{6,2},{7,3},{8,12},{9,13},{10,... | collective-permute-start | bytes 196616 | tf_op jit(solution)/shard_map/ppermute | solution.py:28
  254.7 11.4 %collective-permute-start.43 = (f32[128,128]{0,1:T(8,128)S(1)}, f32[128,128]{0,1:T(8,128)S(1)}, u32[]{:S(2)}, u32[]{:S(2)}) collective-permute-start(f32[128,128]{0,1:T(8,128)S(1)} %add.379), channel_id=1, source_target_pairs={{0,8},{8,0},{16,24},{24,16},{1,9},{9,1},{17,25},{25,17},{2,10},{10... | collective-permute-start | bytes 196616 | tf_op jit(solution)/shard_map/ppermute | solution.py:28
  266.1 4.3 %collective-permute-start.44 = (f32[128,128]{0,1:T(8,128)S(1)}, f32[128,128]{0,1:T(8,128)S(1)}, u32[]{:S(2)}, u32[]{:S(2)}) collective-permute-start(f32[128,128]{0,1:T(8,128)S(1)} %add.380), channel_id=1, source_target_pairs={{0,16},{8,24},{16,0},{24,8},{1,17},{9,25},{17,1},{25,9},{2,18},{10... | collective-permute-start | bytes 196616 | tf_op jit(solution)/shard_map/ppermute | solution.py:28
  (5 other events, 29.0 us)

commit v3 on v2

--- a/solution.py
+++ b/solution.py
@@ -46,6 +46,43 @@
     return total
 
 
+def halving_scatter_sum(value, axis):
+    size = lax.axis_size(axis)
+    if size & (size - 1):
+        return scatter_sum(value, axis)
+    here = lax.axis_index(axis)
+    rows = value.shape[0] // size
+    blocks = value.reshape(size, rows, value.shape[1])
+    step = 1
+    while step < size:
+        bit = (here // step) % 2
+        paired = blocks.reshape(blocks.shape[0] // 2, 2, rows, value.shape[1])
+        kept = lax.dynamic_index_in_dim(paired, bit, axis=1, keepdims=False)
+        sent = lax.dynamic_index_in_dim(paired, 1 - bit, axis=1, keepdims=False)
+        pairs = [(index, index ^ step) for index in range(size)]
+        blocks = kept + lax.ppermute(sent, axis, pairs)
+        step *= 2
+    return blocks.reshape(rows, value.shape[1])
+
+
+def doubling_gather(value, axis):
+    size = lax.axis_size(axis)
+    if size & (size - 1):
+        return lax.all_gather(value, axis, axis=0, tiled=True)
+    here = lax.axis_index(axis)
+    result = value
+    step = 1
+    while step < size:
+        pairs = [(index, index ^ step) for index in range(size)]
+        other = lax.ppermute(result, axis, pairs)
+        low = (here // step) % 2 == 0
+        result = jnp.concatenate(
+            [jnp.where(low, result, other), jnp.where(low, other, result)], axis=0
+        )
+        step *= 2
+    return result
+
+
 def local(tiles, tile_cols, degree_scale, start_block, planted, strengths, bounds):
     piece_rows = start_block.shape[0]
     node_count = piece_rows * lax.axis_size("row") * lax.axis_size("col")
@@ -58,19 +95,19 @@
     dense = dense.reshape(tile_rows * tile_size, n_blocks * tile_size)
     w_hi, w_lo = split_bf16(dense)
 
-    planted_cols = lax.all_gather(planted, "row", axis=0, tiled=True)
-    planted_rows = lax.all_gather(planted, "col", axis=0, tiled=True)
+    planted_cols = doubling_gather(planted, "row")
+    planted_rows = doubling_gather(planted, "col")
 
     def operate(vector):
         scaled = (degree_scale[:, None] * vector).astype(jnp.bfloat16)
-        gathered = lax.all_gather(scaled, "row", axis=0, tiled=True)
+        gathered = doubling_gather(scaled, "row")
         product = jnp.dot(w_hi, gathered, preferred_element_type=jnp.float32)
         product = product + jnp.dot(w_lo, gathered, preferred_element_type=jnp.float32)
         partial = lax.dot_general(
             planted_cols, gathered, (((0,), (0,)), ((), ())), preferred_element_type=jnp.float32
         )
         product = product + split_dot(planted_rows, weights * partial) / node_count
-        summed = scatter_sum(product, "col")
+        summed = halving_scatter_sum(product, "col")
         return degree_scale[:, None] * summed
 
     center = (bounds[1] + bounds[0]) * 0.5

time: 272 us -> 244 us (0.90)
  blocking collectives: 69.6 us -> 0 us
  waiting for transfers between devices: 100 us -> 128 us
  starting transfers between devices: 39.6 us -> 45.8 us
  other arithmetic: 27 us -> 30.9 us
    all_gather x7 -> x0, blocking collectives: 69.6 us -> none  [the longest x5 43.6 us: operate(): gathered = lax.all_gather(scaled, 'row', axis=0, tiled=True)]
    ppermute x35 -> x30, waiting for transfers between devices: 85.3 us -> 101 us  [the longest x15 65.9 us: halving_scatter_sum(): blocks = kept + lax.ppermute(sent, axis, pairs)]
    ppermute x10, waiting for transfers between devices: 14.9 us -> 27.8 us  [butterfly_sum(): value = value + lax.ppermute(value, axis, pairs)]
    dot_general x5, matrix products: 6.35 us -> 10.9 us  [operate(): jnp.dot(w_lo, gathered, preferred_element_type=jnp.float32)]
    ppermute x35 -> x30, starting transfers between devices: 31.4 us -> 35.8 us  [the longest x15 21.8 us: doubling_gather(): other = lax.ppermute(result, axis, pairs)]
  transfers between devices with their start and end apart: 45 -> 40, of which waited for: 21 -> 31; matrix products, arithmetic and copies ran while one was open for 10% -> 18% of each run, Pallas kernels for 0% -> 0%
where the time goes in v3:
time: 244 us
  waiting for transfers between devices  128 us (52%)
  starting transfers between devices  45.8 us (19%)
  matrix products  32.5 us (13%)
  other arithmetic  30.9 us (13%)
  between operations  4.02 us (2%)
  local copies, waits for them, and re-layouts  2.48 us (1%)
    ppermute x15, waiting for transfers between devices, halving_scatter_sum(): blocks = kept + lax.ppermute(sent, axis, pairs)  65.9 us
    ppermute x15, waiting for transfers between devices, doubling_gather(): other = lax.ppermute(result, axis, pairs)  34.8 us
    ppermute x10, waiting for transfers between devices, butterfly_sum(): value = value + lax.ppermute(value, axis, pairs)  27.8 us
    ppermute x15, starting transfers between devices, doubling_gather(): other = lax.ppermute(result, axis, pairs)  21.8 us
    ppermute x15, starting transfers between devices, halving_scatter_sum(): blocks = kept + lax.ppermute(sent, axis, pairs)  14 us
    another operation x3, other arithmetic, local(): factor = jnp.linalg.cholesky(gram_matrix)  12.4 us
    dot_general x5, matrix products, operate(): jnp.dot(w_lo, gathered, preferred_element_type=jnp.float32)  10.9 us
    another operation x2, other arithmetic, local(): lax.linalg.triangular_solve(factor, current, left_side=False, lower=True,...  10.5 us
  transfers between devices with their start and end apart: 40, of which 31 were waited for; matrix products, arithmetic and copies ran while one was open for 18% of the time, Pallas kernels for 0%

profile of v3, /device:TPU:0, one launch (start us, length us, event | category | flops | bytes accessed | tf_op | source)
XLA Modules:
  0.0 244.0 jit_solution(13344917275638687700)
XLA Ops:
  1.2 2.6 %collective-permute-start.5 = (bf16[256,128]{1,0:T(8,128)(2,1)}, bf16[256,128]{1,0:T(8,128)(2,1)S(1)}, u32[]{:S(2)}, u32[]{:S(2)}) collective-permute-start(bf16[256,128]{1,0:T(8,128)(2,1)} %param.11), channel_id=1, source_target_pairs={{0,8},{8,0},{16,24},{24,16},{1,9},{9,1},{17,25},{25,17},{2,10},{10... | collective-permute-start | bytes 196616 | tf_op jit(solution)/shard_map/ppermute | solution.py:77
  4.8 8.2 %fusion.1 = f32[16,8,128,128]{3,1,2,0:T(8,128)S(1)} fusion(bf16[16,16,128,128]{3,2,1,0:T(8,128)(2,1)} %param.7, s32[16,16]{1,0:T(8,128)} %param.8), kind=kOutput, calls=%fused_computation.3 | convolution fusion | flops 67110912 | bytes 16778240 | tf_op jit(solution)/shard_map/rst,rsab->ratb/dot_general | solution.py:94
  13.1 5.3 %fusion = (bf16[2048,1024]{1,0:T(8,128)(2,1)}, bf16[2048,1024]{1,0:T(8,128)(2,1)}) fusion(f32[256,8,8,128]{3,2,1,0:T(8,128)S(1)} %bitcast.137), kind=kLoop, calls=%fused_computation.2 | loop fusion | flops 6291456 | bytes 16777216 | tf_op jit(solution)/shard_map/convert_element_type | solution.py:11
  18.5 2.2 collective-permute-start.3
  20.7 1.6 collective-permute-start.1
  24.3 2.8 %collective-permute-start.4 = (bf16[1024,128]{1,0:T(8,128)(2,1)S(1)}, bf16[1024,128]{1,0:T(8,128)(2,1)S(1)}, u32[]{:S(2)}, u32[]{:S(2)}) collective-permute-start(bf16[1024,128]{1,0:T(8,128)(2,1)S(1)} %pad_maximum_fusion.2), channel_id=1, source_target_pairs={{0,4},{1,5},{2,6},{3,7},{4,0},{5,1},{6,2},{7,3},{8,12},{9,13},{10,... | collective-permute-start | bytes 786440 | tf_op jit(solution)/shard_map/ppermute | solution.py:77
  27.2 3.5 %fusion.34 = f32[2048,128]{1,0:T(8,128)S(1)} fusion(bf16[2048,1024]{1,0:T(8,128)(2,1)} %get-tuple-element.10, bf16[512,128]{1,0:T(8,128)(2,1)S(1)} %get-tuple-element.27, bf16[512,128]{1,0:T(8,128)(2,1)S(1)} %get-tuple-element.26), kind=kOutput, calls=%fused_computation.112 | convolution fusion | flops 537395200 | bytes 5505024 | tf_op jit(solution)/shard_map/dot_general | solution.py:105
  31.0 7.4 %collective-permute-done.4 = bf16[1024,128]{1,0:T(8,128)(2,1)S(1)} collective-permute-done((bf16[1024,128]{1,0:T(8,128)(2,1)S(1)}, bf16[1024,128]{1,0:T(8,128)(2,1)S(1)}, u32[]{:S(2)}, u32[]{:S(2)}) %collective-permute-start.4) | collective-permute-done | bytes 262176 | tf_op jit(solution)/shard_map/ppermute | solution.py:77
  40.5 1.9 collective-permute-done.7
  43.1 7.8 %collective-permute-done.8 = f32[2,256,128]{2,1,0:T(8,128)S(1)} collective-permute-done((f32[2,256,128]{2,1,0:T(8,128)S(1)}, f32[2,256,128]{2,1,0:T(8,128)S(1)}, u32[]{:S(2)}, u32[]{:S(2)}) %collective-permute-start.8) | collective-permute-done | bytes 262176 | tf_op jit(solution)/shard_map/ppermute | solution.py:63
  51.0 2.2 collective-permute-start.9
  56.4 3.0 %collective-permute-done.9 = f32[1,256,128]{2,1,0:T(8,128)S(1)} collective-permute-done((f32[1,256,128]{2,1,0:T(8,128)S(1)}, f32[1,256,128]{2,1,0:T(8,128)S(1)}, u32[]{:S(2)}, u32[]{:S(2)}) %collective-permute-start.9) | collective-permute-done | bytes 131104 | tf_op jit(solution)/shard_map/ppermute | solution.py:63
  61.0 2.9 %collective-permute-done.10 = bf16[256,128]{1,0:T(8,128)(2,1)S(1)} collective-permute-done((bf16[256,128]{1,0:T(8,128)(2,1)S(1)}, bf16[256,128]{1,0:T(8,128)(2,1)S(1)}, u32[]{:S(2)}, u32[]{:S(2)}) %collective-permute-start.10) | collective-permute-done | bytes 65568 | tf_op jit(solution)/shard_map/ppermute | solution.py:77
  63.9 1.4 collective-permute-start.11
  65.4 3.6 %collective-permute-done.11 = bf16[512,128]{1,0:T(8,128)(2,1)S(1)} collective-permute-done((bf16[512,128]{1,0:T(8,128)(2,1)S(1)}, bf16[512,128]{1,0:T(8,128)(2,1)S(1)}, u32[]{:S(2)}, u32[]{:S(2)}) %collective-permute-start.11) | collective-permute-done | bytes 131104 | tf_op jit(solution)/shard_map/ppermute | solution.py:77
  69.0 3.5 %fusion.33 = f32[2048,128]{1,0:T(8,128)S(1)} fusion(bf16[2048,1024]{1,0:T(8,128)(2,1)} %get-tuple-element.10, bf16[512,128]{1,0:T(8,128)(2,1)S(1)} %get-tuple-element.21, bf16[512,128]{1,0:T(8,128)(2,1)S(1)} %get-tuple-element.20), kind=kOutput, calls=%fused_computation.111 | convolution fusion | flops 537395200 | bytes 5505024 | tf_op jit(solution)/shard_map/dot_general | solution.py:105
  76.1 1.9 collective-permute-done.12
  78.7 7.8 %collective-permute-done.13 = f32[2,256,128]{2,1,0:T(8,128)S(1)} collective-permute-done((f32[2,256,128]{2,1,0:T(8,128)S(1)}, f32[2,256,128]{2,1,0:T(8,128)S(1)}, u32[]{:S(2)}, u32[]{:S(2)}) %collective-permute-start.13) | collective-permute-done | bytes 262176 | tf_op jit(solution)/shard_map/ppermute | solution.py:63
  86.6 2.2 collective-permute-start.14
  88.8 6.2 %collective-permute-done.14 = f32[1,256,128]{2,1,0:T(8,128)S(1)} collective-permute-done((f32[1,256,128]{2,1,0:T(8,128)S(1)}, f32[1,256,128]{2,1,0:T(8,128)S(1)}, u32[]{:S(2)}, u32[]{:S(2)}) %collective-permute-start.14) | collective-permute-done | bytes 131104 | tf_op jit(solution)/shard_map/ppermute | solution.py:63
  96.6 2.9 %collective-permute-done.15 = bf16[256,128]{1,0:T(8,128)(2,1)S(1)} collective-permute-done((bf16[256,128]{1,0:T(8,128)(2,1)S(1)}, bf16[256,128]{1,0:T(8,128)(2,1)S(1)}, u32[]{:S(2)}, u32[]{:S(2)}) %collective-permute-start.15) | collective-permute-done | bytes 65568 | tf_op jit(solution)/shard_map/ppermute | solution.py:77
  101.0 3.6 %collective-permute-done.16 = bf16[512,128]{1,0:T(8,128)(2,1)S(1)} collective-permute-done((bf16[512,128]{1,0:T(8,128)(2,1)S(1)}, bf16[512,128]{1,0:T(8,128)(2,1)S(1)}, u32[]{:S(2)}, u32[]{:S(2)}) %collective-permute-start.16) | collective-permute-done | bytes 131104 | tf_op jit(solution)/shard_map/ppermute | solution.py:77
  108.1 1.9 collective-permute-done.17
  110.7 7.8 %collective-permute-done.18 = f32[2,256,128]{2,1,0:T(8,128)S(1)} collective-permute-done((f32[2,256,128]{2,1,0:T(8,128)S(1)}, f32[2,256,128]{2,1,0:T(8,128)S(1)}, u32[]{:S(2)}, u32[]{:S(2)}) %collective-permute-start.18) | collective-permute-done | bytes 262176 | tf_op jit(solution)/shard_map/ppermute | solution.py:63
  118.6 2.2 collective-permute-start.19
  120.8 6.2 %collective-permute-done.19 = f32[1,256,128]{2,1,0:T(8,128)S(1)} collective-permute-done((f32[1,256,128]{2,1,0:T(8,128)S(1)}, f32[1,256,128]{2,1,0:T(8,128)S(1)}, u32[]{:S(2)}, u32[]{:S(2)}) %collective-permute-start.19) | collective-permute-done | bytes 131104 | tf_op jit(solution)/shard_map/ppermute | solution.py:63
  128.6 2.9 %collective-permute-done.20 = bf16[256,128]{1,0:T(8,128)(2,1)S(1)} collective-permute-done((bf16[256,128]{1,0:T(8,128)(2,1)S(1)}, bf16[256,128]{1,0:T(8,128)(2,1)S(1)}, u32[]{:S(2)}, u32[]{:S(2)}) %collective-permute-start.20) | collective-permute-done | bytes 65568 | tf_op jit(solution)/shard_map/ppermute | solution.py:77
  133.0 3.6 %collective-permute-done.21 = bf16[512,128]{1,0:T(8,128)(2,1)S(1)} collective-permute-done((bf16[512,128]{1,0:T(8,128)(2,1)S(1)}, bf16[512,128]{1,0:T(8,128)(2,1)S(1)}, u32[]{:S(2)}, u32[]{:S(2)}) %collective-permute-start.21) | collective-permute-done | bytes 131104 | tf_op jit(solution)/shard_map/ppermute | solution.py:77
  136.6 1.5 fusion.31
  140.4 1.9 collective-permute-done.22
  142.9 7.8 %collective-permute-done.23 = f32[2,256,128]{2,1,0:T(8,128)S(1)} collective-permute-done((f32[2,256,128]{2,1,0:T(8,128)S(1)}, f32[2,256,128]{2,1,0:T(8,128)S(1)}, u32[]{:S(2)}, u32[]{:S(2)}) %collective-permute-start.23) | collective-permute-done | bytes 262176 | tf_op jit(solution)/shard_map/ppermute | solution.py:63
  150.8 2.2 collective-permute-start.24
  153.1 6.2 %collective-permute-done.24 = f32[1,256,128]{2,1,0:T(8,128)S(1)} collective-permute-done((f32[1,256,128]{2,1,0:T(8,128)S(1)}, f32[1,256,128]{2,1,0:T(8,128)S(1)}, u32[]{:S(2)}, u32[]{:S(2)}) %collective-permute-start.24) | collective-permute-done | bytes 131104 | tf_op jit(solution)/shard_map/ppermute | solution.py:63
  160.8 2.9 %collective-permute-done.30 = bf16[256,128]{1,0:T(8,128)(2,1)S(1)} collective-permute-done((bf16[256,128]{1,0:T(8,128)(2,1)S(1)}, bf16[256,128]{1,0:T(8,128)(2,1)S(1)}, u32[]{:S(2)}, u32[]{:S(2)}) %collective-permute-start.30) | collective-permute-done | bytes 65568 | tf_op jit(solution)/shard_map/ppermute | solution.py:77
  165.2 3.6 %collective-permute-done.31 = bf16[512,128]{1,0:T(8,128)(2,1)S(1)} collective-permute-done((bf16[512,128]{1,0:T(8,128)(2,1)S(1)}, bf16[512,128]{1,0:T(8,128)(2,1)S(1)}, u32[]{:S(2)}, u32[]{:S(2)}) %collective-permute-start.31) | collective-permute-done | bytes 131104 | tf_op jit(solution)/shard_map/ppermute | solution.py:77
  175.0 1.6 collective-permute-start.26
  176.5 7.6 %collective-permute-done.26 = f32[128,128]{0,1:T(8,128)S(1)} collective-permute-done((f32[128,128]{0,1:T(8,128)S(1)}, f32[128,128]{0,1:T(8,128)S(1)}, u32[]{:S(2)}, u32[]{:S(2)}) %collective-permute-start.26) | collective-permute-done | bytes 65568 | tf_op jit(solution)/shard_map/ppermute | solution.py:28
  184.2 2.2 collective-permute-start.27
  186.4 3.7 %collective-permute-done.27 = f32[128,128]{0,1:T(8,128)S(1)} collective-permute-done((f32[128,128]{0,1:T(8,128)S(1)}, f32[128,128]{0,1:T(8,128)S(1)}, u32[]{:S(2)}, u32[]{:S(2)}) %collective-permute-start.27) | collective-permute-done | bytes 65568 | tf_op jit(solution)/shard_map/ppermute | solution.py:28
  190.8 3.6 %collective-permute-done.28 = f32[128,128]{0,1:T(8,128)S(1)} collective-permute-done((f32[128,128]{0,1:T(8,128)S(1)}, f32[128,128]{0,1:T(8,128)S(1)}, u32[]{:S(2)}, u32[]{:S(2)}) %collective-permute-start.28) | collective-permute-done | bytes 65568 | tf_op jit(solution)/shard_map/ppermute | solution.py:28
  196.0 1.7 collective-permute-start.34
  198.9 4.4 %collective-permute-done.34 = f32[1,256,128]{2,1,0:T(8,128)S(1)} collective-permute-done((f32[1,256,128]{2,1,0:T(8,128)S(1)}, f32[1,256,128]{2,1,0:T(8,128)S(1)}, u32[]{:S(2)}, u32[]{:S(2)}) %collective-permute-start.34) | collective-permute-done | bytes 131104 | tf_op jit(solution)/shard_map/ppermute | solution.py:63
  203.9 11.7 %cholesky.16 = f32[128,128]{1,0:T(8,128)S(1)} custom-call(f32[128,128]{1,0:T(8,128)S(1)} %fusion.42), custom_call_target="Cholesky" | custom-call | tf_op jit(solution)/shard_map/jit(cholesky)/cholesky | solution.py:128
  215.7 4.4 %collective-permute-done.36 = f32[128,128]{0,1:T(8,128)S(1)} collective-permute-done((f32[128,128]{0,1:T(8,128)S(1)}, f32[128,128]{0,1:T(8,128)S(1)}, u32[]{:S(2)}, u32[]{:S(2)}) %collective-permute-start.36) | collective-permute-done | bytes 65568 | tf_op jit(solution)/shard_map/ppermute | solution.py:28
  222.2 3.9 %collective-permute-done.37 = f32[128,128]{0,1:T(8,128)S(1)} collective-permute-done((f32[128,128]{0,1:T(8,128)S(1)}, f32[128,128]{0,1:T(8,128)S(1)}, u32[]{:S(2)}, u32[]{:S(2)}) %collective-permute-start.37) | collective-permute-done | bytes 65568 | tf_op jit(solution)/shard_map/ppermute | solution.py:28
  226.2 1.8 collective-permute-start.38
  228.7 9.8 %custom-call.10 = f32[1,128,128]{1,2,0:T(8,128)S(1)} custom-call(f32[1,128,128]{2,1,0:T(8,128)S(1)} %fusion.35), custom_call_target="InvertDiagBlocksLowerTriangular" | custom-call | tf_op jit(solution)/shard_map/triangular_solve | solution.py:129
  239.6 3.3 %collective-permute-done.39 = f32[128,128]{0,1:T(8,128)S(1)} collective-permute-done((f32[128,128]{0,1:T(8,128)S(1)}, f32[128,128]{0,1:T(8,128)S(1)}, u32[]{:S(2)}, u32[]{:S(2)}) %collective-permute-start.39) | collective-permute-done | bytes 65568 | tf_op jit(solution)/shard_map/ppermute | solution.py:28
  (148 shorter events, 44.7 us)
Async XLA Ops:
  0.6 17.7 %collective-permute-start.2 = (bf16[256,128]{1,0:T(8,128)(2,1)}, bf16[256,128]{1,0:T(8,128)(2,1)S(1)}, u32[]{:S(2)}, u32[]{:S(2)}) collective-permute-start(bf16[256,128]{1,0:T(8,128)(2,1)} %param.11), channel_id=1, source_target_pairs={{0,1},{1,0},{2,3},{3,2},{4,5},{5,4},{6,7},{7,6},{8,9},{9,8},{10,11... | collective-permute-start | bytes 196616 | tf_op jit(solution)/shard_map/ppermute | solution.py:77
  1.2 17.2 %collective-permute-start.5 = (bf16[256,128]{1,0:T(8,128)(2,1)}, bf16[256,128]{1,0:T(8,128)(2,1)S(1)}, u32[]{:S(2)}, u32[]{:S(2)}) collective-permute-start(bf16[256,128]{1,0:T(8,128)(2,1)} %param.11), channel_id=1, source_target_pairs={{0,8},{8,0},{16,24},{24,16},{1,9},{9,1},{17,25},{25,17},{2,10},{10... | collective-permute-start | bytes 196616 | tf_op jit(solution)/shard_map/ppermute | solution.py:77
  4.8 13.6 %collective-permute-start = (bf16[256,128]{1,0:T(8,128)(2,1)S(1)}, bf16[256,128]{1,0:T(8,128)(2,1)S(1)}, u32[]{:S(2)}, u32[]{:S(2)}) collective-permute-start(bf16[256,128]{1,0:T(8,128)(2,1)S(1)} %multiply_convert_fusion.4), channel_id=1, source_target_pairs={{0,8},{8,0},{16,24},{24,16},{1,9},{9,1},{17,25},{25,17},{2,10},{10... | collective-permute-start | bytes 196616 | tf_op jit(solution)/shard_map/ppermute | solution.py:77
  13.0 5.3 %copy-start.3 = (f32[256,128]{1,0:T(8,128)S(1)}, f32[256,128]{1,0:T(8,128)}, u32[]{:S(2)}) copy-start(f32[256,128]{1,0:T(8,128)} %param.10) | copy-start | bytes 393220
  13.0 5.3 %copy-start.4 = (bf16[256,128]{1,0:T(8,128)(2,1)S(1)}, bf16[256,128]{1,0:T(8,128)(2,1)}, u32[]{:S(2)}) copy-start(bf16[256,128]{1,0:T(8,128)(2,1)} %param.11) | copy-start | bytes 196612
  13.0 5.3 %copy-start.5 = (f32[256]{0:T(256)S(1)}, f32[256]{0:T(256)}, u32[]{:S(2)}) copy-start(f32[256]{0:T(256)} %param.9) | copy-start | bytes 3076
  18.5 5.7 %collective-permute-start.3 = (bf16[512,128]{1,0:T(8,128)(2,1)S(1)}, bf16[512,128]{1,0:T(8,128)(2,1)S(1)}, u32[]{:S(2)}, u32[]{:S(2)}) collective-permute-start(bf16[512,128]{1,0:T(8,128)(2,1)S(1)} %pad_maximum_fusion.9), channel_id=1, source_target_pairs={{0,2},{1,3},{2,0},{3,1},{4,6},{5,7},{6,4},{7,5},{8,10},{9,11},{10,... | collective-permute-start | bytes 393224 | tf_op jit(solution)/shard_map/ppermute | solution.py:77
  20.7 6.4 %collective-permute-start.1 = (bf16[512,128]{1,0:T(8,128)(2,1)S(1)}, bf16[512,128]{1,0:T(8,128)(2,1)S(1)}, u32[]{:S(2)}, u32[]{:S(2)}) collective-permute-start(bf16[512,128]{1,0:T(8,128)(2,1)S(1)} %pad_maximum_fusion.8), channel_id=1, source_target_pairs={{0,16},{8,24},{16,0},{24,8},{1,17},{9,25},{17,1},{25,9},{2,18},{10... | collective-permute-start | bytes 393224 | tf_op jit(solution)/shard_map/ppermute | solution.py:77
  22.3 8.4 %collective-permute-start.6 = (bf16[512,128]{1,0:T(8,128)(2,1)S(1)}, bf16[512,128]{1,0:T(8,128)(2,1)S(1)}, u32[]{:S(2)}, u32[]{:S(2)}) collective-permute-start(bf16[512,128]{1,0:T(8,128)(2,1)S(1)} %pad_maximum_fusion.10), channel_id=1, source_target_pairs={{0,16},{8,24},{16,0},{24,8},{1,17},{9,25},{17,1},{25,9},{2,18},{10... | collective-permute-start | bytes 393224 | tf_op jit(solution)/shard_map/ppermute | solution.py:77
  24.3 6.5 %copy-start.7 = (f32[128]{0:T(128)S(1)}, f32[128]{0:T(128)}, u32[]{:S(2)}) copy-start(f32[128]{0:T(128)} %param.12) | copy-start | bytes 1540
  24.3 14.1 %collective-permute-start.4 = (bf16[1024,128]{1,0:T(8,128)(2,1)S(1)}, bf16[1024,128]{1,0:T(8,128)(2,1)S(1)}, u32[]{:S(2)}, u32[]{:S(2)}) collective-permute-start(bf16[1024,128]{1,0:T(8,128)(2,1)S(1)} %pad_maximum_fusion.2), channel_id=1, source_target_pairs={{0,4},{1,5},{2,6},{3,7},{4,0},{5,1},{6,2},{7,3},{8,12},{9,13},{10,... | collective-permute-start | bytes 786440 | tf_op jit(solution)/shard_map/ppermute | solution.py:77
  30.6 8.4 %copy-start = (bf16[2048,1024]{1,0:T(8,128)(2,1)S(1)}, bf16[2048,1024]{1,0:T(8,128)(2,1)}, u32[]{:S(2)}) copy-start(bf16[2048,1024]{1,0:T(8,128)(2,1)} %get-tuple-element.11) | copy-start | bytes 12582916
  40.4 12.8 %copy-start.6 = (f32[2]{0:T(128)S(1)}, f32[2]{0:T(128)}, u32[]{:S(2)}) copy-start(f32[2]{0:T(128)} %param.13) | copy-start | bytes 28
  40.4 2.0 collective-permute-start.7
  42.5 8.4 %collective-permute-start.8 = (f32[2,256,128]{2,1,0:T(8,128)S(1)}, f32[2,256,128]{2,1,0:T(8,128)S(1)}, u32[]{:S(2)}, u32[]{:S(2)}) collective-permute-start(f32[2,256,128]{2,1,0:T(8,128)S(1)} %dynamic-slice_bitcast_fusion.9), channel_id=1, source_target_pairs={{0,2},{1,3},{2,0},{3,1},{4,6},{5,7},{6,4},{7,5},{8,10},{9,11},{10,... | collective-permute-start | bytes 786440 | tf_op jit(solution)/shard_map/ppermute | solution.py:63
  51.0 8.5 %collective-permute-start.9 = (f32[1,256,128]{2,1,0:T(8,128)S(1)}, f32[1,256,128]{2,1,0:T(8,128)S(1)}, u32[]{:S(2)}, u32[]{:S(2)}) collective-permute-start(f32[1,256,128]{2,1,0:T(8,128)S(1)} %constant_dynamic-slice_fusion.4), channel_id=1, source_target_pairs={{0,4},{1,5},{2,6},{3,7},{4,0},{5,1},{6,2},{7,3},{8,12},{9,13},{10,... | collective-permute-start | bytes 393224 | tf_op jit(solution)/shard_map/ppermute | solution.py:63
  59.5 4.3 %collective-permute-start.10 = (bf16[256,128]{1,0:T(8,128)(2,1)S(1)}, bf16[256,128]{1,0:T(8,128)(2,1)S(1)}, u32[]{:S(2)}, u32[]{:S(2)}) collective-permute-start(bf16[256,128]{1,0:T(8,128)(2,1)S(1)} %get-tuple-element.8), channel_id=1, source_target_pairs={{0,8},{8,0},{16,24},{24,16},{1,9},{9,1},{17,25},{25,17},{2,10},{10... | collective-permute-start | bytes 196616 | tf_op jit(solution)/shard_map/ppermute | solution.py:77
  63.9 5.0 %collective-permute-start.11 = (bf16[512,128]{1,0:T(8,128)(2,1)S(1)}, bf16[512,128]{1,0:T(8,128)(2,1)S(1)}, u32[]{:S(2)}, u32[]{:S(2)}) collective-permute-start(bf16[512,128]{1,0:T(8,128)(2,1)S(1)} %pad_maximum_fusion.11), channel_id=1, source_target_pairs={{0,16},{8,24},{16,0},{24,8},{1,17},{9,25},{17,1},{25,9},{2,18},{10... | collective-permute-start | bytes 393224 | tf_op jit(solution)/shard_map/ppermute | solution.py:77
  72.5 2.2 copy-start.1
  75.9 28.7 %copy-start.2 = (bf16[2048,1024]{1,0:T(8,128)(2,1)S(1)}, bf16[2048,1024]{1,0:T(8,128)(2,1)}, u32[]{:S(2)}) copy-start(bf16[2048,1024]{1,0:T(8,128)(2,1)} %get-tuple-element.10) | copy-start | bytes 12582916
  76.0 2.0 collective-permute-start.12
  78.1 8.4 %collective-permute-start.13 = (f32[2,256,128]{2,1,0:T(8,128)S(1)}, f32[2,256,128]{2,1,0:T(8,128)S(1)}, u32[]{:S(2)}, u32[]{:S(2)}) collective-permute-start(f32[2,256,128]{2,1,0:T(8,128)S(1)} %dynamic-slice_bitcast_fusion.8), channel_id=1, source_target_pairs={{0,2},{1,3},{2,0},{3,1},{4,6},{5,7},{6,4},{7,5},{8,10},{9,11},{10,... | collective-permute-start | bytes 786440 | tf_op jit(solution)/shard_map/ppermute | solution.py:63
  86.6 8.5 %collective-permute-start.14 = (f32[1,256,128]{2,1,0:T(8,128)S(1)}, f32[1,256,128]{2,1,0:T(8,128)S(1)}, u32[]{:S(2)}, u32[]{:S(2)}) collective-permute-start(f32[1,256,128]{2,1,0:T(8,128)S(1)} %constant_dynamic-slice_fusion.3), channel_id=1, source_target_pairs={{0,4},{1,5},{2,6},{3,7},{4,0},{5,1},{6,2},{7,3},{8,12},{9,13},{10,... | collective-permute-start | bytes 393224 | tf_op jit(solution)/shard_map/ppermute | solution.py:63
  95.1 4.3 %collective-permute-start.15 = (bf16[256,128]{1,0:T(8,128)(2,1)S(1)}, bf16[256,128]{1,0:T(8,128)(2,1)S(1)}, u32[]{:S(2)}, u32[]{:S(2)}) collective-permute-start(bf16[256,128]{1,0:T(8,128)(2,1)S(1)} %get-tuple-element.6), channel_id=1, source_target_pairs={{0,8},{8,0},{16,24},{24,16},{1,9},{9,1},{17,25},{25,17},{2,10},{10... | collective-permute-start | bytes 196616 | tf_op jit(solution)/shard_map/ppermute | solution.py:77
  99.5 5.0 %collective-permute-start.16 = (bf16[512,128]{1,0:T(8,128)(2,1)S(1)}, bf16[512,128]{1,0:T(8,128)(2,1)S(1)}, u32[]{:S(2)}, u32[]{:S(2)}) collective-permute-start(bf16[512,128]{1,0:T(8,128)(2,1)S(1)} %pad_maximum_fusion.12), channel_id=1, source_target_pairs={{0,16},{8,24},{16,0},{24,8},{1,17},{9,25},{17,1},{25,9},{2,18},{10... | collective-permute-start | bytes 393224 | tf_op jit(solution)/shard_map/ppermute | solution.py:77
  108.0 2.0 collective-permute-start.17
  110.1 8.4 %collective-permute-start.18 = (f32[2,256,128]{2,1,0:T(8,128)S(1)}, f32[2,256,128]{2,1,0:T(8,128)S(1)}, u32[]{:S(2)}, u32[]{:S(2)}) collective-permute-start(f32[2,256,128]{2,1,0:T(8,128)S(1)} %dynamic-slice_bitcast_fusion.7), channel_id=1, source_target_pairs={{0,2},{1,3},{2,0},{3,1},{4,6},{5,7},{6,4},{7,5},{8,10},{9,11},{10,... | collective-permute-start | bytes 786440 | tf_op jit(solution)/shard_map/ppermute | solution.py:63
  118.6 8.5 %collective-permute-start.19 = (f32[1,256,128]{2,1,0:T(8,128)S(1)}, f32[1,256,128]{2,1,0:T(8,128)S(1)}, u32[]{:S(2)}, u32[]{:S(2)}) collective-permute-start(f32[1,256,128]{2,1,0:T(8,128)S(1)} %constant_dynamic-slice_fusion.2), channel_id=1, source_target_pairs={{0,4},{1,5},{2,6},{3,7},{4,0},{5,1},{6,2},{7,3},{8,12},{9,13},{10,... | collective-permute-start | bytes 393224 | tf_op jit(solution)/shard_map/ppermute | solution.py:63
  127.1 4.3 %collective-permute-start.20 = (bf16[256,128]{1,0:T(8,128)(2,1)S(1)}, bf16[256,128]{1,0:T(8,128)(2,1)S(1)}, u32[]{:S(2)}, u32[]{:S(2)}) collective-permute-start(bf16[256,128]{1,0:T(8,128)(2,1)S(1)} %get-tuple-element.4), channel_id=1, source_target_pairs={{0,8},{8,0},{16,24},{24,16},{1,9},{9,1},{17,25},{25,17},{2,10},{10... | collective-permute-start | bytes 196616 | tf_op jit(solution)/shard_map/ppermute | solution.py:77
  131.5 5.0 %collective-permute-start.21 = (bf16[512,128]{1,0:T(8,128)(2,1)S(1)}, bf16[512,128]{1,0:T(8,128)(2,1)S(1)}, u32[]{:S(2)}, u32[]{:S(2)}) collective-permute-start(bf16[512,128]{1,0:T(8,128)(2,1)S(1)} %pad_maximum_fusion.13), channel_id=1, source_target_pairs={{0,16},{8,24},{16,0},{24,8},{1,17},{9,25},{17,1},{25,9},{2,18},{10... | collective-permute-start | bytes 393224 | tf_op jit(solution)/shard_map/ppermute | solution.py:77
  140.3 2.0 collective-permute-start.22
  142.3 8.4 %collective-permute-start.23 = (f32[2,256,128]{2,1,0:T(8,128)S(1)}, f32[2,256,128]{2,1,0:T(8,128)S(1)}, u32[]{:S(2)}, u32[]{:S(2)}) collective-permute-start(f32[2,256,128]{2,1,0:T(8,128)S(1)} %dynamic-slice_bitcast_fusion.6), channel_id=1, source_target_pairs={{0,2},{1,3},{2,0},{3,1},{4,6},{5,7},{6,4},{7,5},{8,10},{9,11},{10,... | collective-permute-start | bytes 786440 | tf_op jit(solution)/shard_map/ppermute | solution.py:63
  150.8 8.5 %collective-permute-start.24 = (f32[1,256,128]{2,1,0:T(8,128)S(1)}, f32[1,256,128]{2,1,0:T(8,128)S(1)}, u32[]{:S(2)}, u32[]{:S(2)}) collective-permute-start(f32[1,256,128]{2,1,0:T(8,128)S(1)} %constant_dynamic-slice_fusion.1), channel_id=1, source_target_pairs={{0,4},{1,5},{2,6},{3,7},{4,0},{5,1},{6,2},{7,3},{8,12},{9,13},{10,... | collective-permute-start | bytes 393224 | tf_op jit(solution)/shard_map/ppermute | solution.py:63
  159.4 4.3 %collective-permute-start.30 = (bf16[256,128]{1,0:T(8,128)(2,1)S(1)}, bf16[256,128]{1,0:T(8,128)(2,1)S(1)}, u32[]{:S(2)}, u32[]{:S(2)}) collective-permute-start(bf16[256,128]{1,0:T(8,128)(2,1)S(1)} %get-tuple-element.2), channel_id=1, source_target_pairs={{0,8},{8,0},{16,24},{24,16},{1,9},{9,1},{17,25},{25,17},{2,10},{10... | collective-permute-start | bytes 196616 | tf_op jit(solution)/shard_map/ppermute | solution.py:77
  163.8 5.0 %collective-permute-start.31 = (bf16[512,128]{1,0:T(8,128)(2,1)S(1)}, bf16[512,128]{1,0:T(8,128)(2,1)S(1)}, u32[]{:S(2)}, u32[]{:S(2)}) collective-permute-start(bf16[512,128]{1,0:T(8,128)(2,1)S(1)} %pad_maximum_fusion.14), channel_id=1, source_target_pairs={{0,16},{8,24},{16,0},{24,8},{1,17},{9,25},{17,1},{25,9},{2,18},{10... | collective-permute-start | bytes 393224 | tf_op jit(solution)/shard_map/ppermute | solution.py:77
  172.3 2.0 collective-permute-start.32
  172.7 2.2 collective-permute-start.25
  174.4 21.6 %collective-permute-start.33 = (f32[2,256,128]{2,1,0:T(8,128)S(1)}, f32[2,256,128]{2,1,0:T(8,128)S(1)}, u32[]{:S(2)}, u32[]{:S(2)}) collective-permute-start(f32[2,256,128]{2,1,0:T(8,128)S(1)} %dynamic-slice_bitcast_fusion.5), channel_id=1, source_target_pairs={{0,2},{1,3},{2,0},{3,1},{4,6},{5,7},{6,4},{7,5},{8,10},{9,11},{10,... | collective-permute-start | bytes 786440 | tf_op jit(solution)/shard_map/ppermute | solution.py:63
  175.0 9.2 %collective-permute-start.26 = (f32[128,128]{0,1:T(8,128)S(1)}, f32[128,128]{0,1:T(8,128)S(1)}, u32[]{:S(2)}, u32[]{:S(2)}) collective-permute-start(f32[128,128]{0,1:T(8,128)S(1)} %add.269), channel_id=1, source_target_pairs={{0,2},{1,3},{2,0},{3,1},{4,6},{5,7},{6,4},{7,5},{8,10},{9,11},{10,... | collective-permute-start | bytes 196616 | tf_op jit(solution)/shard_map/ppermute | solution.py:28
  184.2 5.9 %collective-permute-start.27 = (f32[128,128]{0,1:T(8,128)S(1)}, f32[128,128]{0,1:T(8,128)S(1)}, u32[]{:S(2)}, u32[]{:S(2)}) collective-permute-start(f32[128,128]{0,1:T(8,128)S(1)} %add.270), channel_id=1, source_target_pairs={{0,4},{1,5},{2,6},{3,7},{4,0},{5,1},{6,2},{7,3},{8,12},{9,13},{10,... | collective-permute-start | bytes 196616 | tf_op jit(solution)/shard_map/ppermute | solution.py:28
  190.1 4.3 %collective-permute-start.28 = (f32[128,128]{0,1:T(8,128)S(1)}, f32[128,128]{0,1:T(8,128)S(1)}, u32[]{:S(2)}, u32[]{:S(2)}) collective-permute-start(f32[128,128]{0,1:T(8,128)S(1)} %add.271), channel_id=1, source_target_pairs={{0,8},{8,0},{16,24},{24,16},{1,9},{9,1},{17,25},{25,17},{2,10},{10... | collective-permute-start | bytes 196616 | tf_op jit(solution)/shard_map/ppermute | solution.py:28
  194.5 4.3 %collective-permute-start.29 = (f32[128,128]{0,1:T(8,128)S(1)}, f32[128,128]{0,1:T(8,128)S(1)}, u32[]{:S(2)}, u32[]{:S(2)}) collective-permute-start(f32[128,128]{0,1:T(8,128)S(1)} %add.272), channel_id=1, source_target_pairs={{0,16},{8,24},{16,0},{24,8},{1,17},{9,25},{17,1},{25,9},{2,18},{10... | collective-permute-start | bytes 196616 | tf_op jit(solution)/shard_map/ppermute | solution.py:28
  196.0 7.3 %collective-permute-start.34 = (f32[1,256,128]{2,1,0:T(8,128)S(1)}, f32[1,256,128]{2,1,0:T(8,128)S(1)}, u32[]{:S(2)}, u32[]{:S(2)}) collective-permute-start(f32[1,256,128]{2,1,0:T(8,128)S(1)} %constant_dynamic-slice_fusion), channel_id=1, source_target_pairs={{0,4},{1,5},{2,6},{3,7},{4,0},{5,1},{6,2},{7,3},{8,12},{9,13},{10,... | collective-permute-start | bytes 393224 | tf_op jit(solution)/shard_map/ppermute | solution.py:63
  203.8 11.8 %collective-permute-start.35 = (f32[128,128]{0,1:T(8,128)S(1)}, f32[128,128]{0,1:T(8,128)S(1)}, u32[]{:S(2)}, u32[]{:S(2)}) collective-permute-start(f32[128,128]{0,1:T(8,128)S(1)} %fusion.13), channel_id=1, source_target_pairs={{0,1},{1,0},{2,3},{3,2},{4,5},{5,4},{6,7},{7,6},{8,9},{9,8},{10,11... | collective-permute-start | bytes 196616 | tf_op jit(solution)/shard_map/ppermute | solution.py:28
  215.6 4.6 %collective-permute-start.36 = (f32[128,128]{0,1:T(8,128)S(1)}, f32[128,128]{0,1:T(8,128)S(1)}, u32[]{:S(2)}, u32[]{:S(2)}) collective-permute-start(f32[128,128]{0,1:T(8,128)S(1)} %add.281), channel_id=1, source_target_pairs={{0,2},{1,3},{2,0},{3,1},{4,6},{5,7},{6,4},{7,5},{8,10},{9,11},{10,... | collective-permute-start | bytes 196616 | tf_op jit(solution)/shard_map/ppermute | solution.py:28
  220.2 6.0 %collective-permute-start.37 = (f32[128,128]{0,1:T(8,128)S(1)}, f32[128,128]{0,1:T(8,128)S(1)}, u32[]{:S(2)}, u32[]{:S(2)}) collective-permute-start(f32[128,128]{0,1:T(8,128)S(1)} %add.282), channel_id=1, source_target_pairs={{0,4},{1,5},{2,6},{3,7},{4,0},{5,1},{6,2},{7,3},{8,12},{9,13},{10,... | collective-permute-start | bytes 196616 | tf_op jit(solution)/shard_map/ppermute | solution.py:28
  226.2 12.3 %collective-permute-start.38 = (f32[128,128]{0,1:T(8,128)S(1)}, f32[128,128]{0,1:T(8,128)S(1)}, u32[]{:S(2)}, u32[]{:S(2)}) collective-permute-start(f32[128,128]{0,1:T(8,128)S(1)} %add.283), channel_id=1, source_target_pairs={{0,8},{8,0},{16,24},{24,16},{1,9},{9,1},{17,25},{25,17},{2,10},{10... | collective-permute-start | bytes 196616 | tf_op jit(solution)/shard_map/ppermute | solution.py:28
  238.5 4.3 %collective-permute-start.39 = (f32[128,128]{0,1:T(8,128)S(1)}, f32[128,128]{0,1:T(8,128)S(1)}, u32[]{:S(2)}, u32[]{:S(2)}) collective-permute-start(f32[128,128]{0,1:T(8,128)S(1)} %add.284), channel_id=1, source_target_pairs={{0,16},{8,24},{16,0},{24,8},{1,17},{9,25},{17,1},{25,9},{2,18},{10... | collective-permute-start | bytes 196616 | tf_op jit(solution)/shard_map/ppermute | solution.py:28

commit v4 on v3

--- a/solution.py
+++ b/solution.py
@@ -119,10 +119,10 @@
         following = 2.0 * (applied - center * current) / half_width - previous
         previous, current = (current, following)
     local_gram = jnp.dot(current.T, current, precision=lax.Precision.HIGHEST)
-    gram_total = all_sum(local_gram)
     applied = operate(current)
     local_rayleigh = jnp.dot(current.T, applied, precision=lax.Precision.HIGHEST)
-    rayleigh_total = all_sum(local_rayleigh)
+    totals = all_sum(jnp.concatenate([local_gram, local_rayleigh], axis=0))
+    gram_total, rayleigh_total = totals[: local_gram.shape[0]], totals[local_gram.shape[0] :]
     gram_matrix = gram_total / node_count
     rayleigh = rayleigh_total / node_count
     factor = jnp.linalg.cholesky(gram_matrix)

time: 244 us -> 243 us (level)
  starting transfers between devices: 45.8 us -> 42.7 us
    ppermute x15, waiting for transfers between devices: 65.9 us -> 75.8 us  [halving_scatter_sum(): blocks = kept + lax.ppermute(sent, axis, pairs)]
    ppermute x10 -> x5, waiting for transfers between devices: 27.8 us -> 19.7 us  [butterfly_sum(): value = value + lax.ppermute(value, axis, pairs)]
    ppermute x10 -> x5, starting transfers between devices: 10 us -> 5.87 us  [butterfly_sum(): value = value + lax.ppermute(value, axis, pairs)]
  transfers between devices with their start and end apart: 40 -> 35, of which waited for: 31 -> 30; matrix products, arithmetic and copies ran while one was open for 18% -> 8% of each run, Pallas kernels for 0% -> 0%
where the time goes in v4:
time: 243 us
  waiting for transfers between devices  130 us (53%)
  starting transfers between devices  42.7 us (18%)
  matrix products  32.4 us (13%)
  other arithmetic  31 us (13%)
  between operations  3.98 us (2%)
  local copies, waits for them, and re-layouts  2.47 us (1%)
    ppermute x15, waiting for transfers between devices, halving_scatter_sum(): blocks = kept + lax.ppermute(sent, axis, pairs)  75.8 us
    ppermute x15, waiting for transfers between devices, doubling_gather(): other = lax.ppermute(result, axis, pairs)  34.5 us
    ppermute x15, starting transfers between devices, doubling_gather(): other = lax.ppermute(result, axis, pairs)  22 us
    ppermute x5, waiting for transfers between devices, butterfly_sum(): value = value + lax.ppermute(value, axis, pairs)  19.7 us
    ppermute x15, starting transfers between devices, halving_scatter_sum(): blocks = kept + lax.ppermute(sent, axis, pairs)  14.8 us
    another operation x3, other arithmetic, local(): factor = jnp.linalg.cholesky(gram_matrix)  12.4 us
    dot_general x5, matrix products, operate(): jnp.dot(w_lo, gathered, preferred_element_type=jnp.float32)  10.9 us
    another operation x2, other arithmetic, local(): lax.linalg.triangular_solve(factor, current, left_side=False, lower=True,...  10.6 us
  transfers between devices with their start and end apart: 35, of which 30 were waited for; matrix products, arithmetic and copies ran while one was open for 8% of the time, Pallas kernels for 0%

profile of v4, /device:TPU:0, one launch (start us, length us, event | category | flops | bytes accessed | tf_op | source)
XLA Modules:
  0.0 242.6 jit_solution(9225020811573849811)
XLA Ops:
  1.2 2.6 %collective-permute-start.5 = (bf16[256,128]{1,0:T(8,128)(2,1)}, bf16[256,128]{1,0:T(8,128)(2,1)S(1)}, u32[]{:S(2)}, u32[]{:S(2)}) collective-permute-start(bf16[256,128]{1,0:T(8,128)(2,1)} %param.11), channel_id=1, source_target_pairs={{0,8},{8,0},{16,24},{24,16},{1,9},{9,1},{17,25},{25,17},{2,10},{10... | collective-permute-start | bytes 196616 | tf_op jit(solution)/shard_map/ppermute | solution.py:77
  4.8 8.2 %fusion.1 = f32[16,8,128,128]{3,1,2,0:T(8,128)S(1)} fusion(bf16[16,16,128,128]{3,2,1,0:T(8,128)(2,1)} %param.7, s32[16,16]{1,0:T(8,128)} %param.8), kind=kOutput, calls=%fused_computation.3 | convolution fusion | flops 67110912 | bytes 16778240 | tf_op jit(solution)/shard_map/rst,rsab->ratb/dot_general | solution.py:94
  13.1 5.2 %fusion = (bf16[2048,1024]{1,0:T(8,128)(2,1)}, bf16[2048,1024]{1,0:T(8,128)(2,1)}) fusion(f32[256,8,8,128]{3,2,1,0:T(8,128)S(1)} %bitcast.137), kind=kLoop, calls=%fused_computation.2 | loop fusion | flops 6291456 | bytes 16777216 | tf_op jit(solution)/shard_map/convert_element_type | solution.py:11
  18.5 2.2 collective-permute-start.3
  20.6 1.6 collective-permute-start.1
  24.3 2.8 %collective-permute-start.4 = (bf16[1024,128]{1,0:T(8,128)(2,1)S(1)}, bf16[1024,128]{1,0:T(8,128)(2,1)S(1)}, u32[]{:S(2)}, u32[]{:S(2)}) collective-permute-start(bf16[1024,128]{1,0:T(8,128)(2,1)S(1)} %pad_maximum_fusion.2), channel_id=1, source_target_pairs={{0,4},{1,5},{2,6},{3,7},{4,0},{5,1},{6,2},{7,3},{8,12},{9,13},{10,... | collective-permute-start | bytes 786440 | tf_op jit(solution)/shard_map/ppermute | solution.py:77
  27.1 3.5 %fusion.34 = f32[2048,128]{1,0:T(8,128)S(1)} fusion(bf16[2048,1024]{1,0:T(8,128)(2,1)} %get-tuple-element.10, bf16[512,128]{1,0:T(8,128)(2,1)S(1)} %get-tuple-element.27, bf16[512,128]{1,0:T(8,128)(2,1)S(1)} %get-tuple-element.26), kind=kOutput, calls=%fused_computation.113 | convolution fusion | flops 537395200 | bytes 5505024 | tf_op jit(solution)/shard_map/dot_general | solution.py:105
  31.0 7.4 %collective-permute-done.4 = bf16[1024,128]{1,0:T(8,128)(2,1)S(1)} collective-permute-done((bf16[1024,128]{1,0:T(8,128)(2,1)S(1)}, bf16[1024,128]{1,0:T(8,128)(2,1)S(1)}, u32[]{:S(2)}, u32[]{:S(2)}) %collective-permute-start.4) | collective-permute-done | bytes 262176 | tf_op jit(solution)/shard_map/ppermute | solution.py:77
  40.5 1.9 collective-permute-done.7
  43.1 7.8 %collective-permute-done.8 = f32[2,256,128]{2,1,0:T(8,128)S(1)} collective-permute-done((f32[2,256,128]{2,1,0:T(8,128)S(1)}, f32[2,256,128]{2,1,0:T(8,128)S(1)}, u32[]{:S(2)}, u32[]{:S(2)}) %collective-permute-start.8) | collective-permute-done | bytes 262176 | tf_op jit(solution)/shard_map/ppermute | solution.py:63
  50.9 2.3 collective-permute-start.9
  56.4 3.0 %collective-permute-done.9 = f32[1,256,128]{2,1,0:T(8,128)S(1)} collective-permute-done((f32[1,256,128]{2,1,0:T(8,128)S(1)}, f32[1,256,128]{2,1,0:T(8,128)S(1)}, u32[]{:S(2)}, u32[]{:S(2)}) %collective-permute-start.9) | collective-permute-done | bytes 131104 | tf_op jit(solution)/shard_map/ppermute | solution.py:63
  60.9 2.9 %collective-permute-done.10 = bf16[256,128]{1,0:T(8,128)(2,1)S(1)} collective-permute-done((bf16[256,128]{1,0:T(8,128)(2,1)S(1)}, bf16[256,128]{1,0:T(8,128)(2,1)S(1)}, u32[]{:S(2)}, u32[]{:S(2)}) %collective-permute-start.10) | collective-permute-done | bytes 65568 | tf_op jit(solution)/shard_map/ppermute | solution.py:77
  63.9 1.5 collective-permute-start.11
  65.3 3.6 %collective-permute-done.11 = bf16[512,128]{1,0:T(8,128)(2,1)S(1)} collective-permute-done((bf16[512,128]{1,0:T(8,128)(2,1)S(1)}, bf16[512,128]{1,0:T(8,128)(2,1)S(1)}, u32[]{:S(2)}, u32[]{:S(2)}) %collective-permute-start.11) | collective-permute-done | bytes 131104 | tf_op jit(solution)/shard_map/ppermute | solution.py:77
  68.9 3.5 %fusion.33 = f32[2048,128]{1,0:T(8,128)S(1)} fusion(bf16[2048,1024]{1,0:T(8,128)(2,1)} %get-tuple-element.10, bf16[512,128]{1,0:T(8,128)(2,1)S(1)} %get-tuple-element.21, bf16[512,128]{1,0:T(8,128)(2,1)S(1)} %get-tuple-element.20), kind=kOutput, calls=%fused_computation.112 | convolution fusion | flops 537395200 | bytes 5505024 | tf_op jit(solution)/shard_map/dot_general | solution.py:105
  76.0 1.9 collective-permute-done.12
  78.7 7.8 %collective-permute-done.13 = f32[2,256,128]{2,1,0:T(8,128)S(1)} collective-permute-done((f32[2,256,128]{2,1,0:T(8,128)S(1)}, f32[2,256,128]{2,1,0:T(8,128)S(1)}, u32[]{:S(2)}, u32[]{:S(2)}) %collective-permute-start.13) | collective-permute-done | bytes 262176 | tf_op jit(solution)/shard_map/ppermute | solution.py:63
  86.5 2.3 collective-permute-start.14
  88.8 6.2 %collective-permute-done.14 = f32[1,256,128]{2,1,0:T(8,128)S(1)} collective-permute-done((f32[1,256,128]{2,1,0:T(8,128)S(1)}, f32[1,256,128]{2,1,0:T(8,128)S(1)}, u32[]{:S(2)}, u32[]{:S(2)}) %collective-permute-start.14) | collective-permute-done | bytes 131104 | tf_op jit(solution)/shard_map/ppermute | solution.py:63
  96.5 2.9 %collective-permute-done.15 = bf16[256,128]{1,0:T(8,128)(2,1)S(1)} collective-permute-done((bf16[256,128]{1,0:T(8,128)(2,1)S(1)}, bf16[256,128]{1,0:T(8,128)(2,1)S(1)}, u32[]{:S(2)}, u32[]{:S(2)}) %collective-permute-start.15) | collective-permute-done | bytes 65568 | tf_op jit(solution)/shard_map/ppermute | solution.py:77
  99.4 1.5 collective-permute-start.16
  100.9 3.6 %collective-permute-done.16 = bf16[512,128]{1,0:T(8,128)(2,1)S(1)} collective-permute-done((bf16[512,128]{1,0:T(8,128)(2,1)S(1)}, bf16[512,128]{1,0:T(8,128)(2,1)S(1)}, u32[]{:S(2)}, u32[]{:S(2)}) %collective-permute-start.16) | collective-permute-done | bytes 131104 | tf_op jit(solution)/shard_map/ppermute | solution.py:77
  108.0 1.9 collective-permute-done.17
  110.7 7.8 %collective-permute-done.18 = f32[2,256,128]{2,1,0:T(8,128)S(1)} collective-permute-done((f32[2,256,128]{2,1,0:T(8,128)S(1)}, f32[2,256,128]{2,1,0:T(8,128)S(1)}, u32[]{:S(2)}, u32[]{:S(2)}) %collective-permute-start.18) | collective-permute-done | bytes 262176 | tf_op jit(solution)/shard_map/ppermute | solution.py:63
  118.5 2.3 collective-permute-start.19
  120.8 6.2 %collective-permute-done.19 = f32[1,256,128]{2,1,0:T(8,128)S(1)} collective-permute-done((f32[1,256,128]{2,1,0:T(8,128)S(1)}, f32[1,256,128]{2,1,0:T(8,128)S(1)}, u32[]{:S(2)}, u32[]{:S(2)}) %collective-permute-start.19) | collective-permute-done | bytes 131104 | tf_op jit(solution)/shard_map/ppermute | solution.py:63
  128.5 2.9 %collective-permute-done.20 = bf16[256,128]{1,0:T(8,128)(2,1)S(1)} collective-permute-done((bf16[256,128]{1,0:T(8,128)(2,1)S(1)}, bf16[256,128]{1,0:T(8,128)(2,1)S(1)}, u32[]{:S(2)}, u32[]{:S(2)}) %collective-permute-start.20) | collective-permute-done | bytes 65568 | tf_op jit(solution)/shard_map/ppermute | solution.py:77
  132.9 3.6 %collective-permute-done.21 = bf16[512,128]{1,0:T(8,128)(2,1)S(1)} collective-permute-done((bf16[512,128]{1,0:T(8,128)(2,1)S(1)}, bf16[512,128]{1,0:T(8,128)(2,1)S(1)}, u32[]{:S(2)}, u32[]{:S(2)}) %collective-permute-start.21) | collective-permute-done | bytes 131104 | tf_op jit(solution)/shard_map/ppermute | solution.py:77
  136.5 1.5 fusion.31
  140.3 1.9 collective-permute-done.22
  142.9 7.8 %collective-permute-done.23 = f32[2,256,128]{2,1,0:T(8,128)S(1)} collective-permute-done((f32[2,256,128]{2,1,0:T(8,128)S(1)}, f32[2,256,128]{2,1,0:T(8,128)S(1)}, u32[]{:S(2)}, u32[]{:S(2)}) %collective-permute-start.23) | collective-permute-done | bytes 262176 | tf_op jit(solution)/shard_map/ppermute | solution.py:63
  150.8 2.3 collective-permute-start.24
  153.0 6.2 %collective-permute-done.24 = f32[1,256,128]{2,1,0:T(8,128)S(1)} collective-permute-done((f32[1,256,128]{2,1,0:T(8,128)S(1)}, f32[1,256,128]{2,1,0:T(8,128)S(1)}, u32[]{:S(2)}, u32[]{:S(2)}) %collective-permute-start.24) | collective-permute-done | bytes 131104 | tf_op jit(solution)/shard_map/ppermute | solution.py:63
  160.8 2.9 %collective-permute-done.25 = bf16[256,128]{1,0:T(8,128)(2,1)S(1)} collective-permute-done((bf16[256,128]{1,0:T(8,128)(2,1)S(1)}, bf16[256,128]{1,0:T(8,128)(2,1)S(1)}, u32[]{:S(2)}, u32[]{:S(2)}) %collective-permute-start.25) | collective-permute-done | bytes 65568 | tf_op jit(solution)/shard_map/ppermute | solution.py:77
  163.7 1.5 collective-permute-start.26
  165.2 3.6 %collective-permute-done.26 = bf16[512,128]{1,0:T(8,128)(2,1)S(1)} collective-permute-done((bf16[512,128]{1,0:T(8,128)(2,1)S(1)}, bf16[512,128]{1,0:T(8,128)(2,1)S(1)}, u32[]{:S(2)}, u32[]{:S(2)}) %collective-permute-start.26) | collective-permute-done | bytes 131104 | tf_op jit(solution)/shard_map/ppermute | solution.py:77
  172.3 1.9 collective-permute-done.27
  174.9 7.8 %collective-permute-done.28 = f32[2,256,128]{2,1,0:T(8,128)S(1)} collective-permute-done((f32[2,256,128]{2,1,0:T(8,128)S(1)}, f32[2,256,128]{2,1,0:T(8,128)S(1)}, u32[]{:S(2)}, u32[]{:S(2)}) %collective-permute-start.28) | collective-permute-done | bytes 262176 | tf_op jit(solution)/shard_map/ppermute | solution.py:63
  182.8 2.3 collective-permute-start.29
  185.4 5.8 %collective-permute-done.29 = f32[1,256,128]{2,1,0:T(8,128)S(1)} collective-permute-done((f32[1,256,128]{2,1,0:T(8,128)S(1)}, f32[1,256,128]{2,1,0:T(8,128)S(1)}, u32[]{:S(2)}, u32[]{:S(2)}) %collective-permute-start.29) | collective-permute-done | bytes 131104 | tf_op jit(solution)/shard_map/ppermute | solution.py:63
  193.7 5.0 %collective-permute-done.31 = f32[256,128]{0,1:T(8,128)S(1)} collective-permute-done((f32[256,128]{0,1:T(8,128)S(1)}, f32[256,128]{0,1:T(8,128)S(1)}, u32[]{:S(2)}, u32[]{:S(2)}) %collective-permute-start.31) | collective-permute-done | bytes 131104 | tf_op jit(solution)/shard_map/ppermute | solution.py:28
  198.8 2.3 collective-permute-start.32
  201.0 6.2 %collective-permute-done.32 = f32[256,128]{0,1:T(8,128)S(1)} collective-permute-done((f32[256,128]{0,1:T(8,128)S(1)}, f32[256,128]{0,1:T(8,128)S(1)}, u32[]{:S(2)}, u32[]{:S(2)}) %collective-permute-start.32) | collective-permute-done | bytes 131104 | tf_op jit(solution)/shard_map/ppermute | solution.py:28
  208.7 3.6 %collective-permute-done.33 = f32[256,128]{0,1:T(8,128)S(1)} collective-permute-done((f32[256,128]{0,1:T(8,128)S(1)}, f32[256,128]{0,1:T(8,128)S(1)}, u32[]{:S(2)}, u32[]{:S(2)}) %collective-permute-start.33) | collective-permute-done | bytes 131104 | tf_op jit(solution)/shard_map/ppermute | solution.py:28
  213.8 3.6 %collective-permute-done.34 = f32[256,128]{0,1:T(8,128)S(1)} collective-permute-done((f32[256,128]{0,1:T(8,128)S(1)}, f32[256,128]{0,1:T(8,128)S(1)}, u32[]{:S(2)}, u32[]{:S(2)}) %collective-permute-start.34) | collective-permute-done | bytes 131104 | tf_op jit(solution)/shard_map/ppermute | solution.py:28
  217.5 11.7 %cholesky.16 = f32[128,128]{1,0:T(8,128)S(1)} custom-call(f32[128,128]{1,0:T(8,128)S(1)} %fusion.42), custom_call_target="Cholesky" | custom-call | tf_op jit(solution)/shard_map/jit(cholesky)/cholesky | solution.py:128
  230.5 10.0 %custom-call.10 = f32[1,128,128]{1,2,0:T(8,128)S(1)} custom-call(f32[1,128,128]{2,1,0:T(8,128)S(1)} %fusion.35), custom_call_target="InvertDiagBlocksLowerTriangular" | custom-call | tf_op jit(solution)/shard_map/triangular_solve | solution.py:129
  (136 shorter events, 40.7 us)
Async XLA Ops:
  0.6 17.7 %collective-permute-start.2 = (bf16[256,128]{1,0:T(8,128)(2,1)}, bf16[256,128]{1,0:T(8,128)(2,1)S(1)}, u32[]{:S(2)}, u32[]{:S(2)}) collective-permute-start(bf16[256,128]{1,0:T(8,128)(2,1)} %param.11), channel_id=1, source_target_pairs={{0,1},{1,0},{2,3},{3,2},{4,5},{5,4},{6,7},{7,6},{8,9},{9,8},{10,11... | collective-permute-start | bytes 196616 | tf_op jit(solution)/shard_map/ppermute | solution.py:77
  1.2 17.1 %collective-permute-start.5 = (bf16[256,128]{1,0:T(8,128)(2,1)}, bf16[256,128]{1,0:T(8,128)(2,1)S(1)}, u32[]{:S(2)}, u32[]{:S(2)}) collective-permute-start(bf16[256,128]{1,0:T(8,128)(2,1)} %param.11), channel_id=1, source_target_pairs={{0,8},{8,0},{16,24},{24,16},{1,9},{9,1},{17,25},{25,17},{2,10},{10... | collective-permute-start | bytes 196616 | tf_op jit(solution)/shard_map/ppermute | solution.py:77
  4.8 13.5 %collective-permute-start = (bf16[256,128]{1,0:T(8,128)(2,1)S(1)}, bf16[256,128]{1,0:T(8,128)(2,1)S(1)}, u32[]{:S(2)}, u32[]{:S(2)}) collective-permute-start(bf16[256,128]{1,0:T(8,128)(2,1)S(1)} %multiply_convert_fusion.4), channel_id=1, source_target_pairs={{0,8},{8,0},{16,24},{24,16},{1,9},{9,1},{17,25},{25,17},{2,10},{10... | collective-permute-start | bytes 196616 | tf_op jit(solution)/shard_map/ppermute | solution.py:77
  13.0 5.3 %copy-start.3 = (f32[256,128]{1,0:T(8,128)S(1)}, f32[256,128]{1,0:T(8,128)}, u32[]{:S(2)}) copy-start(f32[256,128]{1,0:T(8,128)} %param.10) | copy-start | bytes 393220
  13.0 5.3 %copy-start.4 = (bf16[256,128]{1,0:T(8,128)(2,1)S(1)}, bf16[256,128]{1,0:T(8,128)(2,1)}, u32[]{:S(2)}) copy-start(bf16[256,128]{1,0:T(8,128)(2,1)} %param.11) | copy-start | bytes 196612
  13.0 5.3 %copy-start.5 = (f32[256]{0:T(256)S(1)}, f32[256]{0:T(256)}, u32[]{:S(2)}) copy-start(f32[256]{0:T(256)} %param.9) | copy-start | bytes 3076
  18.5 5.7 %collective-permute-start.3 = (bf16[512,128]{1,0:T(8,128)(2,1)S(1)}, bf16[512,128]{1,0:T(8,128)(2,1)S(1)}, u32[]{:S(2)}, u32[]{:S(2)}) collective-permute-start(bf16[512,128]{1,0:T(8,128)(2,1)S(1)} %pad_maximum_fusion.9), channel_id=1, source_target_pairs={{0,2},{1,3},{2,0},{3,1},{4,6},{5,7},{6,4},{7,5},{8,10},{9,11},{10,... | collective-permute-start | bytes 393224 | tf_op jit(solution)/shard_map/ppermute | solution.py:77
  20.6 6.4 %collective-permute-start.1 = (bf16[512,128]{1,0:T(8,128)(2,1)S(1)}, bf16[512,128]{1,0:T(8,128)(2,1)S(1)}, u32[]{:S(2)}, u32[]{:S(2)}) collective-permute-start(bf16[512,128]{1,0:T(8,128)(2,1)S(1)} %pad_maximum_fusion.8), channel_id=1, source_target_pairs={{0,16},{8,24},{16,0},{24,8},{1,17},{9,25},{17,1},{25,9},{2,18},{10... | collective-permute-start | bytes 393224 | tf_op jit(solution)/shard_map/ppermute | solution.py:77
  22.2 8.4 %collective-permute-start.6 = (bf16[512,128]{1,0:T(8,128)(2,1)S(1)}, bf16[512,128]{1,0:T(8,128)(2,1)S(1)}, u32[]{:S(2)}, u32[]{:S(2)}) collective-permute-start(bf16[512,128]{1,0:T(8,128)(2,1)S(1)} %pad_maximum_fusion.10), channel_id=1, source_target_pairs={{0,16},{8,24},{16,0},{24,8},{1,17},{9,25},{17,1},{25,9},{2,18},{10... | collective-permute-start | bytes 393224 | tf_op jit(solution)/shard_map/ppermute | solution.py:77
  24.2 6.5 %copy-start.7 = (f32[128]{0:T(128)S(1)}, f32[128]{0:T(128)}, u32[]{:S(2)}) copy-start(f32[128]{0:T(128)} %param.12) | copy-start | bytes 1540
  24.3 14.1 %collective-permute-start.4 = (bf16[1024,128]{1,0:T(8,128)(2,1)S(1)}, bf16[1024,128]{1,0:T(8,128)(2,1)S(1)}, u32[]{:S(2)}, u32[]{:S(2)}) collective-permute-start(bf16[1024,128]{1,0:T(8,128)(2,1)S(1)} %pad_maximum_fusion.2), channel_id=1, source_target_pairs={{0,4},{1,5},{2,6},{3,7},{4,0},{5,1},{6,2},{7,3},{8,12},{9,13},{10,... | collective-permute-start | bytes 786440 | tf_op jit(solution)/shard_map/ppermute | solution.py:77
  30.6 8.4 %copy-start = (bf16[2048,1024]{1,0:T(8,128)(2,1)S(1)}, bf16[2048,1024]{1,0:T(8,128)(2,1)}, u32[]{:S(2)}) copy-start(bf16[2048,1024]{1,0:T(8,128)(2,1)} %get-tuple-element.11) | copy-start | bytes 12582916
  40.3 12.9 %copy-start.6 = (f32[2]{0:T(128)S(1)}, f32[2]{0:T(128)}, u32[]{:S(2)}) copy-start(f32[2]{0:T(128)} %param.13) | copy-start | bytes 28
  40.4 2.0 collective-permute-start.7
  42.5 8.4 %collective-permute-start.8 = (f32[2,256,128]{2,1,0:T(8,128)S(1)}, f32[2,256,128]{2,1,0:T(8,128)S(1)}, u32[]{:S(2)}, u32[]{:S(2)}) collective-permute-start(f32[2,256,128]{2,1,0:T(8,128)S(1)} %dynamic-slice_bitcast_fusion.9), channel_id=1, source_target_pairs={{0,2},{1,3},{2,0},{3,1},{4,6},{5,7},{6,4},{7,5},{8,10},{9,11},{10,... | collective-permute-start | bytes 786440 | tf_op jit(solution)/shard_map/ppermute | solution.py:63
  50.9 8.5 %collective-permute-start.9 = (f32[1,256,128]{2,1,0:T(8,128)S(1)}, f32[1,256,128]{2,1,0:T(8,128)S(1)}, u32[]{:S(2)}, u32[]{:S(2)}) collective-permute-start(f32[1,256,128]{2,1,0:T(8,128)S(1)} %constant_dynamic-slice_fusion.4), channel_id=1, source_target_pairs={{0,4},{1,5},{2,6},{3,7},{4,0},{5,1},{6,2},{7,3},{8,12},{9,13},{10,... | collective-permute-start | bytes 393224 | tf_op jit(solution)/shard_map/ppermute | solution.py:63
  59.5 4.3 %collective-permute-start.10 = (bf16[256,128]{1,0:T(8,128)(2,1)S(1)}, bf16[256,128]{1,0:T(8,128)(2,1)S(1)}, u32[]{:S(2)}, u32[]{:S(2)}) collective-permute-start(bf16[256,128]{1,0:T(8,128)(2,1)S(1)} %get-tuple-element.8), channel_id=1, source_target_pairs={{0,8},{8,0},{16,24},{24,16},{1,9},{9,1},{17,25},{25,17},{2,10},{10... | collective-permute-start | bytes 196616 | tf_op jit(solution)/shard_map/ppermute | solution.py:77
  63.9 5.0 %collective-permute-start.11 = (bf16[512,128]{1,0:T(8,128)(2,1)S(1)}, bf16[512,128]{1,0:T(8,128)(2,1)S(1)}, u32[]{:S(2)}, u32[]{:S(2)}) collective-permute-start(bf16[512,128]{1,0:T(8,128)(2,1)S(1)} %pad_maximum_fusion.11), channel_id=1, source_target_pairs={{0,16},{8,24},{16,0},{24,8},{1,17},{9,25},{17,1},{25,9},{2,18},{10... | collective-permute-start | bytes 393224 | tf_op jit(solution)/shard_map/ppermute | solution.py:77
  72.4 2.2 copy-start.1
  75.9 28.7 %copy-start.2 = (bf16[2048,1024]{1,0:T(8,128)(2,1)S(1)}, bf16[2048,1024]{1,0:T(8,128)(2,1)}, u32[]{:S(2)}) copy-start(bf16[2048,1024]{1,0:T(8,128)(2,1)} %get-tuple-element.10) | copy-start | bytes 12582916
  75.9 2.0 collective-permute-start.12
  78.0 8.4 %collective-permute-start.13 = (f32[2,256,128]{2,1,0:T(8,128)S(1)}, f32[2,256,128]{2,1,0:T(8,128)S(1)}, u32[]{:S(2)}, u32[]{:S(2)}) collective-permute-start(f32[2,256,128]{2,1,0:T(8,128)S(1)} %dynamic-slice_bitcast_fusion.8), channel_id=1, source_target_pairs={{0,2},{1,3},{2,0},{3,1},{4,6},{5,7},{6,4},{7,5},{8,10},{9,11},{10,... | collective-permute-start | bytes 786440 | tf_op jit(solution)/shard_map/ppermute | solution.py:63
  86.5 8.5 %collective-permute-start.14 = (f32[1,256,128]{2,1,0:T(8,128)S(1)}, f32[1,256,128]{2,1,0:T(8,128)S(1)}, u32[]{:S(2)}, u32[]{:S(2)}) collective-permute-start(f32[1,256,128]{2,1,0:T(8,128)S(1)} %constant_dynamic-slice_fusion.3), channel_id=1, source_target_pairs={{0,4},{1,5},{2,6},{3,7},{4,0},{5,1},{6,2},{7,3},{8,12},{9,13},{10,... | collective-permute-start | bytes 393224 | tf_op jit(solution)/shard_map/ppermute | solution.py:63
  95.1 4.3 %collective-permute-start.15 = (bf16[256,128]{1,0:T(8,128)(2,1)S(1)}, bf16[256,128]{1,0:T(8,128)(2,1)S(1)}, u32[]{:S(2)}, u32[]{:S(2)}) collective-permute-start(bf16[256,128]{1,0:T(8,128)(2,1)S(1)} %get-tuple-element.6), channel_id=1, source_target_pairs={{0,8},{8,0},{16,24},{24,16},{1,9},{9,1},{17,25},{25,17},{2,10},{10... | collective-permute-start | bytes 196616 | tf_op jit(solution)/shard_map/ppermute | solution.py:77
  99.4 5.0 %collective-permute-start.16 = (bf16[512,128]{1,0:T(8,128)(2,1)S(1)}, bf16[512,128]{1,0:T(8,128)(2,1)S(1)}, u32[]{:S(2)}, u32[]{:S(2)}) collective-permute-start(bf16[512,128]{1,0:T(8,128)(2,1)S(1)} %pad_maximum_fusion.12), channel_id=1, source_target_pairs={{0,16},{8,24},{16,0},{24,8},{1,17},{9,25},{17,1},{25,9},{2,18},{10... | collective-permute-start | bytes 393224 | tf_op jit(solution)/shard_map/ppermute | solution.py:77
  108.0 2.0 collective-permute-start.17
  110.0 8.4 %collective-permute-start.18 = (f32[2,256,128]{2,1,0:T(8,128)S(1)}, f32[2,256,128]{2,1,0:T(8,128)S(1)}, u32[]{:S(2)}, u32[]{:S(2)}) collective-permute-start(f32[2,256,128]{2,1,0:T(8,128)S(1)} %dynamic-slice_bitcast_fusion.7), channel_id=1, source_target_pairs={{0,2},{1,3},{2,0},{3,1},{4,6},{5,7},{6,4},{7,5},{8,10},{9,11},{10,... | collective-permute-start | bytes 786440 | tf_op jit(solution)/shard_map/ppermute | solution.py:63
  118.5 8.5 %collective-permute-start.19 = (f32[1,256,128]{2,1,0:T(8,128)S(1)}, f32[1,256,128]{2,1,0:T(8,128)S(1)}, u32[]{:S(2)}, u32[]{:S(2)}) collective-permute-start(f32[1,256,128]{2,1,0:T(8,128)S(1)} %constant_dynamic-slice_fusion.2), channel_id=1, source_target_pairs={{0,4},{1,5},{2,6},{3,7},{4,0},{5,1},{6,2},{7,3},{8,12},{9,13},{10,... | collective-permute-start | bytes 393224 | tf_op jit(solution)/shard_map/ppermute | solution.py:63
  127.1 4.3 %collective-permute-start.20 = (bf16[256,128]{1,0:T(8,128)(2,1)S(1)}, bf16[256,128]{1,0:T(8,128)(2,1)S(1)}, u32[]{:S(2)}, u32[]{:S(2)}) collective-permute-start(bf16[256,128]{1,0:T(8,128)(2,1)S(1)} %get-tuple-element.4), channel_id=1, source_target_pairs={{0,8},{8,0},{16,24},{24,16},{1,9},{9,1},{17,25},{25,17},{2,10},{10... | collective-permute-start | bytes 196616 | tf_op jit(solution)/shard_map/ppermute | solution.py:77
  131.4 5.0 %collective-permute-start.21 = (bf16[512,128]{1,0:T(8,128)(2,1)S(1)}, bf16[512,128]{1,0:T(8,128)(2,1)S(1)}, u32[]{:S(2)}, u32[]{:S(2)}) collective-permute-start(bf16[512,128]{1,0:T(8,128)(2,1)S(1)} %pad_maximum_fusion.13), channel_id=1, source_target_pairs={{0,16},{8,24},{16,0},{24,8},{1,17},{9,25},{17,1},{25,9},{2,18},{10... | collective-permute-start | bytes 393224 | tf_op jit(solution)/shard_map/ppermute | solution.py:77
  140.2 2.0 collective-permute-start.22
  142.3 8.4 %collective-permute-start.23 = (f32[2,256,128]{2,1,0:T(8,128)S(1)}, f32[2,256,128]{2,1,0:T(8,128)S(1)}, u32[]{:S(2)}, u32[]{:S(2)}) collective-permute-start(f32[2,256,128]{2,1,0:T(8,128)S(1)} %dynamic-slice_bitcast_fusion.6), channel_id=1, source_target_pairs={{0,2},{1,3},{2,0},{3,1},{4,6},{5,7},{6,4},{7,5},{8,10},{9,11},{10,... | collective-permute-start | bytes 786440 | tf_op jit(solution)/shard_map/ppermute | solution.py:63
  150.8 8.5 %collective-permute-start.24 = (f32[1,256,128]{2,1,0:T(8,128)S(1)}, f32[1,256,128]{2,1,0:T(8,128)S(1)}, u32[]{:S(2)}, u32[]{:S(2)}) collective-permute-start(f32[1,256,128]{2,1,0:T(8,128)S(1)} %constant_dynamic-slice_fusion.1), channel_id=1, source_target_pairs={{0,4},{1,5},{2,6},{3,7},{4,0},{5,1},{6,2},{7,3},{8,12},{9,13},{10,... | collective-permute-start | bytes 393224 | tf_op jit(solution)/shard_map/ppermute | solution.py:63
  159.3 4.3 %collective-permute-start.25 = (bf16[256,128]{1,0:T(8,128)(2,1)S(1)}, bf16[256,128]{1,0:T(8,128)(2,1)S(1)}, u32[]{:S(2)}, u32[]{:S(2)}) collective-permute-start(bf16[256,128]{1,0:T(8,128)(2,1)S(1)} %get-tuple-element.2), channel_id=1, source_target_pairs={{0,8},{8,0},{16,24},{24,16},{1,9},{9,1},{17,25},{25,17},{2,10},{10... | collective-permute-start | bytes 196616 | tf_op jit(solution)/shard_map/ppermute | solution.py:77
  163.7 5.0 %collective-permute-start.26 = (bf16[512,128]{1,0:T(8,128)(2,1)S(1)}, bf16[512,128]{1,0:T(8,128)(2,1)S(1)}, u32[]{:S(2)}, u32[]{:S(2)}) collective-permute-start(bf16[512,128]{1,0:T(8,128)(2,1)S(1)} %pad_maximum_fusion.14), channel_id=1, source_target_pairs={{0,16},{8,24},{16,0},{24,8},{1,17},{9,25},{17,1},{25,9},{2,18},{10... | collective-permute-start | bytes 393224 | tf_op jit(solution)/shard_map/ppermute | solution.py:77
  172.2 2.0 collective-permute-start.27
  174.3 8.4 %collective-permute-start.28 = (f32[2,256,128]{2,1,0:T(8,128)S(1)}, f32[2,256,128]{2,1,0:T(8,128)S(1)}, u32[]{:S(2)}, u32[]{:S(2)}) collective-permute-start(f32[2,256,128]{2,1,0:T(8,128)S(1)} %dynamic-slice_bitcast_fusion.5), channel_id=1, source_target_pairs={{0,2},{1,3},{2,0},{3,1},{4,6},{5,7},{6,4},{7,5},{8,10},{9,11},{10,... | collective-permute-start | bytes 786440 | tf_op jit(solution)/shard_map/ppermute | solution.py:63
  182.8 8.5 %collective-permute-start.29 = (f32[1,256,128]{2,1,0:T(8,128)S(1)}, f32[1,256,128]{2,1,0:T(8,128)S(1)}, u32[]{:S(2)}, u32[]{:S(2)}) collective-permute-start(f32[1,256,128]{2,1,0:T(8,128)S(1)} %constant_dynamic-slice_fusion), channel_id=1, source_target_pairs={{0,4},{1,5},{2,6},{3,7},{4,0},{5,1},{6,2},{7,3},{8,12},{9,13},{10,... | collective-permute-start | bytes 393224 | tf_op jit(solution)/shard_map/ppermute | solution.py:63
  191.7 1.4 collective-permute-start.30
  193.1 5.6 %collective-permute-start.31 = (f32[256,128]{0,1:T(8,128)S(1)}, f32[256,128]{0,1:T(8,128)S(1)}, u32[]{:S(2)}, u32[]{:S(2)}) collective-permute-start(f32[256,128]{0,1:T(8,128)S(1)} %fusion.80), channel_id=1, source_target_pairs={{0,2},{1,3},{2,0},{3,1},{4,6},{5,7},{6,4},{7,5},{8,10},{9,11},{10,... | collective-permute-start | bytes 393224 | tf_op jit(solution)/shard_map/ppermute | solution.py:28
  198.8 8.5 %collective-permute-start.32 = (f32[256,128]{0,1:T(8,128)S(1)}, f32[256,128]{0,1:T(8,128)S(1)}, u32[]{:S(2)}, u32[]{:S(2)}) collective-permute-start(f32[256,128]{0,1:T(8,128)S(1)} %add.261), channel_id=1, source_target_pairs={{0,4},{1,5},{2,6},{3,7},{4,0},{5,1},{6,2},{7,3},{8,12},{9,13},{10,... | collective-permute-start | bytes 393224 | tf_op jit(solution)/shard_map/ppermute | solution.py:28
  207.2 5.0 %collective-permute-start.33 = (f32[256,128]{0,1:T(8,128)S(1)}, f32[256,128]{0,1:T(8,128)S(1)}, u32[]{:S(2)}, u32[]{:S(2)}) collective-permute-start(f32[256,128]{0,1:T(8,128)S(1)} %add.262), channel_id=1, source_target_pairs={{0,8},{8,0},{16,24},{24,16},{1,9},{9,1},{17,25},{25,17},{2,10},{10... | collective-permute-start | bytes 393224 | tf_op jit(solution)/shard_map/ppermute | solution.py:28
  212.3 5.0 %collective-permute-start.34 = (f32[256,128]{0,1:T(8,128)S(1)}, f32[256,128]{0,1:T(8,128)S(1)}, u32[]{:S(2)}, u32[]{:S(2)}) collective-permute-start(f32[256,128]{0,1:T(8,128)S(1)} %add.263), channel_id=1, source_target_pairs={{0,16},{8,24},{16,0},{24,8},{1,17},{9,25},{17,1},{25,9},{2,18},{10... | collective-permute-start | bytes 393224 | tf_op jit(solution)/shard_map/ppermute | solution.py:28

commit v5 on v4

--- a/solution.py
+++ b/solution.py
@@ -83,6 +83,25 @@
     return result
 
 
+def direct_gather(value, axis):
+    size = lax.axis_size(axis)
+    here = lax.axis_index(axis)
+    parts = [value]
+    for shift in range(1, size):
+        pairs = [(index, (index + shift) % size) for index in range(size)]
+        parts.append(lax.ppermute(value, axis, pairs))
+    stacked = jnp.stack(parts)
+    order = (here - jnp.arange(size, dtype=jnp.int32)) % size
+    return jnp.take(stacked, order, axis=0).reshape(-1, value.shape[1])
+
+
+def exchange_gather(value, axis):
+    size = lax.axis_size(axis)
+    copies = jnp.broadcast_to(value[None], (size,) + value.shape)
+    got = lax.all_to_all(copies, axis, 0, 0, tiled=False)
+    return got.reshape(-1, value.shape[1])
+
+
 def local(tiles, tile_cols, degree_scale, start_block, planted, strengths, bounds):
     piece_rows = start_block.shape[0]
     node_count = piece_rows * lax.axis_size("row") * lax.axis_size("col")
@@ -96,11 +115,11 @@
     w_hi, w_lo = split_bf16(dense)
 
     planted_cols = doubling_gather(planted, "row")
-    planted_rows = doubling_gather(planted, "col")
+    planted_rows = direct_gather(planted, "col")
 
     def operate(vector):
         scaled = (degree_scale[:, None] * vector).astype(jnp.bfloat16)
-        gathered = doubling_gather(scaled, "row")
+        gathered = exchange_gather(scaled, "row")
         product = jnp.dot(w_hi, gathered, preferred_element_type=jnp.float32)
         product = product + jnp.dot(w_lo, gathered, preferred_element_type=jnp.float32)
         partial = lax.dot_general(

time: 243 us -> 256 us (1.053)
  blocking collectives: 0 us -> 35.5 us
  starting transfers between devices: 42.7 us -> 18.1 us
  other arithmetic: 31 us -> 25.3 us
  local copies, waits for them, and re-layouts: 2.47 us -> 7.59 us
    all_to_all x0 -> x4, blocking collectives: none -> 35.5 us  [exchange_gather(): got = lax.all_to_all(copies, axis, 0, 0, tiled=False)]
    ppermute x15 -> x2, waiting for transfers between devices: 34.5 us -> 1.89 us  [doubling_gather(): other = lax.ppermute(result, axis, pairs)]
    ppermute x15 -> x2, starting transfers between devices: 22 us -> 3.44 us  [doubling_gather(): other = lax.ppermute(result, axis, pairs)]
    ppermute x0 -> x7, waiting for transfers between devices: none -> 16.1 us  [direct_gather(): parts.append(lax.ppermute(value, axis, pairs))]
    ppermute x15, starting transfers between devices: 14.8 us -> 1.07 us  [halving_scatter_sum(): blocks = kept + lax.ppermute(sent, axis, pairs)]
    ppermute x15, waiting for transfers between devices: 75.8 us -> 89.4 us  [halving_scatter_sum(): blocks = kept + lax.ppermute(sent, axis, pairs)]
    ppermute x0 -> x7, starting transfers between devices: none -> 7.95 us  [direct_gather(): parts.append(lax.ppermute(value, axis, pairs))]
    convert_element_type x1 -> x0, other arithmetic: 5.24 us -> none  [split_bf16(): lower = (value - upper.astype(jnp.float32)).astype(jnp.bfloat16)]
  transfers between devices with their start and end apart: 35 -> 30, of which waited for: 30 -> 24; matrix products, arithmetic and copies ran while one was open for 8% -> 7% of each run, Pallas kernels for 0% -> 0%
where the time goes in v5:
time: 256 us
  waiting for transfers between devices  131 us (51%)
  blocking collectives  35.5 us (14%)
  matrix products  33.9 us (13%)
  other arithmetic  25.3 us (10%)
  starting transfers between devices  18.1 us (7%)
  local copies, waits for them, and re-layouts  7.59 us (3%)
  between operations  4.18 us (2%)
    ppermute x15, waiting for transfers between devices, halving_scatter_sum(): blocks = kept + lax.ppermute(sent, axis, pairs)  89.4 us
    all_to_all x4, blocking collectives, exchange_gather(): got = lax.all_to_all(copies, axis, 0, 0, tiled=False)  35.5 us
    ppermute x5, waiting for transfers between devices, butterfly_sum(): value = value + lax.ppermute(value, axis, pairs)  23.8 us
    ppermute x7, waiting for transfers between devices, direct_gather(): parts.append(lax.ppermute(value, axis, pairs))  16.1 us
    another operation x3, other arithmetic, local(): factor = jnp.linalg.cholesky(gram_matrix)  12.4 us
    dot_general x1, matrix products, local(): jnp.einsum('rst,rsab->ratb', onehot, tiles, preferred_element_type=jnp.fl...  12.2 us
    another operation x2, other arithmetic, local(): lax.linalg.triangular_solve(factor, current, left_side=False, lower=True,...  10.5 us
    dot_general x5, matrix products, operate(): jnp.dot(w_lo, gathered, preferred_element_type=jnp.float32)  8.43 us
  transfers between devices with their start and end apart: 30, of which 24 were waited for; matrix products, arithmetic and copies ran while one was open for 7% of the time, Pallas kernels for 0%

profile of v5, /device:TPU:0, one launch (start us, length us, event | category | flops | bytes accessed | tf_op | source)
XLA Modules:
  0.0 255.6 jit_solution(16383904368551497504)
XLA Ops:
  0.6 4.6 %collective-permute-start.6 = (bf16[256,128]{1,0:T(8,128)(2,1)}, bf16[256,128]{1,0:T(8,128)(2,1)S(1)}, u32[]{:S(2)}, u32[]{:S(2)}) collective-permute-start(bf16[256,128]{1,0:T(8,128)(2,1)} %param.11), channel_id=1, source_target_pairs={{0,7},{1,0},{2,1},{3,2},{4,3},{5,4},{6,5},{7,6},{8,15},{9,8},{10,9... | collective-permute-start | bytes 196616 | tf_op jit(solution)/shard_map/ppermute | solution.py:92
  5.8 2.7 %collective-permute-start.3 = (bf16[256,128]{1,0:T(8,128)(2,1)}, bf16[256,128]{1,0:T(8,128)(2,1)S(1)}, u32[]{:S(2)}, u32[]{:S(2)}) collective-permute-start(bf16[256,128]{1,0:T(8,128)(2,1)} %param.11), channel_id=1, source_target_pairs={{0,4},{1,5},{2,6},{3,7},{4,0},{5,1},{6,2},{7,3},{8,12},{9,13},{10,... | collective-permute-start | bytes 196616 | tf_op jit(solution)/shard_map/ppermute | solution.py:92
  8.5 1.5 collective-permute-start.7
  11.8 3.4 %all-to-all-start = ((bf16[4,256,128]{2,1,0:T(8,128)(2,1)}), bf16[4,256,128]{2,1,0:T(8,128)(2,1)S(1)}, u32[]{:S(2)}, u32[]{:S(2)}) async-start(bf16[4,256,128]{2,1,0:T(8,128)(2,1)} %broadcast_in_dim.25), calls=%async_computation | async-start | bytes 524288 | tf_op jit(solution)/shard_map/all_to_all | solution.py:101
  16.2 12.2 %fusion = (bf16[16,128,8,128]{3,2,1,0:T(8,128)(2,1)}, bf16[16,128,8,128]{3,2,1,0:T(8,128)(2,1)}) fusion(bf16[16,16,128,128]{3,2,1,0:T(8,128)(2,1)} %param.7, s32[16,16]{1,0:T(8,128)} %param.8), kind=kOutput, calls=%fused_computation.3 | convolution fusion | flops 75499520 | bytes 16778240 | tf_op jit(solution)/shard_map/rst,rsab->ratb/dot_general | solution.py:113
  28.5 5.5 %collective-permute-done = bf16[256,128]{1,0:T(8,128)(2,1)S(1)} collective-permute-done((bf16[256,128]{1,0:T(8,128)(2,1)S(1)}, bf16[256,128]{1,0:T(8,128)(2,1)S(1)}, u32[]{:S(2)}, u32[]{:S(2)}) %collective-permute-start) | collective-permute-done | bytes 65568 | tf_op jit(solution)/shard_map/ppermute | solution.py:92
  34.0 6.0 %collective-permute-done.1 = bf16[256,128]{1,0:T(8,128)(2,1)S(1)} collective-permute-done((bf16[256,128]{1,0:T(8,128)(2,1)S(1)}, bf16[256,128]{1,0:T(8,128)(2,1)S(1)}, u32[]{:S(2)}, u32[]{:S(2)}) %collective-permute-start.1) | collective-permute-done | bytes 65568 | tf_op jit(solution)/shard_map/ppermute | solution.py:92
  40.1 4.6 %collective-permute-done.2 = bf16[256,128]{1,0:T(8,128)(2,1)S(1)} collective-permute-done((bf16[256,128]{1,0:T(8,128)(2,1)S(1)}, bf16[256,128]{1,0:T(8,128)(2,1)S(1)}, u32[]{:S(2)}, u32[]{:S(2)}) %collective-permute-start.2) | collective-permute-done | bytes 65568 | tf_op jit(solution)/shard_map/ppermute | solution.py:92
  44.6 1.9 collective-permute-start.8
  47.7 1.9 collective-permute-done.8
  50.5 1.3 copy-done.2
  51.8 1.3 fusion.11
  54.0 1.3 fusion.26
  55.5 1.9 collective-permute-done.9
  57.6 8.3 %collective-permute-done.10 = f32[2,256,128]{2,1,0:T(8,128)S(1)} collective-permute-done((f32[2,256,128]{2,1,0:T(8,128)S(1)}, f32[2,256,128]{2,1,0:T(8,128)S(1)}, u32[]{:S(2)}, u32[]{:S(2)}) %collective-permute-start.10) | collective-permute-done | bytes 262176 | tf_op jit(solution)/shard_map/ppermute | solution.py:63
  69.2 5.2 %collective-permute-done.11 = f32[1,256,128]{2,1,0:T(8,128)S(1)} collective-permute-done((f32[1,256,128]{2,1,0:T(8,128)S(1)}, f32[1,256,128]{2,1,0:T(8,128)S(1)}, u32[]{:S(2)}, u32[]{:S(2)}) %collective-permute-start.11) | collective-permute-done | bytes 131104 | tf_op jit(solution)/shard_map/ppermute | solution.py:63
  74.5 9.8 %all_to_all.25 = bf16[4,256,128]{2,1,0:T(8,128)(2,1)S(1)} all-to-all(bf16[4,256,128]{2,1,0:T(8,128)(2,1)S(1)} %broadcast_in_dim.30), channel_id=1, replica_groups=mesh['row'=4,'col'=8] {'row'}, dimensions={0} | all-to-all | bytes 524288 | tf_op jit(solution)/shard_map/all_to_all | solution.py:101
  84.6 3.4 %fusion.9 = f32[2048,128]{1,0:T(8,128)S(1)} fusion(bf16[1024,128]{1,0:T(8,128)(2,1)S(1)} %bitcast.259, bf16[256,8,8,128]{3,2,1,0:T(8,128)(2,1)} %bitcast.237), kind=kOutput, calls=%fused_computation.12 | convolution fusion | flops 536870912 | bytes 5505024 | tf_op jit(solution)/shard_map/dot_general | solution.py:124
  88.7 1.6 copy-done.1
  90.3 1.3 fusion.32
  91.7 1.9 collective-permute-done.12
  93.7 8.3 %collective-permute-done.13 = f32[2,256,128]{2,1,0:T(8,128)S(1)} collective-permute-done((f32[2,256,128]{2,1,0:T(8,128)S(1)}, f32[2,256,128]{2,1,0:T(8,128)S(1)}, u32[]{:S(2)}, u32[]{:S(2)}) %collective-permute-start.13) | collective-permute-done | bytes 262176 | tf_op jit(solution)/shard_map/ppermute | solution.py:63
  102.2 8.4 %collective-permute-done.14 = f32[1,256,128]{2,1,0:T(8,128)S(1)} collective-permute-done((f32[1,256,128]{2,1,0:T(8,128)S(1)}, f32[1,256,128]{2,1,0:T(8,128)S(1)}, u32[]{:S(2)}, u32[]{:S(2)}) %collective-permute-start.14) | collective-permute-done | bytes 131104 | tf_op jit(solution)/shard_map/ppermute | solution.py:63
  110.7 8.6 %all_to_all.26 = bf16[4,256,128]{2,1,0:T(8,128)(2,1)S(1)} all-to-all(bf16[4,256,128]{2,1,0:T(8,128)(2,1)S(1)} %broadcast_in_dim.31), channel_id=1, replica_groups=mesh['row'=4,'col'=8] {'row'}, dimensions={0} | all-to-all | bytes 524288 | tf_op jit(solution)/shard_map/all_to_all | solution.py:101
  119.6 1.3 fusion.7
  121.4 1.3 fusion.38
  122.8 1.9 collective-permute-done.15
  124.9 8.3 %collective-permute-done.16 = f32[2,256,128]{2,1,0:T(8,128)S(1)} collective-permute-done((f32[2,256,128]{2,1,0:T(8,128)S(1)}, f32[2,256,128]{2,1,0:T(8,128)S(1)}, u32[]{:S(2)}, u32[]{:S(2)}) %collective-permute-start.16) | collective-permute-done | bytes 262176 | tf_op jit(solution)/shard_map/ppermute | solution.py:63
  133.3 8.4 %collective-permute-done.17 = f32[1,256,128]{2,1,0:T(8,128)S(1)} collective-permute-done((f32[1,256,128]{2,1,0:T(8,128)S(1)}, f32[1,256,128]{2,1,0:T(8,128)S(1)}, u32[]{:S(2)}, u32[]{:S(2)}) %collective-permute-start.17) | collective-permute-done | bytes 131104 | tf_op jit(solution)/shard_map/ppermute | solution.py:63
  141.9 8.6 %all_to_all.27 = bf16[4,256,128]{2,1,0:T(8,128)(2,1)S(1)} all-to-all(bf16[4,256,128]{2,1,0:T(8,128)(2,1)S(1)} %broadcast_in_dim.32), channel_id=1, replica_groups=mesh['row'=4,'col'=8] {'row'}, dimensions={0} | all-to-all | bytes 524288 | tf_op jit(solution)/shard_map/all_to_all | solution.py:101
  150.7 1.2 fusion.5
  152.5 1.3 fusion.44
  153.9 1.9 collective-permute-done.18
  156.0 8.3 %collective-permute-done.19 = f32[2,256,128]{2,1,0:T(8,128)S(1)} collective-permute-done((f32[2,256,128]{2,1,0:T(8,128)S(1)}, f32[2,256,128]{2,1,0:T(8,128)S(1)}, u32[]{:S(2)}, u32[]{:S(2)}) %collective-permute-start.19) | collective-permute-done | bytes 262176 | tf_op jit(solution)/shard_map/ppermute | solution.py:63
  164.5 8.4 %collective-permute-done.20 = f32[1,256,128]{2,1,0:T(8,128)S(1)} collective-permute-done((f32[1,256,128]{2,1,0:T(8,128)S(1)}, f32[1,256,128]{2,1,0:T(8,128)S(1)}, u32[]{:S(2)}, u32[]{:S(2)}) %collective-permute-start.20) | collective-permute-done | bytes 131104 | tf_op jit(solution)/shard_map/ppermute | solution.py:63
  173.0 8.6 %all_to_all.28 = bf16[4,256,128]{2,1,0:T(8,128)(2,1)S(1)} all-to-all(bf16[4,256,128]{2,1,0:T(8,128)(2,1)S(1)} %broadcast_in_dim.33), channel_id=1, replica_groups=mesh['row'=4,'col'=8] {'row'}, dimensions={0} | all-to-all | bytes 524288 | tf_op jit(solution)/shard_map/all_to_all | solution.py:101
  181.6 1.2 fusion.3
  183.7 1.3 fusion.50
  185.1 1.9 collective-permute-done.21
  187.2 8.3 %collective-permute-done.22 = f32[2,256,128]{2,1,0:T(8,128)S(1)} collective-permute-done((f32[2,256,128]{2,1,0:T(8,128)S(1)}, f32[2,256,128]{2,1,0:T(8,128)S(1)}, u32[]{:S(2)}, u32[]{:S(2)}) %collective-permute-start.22) | collective-permute-done | bytes 262176 | tf_op jit(solution)/shard_map/ppermute | solution.py:63
  196.0 8.0 %collective-permute-done.23 = f32[1,256,128]{2,1,0:T(8,128)S(1)} collective-permute-done((f32[1,256,128]{2,1,0:T(8,128)S(1)}, f32[1,256,128]{2,1,0:T(8,128)S(1)}, u32[]{:S(2)}, u32[]{:S(2)}) %collective-permute-start.23) | collective-permute-done | bytes 131104 | tf_op jit(solution)/shard_map/ppermute | solution.py:63
  204.6 1.3 collective-permute-done.24
  206.0 5.5 %collective-permute-done.25 = f32[256,128]{0,1:T(8,128)S(1)} collective-permute-done((f32[256,128]{0,1:T(8,128)S(1)}, f32[256,128]{0,1:T(8,128)S(1)}, u32[]{:S(2)}, u32[]{:S(2)}) %collective-permute-start.25) | collective-permute-done | bytes 131104 | tf_op jit(solution)/shard_map/ppermute | solution.py:28
  211.6 8.4 %collective-permute-done.26 = f32[256,128]{0,1:T(8,128)S(1)} collective-permute-done((f32[256,128]{0,1:T(8,128)S(1)}, f32[256,128]{0,1:T(8,128)S(1)}, u32[]{:S(2)}, u32[]{:S(2)}) %collective-permute-start.26) | collective-permute-done | bytes 131104 | tf_op jit(solution)/shard_map/ppermute | solution.py:28
  221.0 4.5 %collective-permute-done.27 = f32[256,128]{0,1:T(8,128)S(1)} collective-permute-done((f32[256,128]{0,1:T(8,128)S(1)}, f32[256,128]{0,1:T(8,128)S(1)}, u32[]{:S(2)}, u32[]{:S(2)}) %collective-permute-start.27) | collective-permute-done | bytes 131104 | tf_op jit(solution)/shard_map/ppermute | solution.py:28
  226.5 4.0 %collective-permute-done.28 = f32[256,128]{0,1:T(8,128)S(1)} collective-permute-done((f32[256,128]{0,1:T(8,128)S(1)}, f32[256,128]{0,1:T(8,128)S(1)}, u32[]{:S(2)}, u32[]{:S(2)}) %collective-permute-start.28) | collective-permute-done | bytes 131104 | tf_op jit(solution)/shard_map/ppermute | solution.py:28
  230.7 11.7 %cholesky.16 = f32[128,128]{1,0:T(8,128)S(1)} custom-call(f32[128,128]{1,0:T(8,128)S(1)} %fusion.92), custom_call_target="Cholesky" | custom-call | tf_op jit(solution)/shard_map/jit(cholesky)/cholesky | solution.py:147
  243.8 9.8 %custom-call.10 = f32[1,128,128]{1,2,0:T(8,128)S(1)} custom-call(f32[1,128,128]{2,1,0:T(8,128)S(1)} %fusion.85), custom_call_target="InvertDiagBlocksLowerTriangular" | custom-call | tf_op jit(solution)/shard_map/triangular_solve | solution.py:148
  (133 shorter events, 19.4 us)
Async XLA Ops:
  0.6 46.0 %collective-permute-start.6 = (bf16[256,128]{1,0:T(8,128)(2,1)}, bf16[256,128]{1,0:T(8,128)(2,1)S(1)}, u32[]{:S(2)}, u32[]{:S(2)}) collective-permute-start(bf16[256,128]{1,0:T(8,128)(2,1)} %param.11), channel_id=1, source_target_pairs={{0,7},{1,0},{2,1},{3,2},{4,3},{5,4},{6,5},{7,6},{8,15},{9,8},{10,9... | collective-permute-start | bytes 196616 | tf_op jit(solution)/shard_map/ppermute | solution.py:92
  5.2 41.4 %collective-permute-start.5 = (bf16[256,128]{1,0:T(8,128)(2,1)}, bf16[256,128]{1,0:T(8,128)(2,1)S(1)}, u32[]{:S(2)}, u32[]{:S(2)}) collective-permute-start(bf16[256,128]{1,0:T(8,128)(2,1)} %param.11), channel_id=1, source_target_pairs={{0,6},{1,7},{2,0},{3,1},{4,2},{5,3},{6,4},{7,5},{8,14},{9,15},{10,... | collective-permute-start | bytes 196616 | tf_op jit(solution)/shard_map/ppermute | solution.py:92
  5.8 40.8 %collective-permute-start.4 = (bf16[256,128]{1,0:T(8,128)(2,1)}, bf16[256,128]{1,0:T(8,128)(2,1)S(1)}, u32[]{:S(2)}, u32[]{:S(2)}) collective-permute-start(bf16[256,128]{1,0:T(8,128)(2,1)} %param.11), channel_id=1, source_target_pairs={{0,5},{1,6},{2,7},{3,0},{4,1},{5,2},{6,3},{7,4},{8,13},{9,14},{10,... | collective-permute-start | bytes 196616 | tf_op jit(solution)/shard_map/ppermute | solution.py:92
  5.8 40.8 %collective-permute-start.3 = (bf16[256,128]{1,0:T(8,128)(2,1)}, bf16[256,128]{1,0:T(8,128)(2,1)S(1)}, u32[]{:S(2)}, u32[]{:S(2)}) collective-permute-start(bf16[256,128]{1,0:T(8,128)(2,1)} %param.11), channel_id=1, source_target_pairs={{0,4},{1,5},{2,6},{3,7},{4,0},{5,1},{6,2},{7,3},{8,12},{9,13},{10,... | collective-permute-start | bytes 196616 | tf_op jit(solution)/shard_map/ppermute | solution.py:92
  8.5 19.9 %collective-permute-start.7 = (bf16[256,128]{1,0:T(8,128)(2,1)}, bf16[256,128]{1,0:T(8,128)(2,1)S(1)}, u32[]{:S(2)}, u32[]{:S(2)}) collective-permute-start(bf16[256,128]{1,0:T(8,128)(2,1)} %param.11), channel_id=1, source_target_pairs={{0,8},{8,0},{16,24},{24,16},{1,9},{9,1},{17,25},{25,17},{2,10},{10... | collective-permute-start | bytes 196616 | tf_op jit(solution)/shard_map/ppermute | solution.py:77
  11.8 37.9 %all-to-all-start = ((bf16[4,256,128]{2,1,0:T(8,128)(2,1)}), bf16[4,256,128]{2,1,0:T(8,128)(2,1)S(1)}, u32[]{:S(2)}, u32[]{:S(2)}) async-start(bf16[4,256,128]{2,1,0:T(8,128)(2,1)} %broadcast_in_dim.25), calls=%async_computation | async-start | bytes 524288 | tf_op jit(solution)/shard_map/all_to_all | solution.py:101
  16.2 12.2 %copy-start.5 = (bf16[256,128]{1,0:T(8,128)(2,1)S(1)}, bf16[256,128]{1,0:T(8,128)(2,1)}, u32[]{:S(2)}) copy-start(bf16[256,128]{1,0:T(8,128)(2,1)} %param.11) | copy-start | bytes 196612
  16.2 33.5 %copy-start.8 = (f32[128]{0:T(128)S(1)}, f32[128]{0:T(128)}, u32[]{:S(2)}) copy-start(f32[128]{0:T(128)} %param.12) | copy-start | bytes 1540
  28.4 5.5 %collective-permute-start = (bf16[256,128]{1,0:T(8,128)(2,1)S(1)}, bf16[256,128]{1,0:T(8,128)(2,1)S(1)}, u32[]{:S(2)}, u32[]{:S(2)}) collective-permute-start(bf16[256,128]{1,0:T(8,128)(2,1)S(1)} %copy-done.5), channel_id=1, source_target_pairs={{0,1},{1,2},{2,3},{3,4},{4,5},{5,6},{6,7},{7,0},{8,9},{9,10},{10,1... | collective-permute-start | bytes 196616 | tf_op jit(solution)/shard_map/ppermute | solution.py:92
  34.0 6.1 %collective-permute-start.1 = (bf16[256,128]{1,0:T(8,128)(2,1)S(1)}, bf16[256,128]{1,0:T(8,128)(2,1)S(1)}, u32[]{:S(2)}, u32[]{:S(2)}) collective-permute-start(bf16[256,128]{1,0:T(8,128)(2,1)S(1)} %copy-done.5), channel_id=1, source_target_pairs={{0,2},{1,3},{2,4},{3,5},{4,6},{5,7},{6,0},{7,1},{8,10},{9,11},{10,... | collective-permute-start | bytes 196616 | tf_op jit(solution)/shard_map/ppermute | solution.py:92
  40.0 4.6 %collective-permute-start.2 = (bf16[256,128]{1,0:T(8,128)(2,1)S(1)}, bf16[256,128]{1,0:T(8,128)(2,1)S(1)}, u32[]{:S(2)}, u32[]{:S(2)}) collective-permute-start(bf16[256,128]{1,0:T(8,128)(2,1)S(1)} %copy-done.5), channel_id=1, source_target_pairs={{0,3},{1,4},{2,5},{3,6},{4,7},{5,0},{6,1},{7,2},{8,11},{9,12},{10,... | collective-permute-start | bytes 196616 | tf_op jit(solution)/shard_map/ppermute | solution.py:92
  44.6 5.0 %collective-permute-start.8 = (bf16[512,128]{1,0:T(8,128)(2,1)S(1)}, bf16[512,128]{1,0:T(8,128)(2,1)S(1)}, u32[]{:S(2)}, u32[]{:S(2)}) collective-permute-start(bf16[512,128]{1,0:T(8,128)(2,1)S(1)} %pad_maximum_fusion.1), channel_id=1, source_target_pairs={{0,16},{8,24},{16,0},{24,8},{1,17},{9,25},{17,1},{25,9},{2,18},{10... | collective-permute-start | bytes 393224 | tf_op jit(solution)/shard_map/ppermute | solution.py:77
  49.7 2.2 copy-start.2
  51.8 2.2 copy-start
  55.3 10.7 %copy-start.7 = (f32[2]{0:T(128)S(1)}, f32[2]{0:T(128)}, u32[]{:S(2)}) copy-start(f32[2]{0:T(128)} %param.13) | copy-start | bytes 28
  55.3 19.1 %copy-start.4 = (f32[256,128]{1,0:T(8,128)S(1)}, f32[256,128]{1,0:T(8,128)}, u32[]{:S(2)}) copy-start(f32[256,128]{1,0:T(8,128)} %param.10) | copy-start | bytes 393220
  55.3 19.1 %copy-start.6 = (f32[256]{0:T(256)S(1)}, f32[256]{0:T(256)}, u32[]{:S(2)}) copy-start(f32[256]{0:T(256)} %param.9) | copy-start | bytes 3076
  55.4 2.0 collective-permute-start.9
  57.5 8.4 %collective-permute-start.10 = (f32[2,256,128]{2,1,0:T(8,128)S(1)}, f32[2,256,128]{2,1,0:T(8,128)S(1)}, u32[]{:S(2)}, u32[]{:S(2)}) collective-permute-start(f32[2,256,128]{2,1,0:T(8,128)S(1)} %dynamic-slice_bitcast_fusion.9), channel_id=1, source_target_pairs={{0,2},{1,3},{2,0},{3,1},{4,6},{5,7},{6,4},{7,5},{8,10},{9,11},{10,... | collective-permute-start | bytes 786440 | tf_op jit(solution)/shard_map/ppermute | solution.py:63
  65.9 8.5 %collective-permute-start.11 = (f32[1,256,128]{2,1,0:T(8,128)S(1)}, f32[1,256,128]{2,1,0:T(8,128)S(1)}, u32[]{:S(2)}, u32[]{:S(2)}) collective-permute-start(f32[1,256,128]{2,1,0:T(8,128)S(1)} %constant_dynamic-slice_fusion.4), channel_id=1, source_target_pairs={{0,4},{1,5},{2,6},{3,7},{4,0},{5,1},{6,2},{7,3},{8,12},{9,13},{10,... | collective-permute-start | bytes 393224 | tf_op jit(solution)/shard_map/ppermute | solution.py:63
  88.1 2.2 copy-start.1
  91.5 28.1 %copy-start.3 = (bf16[16,128,8,128]{3,2,1,0:T(8,128)(2,1)S(1)}, bf16[16,128,8,128]{3,2,1,0:T(8,128)(2,1)}, u32[]{:S(2)}) copy-start(bf16[16,128,8,128]{3,2,1,0:T(8,128)(2,1)} %get-tuple-element.10) | copy-start | bytes 12582916
  91.6 2.0 collective-permute-start.12
  93.6 8.4 %collective-permute-start.13 = (f32[2,256,128]{2,1,0:T(8,128)S(1)}, f32[2,256,128]{2,1,0:T(8,128)S(1)}, u32[]{:S(2)}, u32[]{:S(2)}) collective-permute-start(f32[2,256,128]{2,1,0:T(8,128)S(1)} %dynamic-slice_bitcast_fusion.8), channel_id=1, source_target_pairs={{0,2},{1,3},{2,0},{3,1},{4,6},{5,7},{6,4},{7,5},{8,10},{9,11},{10,... | collective-permute-start | bytes 786440 | tf_op jit(solution)/shard_map/ppermute | solution.py:63
  102.1 8.5 %collective-permute-start.14 = (f32[1,256,128]{2,1,0:T(8,128)S(1)}, f32[1,256,128]{2,1,0:T(8,128)S(1)}, u32[]{:S(2)}, u32[]{:S(2)}) collective-permute-start(f32[1,256,128]{2,1,0:T(8,128)S(1)} %constant_dynamic-slice_fusion.3), channel_id=1, source_target_pairs={{0,4},{1,5},{2,6},{3,7},{4,0},{5,1},{6,2},{7,3},{8,12},{9,13},{10,... | collective-permute-start | bytes 393224 | tf_op jit(solution)/shard_map/ppermute | solution.py:63
  122.7 2.0 collective-permute-start.15
  124.8 8.4 %collective-permute-start.16 = (f32[2,256,128]{2,1,0:T(8,128)S(1)}, f32[2,256,128]{2,1,0:T(8,128)S(1)}, u32[]{:S(2)}, u32[]{:S(2)}) collective-permute-start(f32[2,256,128]{2,1,0:T(8,128)S(1)} %dynamic-slice_bitcast_fusion.7), channel_id=1, source_target_pairs={{0,2},{1,3},{2,0},{3,1},{4,6},{5,7},{6,4},{7,5},{8,10},{9,11},{10,... | collective-permute-start | bytes 786440 | tf_op jit(solution)/shard_map/ppermute | solution.py:63
  133.3 8.5 %collective-permute-start.17 = (f32[1,256,128]{2,1,0:T(8,128)S(1)}, f32[1,256,128]{2,1,0:T(8,128)S(1)}, u32[]{:S(2)}, u32[]{:S(2)}) collective-permute-start(f32[1,256,128]{2,1,0:T(8,128)S(1)} %constant_dynamic-slice_fusion.2), channel_id=1, source_target_pairs={{0,4},{1,5},{2,6},{3,7},{4,0},{5,1},{6,2},{7,3},{8,12},{9,13},{10,... | collective-permute-start | bytes 393224 | tf_op jit(solution)/shard_map/ppermute | solution.py:63
  153.9 2.0 collective-permute-start.18
  155.9 8.4 %collective-permute-start.19 = (f32[2,256,128]{2,1,0:T(8,128)S(1)}, f32[2,256,128]{2,1,0:T(8,128)S(1)}, u32[]{:S(2)}, u32[]{:S(2)}) collective-permute-start(f32[2,256,128]{2,1,0:T(8,128)S(1)} %dynamic-slice_bitcast_fusion.6), channel_id=1, source_target_pairs={{0,2},{1,3},{2,0},{3,1},{4,6},{5,7},{6,4},{7,5},{8,10},{9,11},{10,... | collective-permute-start | bytes 786440 | tf_op jit(solution)/shard_map/ppermute | solution.py:63
  164.4 8.5 %collective-permute-start.20 = (f32[1,256,128]{2,1,0:T(8,128)S(1)}, f32[1,256,128]{2,1,0:T(8,128)S(1)}, u32[]{:S(2)}, u32[]{:S(2)}) collective-permute-start(f32[1,256,128]{2,1,0:T(8,128)S(1)} %constant_dynamic-slice_fusion.1), channel_id=1, source_target_pairs={{0,4},{1,5},{2,6},{3,7},{4,0},{5,1},{6,2},{7,3},{8,12},{9,13},{10,... | collective-permute-start | bytes 393224 | tf_op jit(solution)/shard_map/ppermute | solution.py:63
  185.0 2.0 collective-permute-start.21
  187.1 8.4 %collective-permute-start.22 = (f32[2,256,128]{2,1,0:T(8,128)S(1)}, f32[2,256,128]{2,1,0:T(8,128)S(1)}, u32[]{:S(2)}, u32[]{:S(2)}) collective-permute-start(f32[2,256,128]{2,1,0:T(8,128)S(1)} %dynamic-slice_bitcast_fusion.5), channel_id=1, source_target_pairs={{0,2},{1,3},{2,0},{3,1},{4,6},{5,7},{6,4},{7,5},{8,10},{9,11},{10,... | collective-permute-start | bytes 786440 | tf_op jit(solution)/shard_map/ppermute | solution.py:63
  195.5 8.5 %collective-permute-start.23 = (f32[1,256,128]{2,1,0:T(8,128)S(1)}, f32[1,256,128]{2,1,0:T(8,128)S(1)}, u32[]{:S(2)}, u32[]{:S(2)}) collective-permute-start(f32[1,256,128]{2,1,0:T(8,128)S(1)} %constant_dynamic-slice_fusion), channel_id=1, source_target_pairs={{0,4},{1,5},{2,6},{3,7},{4,0},{5,1},{6,2},{7,3},{8,12},{9,13},{10,... | collective-permute-start | bytes 393224 | tf_op jit(solution)/shard_map/ppermute | solution.py:63
  204.5 1.4 collective-permute-start.24
  205.9 5.6 %collective-permute-start.25 = (f32[256,128]{0,1:T(8,128)S(1)}, f32[256,128]{0,1:T(8,128)S(1)}, u32[]{:S(2)}, u32[]{:S(2)}) collective-permute-start(f32[256,128]{0,1:T(8,128)S(1)} %fusion.118), channel_id=1, source_target_pairs={{0,2},{1,3},{2,0},{3,1},{4,6},{5,7},{6,4},{7,5},{8,10},{9,11},{10,... | collective-permute-start | bytes 393224 | tf_op jit(solution)/shard_map/ppermute | solution.py:28
  211.6 8.5 %collective-permute-start.26 = (f32[256,128]{0,1:T(8,128)S(1)}, f32[256,128]{0,1:T(8,128)S(1)}, u32[]{:S(2)}, u32[]{:S(2)}) collective-permute-start(f32[256,128]{0,1:T(8,128)S(1)} %add.284), channel_id=1, source_target_pairs={{0,4},{1,5},{2,6},{3,7},{4,0},{5,1},{6,2},{7,3},{8,12},{9,13},{10,... | collective-permute-start | bytes 393224 | tf_op jit(solution)/shard_map/ppermute | solution.py:28
  220.0 5.5 %collective-permute-start.27 = (f32[256,128]{0,1:T(8,128)S(1)}, f32[256,128]{0,1:T(8,128)S(1)}, u32[]{:S(2)}, u32[]{:S(2)}) collective-permute-start(f32[256,128]{0,1:T(8,128)S(1)} %add.285), channel_id=1, source_target_pairs={{0,8},{8,0},{16,24},{24,16},{1,9},{9,1},{17,25},{25,17},{2,10},{10... | collective-permute-start | bytes 393224 | tf_op jit(solution)/shard_map/ppermute | solution.py:28
  225.5 5.0 %collective-permute-start.28 = (f32[256,128]{0,1:T(8,128)S(1)}, f32[256,128]{0,1:T(8,128)S(1)}, u32[]{:S(2)}, u32[]{:S(2)}) collective-permute-start(f32[256,128]{0,1:T(8,128)S(1)} %add.286), channel_id=1, source_target_pairs={{0,16},{8,24},{16,0},{24,8},{1,17},{9,25},{17,1},{25,9},{2,18},{10... | collective-permute-start | bytes 393224 | tf_op jit(solution)/shard_map/ppermute | solution.py:28

commit v6 on v4

--- a/solution.py
+++ b/solution.py
@@ -83,6 +83,26 @@
     return result
 
 
+def far_first_gather(value, axis):
+    size = lax.axis_size(axis)
+    if size & (size - 1):
+        return lax.all_gather(value, axis, axis=0, tiled=True)
+    here = lax.axis_index(axis)
+    result = value[None]
+    step = size // 2
+    while step >= 1:
+        pairs = [(index, index ^ step) for index in range(size)]
+        other = lax.ppermute(result, axis, pairs)
+        low = (here // step) % 2 == 0
+        result = jnp.concatenate(
+            [jnp.where(low, result, other), jnp.where(low, other, result)], axis=0
+        )
+        step //= 2
+    bits = size.bit_length() - 1
+    order = [int(format(index, f"0{bits}b")[::-1], 2) if bits else 0 for index in range(size)]
+    return result[jnp.array(order)].reshape(-1, value.shape[1])
+
+
 def local(tiles, tile_cols, degree_scale, start_block, planted, strengths, bounds):
     piece_rows = start_block.shape[0]
     node_count = piece_rows * lax.axis_size("row") * lax.axis_size("col")
@@ -96,7 +116,7 @@
     w_hi, w_lo = split_bf16(dense)
 
     planted_cols = doubling_gather(planted, "row")
-    planted_rows = doubling_gather(planted, "col")
+    planted_rows = far_first_gather(planted, "col")
 
     def operate(vector):
         scaled = (degree_scale[:, None] * vector).astype(jnp.bfloat16)

time: 243 us -> 240 us (0.988)
  starting transfers between devices: 42.7 us -> 23.5 us
  waiting for transfers between devices: 130 us -> 144 us
    ppermute x15, waiting for transfers between devices: 75.8 us -> 87.5 us  [halving_scatter_sum(): blocks = kept + lax.ppermute(sent, axis, pairs)]
    ppermute x15, starting transfers between devices: 14.8 us -> 3.67 us  [halving_scatter_sum(): blocks = kept + lax.ppermute(sent, axis, pairs)]
    ppermute x15 -> x12, starting transfers between devices: 22 us -> 12.9 us  [doubling_gather(): other = lax.ppermute(result, axis, pairs)]
    ppermute x0 -> x3, starting transfers between devices: none -> 4.76 us  [far_first_gather(): other = lax.ppermute(result, axis, pairs)]
    ppermute x15 -> x12, waiting for transfers between devices: 34.5 us -> 29.8 us  [doubling_gather(): other = lax.ppermute(result, axis, pairs)]
    ppermute x5, waiting for transfers between devices: 19.7 us -> 23.8 us  [butterfly_sum(): value = value + lax.ppermute(value, axis, pairs)]
    ppermute x5, starting transfers between devices: 5.87 us -> 2.19 us  [butterfly_sum(): value = value + lax.ppermute(value, axis, pairs)]
    ppermute x0 -> x3, waiting for transfers between devices: none -> 2.78 us  [far_first_gather(): other = lax.ppermute(result, axis, pairs)]
  transfers between devices with their start and end apart: 35 -> 35, of which waited for: 30 -> 29; matrix products, arithmetic and copies ran while one was open for 8% -> 8% of each run, Pallas kernels for 0% -> 0%
where the time goes in v6:
time: 240 us
  waiting for transfers between devices  144 us (60%)
  matrix products  32.4 us (14%)
  other arithmetic  31 us (13%)
  starting transfers between devices  23.5 us (10%)
  local copies, waits for them, and re-layouts  4.72 us (2%)
  between operations  4.04 us (2%)
    ppermute x15, waiting for transfers between devices, halving_scatter_sum(): blocks = kept + lax.ppermute(sent, axis, pairs)  87.5 us
    ppermute x12, waiting for transfers between devices, doubling_gather(): other = lax.ppermute(result, axis, pairs)  29.8 us
    ppermute x5, waiting for transfers between devices, butterfly_sum(): value = value + lax.ppermute(value, axis, pairs)  23.8 us
    ppermute x12, starting transfers between devices, doubling_gather(): other = lax.ppermute(result, axis, pairs)  12.9 us
    another operation x3, other arithmetic, local(): factor = jnp.linalg.cholesky(gram_matrix)  12.4 us
    dot_general x5, matrix products, operate(): jnp.dot(w_lo, gathered, preferred_element_type=jnp.float32)  10.9 us
    another operation x2, other arithmetic, local(): lax.linalg.triangular_solve(factor, current, left_side=False, lower=True,...  10.6 us
    dot_general x1, matrix products, local(): jnp.einsum('rst,rsab->ratb', onehot, tiles, preferred_element_type=jnp.fl...  8.2 us
  transfers between devices with their start and end apart: 35, of which 29 were waited for; matrix products, arithmetic and copies ran while one was open for 8% of the time, Pallas kernels for 0%

profile of v6, /device:TPU:0, one launch (start us, length us, event | category | flops | bytes accessed | tf_op | source)
XLA Modules:
  0.0 239.7 jit_solution(14344106282198867164)
XLA Ops:
  1.6 3.0 %collective-permute-start = (bf16[256,128]{1,0:T(8,128)(2,1)S(1)}, bf16[256,128]{1,0:T(8,128)(2,1)S(1)}, u32[]{:S(2)}, u32[]{:S(2)}) collective-permute-start(bf16[256,128]{1,0:T(8,128)(2,1)S(1)} %multiply_convert_fusion.4), channel_id=1, source_target_pairs={{0,8},{8,0},{16,24},{24,16},{1,9},{9,1},{17,25},{25,17},{2,10},{10... | collective-permute-start | bytes 196616 | tf_op jit(solution)/shard_map/ppermute | solution.py:77
  4.8 3.0 %collective-permute-start.2 = (bf16[1,256,128]{2,1,0:T(8,128)(2,1)}, bf16[1,256,128]{2,1,0:T(8,128)(2,1)S(1)}, u32[]{:S(2)}, u32[]{:S(2)}) collective-permute-start(bf16[1,256,128]{2,1,0:T(8,128)(2,1)} %bitcast.182), channel_id=1, source_target_pairs={{0,4},{1,5},{2,6},{3,7},{4,0},{5,1},{6,2},{7,3},{8,12},{9,13},{10,... | collective-permute-start | bytes 196616 | tf_op jit(solution)/shard_map/ppermute | solution.py:95
  7.8 8.2 %fusion.1 = f32[16,8,128,128]{3,1,2,0:T(8,128)S(1)} fusion(bf16[16,16,128,128]{3,2,1,0:T(8,128)(2,1)} %param.8, s32[16,16]{1,0:T(8,128)} %param.9), kind=kOutput, calls=%fused_computation.4 | convolution fusion | flops 67110912 | bytes 16778240 | tf_op jit(solution)/shard_map/rst,rsab->ratb/dot_general | solution.py:114
  16.0 5.3 %fusion = (bf16[2048,1024]{1,0:T(8,128)(2,1)}, bf16[2048,1024]{1,0:T(8,128)(2,1)}) fusion(f32[256,8,8,128]{3,2,1,0:T(8,128)S(1)} %bitcast.161), kind=kLoop, calls=%fused_computation.3 | loop fusion | flops 6291456 | bytes 16777216 | tf_op jit(solution)/shard_map/convert_element_type | solution.py:11
  21.5 1.6 collective-permute-start.1
  23.1 1.6 collective-permute-start.3
  25.3 2.8 %collective-permute-done.3 = bf16[2,256,128]{2,1,0:T(8,128)(2,1)S(1)} collective-permute-done((bf16[2,256,128]{2,1,0:T(8,128)(2,1)S(1)}, bf16[2,256,128]{2,1,0:T(8,128)(2,1)S(1)}, u32[]{:S(2)}, u32[]{:S(2)}) %collective-permute-start.3) | collective-permute-done | bytes 131104 | tf_op jit(solution)/shard_map/ppermute | solution.py:95
  28.4 3.4 %fusion.34 = f32[2048,128]{1,0:T(8,128)S(1)} fusion(bf16[2048,1024]{1,0:T(8,128)(2,1)} %get-tuple-element.10, bf16[512,128]{1,0:T(8,128)(2,1)S(1)} %get-tuple-element.25, bf16[512,128]{1,0:T(8,128)(2,1)S(1)} %get-tuple-element.24), kind=kOutput, calls=%fused_computation.114 | convolution fusion | flops 537395200 | bytes 5505024 | tf_op jit(solution)/shard_map/dot_general | solution.py:125
  33.5 1.6 copy-done
  37.0 1.5 collective-permute-done.7
  38.6 1.6 collective-permute-start.8
  40.3 7.0 %collective-permute-done.8 = f32[2,256,128]{2,1,0:T(8,128)S(1)} collective-permute-done((f32[2,256,128]{2,1,0:T(8,128)S(1)}, f32[2,256,128]{2,1,0:T(8,128)S(1)}, u32[]{:S(2)}, u32[]{:S(2)}) %collective-permute-start.8) | collective-permute-done | bytes 262176 | tf_op jit(solution)/shard_map/ppermute | solution.py:63
  50.9 5.1 %collective-permute-done.9 = f32[1,256,128]{2,1,0:T(8,128)S(1)} collective-permute-done((f32[1,256,128]{2,1,0:T(8,128)S(1)}, f32[1,256,128]{2,1,0:T(8,128)S(1)}, u32[]{:S(2)}, u32[]{:S(2)}) %collective-permute-start.9) | collective-permute-done | bytes 131104 | tf_op jit(solution)/shard_map/ppermute | solution.py:63
  56.2 1.5 collective-permute-start.10
  57.7 2.8 %collective-permute-done.10 = bf16[256,128]{1,0:T(8,128)(2,1)S(1)} collective-permute-done((bf16[256,128]{1,0:T(8,128)(2,1)S(1)}, bf16[256,128]{1,0:T(8,128)(2,1)S(1)}, u32[]{:S(2)}, u32[]{:S(2)}) %collective-permute-start.10) | collective-permute-done | bytes 65568 | tf_op jit(solution)/shard_map/ppermute | solution.py:77
  60.9 4.7 %collective-permute-done.11 = bf16[512,128]{1,0:T(8,128)(2,1)S(1)} collective-permute-done((bf16[512,128]{1,0:T(8,128)(2,1)S(1)}, bf16[512,128]{1,0:T(8,128)(2,1)S(1)}, u32[]{:S(2)}, u32[]{:S(2)}) %collective-permute-start.11) | collective-permute-done | bytes 131104 | tf_op jit(solution)/shard_map/ppermute | solution.py:77
  65.6 3.5 %fusion.33 = f32[2048,128]{1,0:T(8,128)S(1)} fusion(bf16[2048,1024]{1,0:T(8,128)(2,1)} %get-tuple-element.10, bf16[512,128]{1,0:T(8,128)(2,1)S(1)} %get-tuple-element.21, bf16[512,128]{1,0:T(8,128)(2,1)S(1)} %get-tuple-element.20), kind=kOutput, calls=%fused_computation.113 | convolution fusion | flops 537395200 | bytes 5505024 | tf_op jit(solution)/shard_map/dot_general | solution.py:125
  69.9 1.3 copy-done.1
  72.7 1.9 collective-permute-done.12
  74.8 8.3 %collective-permute-done.13 = f32[2,256,128]{2,1,0:T(8,128)S(1)} collective-permute-done((f32[2,256,128]{2,1,0:T(8,128)S(1)}, f32[2,256,128]{2,1,0:T(8,128)S(1)}, u32[]{:S(2)}, u32[]{:S(2)}) %collective-permute-start.13) | collective-permute-done | bytes 262176 | tf_op jit(solution)/shard_map/ppermute | solution.py:63
  83.3 8.3 %collective-permute-done.14 = f32[1,256,128]{2,1,0:T(8,128)S(1)} collective-permute-done((f32[1,256,128]{2,1,0:T(8,128)S(1)}, f32[1,256,128]{2,1,0:T(8,128)S(1)}, u32[]{:S(2)}, u32[]{:S(2)}) %collective-permute-start.14) | collective-permute-done | bytes 131104 | tf_op jit(solution)/shard_map/ppermute | solution.py:63
  91.7 1.5 collective-permute-start.15
  93.3 2.8 %collective-permute-done.15 = bf16[256,128]{1,0:T(8,128)(2,1)S(1)} collective-permute-done((bf16[256,128]{1,0:T(8,128)(2,1)S(1)}, bf16[256,128]{1,0:T(8,128)(2,1)S(1)}, u32[]{:S(2)}, u32[]{:S(2)}) %collective-permute-start.15) | collective-permute-done | bytes 65568 | tf_op jit(solution)/shard_map/ppermute | solution.py:77
  96.5 4.7 %collective-permute-done.16 = bf16[512,128]{1,0:T(8,128)(2,1)S(1)} collective-permute-done((bf16[512,128]{1,0:T(8,128)(2,1)S(1)}, bf16[512,128]{1,0:T(8,128)(2,1)S(1)}, u32[]{:S(2)}, u32[]{:S(2)}) %collective-permute-start.16) | collective-permute-done | bytes 131104 | tf_op jit(solution)/shard_map/ppermute | solution.py:77
  104.7 1.9 collective-permute-done.17
  106.8 8.3 %collective-permute-done.18 = f32[2,256,128]{2,1,0:T(8,128)S(1)} collective-permute-done((f32[2,256,128]{2,1,0:T(8,128)S(1)}, f32[2,256,128]{2,1,0:T(8,128)S(1)}, u32[]{:S(2)}, u32[]{:S(2)}) %collective-permute-start.18) | collective-permute-done | bytes 262176 | tf_op jit(solution)/shard_map/ppermute | solution.py:63
  115.3 8.3 %collective-permute-done.19 = f32[1,256,128]{2,1,0:T(8,128)S(1)} collective-permute-done((f32[1,256,128]{2,1,0:T(8,128)S(1)}, f32[1,256,128]{2,1,0:T(8,128)S(1)}, u32[]{:S(2)}, u32[]{:S(2)}) %collective-permute-start.19) | collective-permute-done | bytes 131104 | tf_op jit(solution)/shard_map/ppermute | solution.py:63
  123.7 1.5 collective-permute-start.20
  125.3 2.8 %collective-permute-done.20 = bf16[256,128]{1,0:T(8,128)(2,1)S(1)} collective-permute-done((bf16[256,128]{1,0:T(8,128)(2,1)S(1)}, bf16[256,128]{1,0:T(8,128)(2,1)S(1)}, u32[]{:S(2)}, u32[]{:S(2)}) %collective-permute-start.20) | collective-permute-done | bytes 65568 | tf_op jit(solution)/shard_map/ppermute | solution.py:77
  128.5 4.7 %collective-permute-done.21 = bf16[512,128]{1,0:T(8,128)(2,1)S(1)} collective-permute-done((bf16[512,128]{1,0:T(8,128)(2,1)S(1)}, bf16[512,128]{1,0:T(8,128)(2,1)S(1)}, u32[]{:S(2)}, u32[]{:S(2)}) %collective-permute-start.21) | collective-permute-done | bytes 131104 | tf_op jit(solution)/shard_map/ppermute | solution.py:77
  133.2 1.5 fusion.31
  136.9 1.9 collective-permute-done.22
  139.0 8.3 %collective-permute-done.23 = f32[2,256,128]{2,1,0:T(8,128)S(1)} collective-permute-done((f32[2,256,128]{2,1,0:T(8,128)S(1)}, f32[2,256,128]{2,1,0:T(8,128)S(1)}, u32[]{:S(2)}, u32[]{:S(2)}) %collective-permute-start.23) | collective-permute-done | bytes 262176 | tf_op jit(solution)/shard_map/ppermute | solution.py:63
  147.5 8.3 %collective-permute-done.24 = f32[1,256,128]{2,1,0:T(8,128)S(1)} collective-permute-done((f32[1,256,128]{2,1,0:T(8,128)S(1)}, f32[1,256,128]{2,1,0:T(8,128)S(1)}, u32[]{:S(2)}, u32[]{:S(2)}) %collective-permute-start.24) | collective-permute-done | bytes 131104 | tf_op jit(solution)/shard_map/ppermute | solution.py:63
  156.0 1.5 collective-permute-start.25
  157.5 2.8 %collective-permute-done.25 = bf16[256,128]{1,0:T(8,128)(2,1)S(1)} collective-permute-done((bf16[256,128]{1,0:T(8,128)(2,1)S(1)}, bf16[256,128]{1,0:T(8,128)(2,1)S(1)}, u32[]{:S(2)}, u32[]{:S(2)}) %collective-permute-start.25) | collective-permute-done | bytes 65568 | tf_op jit(solution)/shard_map/ppermute | solution.py:77
  160.7 4.7 %collective-permute-done.26 = bf16[512,128]{1,0:T(8,128)(2,1)S(1)} collective-permute-done((bf16[512,128]{1,0:T(8,128)(2,1)S(1)}, bf16[512,128]{1,0:T(8,128)(2,1)S(1)}, u32[]{:S(2)}, u32[]{:S(2)}) %collective-permute-start.26) | collective-permute-done | bytes 131104 | tf_op jit(solution)/shard_map/ppermute | solution.py:77
  168.9 1.9 collective-permute-done.27
  171.0 8.3 %collective-permute-done.28 = f32[2,256,128]{2,1,0:T(8,128)S(1)} collective-permute-done((f32[2,256,128]{2,1,0:T(8,128)S(1)}, f32[2,256,128]{2,1,0:T(8,128)S(1)}, u32[]{:S(2)}, u32[]{:S(2)}) %collective-permute-start.28) | collective-permute-done | bytes 262176 | tf_op jit(solution)/shard_map/ppermute | solution.py:63
  179.9 7.9 %collective-permute-done.29 = f32[1,256,128]{2,1,0:T(8,128)S(1)} collective-permute-done((f32[1,256,128]{2,1,0:T(8,128)S(1)}, f32[1,256,128]{2,1,0:T(8,128)S(1)}, u32[]{:S(2)}, u32[]{:S(2)}) %collective-permute-start.29) | collective-permute-done | bytes 131104 | tf_op jit(solution)/shard_map/ppermute | solution.py:63
  188.4 1.3 collective-permute-done.30
  189.9 5.5 %collective-permute-done.31 = f32[256,128]{0,1:T(8,128)S(1)} collective-permute-done((f32[256,128]{0,1:T(8,128)S(1)}, f32[256,128]{0,1:T(8,128)S(1)}, u32[]{:S(2)}, u32[]{:S(2)}) %collective-permute-start.31) | collective-permute-done | bytes 131104 | tf_op jit(solution)/shard_map/ppermute | solution.py:28
  195.5 8.3 %collective-permute-done.32 = f32[256,128]{0,1:T(8,128)S(1)} collective-permute-done((f32[256,128]{0,1:T(8,128)S(1)}, f32[256,128]{0,1:T(8,128)S(1)}, u32[]{:S(2)}, u32[]{:S(2)}) %collective-permute-start.32) | collective-permute-done | bytes 131104 | tf_op jit(solution)/shard_map/ppermute | solution.py:28
  203.9 1.5 collective-permute-start.33
  205.5 3.9 %collective-permute-done.33 = f32[256,128]{0,1:T(8,128)S(1)} collective-permute-done((f32[256,128]{0,1:T(8,128)S(1)}, f32[256,128]{0,1:T(8,128)S(1)}, u32[]{:S(2)}, u32[]{:S(2)}) %collective-permute-start.33) | collective-permute-done | bytes 131104 | tf_op jit(solution)/shard_map/ppermute | solution.py:28
  209.8 4.7 %collective-permute-done.34 = f32[256,128]{0,1:T(8,128)S(1)} collective-permute-done((f32[256,128]{0,1:T(8,128)S(1)}, f32[256,128]{0,1:T(8,128)S(1)}, u32[]{:S(2)}, u32[]{:S(2)}) %collective-permute-start.34) | collective-permute-done | bytes 131104 | tf_op jit(solution)/shard_map/ppermute | solution.py:28
  214.6 11.7 %cholesky.16 = f32[128,128]{1,0:T(8,128)S(1)} custom-call(f32[128,128]{1,0:T(8,128)S(1)} %fusion.42), custom_call_target="Cholesky" | custom-call | tf_op jit(solution)/shard_map/jit(cholesky)/cholesky | solution.py:148
  227.6 10.0 %custom-call.10 = f32[1,128,128]{1,2,0:T(8,128)S(1)} custom-call(f32[1,128,128]{2,1,0:T(8,128)S(1)} %fusion.35), custom_call_target="InvertDiagBlocksLowerTriangular" | custom-call | tf_op jit(solution)/shard_map/triangular_solve | solution.py:149
  (143 shorter events, 26.6 us)
Async XLA Ops:
  1.6 19.7 %collective-permute-start = (bf16[256,128]{1,0:T(8,128)(2,1)S(1)}, bf16[256,128]{1,0:T(8,128)(2,1)S(1)}, u32[]{:S(2)}, u32[]{:S(2)}) collective-permute-start(bf16[256,128]{1,0:T(8,128)(2,1)S(1)} %multiply_convert_fusion.4), channel_id=1, source_target_pairs={{0,8},{8,0},{16,24},{24,16},{1,9},{9,1},{17,25},{25,17},{2,10},{10... | collective-permute-start | bytes 196616 | tf_op jit(solution)/shard_map/ppermute | solution.py:77
  4.7 20.1 %collective-permute-start.5 = (bf16[256,128]{1,0:T(8,128)(2,1)}, bf16[256,128]{1,0:T(8,128)(2,1)S(1)}, u32[]{:S(2)}, u32[]{:S(2)}) collective-permute-start(bf16[256,128]{1,0:T(8,128)(2,1)} %param.12), channel_id=1, source_target_pairs={{0,8},{8,0},{16,24},{24,16},{1,9},{9,1},{17,25},{25,17},{2,10},{10... | collective-permute-start | bytes 196616 | tf_op jit(solution)/shard_map/ppermute | solution.py:77
  4.8 18.3 %collective-permute-start.2 = (bf16[1,256,128]{2,1,0:T(8,128)(2,1)}, bf16[1,256,128]{2,1,0:T(8,128)(2,1)S(1)}, u32[]{:S(2)}, u32[]{:S(2)}) collective-permute-start(bf16[1,256,128]{2,1,0:T(8,128)(2,1)} %bitcast.182), channel_id=1, source_target_pairs={{0,4},{1,5},{2,6},{3,7},{4,0},{5,1},{6,2},{7,3},{8,12},{9,13},{10,... | collective-permute-start | bytes 196616 | tf_op jit(solution)/shard_map/ppermute | solution.py:95
  16.0 5.3 %copy-start.7 = (s32[8]{0:T(128)S(1)}, s32[8]{0:T(128)}, u32[]{:S(2)}) copy-start(s32[8]{0:T(128)} %constant.326) | copy-start | bytes 100
  16.0 5.3 %copy-start.3 = (f32[256,128]{1,0:T(8,128)S(1)}, f32[256,128]{1,0:T(8,128)}, u32[]{:S(2)}) copy-start(f32[256,128]{1,0:T(8,128)} %param.11) | copy-start | bytes 393220
  16.0 5.3 %copy-start.5 = (f32[256]{0:T(256)S(1)}, f32[256]{0:T(256)}, u32[]{:S(2)}) copy-start(f32[256]{0:T(256)} %param.10) | copy-start | bytes 3076
  16.0 7.0 %copy-start.4 = (bf16[256,128]{1,0:T(8,128)(2,1)S(1)}, bf16[256,128]{1,0:T(8,128)(2,1)}, u32[]{:S(2)}) copy-start(bf16[256,128]{1,0:T(8,128)(2,1)} %param.12) | copy-start | bytes 196612
  21.5 6.8 %collective-permute-start.1 = (bf16[512,128]{1,0:T(8,128)(2,1)S(1)}, bf16[512,128]{1,0:T(8,128)(2,1)S(1)}, u32[]{:S(2)}, u32[]{:S(2)}) collective-permute-start(bf16[512,128]{1,0:T(8,128)(2,1)S(1)} %pad_maximum_fusion.8), channel_id=1, source_target_pairs={{0,16},{8,24},{16,0},{24,8},{1,17},{9,25},{17,1},{25,9},{2,18},{10... | collective-permute-start | bytes 393224 | tf_op jit(solution)/shard_map/ppermute | solution.py:77
  23.1 5.0 %collective-permute-start.3 = (bf16[2,256,128]{2,1,0:T(8,128)(2,1)S(1)}, bf16[2,256,128]{2,1,0:T(8,128)(2,1)S(1)}, u32[]{:S(2)}, u32[]{:S(2)}) collective-permute-start(bf16[2,256,128]{2,1,0:T(8,128)(2,1)S(1)} %pad_maximum_fusion.9), channel_id=1, source_target_pairs={{0,2},{1,3},{2,0},{3,1},{4,6},{5,7},{6,4},{7,5},{8,10},{9,11},{10,... | collective-permute-start | bytes 393224 | tf_op jit(solution)/shard_map/ppermute | solution.py:95
  24.8 7.0 %collective-permute-start.6 = (bf16[512,128]{1,0:T(8,128)(2,1)S(1)}, bf16[512,128]{1,0:T(8,128)(2,1)S(1)}, u32[]{:S(2)}, u32[]{:S(2)}) collective-permute-start(bf16[512,128]{1,0:T(8,128)(2,1)S(1)} %pad_maximum_fusion.10), channel_id=1, source_target_pairs={{0,16},{8,24},{16,0},{24,8},{1,17},{9,25},{17,1},{25,9},{2,18},{10... | collective-permute-start | bytes 393224 | tf_op jit(solution)/shard_map/ppermute | solution.py:77
  28.2 3.7 %copy-start.8 = (f32[128]{0:T(128)S(1)}, f32[128]{0:T(128)}, u32[]{:S(2)}) copy-start(f32[128]{0:T(128)} %param.13) | copy-start | bytes 1540
  28.2 4.0 %collective-permute-start.4 = (bf16[4,256,128]{2,1,0:T(8,128)(2,1)S(1)}, bf16[4,256,128]{2,1,0:T(8,128)(2,1)S(1)}, u32[]{:S(2)}, u32[]{:S(2)}) collective-permute-start(bf16[4,256,128]{2,1,0:T(8,128)(2,1)S(1)} %pad_maximum_fusion.2), channel_id=1, source_target_pairs={{0,1},{1,0},{2,3},{3,2},{4,5},{5,4},{6,7},{7,6},{8,9},{9,8},{10,11... | collective-permute-start | bytes 786440 | tf_op jit(solution)/shard_map/ppermute | solution.py:95
  32.9 2.2 copy-start
  36.4 11.4 %copy-start.6 = (f32[2]{0:T(128)S(1)}, f32[2]{0:T(128)}, u32[]{:S(2)}) copy-start(f32[2]{0:T(128)} %param.14) | copy-start | bytes 28
  36.5 2.1 collective-permute-start.7
  38.6 8.7 %collective-permute-start.8 = (f32[2,256,128]{2,1,0:T(8,128)S(1)}, f32[2,256,128]{2,1,0:T(8,128)S(1)}, u32[]{:S(2)}, u32[]{:S(2)}) collective-permute-start(f32[2,256,128]{2,1,0:T(8,128)S(1)} %dynamic-slice_bitcast_fusion.9), channel_id=1, source_target_pairs={{0,2},{1,3},{2,0},{3,1},{4,6},{5,7},{6,4},{7,5},{8,10},{9,11},{10,... | collective-permute-start | bytes 786440 | tf_op jit(solution)/shard_map/ppermute | solution.py:63
  47.4 8.7 %collective-permute-start.9 = (f32[1,256,128]{2,1,0:T(8,128)S(1)}, f32[1,256,128]{2,1,0:T(8,128)S(1)}, u32[]{:S(2)}, u32[]{:S(2)}) collective-permute-start(f32[1,256,128]{2,1,0:T(8,128)S(1)} %constant_dynamic-slice_fusion.3), channel_id=1, source_target_pairs={{0,4},{1,5},{2,6},{3,7},{4,0},{5,1},{6,2},{7,3},{8,12},{9,13},{10,... | collective-permute-start | bytes 393224 | tf_op jit(solution)/shard_map/ppermute | solution.py:63
  56.2 4.3 %collective-permute-start.10 = (bf16[256,128]{1,0:T(8,128)(2,1)S(1)}, bf16[256,128]{1,0:T(8,128)(2,1)S(1)}, u32[]{:S(2)}, u32[]{:S(2)}) collective-permute-start(bf16[256,128]{1,0:T(8,128)(2,1)S(1)} %get-tuple-element.8), channel_id=1, source_target_pairs={{0,8},{8,0},{16,24},{24,16},{1,9},{9,1},{17,25},{25,17},{2,10},{10... | collective-permute-start | bytes 196616 | tf_op jit(solution)/shard_map/ppermute | solution.py:77
  60.5 5.0 %collective-permute-start.11 = (bf16[512,128]{1,0:T(8,128)(2,1)S(1)}, bf16[512,128]{1,0:T(8,128)(2,1)S(1)}, u32[]{:S(2)}, u32[]{:S(2)}) collective-permute-start(bf16[512,128]{1,0:T(8,128)(2,1)S(1)} %pad_maximum_fusion.11), channel_id=1, source_target_pairs={{0,16},{8,24},{16,0},{24,8},{1,17},{9,25},{17,1},{25,9},{2,18},{10... | collective-permute-start | bytes 393224 | tf_op jit(solution)/shard_map/ppermute | solution.py:77
  69.1 2.2 copy-start.1
  72.5 28.7 %copy-start.2 = (bf16[2048,1024]{1,0:T(8,128)(2,1)S(1)}, bf16[2048,1024]{1,0:T(8,128)(2,1)}, u32[]{:S(2)}) copy-start(bf16[2048,1024]{1,0:T(8,128)(2,1)} %get-tuple-element.10) | copy-start | bytes 12582916
  72.6 2.0 collective-permute-start.12
  74.7 8.4 %collective-permute-start.13 = (f32[2,256,128]{2,1,0:T(8,128)S(1)}, f32[2,256,128]{2,1,0:T(8,128)S(1)}, u32[]{:S(2)}, u32[]{:S(2)}) collective-permute-start(f32[2,256,128]{2,1,0:T(8,128)S(1)} %dynamic-slice_bitcast_fusion.8), channel_id=1, source_target_pairs={{0,2},{1,3},{2,0},{3,1},{4,6},{5,7},{6,4},{7,5},{8,10},{9,11},{10,... | collective-permute-start | bytes 786440 | tf_op jit(solution)/shard_map/ppermute | solution.py:63
  83.2 8.5 %collective-permute-start.14 = (f32[1,256,128]{2,1,0:T(8,128)S(1)}, f32[1,256,128]{2,1,0:T(8,128)S(1)}, u32[]{:S(2)}, u32[]{:S(2)}) collective-permute-start(f32[1,256,128]{2,1,0:T(8,128)S(1)} %constant_dynamic-slice_fusion.2), channel_id=1, source_target_pairs={{0,4},{1,5},{2,6},{3,7},{4,0},{5,1},{6,2},{7,3},{8,12},{9,13},{10,... | collective-permute-start | bytes 393224 | tf_op jit(solution)/shard_map/ppermute | solution.py:63
  91.7 4.3 %collective-permute-start.15 = (bf16[256,128]{1,0:T(8,128)(2,1)S(1)}, bf16[256,128]{1,0:T(8,128)(2,1)S(1)}, u32[]{:S(2)}, u32[]{:S(2)}) collective-permute-start(bf16[256,128]{1,0:T(8,128)(2,1)S(1)} %get-tuple-element.6), channel_id=1, source_target_pairs={{0,8},{8,0},{16,24},{24,16},{1,9},{9,1},{17,25},{25,17},{2,10},{10... | collective-permute-start | bytes 196616 | tf_op jit(solution)/shard_map/ppermute | solution.py:77
  96.1 5.0 %collective-permute-start.16 = (bf16[512,128]{1,0:T(8,128)(2,1)S(1)}, bf16[512,128]{1,0:T(8,128)(2,1)S(1)}, u32[]{:S(2)}, u32[]{:S(2)}) collective-permute-start(bf16[512,128]{1,0:T(8,128)(2,1)S(1)} %pad_maximum_fusion.12), channel_id=1, source_target_pairs={{0,16},{8,24},{16,0},{24,8},{1,17},{9,25},{17,1},{25,9},{2,18},{10... | collective-permute-start | bytes 393224 | tf_op jit(solution)/shard_map/ppermute | solution.py:77
  104.6 2.0 collective-permute-start.17
  106.7 8.4 %collective-permute-start.18 = (f32[2,256,128]{2,1,0:T(8,128)S(1)}, f32[2,256,128]{2,1,0:T(8,128)S(1)}, u32[]{:S(2)}, u32[]{:S(2)}) collective-permute-start(f32[2,256,128]{2,1,0:T(8,128)S(1)} %dynamic-slice_bitcast_fusion.7), channel_id=1, source_target_pairs={{0,2},{1,3},{2,0},{3,1},{4,6},{5,7},{6,4},{7,5},{8,10},{9,11},{10,... | collective-permute-start | bytes 786440 | tf_op jit(solution)/shard_map/ppermute | solution.py:63
  115.2 8.5 %collective-permute-start.19 = (f32[1,256,128]{2,1,0:T(8,128)S(1)}, f32[1,256,128]{2,1,0:T(8,128)S(1)}, u32[]{:S(2)}, u32[]{:S(2)}) collective-permute-start(f32[1,256,128]{2,1,0:T(8,128)S(1)} %constant_dynamic-slice_fusion.1), channel_id=1, source_target_pairs={{0,4},{1,5},{2,6},{3,7},{4,0},{5,1},{6,2},{7,3},{8,12},{9,13},{10,... | collective-permute-start | bytes 393224 | tf_op jit(solution)/shard_map/ppermute | solution.py:63
  123.7 4.3 %collective-permute-start.20 = (bf16[256,128]{1,0:T(8,128)(2,1)S(1)}, bf16[256,128]{1,0:T(8,128)(2,1)S(1)}, u32[]{:S(2)}, u32[]{:S(2)}) collective-permute-start(bf16[256,128]{1,0:T(8,128)(2,1)S(1)} %get-tuple-element.4), channel_id=1, source_target_pairs={{0,8},{8,0},{16,24},{24,16},{1,9},{9,1},{17,25},{25,17},{2,10},{10... | collective-permute-start | bytes 196616 | tf_op jit(solution)/shard_map/ppermute | solution.py:77
  128.1 5.0 %collective-permute-start.21 = (bf16[512,128]{1,0:T(8,128)(2,1)S(1)}, bf16[512,128]{1,0:T(8,128)(2,1)S(1)}, u32[]{:S(2)}, u32[]{:S(2)}) collective-permute-start(bf16[512,128]{1,0:T(8,128)(2,1)S(1)} %pad_maximum_fusion.13), channel_id=1, source_target_pairs={{0,16},{8,24},{16,0},{24,8},{1,17},{9,25},{17,1},{25,9},{2,18},{10... | collective-permute-start | bytes 393224 | tf_op jit(solution)/shard_map/ppermute | solution.py:77
  136.9 2.0 collective-permute-start.22
  138.9 8.4 %collective-permute-start.23 = (f32[2,256,128]{2,1,0:T(8,128)S(1)}, f32[2,256,128]{2,1,0:T(8,128)S(1)}, u32[]{:S(2)}, u32[]{:S(2)}) collective-permute-start(f32[2,256,128]{2,1,0:T(8,128)S(1)} %dynamic-slice_bitcast_fusion.6), channel_id=1, source_target_pairs={{0,2},{1,3},{2,0},{3,1},{4,6},{5,7},{6,4},{7,5},{8,10},{9,11},{10,... | collective-permute-start | bytes 786440 | tf_op jit(solution)/shard_map/ppermute | solution.py:63
  147.4 8.5 %collective-permute-start.24 = (f32[1,256,128]{2,1,0:T(8,128)S(1)}, f32[1,256,128]{2,1,0:T(8,128)S(1)}, u32[]{:S(2)}, u32[]{:S(2)}) collective-permute-start(f32[1,256,128]{2,1,0:T(8,128)S(1)} %constant_dynamic-slice_fusion), channel_id=1, source_target_pairs={{0,4},{1,5},{2,6},{3,7},{4,0},{5,1},{6,2},{7,3},{8,12},{9,13},{10,... | collective-permute-start | bytes 393224 | tf_op jit(solution)/shard_map/ppermute | solution.py:63
  156.0 4.3 %collective-permute-start.25 = (bf16[256,128]{1,0:T(8,128)(2,1)S(1)}, bf16[256,128]{1,0:T(8,128)(2,1)S(1)}, u32[]{:S(2)}, u32[]{:S(2)}) collective-permute-start(bf16[256,128]{1,0:T(8,128)(2,1)S(1)} %get-tuple-element.2), channel_id=1, source_target_pairs={{0,8},{8,0},{16,24},{24,16},{1,9},{9,1},{17,25},{25,17},{2,10},{10... | collective-permute-start | bytes 196616 | tf_op jit(solution)/shard_map/ppermute | solution.py:77
  160.4 5.0 %collective-permute-start.26 = (bf16[512,128]{1,0:T(8,128)(2,1)S(1)}, bf16[512,128]{1,0:T(8,128)(2,1)S(1)}, u32[]{:S(2)}, u32[]{:S(2)}) collective-permute-start(bf16[512,128]{1,0:T(8,128)(2,1)S(1)} %pad_maximum_fusion.14), channel_id=1, source_target_pairs={{0,16},{8,24},{16,0},{24,8},{1,17},{9,25},{17,1},{25,9},{2,18},{10... | collective-permute-start | bytes 393224 | tf_op jit(solution)/shard_map/ppermute | solution.py:77
  168.9 2.0 collective-permute-start.27
  170.9 8.4 %collective-permute-start.28 = (f32[2,256,128]{2,1,0:T(8,128)S(1)}, f32[2,256,128]{2,1,0:T(8,128)S(1)}, u32[]{:S(2)}, u32[]{:S(2)}) collective-permute-start(f32[2,256,128]{2,1,0:T(8,128)S(1)} %dynamic-slice_bitcast_fusion.5), channel_id=1, source_target_pairs={{0,2},{1,3},{2,0},{3,1},{4,6},{5,7},{6,4},{7,5},{8,10},{9,11},{10,... | collective-permute-start | bytes 786440 | tf_op jit(solution)/shard_map/ppermute | solution.py:63
  179.4 8.5 %collective-permute-start.29 = (f32[1,256,128]{2,1,0:T(8,128)S(1)}, f32[1,256,128]{2,1,0:T(8,128)S(1)}, u32[]{:S(2)}, u32[]{:S(2)}) collective-permute-start(f32[1,256,128]{2,1,0:T(8,128)S(1)} %constant_dynamic-slice_fusion.4), channel_id=1, source_target_pairs={{0,4},{1,5},{2,6},{3,7},{4,0},{5,1},{6,2},{7,3},{8,12},{9,13},{10,... | collective-permute-start | bytes 393224 | tf_op jit(solution)/shard_map/ppermute | solution.py:63
  188.3 1.4 collective-permute-start.30
  189.8 5.6 %collective-permute-start.31 = (f32[256,128]{0,1:T(8,128)S(1)}, f32[256,128]{0,1:T(8,128)S(1)}, u32[]{:S(2)}, u32[]{:S(2)}) collective-permute-start(f32[256,128]{0,1:T(8,128)S(1)} %fusion.80), channel_id=1, source_target_pairs={{0,2},{1,3},{2,0},{3,1},{4,6},{5,7},{6,4},{7,5},{8,10},{9,11},{10,... | collective-permute-start | bytes 393224 | tf_op jit(solution)/shard_map/ppermute | solution.py:28
  195.4 8.5 %collective-permute-start.32 = (f32[256,128]{0,1:T(8,128)S(1)}, f32[256,128]{0,1:T(8,128)S(1)}, u32[]{:S(2)}, u32[]{:S(2)}) collective-permute-start(f32[256,128]{0,1:T(8,128)S(1)} %add.265), channel_id=1, source_target_pairs={{0,4},{1,5},{2,6},{3,7},{4,0},{5,1},{6,2},{7,3},{8,12},{9,13},{10,... | collective-permute-start | bytes 393224 | tf_op jit(solution)/shard_map/ppermute | solution.py:28
  203.9 5.5 %collective-permute-start.33 = (f32[256,128]{0,1:T(8,128)S(1)}, f32[256,128]{0,1:T(8,128)S(1)}, u32[]{:S(2)}, u32[]{:S(2)}) collective-permute-start(f32[256,128]{0,1:T(8,128)S(1)} %add.266), channel_id=1, source_target_pairs={{0,8},{8,0},{16,24},{24,16},{1,9},{9,1},{17,25},{25,17},{2,10},{10... | collective-permute-start | bytes 393224 | tf_op jit(solution)/shard_map/ppermute | solution.py:28
  209.4 5.0 %collective-permute-start.34 = (f32[256,128]{0,1:T(8,128)S(1)}, f32[256,128]{0,1:T(8,128)S(1)}, u32[]{:S(2)}, u32[]{:S(2)}) collective-permute-start(f32[256,128]{0,1:T(8,128)S(1)} %add.267), channel_id=1, source_target_pairs={{0,16},{8,24},{16,0},{24,8},{1,17},{9,25},{17,1},{25,9},{2,18},{10... | collective-permute-start | bytes 393224 | tf_op jit(solution)/shard_map/ppermute | solution.py:28

commit v7 on v6

--- a/solution.py
+++ b/solution.py
@@ -1,6 +1,8 @@
 import jax
 import jax.numpy as jnp
 from jax import lax
+from jax.experimental import pallas as pl
+from jax.experimental.pallas import tpu as pltpu
 from jax.sharding import PartitionSpec as P
 
 DEGREE = 4
@@ -103,6 +105,41 @@
     return result[jnp.array(order)].reshape(-1, value.shape[1])
 
 
+def dense_parts(tiles, tile_cols, n_blocks):
+    tile_rows, slots, tile_size = tiles.shape[0], tiles.shape[1], tiles.shape[2]
+    width = n_blocks * tile_size
+
+    def kernel(cols_ref, tiles_ref, hi_ref, lo_ref, acc_ref):
+        row = pl.program_id(0)
+        acc_ref[...] = jnp.zeros_like(acc_ref)
+        for slot in range(slots):
+            start = pl.multiple_of(cols_ref[row, slot] * tile_size, tile_size)
+            window = pl.ds(start, tile_size)
+            acc_ref[:, window] = acc_ref[:, window] + tiles_ref[0, slot].astype(jnp.float32)
+        total = acc_ref[...]
+        upper = total.astype(jnp.bfloat16)
+        hi_ref[...] = upper
+        lo_ref[...] = (total - upper.astype(jnp.float32)).astype(jnp.bfloat16)
+
+    grid_spec = pltpu.PrefetchScalarGridSpec(
+        num_scalar_prefetch=1,
+        grid=(tile_rows,),
+        in_specs=[pl.BlockSpec((1, slots, tile_size, tile_size), lambda r, cols: (r, 0, 0, 0))],
+        out_specs=[
+            pl.BlockSpec((tile_size, width), lambda r, cols: (r, 0)),
+            pl.BlockSpec((tile_size, width), lambda r, cols: (r, 0)),
+        ],
+        scratch_shapes=[pltpu.VMEM((tile_size, width), jnp.float32)],
+    )
+    shape = jax.ShapeDtypeStruct((tile_rows * tile_size, width), jnp.bfloat16)
+    return pl.pallas_call(
+        kernel,
+        grid_spec=grid_spec,
+        out_shape=(shape, shape),
+        compiler_params=pltpu.CompilerParams(dimension_semantics=("arbitrary",)),
+    )(tile_cols, tiles)
+
+
 def local(tiles, tile_cols, degree_scale, start_block, planted, strengths, bounds):
     piece_rows = start_block.shape[0]
     node_count = piece_rows * lax.axis_size("row") * lax.axis_size("col")
@@ -110,10 +147,7 @@
     n_blocks = lax.axis_size("row") * piece_rows // tile_size
     weights = strengths[:, None]
 
-    onehot = (tile_cols[:, :, None] == jnp.arange(n_blocks, dtype=jnp.int32)[None, None, :]).astype(jnp.bfloat16)
-    dense = jnp.einsum("rst,rsab->ratb", onehot, tiles, preferred_element_type=jnp.float32)
-    dense = dense.reshape(tile_rows * tile_size, n_blocks * tile_size)
-    w_hi, w_lo = split_bf16(dense)
+    w_hi, w_lo = dense_parts(tiles, tile_cols, n_blocks)
 
     planted_cols = doubling_gather(planted, "row")
     planted_rows = far_first_gather(planted, "col")

time: 240 us -> 240 us (level)
  Pallas kernels: 0 us -> 14.8 us
  matrix products: 32.4 us -> 24.3 us
  other arithmetic: 31 us -> 25.7 us
    pallas_call x0 -> x1, Pallas kernels: none -> 14.8 us  [dense_parts(): pl.pallas_call(kernel, grid_spec=grid_spec, out_shape=(shape, shape), com...]
    dot_general x1 -> x0, matrix products: 8.2 us -> none  [local(): jnp.einsum('rst,rsab->ratb', onehot, tiles, preferred_element_type=jnp.fl...]
    convert_element_type x1 -> x0, other arithmetic: 5.26 us -> none  [split_bf16(): lower = (value - upper.astype(jnp.float32)).astype(jnp.bfloat16)]
  transfers between devices with their start and end apart: 35 -> 35, of which waited for: 29 -> 29; matrix products, arithmetic and copies ran while one was open for 8% -> 2% of each run, Pallas kernels for 0% -> 6%
where the time goes in v7:
time: 240 us
  waiting for transfers between devices  144 us (60%)
  other arithmetic  25.7 us (11%)
  matrix products  24.3 us (10%)
  starting transfers between devices  23.6 us (10%)
  Pallas kernels  14.8 us (6%)
  between operations  4.03 us (2%)
  local copies, waits for them, and re-layouts  3.39 us (1%)
    ppermute x15, waiting for transfers between devices, halving_scatter_sum(): blocks = kept + lax.ppermute(sent, axis, pairs)  87.6 us
    ppermute x12, waiting for transfers between devices, doubling_gather(): other = lax.ppermute(result, axis, pairs)  29.7 us
    ppermute x5, waiting for transfers between devices, butterfly_sum(): value = value + lax.ppermute(value, axis, pairs)  23.8 us
    pallas_call x1, Pallas kernels, dense_parts(): pl.pallas_call(kernel, grid_spec=grid_spec, out_shape=(shape, shape), com...  14.8 us
    ppermute x12, starting transfers between devices, doubling_gather(): other = lax.ppermute(result, axis, pairs)  13 us
    another operation x3, other arithmetic, local(): factor = jnp.linalg.cholesky(gram_matrix)  12.4 us
    dot_general x5, matrix products, operate(): jnp.dot(w_lo, gathered, preferred_element_type=jnp.float32)  11 us
    another operation x2, other arithmetic, local(): lax.linalg.triangular_solve(factor, current, left_side=False, lower=True,...  10.6 us
  transfers between devices with their start and end apart: 35, of which 29 were waited for; matrix products, arithmetic and copies ran while one was open for 2% of the time, Pallas kernels for 6%

profile of v7, /device:TPU:0, one launch (start us, length us, event | category | flops | bytes accessed | tf_op | source)
XLA Modules:
  0.0 239.7 jit_solution(4140481366568305112)
XLA Ops:
  1.6 3.0 %collective-permute-start = (bf16[256,128]{1,0:T(8,128)(2,1)S(1)}, bf16[256,128]{1,0:T(8,128)(2,1)S(1)}, u32[]{:S(2)}, u32[]{:S(2)}) collective-permute-start(bf16[256,128]{1,0:T(8,128)(2,1)S(1)} %multiply_convert_fusion.4), channel_id=1, source_target_pairs={{0,8},{8,0},{16,24},{24,16},{1,9},{9,1},{17,25},{25,17},{2,10},{10... | collective-permute-start | bytes 196616 | tf_op jit(solution)/shard_map/ppermute | solution.py:79
  4.8 3.0 %collective-permute-start.2 = (bf16[1,256,128]{2,1,0:T(8,128)(2,1)}, bf16[1,256,128]{2,1,0:T(8,128)(2,1)S(1)}, u32[]{:S(2)}, u32[]{:S(2)}) collective-permute-start(bf16[1,256,128]{2,1,0:T(8,128)(2,1)} %bitcast.167), channel_id=1, source_target_pairs={{0,4},{1,5},{2,6},{3,7},{4,0},{5,1},{6,2},{7,3},{8,12},{9,13},{10,... | collective-permute-start | bytes 196616 | tf_op jit(solution)/shard_map/ppermute | solution.py:97
  7.8 14.8 %shard_map.95 = (bf16[2048,1024]{1,0:T(8,128)(2,1)}, bf16[2048,1024]{1,0:T(8,128)(2,1)}) custom-call(s32[16,16]{1,0:T(8,128)} %cols_ref.1, bf16[16,16,128,128]{3,2,1,0:T(8,128)(2,1)} %tiles_ref.1), custom_call_target="tpu_custom_call" | custom-call | tf_op jit(solution)/shard_map/pallas_call | solution.py:135
  22.8 1.6 collective-permute-start.1
  24.4 1.7 collective-permute-start.3
  26.7 2.7 %collective-permute-done.3 = bf16[2,256,128]{2,1,0:T(8,128)(2,1)S(1)} collective-permute-done((bf16[2,256,128]{2,1,0:T(8,128)(2,1)S(1)}, bf16[2,256,128]{2,1,0:T(8,128)(2,1)S(1)}, u32[]{:S(2)}, u32[]{:S(2)}) %collective-permute-start.3) | collective-permute-done | bytes 131104 | tf_op jit(solution)/shard_map/ppermute | solution.py:97
  29.7 3.4 %fusion.31 = f32[2048,128]{1,0:T(8,128)S(1)} fusion(bf16[2048,1024]{1,0:T(8,128)(2,1)} %get-tuple-element.5, bf16[512,128]{1,0:T(8,128)(2,1)S(1)} %get-tuple-element.27, bf16[512,128]{1,0:T(8,128)(2,1)S(1)} %get-tuple-element.26), kind=kOutput, calls=%fused_computation.109 | convolution fusion | flops 537395200 | bytes 5505024 | tf_op jit(solution)/shard_map/dot_general | solution.py:159
  34.8 1.6 copy-done
  36.4 1.3 fusion.9
  38.3 1.5 collective-permute-done.7
  40.0 1.7 collective-permute-start.8
  41.6 7.0 %collective-permute-done.8 = f32[2,256,128]{2,1,0:T(8,128)S(1)} collective-permute-done((f32[2,256,128]{2,1,0:T(8,128)S(1)}, f32[2,256,128]{2,1,0:T(8,128)S(1)}, u32[]{:S(2)}, u32[]{:S(2)}) %collective-permute-start.8) | collective-permute-done | bytes 262176 | tf_op jit(solution)/shard_map/ppermute | solution.py:65
  52.2 5.1 %collective-permute-done.9 = f32[1,256,128]{2,1,0:T(8,128)S(1)} collective-permute-done((f32[1,256,128]{2,1,0:T(8,128)S(1)}, f32[1,256,128]{2,1,0:T(8,128)S(1)}, u32[]{:S(2)}, u32[]{:S(2)}) %collective-permute-start.9) | collective-permute-done | bytes 131104 | tf_op jit(solution)/shard_map/ppermute | solution.py:65
  57.5 1.6 collective-permute-start.10
  59.0 2.8 %collective-permute-done.10 = bf16[256,128]{1,0:T(8,128)(2,1)S(1)} collective-permute-done((bf16[256,128]{1,0:T(8,128)(2,1)S(1)}, bf16[256,128]{1,0:T(8,128)(2,1)S(1)}, u32[]{:S(2)}, u32[]{:S(2)}) %collective-permute-start.10) | collective-permute-done | bytes 65568 | tf_op jit(solution)/shard_map/ppermute | solution.py:79
  62.2 4.7 %collective-permute-done.11 = bf16[512,128]{1,0:T(8,128)(2,1)S(1)} collective-permute-done((bf16[512,128]{1,0:T(8,128)(2,1)S(1)}, bf16[512,128]{1,0:T(8,128)(2,1)S(1)}, u32[]{:S(2)}, u32[]{:S(2)}) %collective-permute-start.11) | collective-permute-done | bytes 131104 | tf_op jit(solution)/shard_map/ppermute | solution.py:79
  67.2 3.6 %fusion.30 = f32[2048,128]{1,0:T(8,128)S(1)} fusion(bf16[2048,1024]{1,0:T(8,128)(2,1)} %get-tuple-element.5, bf16[512,128]{1,0:T(8,128)(2,1)S(1)} %get-tuple-element.23, bf16[512,128]{1,0:T(8,128)(2,1)S(1)} %get-tuple-element.22), kind=kOutput, calls=%fused_computation.108 | convolution fusion | flops 537395200 | bytes 5505024 | tf_op jit(solution)/shard_map/dot_general | solution.py:159
  72.8 1.9 collective-permute-done.12
  74.9 8.3 %collective-permute-done.13 = f32[2,256,128]{2,1,0:T(8,128)S(1)} collective-permute-done((f32[2,256,128]{2,1,0:T(8,128)S(1)}, f32[2,256,128]{2,1,0:T(8,128)S(1)}, u32[]{:S(2)}, u32[]{:S(2)}) %collective-permute-start.13) | collective-permute-done | bytes 262176 | tf_op jit(solution)/shard_map/ppermute | solution.py:65
  83.4 8.4 %collective-permute-done.14 = f32[1,256,128]{2,1,0:T(8,128)S(1)} collective-permute-done((f32[1,256,128]{2,1,0:T(8,128)S(1)}, f32[1,256,128]{2,1,0:T(8,128)S(1)}, u32[]{:S(2)}, u32[]{:S(2)}) %collective-permute-start.14) | collective-permute-done | bytes 131104 | tf_op jit(solution)/shard_map/ppermute | solution.py:65
  91.9 1.6 collective-permute-start.15
  93.4 2.8 %collective-permute-done.15 = bf16[256,128]{1,0:T(8,128)(2,1)S(1)} collective-permute-done((bf16[256,128]{1,0:T(8,128)(2,1)S(1)}, bf16[256,128]{1,0:T(8,128)(2,1)S(1)}, u32[]{:S(2)}, u32[]{:S(2)}) %collective-permute-start.15) | collective-permute-done | bytes 65568 | tf_op jit(solution)/shard_map/ppermute | solution.py:79
  96.6 4.6 %collective-permute-done.16 = bf16[512,128]{1,0:T(8,128)(2,1)S(1)} collective-permute-done((bf16[512,128]{1,0:T(8,128)(2,1)S(1)}, bf16[512,128]{1,0:T(8,128)(2,1)S(1)}, u32[]{:S(2)}, u32[]{:S(2)}) %collective-permute-start.16) | collective-permute-done | bytes 131104 | tf_op jit(solution)/shard_map/ppermute | solution.py:79
  104.8 1.9 collective-permute-done.17
  106.9 8.3 %collective-permute-done.18 = f32[2,256,128]{2,1,0:T(8,128)S(1)} collective-permute-done((f32[2,256,128]{2,1,0:T(8,128)S(1)}, f32[2,256,128]{2,1,0:T(8,128)S(1)}, u32[]{:S(2)}, u32[]{:S(2)}) %collective-permute-start.18) | collective-permute-done | bytes 262176 | tf_op jit(solution)/shard_map/ppermute | solution.py:65
  115.4 8.4 %collective-permute-done.19 = f32[1,256,128]{2,1,0:T(8,128)S(1)} collective-permute-done((f32[1,256,128]{2,1,0:T(8,128)S(1)}, f32[1,256,128]{2,1,0:T(8,128)S(1)}, u32[]{:S(2)}, u32[]{:S(2)}) %collective-permute-start.19) | collective-permute-done | bytes 131104 | tf_op jit(solution)/shard_map/ppermute | solution.py:65
  123.9 1.6 collective-permute-start.20
  125.4 2.8 %collective-permute-done.20 = bf16[256,128]{1,0:T(8,128)(2,1)S(1)} collective-permute-done((bf16[256,128]{1,0:T(8,128)(2,1)S(1)}, bf16[256,128]{1,0:T(8,128)(2,1)S(1)}, u32[]{:S(2)}, u32[]{:S(2)}) %collective-permute-start.20) | collective-permute-done | bytes 65568 | tf_op jit(solution)/shard_map/ppermute | solution.py:79
  128.6 4.6 %collective-permute-done.21 = bf16[512,128]{1,0:T(8,128)(2,1)S(1)} collective-permute-done((bf16[512,128]{1,0:T(8,128)(2,1)S(1)}, bf16[512,128]{1,0:T(8,128)(2,1)S(1)}, u32[]{:S(2)}, u32[]{:S(2)}) %collective-permute-start.21) | collective-permute-done | bytes 131104 | tf_op jit(solution)/shard_map/ppermute | solution.py:79
  133.6 1.5 fusion.28
  135.7 1.3 fusion.3
  137.0 1.9 collective-permute-done.22
  139.1 8.3 %collective-permute-done.23 = f32[2,256,128]{2,1,0:T(8,128)S(1)} collective-permute-done((f32[2,256,128]{2,1,0:T(8,128)S(1)}, f32[2,256,128]{2,1,0:T(8,128)S(1)}, u32[]{:S(2)}, u32[]{:S(2)}) %collective-permute-start.23) | collective-permute-done | bytes 262176 | tf_op jit(solution)/shard_map/ppermute | solution.py:65
  147.6 8.4 %collective-permute-done.24 = f32[1,256,128]{2,1,0:T(8,128)S(1)} collective-permute-done((f32[1,256,128]{2,1,0:T(8,128)S(1)}, f32[1,256,128]{2,1,0:T(8,128)S(1)}, u32[]{:S(2)}, u32[]{:S(2)}) %collective-permute-start.24) | collective-permute-done | bytes 131104 | tf_op jit(solution)/shard_map/ppermute | solution.py:65
  156.1 1.6 collective-permute-start.25
  157.6 2.8 %collective-permute-done.25 = bf16[256,128]{1,0:T(8,128)(2,1)S(1)} collective-permute-done((bf16[256,128]{1,0:T(8,128)(2,1)S(1)}, bf16[256,128]{1,0:T(8,128)(2,1)S(1)}, u32[]{:S(2)}, u32[]{:S(2)}) %collective-permute-start.25) | collective-permute-done | bytes 65568 | tf_op jit(solution)/shard_map/ppermute | solution.py:79
  160.8 4.6 %collective-permute-done.26 = bf16[512,128]{1,0:T(8,128)(2,1)S(1)} collective-permute-done((bf16[512,128]{1,0:T(8,128)(2,1)S(1)}, bf16[512,128]{1,0:T(8,128)(2,1)S(1)}, u32[]{:S(2)}, u32[]{:S(2)}) %collective-permute-start.26) | collective-permute-done | bytes 131104 | tf_op jit(solution)/shard_map/ppermute | solution.py:79
  169.0 1.9 collective-permute-done.27
  171.1 8.3 %collective-permute-done.28 = f32[2,256,128]{2,1,0:T(8,128)S(1)} collective-permute-done((f32[2,256,128]{2,1,0:T(8,128)S(1)}, f32[2,256,128]{2,1,0:T(8,128)S(1)}, u32[]{:S(2)}, u32[]{:S(2)}) %collective-permute-start.28) | collective-permute-done | bytes 262176 | tf_op jit(solution)/shard_map/ppermute | solution.py:65
  180.0 8.0 %collective-permute-done.29 = f32[1,256,128]{2,1,0:T(8,128)S(1)} collective-permute-done((f32[1,256,128]{2,1,0:T(8,128)S(1)}, f32[1,256,128]{2,1,0:T(8,128)S(1)}, u32[]{:S(2)}, u32[]{:S(2)}) %collective-permute-start.29) | collective-permute-done | bytes 131104 | tf_op jit(solution)/shard_map/ppermute | solution.py:65
  188.5 1.3 collective-permute-done.30
  190.0 5.5 %collective-permute-done.31 = f32[256,128]{0,1:T(8,128)S(1)} collective-permute-done((f32[256,128]{0,1:T(8,128)S(1)}, f32[256,128]{0,1:T(8,128)S(1)}, u32[]{:S(2)}, u32[]{:S(2)}) %collective-permute-start.31) | collective-permute-done | bytes 131104 | tf_op jit(solution)/shard_map/ppermute | solution.py:30
  195.6 8.4 %collective-permute-done.32 = f32[256,128]{0,1:T(8,128)S(1)} collective-permute-done((f32[256,128]{0,1:T(8,128)S(1)}, f32[256,128]{0,1:T(8,128)S(1)}, u32[]{:S(2)}, u32[]{:S(2)}) %collective-permute-start.32) | collective-permute-done | bytes 131104 | tf_op jit(solution)/shard_map/ppermute | solution.py:30
  204.0 1.6 collective-permute-start.33
  205.6 3.9 %collective-permute-done.33 = f32[256,128]{0,1:T(8,128)S(1)} collective-permute-done((f32[256,128]{0,1:T(8,128)S(1)}, f32[256,128]{0,1:T(8,128)S(1)}, u32[]{:S(2)}, u32[]{:S(2)}) %collective-permute-start.33) | collective-permute-done | bytes 131104 | tf_op jit(solution)/shard_map/ppermute | solution.py:30
  209.9 4.6 %collective-permute-done.34 = f32[256,128]{0,1:T(8,128)S(1)} collective-permute-done((f32[256,128]{0,1:T(8,128)S(1)}, f32[256,128]{0,1:T(8,128)S(1)}, u32[]{:S(2)}, u32[]{:S(2)}) %collective-permute-start.34) | collective-permute-done | bytes 131104 | tf_op jit(solution)/shard_map/ppermute | solution.py:30
  214.7 11.7 %cholesky.16 = f32[128,128]{1,0:T(8,128)S(1)} custom-call(f32[128,128]{1,0:T(8,128)S(1)} %fusion.39), custom_call_target="Cholesky" | custom-call | tf_op jit(solution)/shard_map/jit(cholesky)/cholesky | solution.py:182
  227.7 9.9 %custom-call.10 = f32[1,128,128]{1,2,0:T(8,128)S(1)} custom-call(f32[1,128,128]{2,1,0:T(8,128)S(1)} %fusion.32), custom_call_target="InvertDiagBlocksLowerTriangular" | custom-call | tf_op jit(solution)/shard_map/triangular_solve | solution.py:183
  (142 shorter events, 24.0 us)
Async XLA Ops:
  1.6 21.0 %collective-permute-start = (bf16[256,128]{1,0:T(8,128)(2,1)S(1)}, bf16[256,128]{1,0:T(8,128)(2,1)S(1)}, u32[]{:S(2)}, u32[]{:S(2)}) collective-permute-start(bf16[256,128]{1,0:T(8,128)(2,1)S(1)} %multiply_convert_fusion.4), channel_id=1, source_target_pairs={{0,8},{8,0},{16,24},{24,16},{1,9},{9,1},{17,25},{25,17},{2,10},{10... | collective-permute-start | bytes 196616 | tf_op jit(solution)/shard_map/ppermute | solution.py:79
  4.7 21.4 %collective-permute-start.5 = (bf16[256,128]{1,0:T(8,128)(2,1)}, bf16[256,128]{1,0:T(8,128)(2,1)S(1)}, u32[]{:S(2)}, u32[]{:S(2)}) collective-permute-start(bf16[256,128]{1,0:T(8,128)(2,1)} %param.12), channel_id=1, source_target_pairs={{0,8},{8,0},{16,24},{24,16},{1,9},{9,1},{17,25},{25,17},{2,10},{10... | collective-permute-start | bytes 196616 | tf_op jit(solution)/shard_map/ppermute | solution.py:79
  4.8 19.6 %collective-permute-start.2 = (bf16[1,256,128]{2,1,0:T(8,128)(2,1)}, bf16[1,256,128]{2,1,0:T(8,128)(2,1)S(1)}, u32[]{:S(2)}, u32[]{:S(2)}) collective-permute-start(bf16[1,256,128]{2,1,0:T(8,128)(2,1)} %bitcast.167), channel_id=1, source_target_pairs={{0,4},{1,5},{2,6},{3,7},{4,0},{5,1},{6,2},{7,3},{8,12},{9,13},{10,... | collective-permute-start | bytes 196616 | tf_op jit(solution)/shard_map/ppermute | solution.py:97
  7.8 14.8 %copy-start.7 = (s32[8]{0:T(128)S(1)}, s32[8]{0:T(128)}, u32[]{:S(2)}) copy-start(s32[8]{0:T(128)} %constant.326) | copy-start | bytes 100
  7.8 14.8 %copy-start.3 = (f32[256,128]{1,0:T(8,128)S(1)}, f32[256,128]{1,0:T(8,128)}, u32[]{:S(2)}) copy-start(f32[256,128]{1,0:T(8,128)} %param.11) | copy-start | bytes 393220
  7.8 14.9 %copy-start.5 = (f32[256]{0:T(256)S(1)}, f32[256]{0:T(256)}, u32[]{:S(2)}) copy-start(f32[256]{0:T(256)} %param.10) | copy-start | bytes 3076
  7.8 16.6 %copy-start.4 = (bf16[256,128]{1,0:T(8,128)(2,1)S(1)}, bf16[256,128]{1,0:T(8,128)(2,1)}, u32[]{:S(2)}) copy-start(bf16[256,128]{1,0:T(8,128)(2,1)} %param.12) | copy-start | bytes 196612
  22.8 6.8 %collective-permute-start.1 = (bf16[512,128]{1,0:T(8,128)(2,1)S(1)}, bf16[512,128]{1,0:T(8,128)(2,1)S(1)}, u32[]{:S(2)}, u32[]{:S(2)}) collective-permute-start(bf16[512,128]{1,0:T(8,128)(2,1)S(1)} %pad_maximum_fusion.8), channel_id=1, source_target_pairs={{0,16},{8,24},{16,0},{24,8},{1,17},{9,25},{17,1},{25,9},{2,18},{10... | collective-permute-start | bytes 393224 | tf_op jit(solution)/shard_map/ppermute | solution.py:79
  24.4 5.0 %collective-permute-start.3 = (bf16[2,256,128]{2,1,0:T(8,128)(2,1)S(1)}, bf16[2,256,128]{2,1,0:T(8,128)(2,1)S(1)}, u32[]{:S(2)}, u32[]{:S(2)}) collective-permute-start(bf16[2,256,128]{2,1,0:T(8,128)(2,1)S(1)} %pad_maximum_fusion.9), channel_id=1, source_target_pairs={{0,2},{1,3},{2,0},{3,1},{4,6},{5,7},{6,4},{7,5},{8,10},{9,11},{10,... | collective-permute-start | bytes 393224 | tf_op jit(solution)/shard_map/ppermute | solution.py:97
  26.1 7.0 %collective-permute-start.6 = (bf16[512,128]{1,0:T(8,128)(2,1)S(1)}, bf16[512,128]{1,0:T(8,128)(2,1)S(1)}, u32[]{:S(2)}, u32[]{:S(2)}) collective-permute-start(bf16[512,128]{1,0:T(8,128)(2,1)S(1)} %pad_maximum_fusion.10), channel_id=1, source_target_pairs={{0,16},{8,24},{16,0},{24,8},{1,17},{9,25},{17,1},{25,9},{2,18},{10... | collective-permute-start | bytes 393224 | tf_op jit(solution)/shard_map/ppermute | solution.py:79
  29.5 3.7 %copy-start.8 = (f32[128]{0:T(128)S(1)}, f32[128]{0:T(128)}, u32[]{:S(2)}) copy-start(f32[128]{0:T(128)} %param.13) | copy-start | bytes 1540
  29.5 4.0 %collective-permute-start.4 = (bf16[4,256,128]{2,1,0:T(8,128)(2,1)S(1)}, bf16[4,256,128]{2,1,0:T(8,128)(2,1)S(1)}, u32[]{:S(2)}, u32[]{:S(2)}) collective-permute-start(bf16[4,256,128]{2,1,0:T(8,128)(2,1)S(1)} %pad_maximum_fusion.2), channel_id=1, source_target_pairs={{0,1},{1,0},{2,3},{3,2},{4,5},{5,4},{6,7},{7,6},{8,9},{9,8},{10,11... | collective-permute-start | bytes 786440 | tf_op jit(solution)/shard_map/ppermute | solution.py:97
  34.2 2.2 copy-start
  37.7 11.3 %copy-start.6 = (f32[2]{0:T(128)S(1)}, f32[2]{0:T(128)}, u32[]{:S(2)}) copy-start(f32[2]{0:T(128)} %param.14) | copy-start | bytes 28
  37.8 2.1 collective-permute-start.7
  40.0 8.7 %collective-permute-start.8 = (f32[2,256,128]{2,1,0:T(8,128)S(1)}, f32[2,256,128]{2,1,0:T(8,128)S(1)}, u32[]{:S(2)}, u32[]{:S(2)}) collective-permute-start(f32[2,256,128]{2,1,0:T(8,128)S(1)} %dynamic-slice_bitcast_fusion.9), channel_id=1, source_target_pairs={{0,2},{1,3},{2,0},{3,1},{4,6},{5,7},{6,4},{7,5},{8,10},{9,11},{10,... | collective-permute-start | bytes 786440 | tf_op jit(solution)/shard_map/ppermute | solution.py:65
  48.7 8.7 %collective-permute-start.9 = (f32[1,256,128]{2,1,0:T(8,128)S(1)}, f32[1,256,128]{2,1,0:T(8,128)S(1)}, u32[]{:S(2)}, u32[]{:S(2)}) collective-permute-start(f32[1,256,128]{2,1,0:T(8,128)S(1)} %constant_dynamic-slice_fusion.3), channel_id=1, source_target_pairs={{0,4},{1,5},{2,6},{3,7},{4,0},{5,1},{6,2},{7,3},{8,12},{9,13},{10,... | collective-permute-start | bytes 393224 | tf_op jit(solution)/shard_map/ppermute | solution.py:65
  57.5 4.3 %collective-permute-start.10 = (bf16[256,128]{1,0:T(8,128)(2,1)S(1)}, bf16[256,128]{1,0:T(8,128)(2,1)S(1)}, u32[]{:S(2)}, u32[]{:S(2)}) collective-permute-start(bf16[256,128]{1,0:T(8,128)(2,1)S(1)} %get-tuple-element.12), channel_id=1, source_target_pairs={{0,8},{8,0},{16,24},{24,16},{1,9},{9,1},{17,25},{25,17},{2,10},{10... | collective-permute-start | bytes 196616 | tf_op jit(solution)/shard_map/ppermute | solution.py:79
  61.8 5.0 %collective-permute-start.11 = (bf16[512,128]{1,0:T(8,128)(2,1)S(1)}, bf16[512,128]{1,0:T(8,128)(2,1)S(1)}, u32[]{:S(2)}, u32[]{:S(2)}) collective-permute-start(bf16[512,128]{1,0:T(8,128)(2,1)S(1)} %pad_maximum_fusion.11), channel_id=1, source_target_pairs={{0,16},{8,24},{16,0},{24,8},{1,17},{9,25},{17,1},{25,9},{2,18},{10... | collective-permute-start | bytes 393224 | tf_op jit(solution)/shard_map/ppermute | solution.py:79
  67.2 4.2 %copy-start.1 = (bf16[2048,1024]{1,0:T(8,128)(2,1)S(1)}, bf16[2048,1024]{1,0:T(8,128)(2,1)}, u32[]{:S(2)}) copy-start(bf16[2048,1024]{1,0:T(8,128)(2,1)} %get-tuple-element.4) | copy-start | bytes 12582916
  72.7 28.9 %copy-start.2 = (bf16[2048,1024]{1,0:T(8,128)(2,1)S(1)}, bf16[2048,1024]{1,0:T(8,128)(2,1)}, u32[]{:S(2)}) copy-start(bf16[2048,1024]{1,0:T(8,128)(2,1)} %get-tuple-element.5) | copy-start | bytes 12582916
  72.7 2.0 collective-permute-start.12
  74.8 8.4 %collective-permute-start.13 = (f32[2,256,128]{2,1,0:T(8,128)S(1)}, f32[2,256,128]{2,1,0:T(8,128)S(1)}, u32[]{:S(2)}, u32[]{:S(2)}) collective-permute-start(f32[2,256,128]{2,1,0:T(8,128)S(1)} %dynamic-slice_bitcast_fusion.8), channel_id=1, source_target_pairs={{0,2},{1,3},{2,0},{3,1},{4,6},{5,7},{6,4},{7,5},{8,10},{9,11},{10,... | collective-permute-start | bytes 786440 | tf_op jit(solution)/shard_map/ppermute | solution.py:65
  83.3 8.5 %collective-permute-start.14 = (f32[1,256,128]{2,1,0:T(8,128)S(1)}, f32[1,256,128]{2,1,0:T(8,128)S(1)}, u32[]{:S(2)}, u32[]{:S(2)}) collective-permute-start(f32[1,256,128]{2,1,0:T(8,128)S(1)} %constant_dynamic-slice_fusion.2), channel_id=1, source_target_pairs={{0,4},{1,5},{2,6},{3,7},{4,0},{5,1},{6,2},{7,3},{8,12},{9,13},{10,... | collective-permute-start | bytes 393224 | tf_op jit(solution)/shard_map/ppermute | solution.py:65
  91.9 4.3 %collective-permute-start.15 = (bf16[256,128]{1,0:T(8,128)(2,1)S(1)}, bf16[256,128]{1,0:T(8,128)(2,1)S(1)}, u32[]{:S(2)}, u32[]{:S(2)}) collective-permute-start(bf16[256,128]{1,0:T(8,128)(2,1)S(1)} %get-tuple-element.10), channel_id=1, source_target_pairs={{0,8},{8,0},{16,24},{24,16},{1,9},{9,1},{17,25},{25,17},{2,10},{10... | collective-permute-start | bytes 196616 | tf_op jit(solution)/shard_map/ppermute | solution.py:79
  96.2 5.0 %collective-permute-start.16 = (bf16[512,128]{1,0:T(8,128)(2,1)S(1)}, bf16[512,128]{1,0:T(8,128)(2,1)S(1)}, u32[]{:S(2)}, u32[]{:S(2)}) collective-permute-start(bf16[512,128]{1,0:T(8,128)(2,1)S(1)} %pad_maximum_fusion.12), channel_id=1, source_target_pairs={{0,16},{8,24},{16,0},{24,8},{1,17},{9,25},{17,1},{25,9},{2,18},{10... | collective-permute-start | bytes 393224 | tf_op jit(solution)/shard_map/ppermute | solution.py:79
  104.8 2.0 collective-permute-start.17
  106.8 8.4 %collective-permute-start.18 = (f32[2,256,128]{2,1,0:T(8,128)S(1)}, f32[2,256,128]{2,1,0:T(8,128)S(1)}, u32[]{:S(2)}, u32[]{:S(2)}) collective-permute-start(f32[2,256,128]{2,1,0:T(8,128)S(1)} %dynamic-slice_bitcast_fusion.7), channel_id=1, source_target_pairs={{0,2},{1,3},{2,0},{3,1},{4,6},{5,7},{6,4},{7,5},{8,10},{9,11},{10,... | collective-permute-start | bytes 786440 | tf_op jit(solution)/shard_map/ppermute | solution.py:65
  115.3 8.5 %collective-permute-start.19 = (f32[1,256,128]{2,1,0:T(8,128)S(1)}, f32[1,256,128]{2,1,0:T(8,128)S(1)}, u32[]{:S(2)}, u32[]{:S(2)}) collective-permute-start(f32[1,256,128]{2,1,0:T(8,128)S(1)} %constant_dynamic-slice_fusion.1), channel_id=1, source_target_pairs={{0,4},{1,5},{2,6},{3,7},{4,0},{5,1},{6,2},{7,3},{8,12},{9,13},{10,... | collective-permute-start | bytes 393224 | tf_op jit(solution)/shard_map/ppermute | solution.py:65
  123.9 4.3 %collective-permute-start.20 = (bf16[256,128]{1,0:T(8,128)(2,1)S(1)}, bf16[256,128]{1,0:T(8,128)(2,1)S(1)}, u32[]{:S(2)}, u32[]{:S(2)}) collective-permute-start(bf16[256,128]{1,0:T(8,128)(2,1)S(1)} %get-tuple-element.8), channel_id=1, source_target_pairs={{0,8},{8,0},{16,24},{24,16},{1,9},{9,1},{17,25},{25,17},{2,10},{10... | collective-permute-start | bytes 196616 | tf_op jit(solution)/shard_map/ppermute | solution.py:79
  128.2 5.0 %collective-permute-start.21 = (bf16[512,128]{1,0:T(8,128)(2,1)S(1)}, bf16[512,128]{1,0:T(8,128)(2,1)S(1)}, u32[]{:S(2)}, u32[]{:S(2)}) collective-permute-start(bf16[512,128]{1,0:T(8,128)(2,1)S(1)} %pad_maximum_fusion.13), channel_id=1, source_target_pairs={{0,16},{8,24},{16,0},{24,8},{1,17},{9,25},{17,1},{25,9},{2,18},{10... | collective-permute-start | bytes 393224 | tf_op jit(solution)/shard_map/ppermute | solution.py:79
  137.0 2.0 collective-permute-start.22
  139.0 8.4 %collective-permute-start.23 = (f32[2,256,128]{2,1,0:T(8,128)S(1)}, f32[2,256,128]{2,1,0:T(8,128)S(1)}, u32[]{:S(2)}, u32[]{:S(2)}) collective-permute-start(f32[2,256,128]{2,1,0:T(8,128)S(1)} %dynamic-slice_bitcast_fusion.6), channel_id=1, source_target_pairs={{0,2},{1,3},{2,0},{3,1},{4,6},{5,7},{6,4},{7,5},{8,10},{9,11},{10,... | collective-permute-start | bytes 786440 | tf_op jit(solution)/shard_map/ppermute | solution.py:65
  147.5 8.5 %collective-permute-start.24 = (f32[1,256,128]{2,1,0:T(8,128)S(1)}, f32[1,256,128]{2,1,0:T(8,128)S(1)}, u32[]{:S(2)}, u32[]{:S(2)}) collective-permute-start(f32[1,256,128]{2,1,0:T(8,128)S(1)} %constant_dynamic-slice_fusion), channel_id=1, source_target_pairs={{0,4},{1,5},{2,6},{3,7},{4,0},{5,1},{6,2},{7,3},{8,12},{9,13},{10,... | collective-permute-start | bytes 393224 | tf_op jit(solution)/shard_map/ppermute | solution.py:65
  156.1 4.3 %collective-permute-start.25 = (bf16[256,128]{1,0:T(8,128)(2,1)S(1)}, bf16[256,128]{1,0:T(8,128)(2,1)S(1)}, u32[]{:S(2)}, u32[]{:S(2)}) collective-permute-start(bf16[256,128]{1,0:T(8,128)(2,1)S(1)} %get-tuple-element.6), channel_id=1, source_target_pairs={{0,8},{8,0},{16,24},{24,16},{1,9},{9,1},{17,25},{25,17},{2,10},{10... | collective-permute-start | bytes 196616 | tf_op jit(solution)/shard_map/ppermute | solution.py:79
  160.5 5.0 %collective-permute-start.26 = (bf16[512,128]{1,0:T(8,128)(2,1)S(1)}, bf16[512,128]{1,0:T(8,128)(2,1)S(1)}, u32[]{:S(2)}, u32[]{:S(2)}) collective-permute-start(bf16[512,128]{1,0:T(8,128)(2,1)S(1)} %pad_maximum_fusion.14), channel_id=1, source_target_pairs={{0,16},{8,24},{16,0},{24,8},{1,17},{9,25},{17,1},{25,9},{2,18},{10... | collective-permute-start | bytes 393224 | tf_op jit(solution)/shard_map/ppermute | solution.py:79
  169.0 2.0 collective-permute-start.27
  171.0 8.4 %collective-permute-start.28 = (f32[2,256,128]{2,1,0:T(8,128)S(1)}, f32[2,256,128]{2,1,0:T(8,128)S(1)}, u32[]{:S(2)}, u32[]{:S(2)}) collective-permute-start(f32[2,256,128]{2,1,0:T(8,128)S(1)} %dynamic-slice_bitcast_fusion.5), channel_id=1, source_target_pairs={{0,2},{1,3},{2,0},{3,1},{4,6},{5,7},{6,4},{7,5},{8,10},{9,11},{10,... | collective-permute-start | bytes 786440 | tf_op jit(solution)/shard_map/ppermute | solution.py:65
  179.5 8.5 %collective-permute-start.29 = (f32[1,256,128]{2,1,0:T(8,128)S(1)}, f32[1,256,128]{2,1,0:T(8,128)S(1)}, u32[]{:S(2)}, u32[]{:S(2)}) collective-permute-start(f32[1,256,128]{2,1,0:T(8,128)S(1)} %constant_dynamic-slice_fusion.4), channel_id=1, source_target_pairs={{0,4},{1,5},{2,6},{3,7},{4,0},{5,1},{6,2},{7,3},{8,12},{9,13},{10,... | collective-permute-start | bytes 393224 | tf_op jit(solution)/shard_map/ppermute | solution.py:65
  188.4 1.4 collective-permute-start.30
  189.9 5.6 %collective-permute-start.31 = (f32[256,128]{0,1:T(8,128)S(1)}, f32[256,128]{0,1:T(8,128)S(1)}, u32[]{:S(2)}, u32[]{:S(2)}) collective-permute-start(f32[256,128]{0,1:T(8,128)S(1)} %fusion.74), channel_id=1, source_target_pairs={{0,2},{1,3},{2,0},{3,1},{4,6},{5,7},{6,4},{7,5},{8,10},{9,11},{10,... | collective-permute-start | bytes 393224 | tf_op jit(solution)/shard_map/ppermute | solution.py:30
  195.5 8.5 %collective-permute-start.32 = (f32[256,128]{0,1:T(8,128)S(1)}, f32[256,128]{0,1:T(8,128)S(1)}, u32[]{:S(2)}, u32[]{:S(2)}) collective-permute-start(f32[256,128]{0,1:T(8,128)S(1)} %add.265), channel_id=1, source_target_pairs={{0,4},{1,5},{2,6},{3,7},{4,0},{5,1},{6,2},{7,3},{8,12},{9,13},{10,... | collective-permute-start | bytes 393224 | tf_op jit(solution)/shard_map/ppermute | solution.py:30
  204.0 5.5 %collective-permute-start.33 = (f32[256,128]{0,1:T(8,128)S(1)}, f32[256,128]{0,1:T(8,128)S(1)}, u32[]{:S(2)}, u32[]{:S(2)}) collective-permute-start(f32[256,128]{0,1:T(8,128)S(1)} %add.266), channel_id=1, source_target_pairs={{0,8},{8,0},{16,24},{24,16},{1,9},{9,1},{17,25},{25,17},{2,10},{10... | collective-permute-start | bytes 393224 | tf_op jit(solution)/shard_map/ppermute | solution.py:30
  209.5 5.0 %collective-permute-start.34 = (f32[256,128]{0,1:T(8,128)S(1)}, f32[256,128]{0,1:T(8,128)S(1)}, u32[]{:S(2)}, u32[]{:S(2)}) collective-permute-start(f32[256,128]{0,1:T(8,128)S(1)} %add.267), channel_id=1, source_target_pairs={{0,16},{8,24},{16,0},{24,8},{1,17},{9,25},{17,1},{25,9},{2,18},{10... | collective-permute-start | bytes 393224 | tf_op jit(solution)/shard_map/ppermute | solution.py:30

commit v8 on v6

--- a/solution.py
+++ b/solution.py
@@ -103,6 +103,37 @@
     return result[jnp.array(order)].reshape(-1, value.shape[1])
 
 
+def gather_segments(value, axis):
+    size = lax.axis_size(axis)
+    here = lax.axis_index(axis)
+    segments = [value]
+    result = value
+    step = 1
+    while step < size:
+        pairs = [(index, index ^ step) for index in range(size)]
+        other = lax.ppermute(result, axis, pairs)
+        segments.append(other)
+        if step * 2 < size:
+            low = (here // step) % 2 == 0
+            result = jnp.concatenate(
+                [jnp.where(low, result, other), jnp.where(low, other, result)], axis=0
+            )
+        step *= 2
+    return segments
+
+
+def segment_pieces(axis):
+    size = lax.axis_size(axis)
+    here = lax.axis_index(axis)
+    pieces = [here[None]]
+    step = 1
+    while step < size:
+        start = ((here ^ step) // step) * step
+        pieces.append(start + jnp.arange(step, dtype=jnp.int32))
+        step *= 2
+    return jnp.concatenate(pieces).astype(jnp.int32)
+
+
 def local(tiles, tile_cols, degree_scale, start_block, planted, strengths, bounds):
     piece_rows = start_block.shape[0]
     node_count = piece_rows * lax.axis_size("row") * lax.axis_size("col")
@@ -110,22 +141,45 @@
     n_blocks = lax.axis_size("row") * piece_rows // tile_size
     weights = strengths[:, None]
 
-    onehot = (tile_cols[:, :, None] == jnp.arange(n_blocks, dtype=jnp.int32)[None, None, :]).astype(jnp.bfloat16)
+    row_size = lax.axis_size("row")
+    in_order = row_size & (row_size - 1) == 0
+    per_piece = piece_rows // tile_size
+    if in_order:
+        pieces = segment_pieces("row")
+        block_order = (pieces[:, None] * per_piece + jnp.arange(per_piece, dtype=jnp.int32)[None, :]).reshape(-1)
+    else:
+        block_order = jnp.arange(n_blocks, dtype=jnp.int32)
+
+    onehot = (tile_cols[:, :, None] == block_order[None, None, :]).astype(jnp.bfloat16)
     dense = jnp.einsum("rst,rsab->ratb", onehot, tiles, preferred_element_type=jnp.float32)
     dense = dense.reshape(tile_rows * tile_size, n_blocks * tile_size)
     w_hi, w_lo = split_bf16(dense)
 
-    planted_cols = doubling_gather(planted, "row")
+    if in_order:
+        planted_segments = gather_segments(planted, "row")
+    else:
+        planted_segments = [lax.all_gather(planted, "row", axis=0, tiled=True)]
     planted_rows = far_first_gather(planted, "col")
 
     def operate(vector):
         scaled = (degree_scale[:, None] * vector).astype(jnp.bfloat16)
-        gathered = doubling_gather(scaled, "row")
-        product = jnp.dot(w_hi, gathered, preferred_element_type=jnp.float32)
-        product = product + jnp.dot(w_lo, gathered, preferred_element_type=jnp.float32)
-        partial = lax.dot_general(
-            planted_cols, gathered, (((0,), (0,)), ((), ())), preferred_element_type=jnp.float32
-        )
+        if in_order:
+            segments = gather_segments(scaled, "row")
+        else:
+            segments = [lax.all_gather(scaled, "row", axis=0, tiled=True)]
+        product = None
+        partial = None
+        offset = 0
+        for segment, planted_part in zip(segments, planted_segments):
+            columns = slice(offset, offset + segment.shape[0])
+            offset += segment.shape[0]
+            piece = jnp.dot(w_hi[:, columns], segment, preferred_element_type=jnp.float32)
+            piece = piece + jnp.dot(w_lo[:, columns], segment, preferred_element_type=jnp.float32)
+            inner = lax.dot_general(
+                planted_part, segment, (((0,), (0,)), ((), ())), preferred_element_type=jnp.float32
+            )
+            product = piece if product is None else product + piece
+            partial = inner if partial is None else partial + inner
         product = product + split_dot(planted_rows, weights * partial) / node_count
         summed = halving_scatter_sum(product, "col")
         return degree_scale[:, None] * summed

time: 240 us -> 253 us (1.054); the launches traced: 240 us -> 249 us
  matrix products: 32.4 us -> 53.7 us
  waiting for transfers between devices: 144 us -> 128 us
  local copies, waits for them, and re-layouts: 4.72 us -> 7.55 us
    ppermute x12, waiting for transfers between devices: 29.8 us -> 16.3 us  [gather_segments(): other = lax.ppermute(result, axis, pairs)]
    dot_general x15 -> x45, matrix products: 18.6 us -> 29.8 us  [the longest x15 13.6 us: operate(): jnp.dot(w_lo[:, columns], segment, preferred_element_type=jnp.float32)]
    dot_general x5, matrix products: 1.43 us -> 11.3 us  [split_dot(): return first + jnp.dot(left, lower, preferred_element_type=jnp.float32)]
    ppermute x12, starting transfers between devices: 12.9 us -> 15.8 us  [gather_segments(): other = lax.ppermute(result, axis, pairs)]
    ppermute x3, waiting for transfers between devices: 2.78 us -> 0.01 us  [far_first_gather(): other = lax.ppermute(result, axis, pairs)]
    unnamed x18 -> x23, local copies, waits for them, and re-layouts: 2.97 us -> 5.71 us
  transfers between devices with their start and end apart: 35 -> 35, of which waited for: 29 -> 27; matrix products, arithmetic and copies ran while one was open for 8% -> 16% of each run, Pallas kernels for 0% -> 0%
where the time goes in v8:
time: 253 us; the launch traced here: 249 us
  waiting for transfers between devices  128 us (51%)
  matrix products  53.7 us (21%)
  other arithmetic  29.1 us (12%)
  starting transfers between devices  26 us (10%)
  local copies, waits for them, and re-layouts  7.55 us (3%)
  between operations  4.42 us (2%)
    ppermute x15, waiting for transfers between devices, halving_scatter_sum(): blocks = kept + lax.ppermute(sent, axis, pairs)  88.4 us
    ppermute x5, waiting for transfers between devices, butterfly_sum(): value = value + lax.ppermute(value, axis, pairs)  23.3 us
    ppermute x12, waiting for transfers between devices, gather_segments(): other = lax.ppermute(result, axis, pairs)  16.3 us
    ppermute x12, starting transfers between devices, gather_segments(): other = lax.ppermute(result, axis, pairs)  15.8 us
    dot_general x15, matrix products, operate(): jnp.dot(w_lo[:, columns], segment, preferred_element_type=jnp.float32)  13.6 us
    dot_general x15, matrix products, operate(): jnp.dot(w_hi[:, columns], segment, preferred_element_type=jnp.float32)  12.9 us
    another operation x3, other arithmetic, local(): factor = jnp.linalg.cholesky(gram_matrix)  12.4 us
    dot_general x5, matrix products, split_dot(): return first + jnp.dot(left, lower, preferred_element_type=jnp.float32)  11.3 us
  transfers between devices with their start and end apart: 35, of which 27 were waited for; matrix products, arithmetic and copies ran while one was open for 16% of the time, Pallas kernels for 0%

profile of v8, /device:TPU:0, one launch (start us, length us, event | category | flops | bytes accessed | tf_op | source)
XLA Modules:
  0.0 248.8 jit_solution(16819205687251136853)
XLA Ops:
  1.6 3.0 %collective-permute-start = (bf16[256,128]{1,0:T(8,128)(2,1)S(1)}, bf16[256,128]{1,0:T(8,128)(2,1)S(1)}, u32[]{:S(2)}, u32[]{:S(2)}) collective-permute-start(bf16[256,128]{1,0:T(8,128)(2,1)S(1)} %multiply_convert_fusion.4), channel_id=1, source_target_pairs={{0,8},{8,0},{16,24},{24,16},{1,9},{9,1},{17,25},{25,17},{2,10},{10... | collective-permute-start | bytes 196616 | tf_op jit(solution)/shard_map/ppermute | solution.py:114
  4.8 3.0 %collective-permute-start.2 = (bf16[1,256,128]{2,1,0:T(8,128)(2,1)}, bf16[1,256,128]{2,1,0:T(8,128)(2,1)S(1)}, u32[]{:S(2)}, u32[]{:S(2)}) collective-permute-start(bf16[1,256,128]{2,1,0:T(8,128)(2,1)} %bitcast.252), channel_id=1, source_target_pairs={{0,4},{1,5},{2,6},{3,7},{4,0},{5,1},{6,2},{7,3},{8,12},{9,13},{10,... | collective-permute-start | bytes 196616 | tf_op jit(solution)/shard_map/ppermute | solution.py:95
  8.0 8.2 %fusion.1 = f32[16,8,128,128]{3,1,2,0:T(8,128)S(1)} fusion(bf16[16,16,128,128]{3,2,1,0:T(8,128)(2,1)} %param.8, s32[16,16]{1,0:T(8,128)} %param.9, s32[8]{0:T(128)S(1)} %add.353), kind=kOutput, calls=%fused_computation.4 | convolution fusion | flops 67110912 | bytes 16778272 | tf_op jit(solution)/shard_map/rst,rsab->ratb/dot_general | solution.py:154
  16.3 4.1 %copy.43 = bf16[256,8,8,128]{3,1,2,0:T(8,128)(2,1)} copy(f32[256,8,8,128]{3,2,1,0:T(8,128)S(1)} %bitcast.230) | data formatting | bytes 12582912
  20.4 3.7 %fusion = bf16[2048,1024]{1,0:T(8,128)(2,1)} fusion(f32[256,8,8,128]{3,2,1,0:T(8,128)S(1)} %bitcast.231), kind=kLoop, calls=%fused_computation.3 | loop fusion | flops 8388608 | bytes 12582912 | tf_op jit(solution)/shard_map/convert_element_type | solution.py:11
  24.3 1.6 fusion.76
  26.0 2.6 %convolution_add_fusion.19 = f32[2048,128]{1,0:T(8,128)} fusion(f32[2048,128]{1,0:T(8,128)S(1)} %fusion.76, bf16[256,128]{1,0:T(8,128)(2,1)S(1)} %multiply_convert_fusion.4, bf16[2048,1024]{1,0:T(8,128)(2,1)} %fusion), kind=kOutput, calls=%fused_computation.45 | convolution fusion | flops 134479872 | bytes 3211264 | tf_op jit(solution)/shard_map/dot_general | solution.py:177
  28.8 1.6 collective-permute-start.1
  30.4 1.6 collective-permute-start.3
  32.7 1.6 fusion.56
  34.3 1.7 fusion.22
  36.4 1.7 fusion.41
  39.9 1.6 copy-done
  41.5 2.0 fusion.17
  46.6 7.8 %collective-permute-done.8 = f32[2,256,128]{2,1,0:T(8,128)S(1)} collective-permute-done((f32[2,256,128]{2,1,0:T(8,128)S(1)}, f32[2,256,128]{2,1,0:T(8,128)S(1)}, u32[]{:S(2)}, u32[]{:S(2)}) %collective-permute-start.8) | collective-permute-done | bytes 262176 | tf_op jit(solution)/shard_map/ppermute | solution.py:63
  58.0 5.1 %collective-permute-done.9 = f32[1,256,128]{2,1,0:T(8,128)S(1)} collective-permute-done((f32[1,256,128]{2,1,0:T(8,128)S(1)}, f32[1,256,128]{2,1,0:T(8,128)S(1)}, u32[]{:S(2)}, u32[]{:S(2)}) %collective-permute-start.9) | collective-permute-done | bytes 131104 | tf_op jit(solution)/shard_map/ppermute | solution.py:63
  64.8 1.6 fusion.74
  66.4 1.7 convolution_add_fusion.17
  71.0 2.4 collective-permute-done.11
  75.8 1.9 collective-permute-done.12
  77.9 8.3 %collective-permute-done.13 = f32[2,256,128]{2,1,0:T(8,128)S(1)} collective-permute-done((f32[2,256,128]{2,1,0:T(8,128)S(1)}, f32[2,256,128]{2,1,0:T(8,128)S(1)}, u32[]{:S(2)}, u32[]{:S(2)}) %collective-permute-start.13) | collective-permute-done | bytes 262176 | tf_op jit(solution)/shard_map/ppermute | solution.py:63
  86.3 8.4 %collective-permute-done.14 = f32[1,256,128]{2,1,0:T(8,128)S(1)} collective-permute-done((f32[1,256,128]{2,1,0:T(8,128)S(1)}, f32[1,256,128]{2,1,0:T(8,128)S(1)}, u32[]{:S(2)}, u32[]{:S(2)}) %collective-permute-start.14) | collective-permute-done | bytes 131104 | tf_op jit(solution)/shard_map/ppermute | solution.py:63
  96.8 2.3 collective-permute-done.15
  99.2 1.6 collective-permute-start.16
  101.9 2.3 collective-permute-done.16
  106.6 1.9 collective-permute-done.17
  108.7 8.3 %collective-permute-done.18 = f32[2,256,128]{2,1,0:T(8,128)S(1)} collective-permute-done((f32[2,256,128]{2,1,0:T(8,128)S(1)}, f32[2,256,128]{2,1,0:T(8,128)S(1)}, u32[]{:S(2)}, u32[]{:S(2)}) %collective-permute-start.18) | collective-permute-done | bytes 262176 | tf_op jit(solution)/shard_map/ppermute | solution.py:63
  117.2 8.4 %collective-permute-done.19 = f32[1,256,128]{2,1,0:T(8,128)S(1)} collective-permute-done((f32[1,256,128]{2,1,0:T(8,128)S(1)}, f32[1,256,128]{2,1,0:T(8,128)S(1)}, u32[]{:S(2)}, u32[]{:S(2)}) %collective-permute-start.19) | collective-permute-done | bytes 131104 | tf_op jit(solution)/shard_map/ppermute | solution.py:63
  127.7 2.3 collective-permute-done.20
  130.0 1.6 collective-permute-start.21
  132.8 2.3 collective-permute-done.21
  135.6 10.1 %fusion.6 = f32[2048,128]{1,0:T(8,128)S(1)} fusion(f32[2048,128]{1,0:T(8,128)S(1)} %fusion.113, bf16[2048,128]{1,0:T(8,128)(2,1)S(1)} %bitcast.239, f32[128,128]{0,1:T(8,128)S(1)} %fusion.31), kind=kOutput, calls=%fused_computation.12 | convolution fusion | flops 67698688 | bytes 2686976 | tf_op jit(solution)/shard_map/dot_general | solution.py:18
  147.2 1.9 collective-permute-done.22
  149.3 8.3 %collective-permute-done.23 = f32[2,256,128]{2,1,0:T(8,128)S(1)} collective-permute-done((f32[2,256,128]{2,1,0:T(8,128)S(1)}, f32[2,256,128]{2,1,0:T(8,128)S(1)}, u32[]{:S(2)}, u32[]{:S(2)}) %collective-permute-start.23) | collective-permute-done | bytes 262176 | tf_op jit(solution)/shard_map/ppermute | solution.py:63
  157.8 8.4 %collective-permute-done.24 = f32[1,256,128]{2,1,0:T(8,128)S(1)} collective-permute-done((f32[1,256,128]{2,1,0:T(8,128)S(1)}, f32[1,256,128]{2,1,0:T(8,128)S(1)}, u32[]{:S(2)}, u32[]{:S(2)}) %collective-permute-start.24) | collective-permute-done | bytes 131104 | tf_op jit(solution)/shard_map/ppermute | solution.py:63
  168.3 2.3 collective-permute-done.25
  170.6 1.6 collective-permute-start.26
  173.4 2.3 collective-permute-done.26
  178.1 1.9 collective-permute-done.27
  180.2 8.3 %collective-permute-done.28 = f32[2,256,128]{2,1,0:T(8,128)S(1)} collective-permute-done((f32[2,256,128]{2,1,0:T(8,128)S(1)}, f32[2,256,128]{2,1,0:T(8,128)S(1)}, u32[]{:S(2)}, u32[]{:S(2)}) %collective-permute-start.28) | collective-permute-done | bytes 262176 | tf_op jit(solution)/shard_map/ppermute | solution.py:63
  189.0 8.0 %collective-permute-done.29 = f32[1,256,128]{2,1,0:T(8,128)S(1)} collective-permute-done((f32[1,256,128]{2,1,0:T(8,128)S(1)}, f32[1,256,128]{2,1,0:T(8,128)S(1)}, u32[]{:S(2)}, u32[]{:S(2)}) %collective-permute-start.29) | collective-permute-done | bytes 131104 | tf_op jit(solution)/shard_map/ppermute | solution.py:63
  199.0 5.5 %collective-permute-done.31 = f32[256,128]{0,1:T(8,128)S(1)} collective-permute-done((f32[256,128]{0,1:T(8,128)S(1)}, f32[256,128]{0,1:T(8,128)S(1)}, u32[]{:S(2)}, u32[]{:S(2)}) %collective-permute-start.31) | collective-permute-done | bytes 131104 | tf_op jit(solution)/shard_map/ppermute | solution.py:28
  204.6 8.4 %collective-permute-done.32 = f32[256,128]{0,1:T(8,128)S(1)} collective-permute-done((f32[256,128]{0,1:T(8,128)S(1)}, f32[256,128]{0,1:T(8,128)S(1)}, u32[]{:S(2)}, u32[]{:S(2)}) %collective-permute-start.32) | collective-permute-done | bytes 131104 | tf_op jit(solution)/shard_map/ppermute | solution.py:28
  213.9 4.6 %collective-permute-done.33 = f32[256,128]{0,1:T(8,128)S(1)} collective-permute-done((f32[256,128]{0,1:T(8,128)S(1)}, f32[256,128]{0,1:T(8,128)S(1)}, u32[]{:S(2)}, u32[]{:S(2)}) %collective-permute-start.33) | collective-permute-done | bytes 131104 | tf_op jit(solution)/shard_map/ppermute | solution.py:28
  218.5 1.6 collective-permute-start.34
  220.2 3.4 %collective-permute-done.34 = f32[256,128]{0,1:T(8,128)S(1)} collective-permute-done((f32[256,128]{0,1:T(8,128)S(1)}, f32[256,128]{0,1:T(8,128)S(1)}, u32[]{:S(2)}, u32[]{:S(2)}) %collective-permute-start.34) | collective-permute-done | bytes 131104 | tf_op jit(solution)/shard_map/ppermute | solution.py:28
  223.7 11.7 %cholesky.16 = f32[128,128]{1,0:T(8,128)S(1)} custom-call(f32[128,128]{1,0:T(8,128)S(1)} %fusion.102), custom_call_target="Cholesky" | custom-call | tf_op jit(solution)/shard_map/jit(cholesky)/cholesky | solution.py:202
  236.8 9.8 %custom-call.10 = f32[1,128,128]{1,2,0:T(8,128)S(1)} custom-call(f32[1,128,128]{2,1,0:T(8,128)S(1)} %fusion.95), custom_call_target="InvertDiagBlocksLowerTriangular" | custom-call | tf_op jit(solution)/shard_map/triangular_solve | solution.py:203
  (176 shorter events, 39.8 us)
Async XLA Ops:
  1.6 27.0 %collective-permute-start = (bf16[256,128]{1,0:T(8,128)(2,1)S(1)}, bf16[256,128]{1,0:T(8,128)(2,1)S(1)}, u32[]{:S(2)}, u32[]{:S(2)}) collective-permute-start(bf16[256,128]{1,0:T(8,128)(2,1)S(1)} %multiply_convert_fusion.4), channel_id=1, source_target_pairs={{0,8},{8,0},{16,24},{24,16},{1,9},{9,1},{17,25},{25,17},{2,10},{10... | collective-permute-start | bytes 196616 | tf_op jit(solution)/shard_map/ppermute | solution.py:114
  4.7 27.4 %collective-permute-start.5 = (bf16[256,128]{1,0:T(8,128)(2,1)}, bf16[256,128]{1,0:T(8,128)(2,1)S(1)}, u32[]{:S(2)}, u32[]{:S(2)}) collective-permute-start(bf16[256,128]{1,0:T(8,128)(2,1)} %param.12), channel_id=1, source_target_pairs={{0,8},{8,0},{16,24},{24,16},{1,9},{9,1},{17,25},{25,17},{2,10},{10... | collective-permute-start | bytes 196616 | tf_op jit(solution)/shard_map/ppermute | solution.py:114
  4.8 25.6 %collective-permute-start.2 = (bf16[1,256,128]{2,1,0:T(8,128)(2,1)}, bf16[1,256,128]{2,1,0:T(8,128)(2,1)S(1)}, u32[]{:S(2)}, u32[]{:S(2)}) collective-permute-start(bf16[1,256,128]{2,1,0:T(8,128)(2,1)} %bitcast.252), channel_id=1, source_target_pairs={{0,4},{1,5},{2,6},{3,7},{4,0},{5,1},{6,2},{7,3},{8,12},{9,13},{10,... | collective-permute-start | bytes 196616 | tf_op jit(solution)/shard_map/ppermute | solution.py:95
  20.4 3.7 %copy-start.5 = (bf16[256,128]{1,0:T(8,128)(2,1)S(1)}, bf16[256,128]{1,0:T(8,128)(2,1)}, u32[]{:S(2)}) copy-start(bf16[256,128]{1,0:T(8,128)(2,1)} %param.12) | copy-start | bytes 196612
  24.1 4.5 %copy-start.10 = (s32[8]{0:T(128)S(1)}, s32[8]{0:T(128)}, u32[]{:S(2)}) copy-start(s32[8]{0:T(128)} %constant.310) | copy-start | bytes 100
  24.1 4.6 %copy-start.6 = (f32[256,128]{1,0:T(8,128)S(1)}, f32[256,128]{1,0:T(8,128)}, u32[]{:S(2)}) copy-start(f32[256,128]{1,0:T(8,128)} %param.11) | copy-start | bytes 393220
  24.1 4.6 %copy-start.7 = (f32[256]{0:T(256)S(1)}, f32[256]{0:T(256)}, u32[]{:S(2)}) copy-start(f32[256]{0:T(256)} %param.10) | copy-start | bytes 3076
  28.6 5.7 %copy-start.4 = (f32[2048,128]{1,0:T(8,128)S(1)}, f32[2048,128]{1,0:T(8,128)}, u32[]{:S(2)}) copy-start(f32[2048,128]{1,0:T(8,128)} %convolution_add_fusion.19) | copy-start | bytes 3145732
  28.8 7.6 %collective-permute-start.1 = (bf16[512,128]{1,0:T(8,128)(2,1)S(1)}, bf16[512,128]{1,0:T(8,128)(2,1)S(1)}, u32[]{:S(2)}, u32[]{:S(2)}) collective-permute-start(bf16[512,128]{1,0:T(8,128)(2,1)S(1)} %pad_maximum_fusion.2), channel_id=1, source_target_pairs={{0,16},{8,24},{16,0},{24,8},{1,17},{9,25},{17,1},{25,9},{2,18},{10... | collective-permute-start | bytes 393224 | tf_op jit(solution)/shard_map/ppermute | solution.py:114
  30.4 6.0 %copy-start.2 = (bf16[2048,1024]{1,0:T(8,128)(2,1)S(1)}, bf16[2048,1024]{1,0:T(8,128)(2,1)}, u32[]{:S(2)}) copy-start(bf16[2048,1024]{1,0:T(8,128)(2,1)} %fusion) | copy-start | bytes 12582916
  30.4 5.8 %collective-permute-start.3 = (bf16[2,256,128]{2,1,0:T(8,128)(2,1)S(1)}, bf16[2,256,128]{2,1,0:T(8,128)(2,1)S(1)}, u32[]{:S(2)}, u32[]{:S(2)}) collective-permute-start(bf16[2,256,128]{2,1,0:T(8,128)(2,1)S(1)} %pad_maximum_fusion.3), channel_id=1, source_target_pairs={{0,2},{1,3},{2,0},{3,1},{4,6},{5,7},{6,4},{7,5},{8,10},{9,11},{10,... | collective-permute-start | bytes 393224 | tf_op jit(solution)/shard_map/ppermute | solution.py:95
  32.1 6.0 %collective-permute-start.6 = (bf16[512,128]{1,0:T(8,128)(2,1)S(1)}, bf16[512,128]{1,0:T(8,128)(2,1)S(1)}, u32[]{:S(2)}, u32[]{:S(2)}) collective-permute-start(bf16[512,128]{1,0:T(8,128)(2,1)S(1)} %pad_maximum_fusion.4), channel_id=1, source_target_pairs={{0,16},{8,24},{16,0},{24,8},{1,17},{9,25},{17,1},{25,9},{2,18},{10... | collective-permute-start | bytes 393224 | tf_op jit(solution)/shard_map/ppermute | solution.py:114
  34.3 3.7 %copy-start.8 = (f32[128]{0:T(128)S(1)}, f32[128]{0:T(128)}, u32[]{:S(2)}) copy-start(f32[128]{0:T(128)} %param.13) | copy-start | bytes 1540
  36.3 2.3 collective-permute-start.4
  39.3 2.2 copy-start
  41.5 13.3 %copy-start.9 = (f32[2]{0:T(128)S(1)}, f32[2]{0:T(128)}, u32[]{:S(2)}) copy-start(f32[2]{0:T(128)} %param.14) | copy-start | bytes 28
  43.5 2.1 collective-permute-start.7
  45.7 8.7 %collective-permute-start.8 = (f32[2,256,128]{2,1,0:T(8,128)S(1)}, f32[2,256,128]{2,1,0:T(8,128)S(1)}, u32[]{:S(2)}, u32[]{:S(2)}) collective-permute-start(f32[2,256,128]{2,1,0:T(8,128)S(1)} %dynamic-slice_bitcast_fusion.9), channel_id=1, source_target_pairs={{0,2},{1,3},{2,0},{3,1},{4,6},{5,7},{6,4},{7,5},{8,10},{9,11},{10,... | collective-permute-start | bytes 786440 | tf_op jit(solution)/shard_map/ppermute | solution.py:63
  54.4 8.7 %collective-permute-start.9 = (f32[1,256,128]{2,1,0:T(8,128)S(1)}, f32[1,256,128]{2,1,0:T(8,128)S(1)}, u32[]{:S(2)}, u32[]{:S(2)}) collective-permute-start(f32[1,256,128]{2,1,0:T(8,128)S(1)} %constant_dynamic-slice_fusion.3), channel_id=1, source_target_pairs={{0,4},{1,5},{2,6},{3,7},{4,0},{5,1},{6,2},{7,3},{8,12},{9,13},{10,... | collective-permute-start | bytes 393224 | tf_op jit(solution)/shard_map/ppermute | solution.py:63
  58.0 11.8 %copy-start.3 = (bf16[2048,1024]{1,0:T(8,128)(2,1)S(1)}, bf16[2048,1024]{1,0:T(8,128)(2,1)}, u32[]{:S(2)}) copy-start(bf16[2048,1024]{1,0:T(8,128)(2,1)} %fusion) | copy-start | bytes 12582916
  63.2 7.1 %copy-start.1 = (bf16[256,8,8,128]{3,1,2,0:T(8,128)(2,1)S(1)}, bf16[256,8,8,128]{3,1,2,0:T(8,128)(2,1)}, u32[]{:S(2)}) copy-start(bf16[256,8,8,128]{3,1,2,0:T(8,128)(2,1)} %copy.43) | copy-start | bytes 12582916
  63.2 5.1 %collective-permute-start.10 = (bf16[256,128]{1,0:T(8,128)(2,1)S(1)}, bf16[256,128]{1,0:T(8,128)(2,1)S(1)}, u32[]{:S(2)}, u32[]{:S(2)}) collective-permute-start(bf16[256,128]{1,0:T(8,128)(2,1)S(1)} %get-tuple-element.8), channel_id=1, source_target_pairs={{0,8},{8,0},{16,24},{24,16},{1,9},{9,1},{17,25},{25,17},{2,10},{10... | collective-permute-start | bytes 196616 | tf_op jit(solution)/shard_map/ppermute | solution.py:114
  68.4 5.0 %collective-permute-start.11 = (bf16[512,128]{1,0:T(8,128)(2,1)S(1)}, bf16[512,128]{1,0:T(8,128)(2,1)S(1)}, u32[]{:S(2)}, u32[]{:S(2)}) collective-permute-start(bf16[512,128]{1,0:T(8,128)(2,1)S(1)} %pad_maximum_fusion.5), channel_id=1, source_target_pairs={{0,16},{8,24},{16,0},{24,8},{1,17},{9,25},{17,1},{25,9},{2,18},{10... | collective-permute-start | bytes 393224 | tf_op jit(solution)/shard_map/ppermute | solution.py:114
  75.7 2.0 collective-permute-start.12
  77.8 8.4 %collective-permute-start.13 = (f32[2,256,128]{2,1,0:T(8,128)S(1)}, f32[2,256,128]{2,1,0:T(8,128)S(1)}, u32[]{:S(2)}, u32[]{:S(2)}) collective-permute-start(f32[2,256,128]{2,1,0:T(8,128)S(1)} %dynamic-slice_bitcast_fusion.8), channel_id=1, source_target_pairs={{0,2},{1,3},{2,0},{3,1},{4,6},{5,7},{6,4},{7,5},{8,10},{9,11},{10,... | collective-permute-start | bytes 786440 | tf_op jit(solution)/shard_map/ppermute | solution.py:63
  86.3 8.5 %collective-permute-start.14 = (f32[1,256,128]{2,1,0:T(8,128)S(1)}, f32[1,256,128]{2,1,0:T(8,128)S(1)}, u32[]{:S(2)}, u32[]{:S(2)}) collective-permute-start(f32[1,256,128]{2,1,0:T(8,128)S(1)} %constant_dynamic-slice_fusion.2), channel_id=1, source_target_pairs={{0,4},{1,5},{2,6},{3,7},{4,0},{5,1},{6,2},{7,3},{8,12},{9,13},{10,... | collective-permute-start | bytes 393224 | tf_op jit(solution)/shard_map/ppermute | solution.py:63
  94.8 4.3 %collective-permute-start.15 = (bf16[256,128]{1,0:T(8,128)(2,1)S(1)}, bf16[256,128]{1,0:T(8,128)(2,1)S(1)}, u32[]{:S(2)}, u32[]{:S(2)}) collective-permute-start(bf16[256,128]{1,0:T(8,128)(2,1)S(1)} %get-tuple-element.6), channel_id=1, source_target_pairs={{0,8},{8,0},{16,24},{24,16},{1,9},{9,1},{17,25},{25,17},{2,10},{10... | collective-permute-start | bytes 196616 | tf_op jit(solution)/shard_map/ppermute | solution.py:114
  99.2 5.0 %collective-permute-start.16 = (bf16[512,128]{1,0:T(8,128)(2,1)S(1)}, bf16[512,128]{1,0:T(8,128)(2,1)S(1)}, u32[]{:S(2)}, u32[]{:S(2)}) collective-permute-start(bf16[512,128]{1,0:T(8,128)(2,1)S(1)} %pad_maximum_fusion.6), channel_id=1, source_target_pairs={{0,16},{8,24},{16,0},{24,8},{1,17},{9,25},{17,1},{25,9},{2,18},{10... | collective-permute-start | bytes 393224 | tf_op jit(solution)/shard_map/ppermute | solution.py:114
  106.6 2.0 collective-permute-start.17
  108.6 8.4 %collective-permute-start.18 = (f32[2,256,128]{2,1,0:T(8,128)S(1)}, f32[2,256,128]{2,1,0:T(8,128)S(1)}, u32[]{:S(2)}, u32[]{:S(2)}) collective-permute-start(f32[2,256,128]{2,1,0:T(8,128)S(1)} %dynamic-slice_bitcast_fusion.7), channel_id=1, source_target_pairs={{0,2},{1,3},{2,0},{3,1},{4,6},{5,7},{6,4},{7,5},{8,10},{9,11},{10,... | collective-permute-start | bytes 786440 | tf_op jit(solution)/shard_map/ppermute | solution.py:63
  117.1 8.5 %collective-permute-start.19 = (f32[1,256,128]{2,1,0:T(8,128)S(1)}, f32[1,256,128]{2,1,0:T(8,128)S(1)}, u32[]{:S(2)}, u32[]{:S(2)}) collective-permute-start(f32[1,256,128]{2,1,0:T(8,128)S(1)} %constant_dynamic-slice_fusion.1), channel_id=1, source_target_pairs={{0,4},{1,5},{2,6},{3,7},{4,0},{5,1},{6,2},{7,3},{8,12},{9,13},{10,... | collective-permute-start | bytes 393224 | tf_op jit(solution)/shard_map/ppermute | solution.py:63
  125.7 4.3 %collective-permute-start.20 = (bf16[256,128]{1,0:T(8,128)(2,1)S(1)}, bf16[256,128]{1,0:T(8,128)(2,1)S(1)}, u32[]{:S(2)}, u32[]{:S(2)}) collective-permute-start(bf16[256,128]{1,0:T(8,128)(2,1)S(1)} %get-tuple-element.4), channel_id=1, source_target_pairs={{0,8},{8,0},{16,24},{24,16},{1,9},{9,1},{17,25},{25,17},{2,10},{10... | collective-permute-start | bytes 196616 | tf_op jit(solution)/shard_map/ppermute | solution.py:114
  130.0 5.0 %collective-permute-start.21 = (bf16[512,128]{1,0:T(8,128)(2,1)S(1)}, bf16[512,128]{1,0:T(8,128)(2,1)S(1)}, u32[]{:S(2)}, u32[]{:S(2)}) collective-permute-start(bf16[512,128]{1,0:T(8,128)(2,1)S(1)} %pad_maximum_fusion.7), channel_id=1, source_target_pairs={{0,16},{8,24},{16,0},{24,8},{1,17},{9,25},{17,1},{25,9},{2,18},{10... | collective-permute-start | bytes 393224 | tf_op jit(solution)/shard_map/ppermute | solution.py:114
  147.2 2.0 collective-permute-start.22
  149.2 8.4 %collective-permute-start.23 = (f32[2,256,128]{2,1,0:T(8,128)S(1)}, f32[2,256,128]{2,1,0:T(8,128)S(1)}, u32[]{:S(2)}, u32[]{:S(2)}) collective-permute-start(f32[2,256,128]{2,1,0:T(8,128)S(1)} %dynamic-slice_bitcast_fusion.6), channel_id=1, source_target_pairs={{0,2},{1,3},{2,0},{3,1},{4,6},{5,7},{6,4},{7,5},{8,10},{9,11},{10,... | collective-permute-start | bytes 786440 | tf_op jit(solution)/shard_map/ppermute | solution.py:63
  157.7 8.5 %collective-permute-start.24 = (f32[1,256,128]{2,1,0:T(8,128)S(1)}, f32[1,256,128]{2,1,0:T(8,128)S(1)}, u32[]{:S(2)}, u32[]{:S(2)}) collective-permute-start(f32[1,256,128]{2,1,0:T(8,128)S(1)} %constant_dynamic-slice_fusion), channel_id=1, source_target_pairs={{0,4},{1,5},{2,6},{3,7},{4,0},{5,1},{6,2},{7,3},{8,12},{9,13},{10,... | collective-permute-start | bytes 393224 | tf_op jit(solution)/shard_map/ppermute | solution.py:63
  166.3 4.3 %collective-permute-start.25 = (bf16[256,128]{1,0:T(8,128)(2,1)S(1)}, bf16[256,128]{1,0:T(8,128)(2,1)S(1)}, u32[]{:S(2)}, u32[]{:S(2)}) collective-permute-start(bf16[256,128]{1,0:T(8,128)(2,1)S(1)} %get-tuple-element.2), channel_id=1, source_target_pairs={{0,8},{8,0},{16,24},{24,16},{1,9},{9,1},{17,25},{25,17},{2,10},{10... | collective-permute-start | bytes 196616 | tf_op jit(solution)/shard_map/ppermute | solution.py:114
  170.6 5.0 %collective-permute-start.26 = (bf16[512,128]{1,0:T(8,128)(2,1)S(1)}, bf16[512,128]{1,0:T(8,128)(2,1)S(1)}, u32[]{:S(2)}, u32[]{:S(2)}) collective-permute-start(bf16[512,128]{1,0:T(8,128)(2,1)S(1)} %pad_maximum_fusion.8), channel_id=1, source_target_pairs={{0,16},{8,24},{16,0},{24,8},{1,17},{9,25},{17,1},{25,9},{2,18},{10... | collective-permute-start | bytes 393224 | tf_op jit(solution)/shard_map/ppermute | solution.py:114
  178.0 2.0 collective-permute-start.27
  180.1 8.4 %collective-permute-start.28 = (f32[2,256,128]{2,1,0:T(8,128)S(1)}, f32[2,256,128]{2,1,0:T(8,128)S(1)}, u32[]{:S(2)}, u32[]{:S(2)}) collective-permute-start(f32[2,256,128]{2,1,0:T(8,128)S(1)} %dynamic-slice_bitcast_fusion.5), channel_id=1, source_target_pairs={{0,2},{1,3},{2,0},{3,1},{4,6},{5,7},{6,4},{7,5},{8,10},{9,11},{10,... | collective-permute-start | bytes 786440 | tf_op jit(solution)/shard_map/ppermute | solution.py:63
  188.6 8.5 %collective-permute-start.29 = (f32[1,256,128]{2,1,0:T(8,128)S(1)}, f32[1,256,128]{2,1,0:T(8,128)S(1)}, u32[]{:S(2)}, u32[]{:S(2)}) collective-permute-start(f32[1,256,128]{2,1,0:T(8,128)S(1)} %constant_dynamic-slice_fusion.4), channel_id=1, source_target_pairs={{0,4},{1,5},{2,6},{3,7},{4,0},{5,1},{6,2},{7,3},{8,12},{9,13},{10,... | collective-permute-start | bytes 393224 | tf_op jit(solution)/shard_map/ppermute | solution.py:63
  197.5 1.4 collective-permute-start.30
  198.9 5.6 %collective-permute-start.31 = (f32[256,128]{0,1:T(8,128)S(1)}, f32[256,128]{0,1:T(8,128)S(1)}, u32[]{:S(2)}, u32[]{:S(2)}) collective-permute-start(f32[256,128]{0,1:T(8,128)S(1)} %fusion.126), channel_id=1, source_target_pairs={{0,2},{1,3},{2,0},{3,1},{4,6},{5,7},{6,4},{7,5},{8,10},{9,11},{10,... | collective-permute-start | bytes 393224 | tf_op jit(solution)/shard_map/ppermute | solution.py:28
  204.6 8.5 %collective-permute-start.32 = (f32[256,128]{0,1:T(8,128)S(1)}, f32[256,128]{0,1:T(8,128)S(1)}, u32[]{:S(2)}, u32[]{:S(2)}) collective-permute-start(f32[256,128]{0,1:T(8,128)S(1)} %add.432), channel_id=1, source_target_pairs={{0,4},{1,5},{2,6},{3,7},{4,0},{5,1},{6,2},{7,3},{8,12},{9,13},{10,... | collective-permute-start | bytes 393224 | tf_op jit(solution)/shard_map/ppermute | solution.py:28
  213.0 5.5 %collective-permute-start.33 = (f32[256,128]{0,1:T(8,128)S(1)}, f32[256,128]{0,1:T(8,128)S(1)}, u32[]{:S(2)}, u32[]{:S(2)}) collective-permute-start(f32[256,128]{0,1:T(8,128)S(1)} %add.433), channel_id=1, source_target_pairs={{0,8},{8,0},{16,24},{24,16},{1,9},{9,1},{17,25},{25,17},{2,10},{10... | collective-permute-start | bytes 393224 | tf_op jit(solution)/shard_map/ppermute | solution.py:28
  218.5 5.0 %collective-permute-start.34 = (f32[256,128]{0,1:T(8,128)S(1)}, f32[256,128]{0,1:T(8,128)S(1)}, u32[]{:S(2)}, u32[]{:S(2)}) collective-permute-start(f32[256,128]{0,1:T(8,128)S(1)} %add.434), channel_id=1, source_target_pairs={{0,16},{8,24},{16,0},{24,8},{1,17},{9,25},{17,1},{25,9},{2,18},{10... | collective-permute-start | bytes 393224 | tf_op jit(solution)/shard_map/ppermute | solution.py:28

commit v9 on v8

--- a/solution.py
+++ b/solution.py
@@ -147,10 +147,11 @@
     if in_order:
         pieces = segment_pieces("row")
         block_order = (pieces[:, None] * per_piece + jnp.arange(per_piece, dtype=jnp.int32)[None, :]).reshape(-1)
+        arrival = jnp.argsort(block_order).astype(jnp.int32)[tile_cols]
     else:
-        block_order = jnp.arange(n_blocks, dtype=jnp.int32)
-
-    onehot = (tile_cols[:, :, None] == block_order[None, None, :]).astype(jnp.bfloat16)
+        arrival = tile_cols
+
+    onehot = (arrival[:, :, None] == jnp.arange(n_blocks, dtype=jnp.int32)[None, None, :]).astype(jnp.bfloat16)
     dense = jnp.einsum("rst,rsab->ratb", onehot, tiles, preferred_element_type=jnp.float32)
     dense = dense.reshape(tile_rows * tile_size, n_blocks * tile_size)
     w_hi, w_lo = split_bf16(dense)

time: 253 us -> 257 us (1.016)
    dot_general x5, matrix products: 11.3 us -> 1.47 us  [split_dot(): return first + jnp.dot(left, lower, preferred_element_type=jnp.float32)]
    dot_general x15, matrix products: 13.6 us -> 23.1 us  [operate(): jnp.dot(w_lo[:, columns], segment, preferred_element_type=jnp.float32)]
  transfers between devices with their start and end apart: 35 -> 35, of which waited for: 27 -> 27; matrix products, arithmetic and copies ran while one was open for 16% -> 17% of each run, Pallas kernels for 0% -> 0%
where the time goes in v9:
time: 257 us; the launch traced here: 252 us
  waiting for transfers between devices  128 us (50%)
  matrix products  53.1 us (21%)
  other arithmetic  30.8 us (12%)
  starting transfers between devices  26.2 us (10%)
  local copies, waits for them, and re-layouts  9.3 us (4%)
  between operations  4.69 us (2%)
    ppermute x15, waiting for transfers between devices, halving_scatter_sum(): blocks = kept + lax.ppermute(sent, axis, pairs)  88.5 us
    ppermute x5, waiting for transfers between devices, butterfly_sum(): value = value + lax.ppermute(value, axis, pairs)  23.2 us
    dot_general x15, matrix products, operate(): jnp.dot(w_lo[:, columns], segment, preferred_element_type=jnp.float32)  23.1 us
    ppermute x12, waiting for transfers between devices, gather_segments(): other = lax.ppermute(result, axis, pairs)  16.2 us
    ppermute x12, starting transfers between devices, gather_segments(): other = lax.ppermute(result, axis, pairs)  16 us
    dot_general x15, matrix products, operate(): jnp.dot(w_hi[:, columns], segment, preferred_element_type=jnp.float32)  12.9 us
    another operation x3, other arithmetic, local(): factor = jnp.linalg.cholesky(gram_matrix)  12.4 us
    another operation x2, other arithmetic, local(): lax.linalg.triangular_solve(factor, current, left_side=False, lower=True,...  10.5 us
  transfers between devices with their start and end apart: 35, of which 27 were waited for; matrix products, arithmetic and copies ran while one was open for 17% of the time, Pallas kernels for 0%

profile of v9, /device:TPU:0, one launch (start us, length us, event | category | flops | bytes accessed | tf_op | source)
XLA Modules:
  0.0 252.0 jit_solution(11628307000262557738)
XLA Ops:
  1.6 3.0 %collective-permute-start = (bf16[256,128]{1,0:T(8,128)(2,1)S(1)}, bf16[256,128]{1,0:T(8,128)(2,1)S(1)}, u32[]{:S(2)}, u32[]{:S(2)}) collective-permute-start(bf16[256,128]{1,0:T(8,128)(2,1)S(1)} %multiply_convert_fusion.4), channel_id=1, source_target_pairs={{0,8},{8,0},{16,24},{24,16},{1,9},{9,1},{17,25},{25,17},{2,10},{10... | collective-permute-start | bytes 196616 | tf_op jit(solution)/shard_map/ppermute | solution.py:114
  4.8 3.0 %collective-permute-start.2 = (bf16[1,256,128]{2,1,0:T(8,128)(2,1)}, bf16[1,256,128]{2,1,0:T(8,128)(2,1)S(1)}, u32[]{:S(2)}, u32[]{:S(2)}) collective-permute-start(bf16[1,256,128]{2,1,0:T(8,128)(2,1)} %bitcast.252), channel_id=1, source_target_pairs={{0,4},{1,5},{2,6},{3,7},{4,0},{5,1},{6,2},{7,3},{8,12},{9,13},{10,... | collective-permute-start | bytes 196616 | tf_op jit(solution)/shard_map/ppermute | solution.py:95
  9.8 1.9 gather_fusion
  11.8 8.2 %fusion.1 = f32[16,8,128,128]{3,1,2,0:T(8,128)S(1)} fusion(bf16[16,16,128,128]{3,2,1,0:T(8,128)(2,1)} %param.8, s32[16,16]{1,0:T(8,128)S(1)} %reshape.128), kind=kOutput, calls=%fused_computation.5 | convolution fusion | flops 67110912 | bytes 16778240 | tf_op jit(solution)/shard_map/rst,rsab->ratb/dot_general | solution.py:155
  19.9 4.1 %copy.43 = bf16[256,8,8,128]{3,1,2,0:T(8,128)(2,1)} copy(f32[256,8,8,128]{3,2,1,0:T(8,128)S(1)} %bitcast.230) | data formatting | bytes 12582912
  24.0 3.7 %fusion = bf16[2048,1024]{1,0:T(8,128)(2,1)} fusion(f32[256,8,8,128]{3,2,1,0:T(8,128)S(1)} %bitcast.231), kind=kLoop, calls=%fused_computation.4 | loop fusion | flops 8388608 | bytes 12582912 | tf_op jit(solution)/shard_map/convert_element_type | solution.py:11
  27.9 1.6 fusion.76
  29.6 2.6 %convolution_add_fusion.19 = f32[2048,128]{1,0:T(8,128)} fusion(f32[2048,128]{1,0:T(8,128)S(1)} %fusion.76, bf16[256,128]{1,0:T(8,128)(2,1)S(1)} %multiply_convert_fusion.4, bf16[2048,1024]{1,0:T(8,128)(2,1)} %fusion), kind=kOutput, calls=%fused_computation.46 | convolution fusion | flops 134479872 | bytes 3211264 | tf_op jit(solution)/shard_map/dot_general | solution.py:178
  32.4 1.6 collective-permute-start.1
  34.1 1.6 collective-permute-start.3
  36.3 1.6 fusion.56
  38.0 1.7 fusion.22
  40.0 1.7 fusion.41
  44.9 2.0 fusion.17
  50.0 7.8 %collective-permute-done.8 = f32[2,256,128]{2,1,0:T(8,128)S(1)} collective-permute-done((f32[2,256,128]{2,1,0:T(8,128)S(1)}, f32[2,256,128]{2,1,0:T(8,128)S(1)}, u32[]{:S(2)}, u32[]{:S(2)}) %collective-permute-start.8) | collective-permute-done | bytes 262176 | tf_op jit(solution)/shard_map/ppermute | solution.py:63
  61.5 5.1 %collective-permute-done.9 = f32[1,256,128]{2,1,0:T(8,128)S(1)} collective-permute-done((f32[1,256,128]{2,1,0:T(8,128)S(1)}, f32[1,256,128]{2,1,0:T(8,128)S(1)}, u32[]{:S(2)}, u32[]{:S(2)}) %collective-permute-start.9) | collective-permute-done | bytes 131104 | tf_op jit(solution)/shard_map/ppermute | solution.py:63
  68.2 1.6 fusion.74
  69.9 1.7 convolution_add_fusion.17
  74.4 2.4 collective-permute-done.11
  79.2 1.9 collective-permute-done.12
  81.3 8.3 %collective-permute-done.13 = f32[2,256,128]{2,1,0:T(8,128)S(1)} collective-permute-done((f32[2,256,128]{2,1,0:T(8,128)S(1)}, f32[2,256,128]{2,1,0:T(8,128)S(1)}, u32[]{:S(2)}, u32[]{:S(2)}) %collective-permute-start.13) | collective-permute-done | bytes 262176 | tf_op jit(solution)/shard_map/ppermute | solution.py:63
  89.8 8.4 %collective-permute-done.14 = f32[1,256,128]{2,1,0:T(8,128)S(1)} collective-permute-done((f32[1,256,128]{2,1,0:T(8,128)S(1)}, f32[1,256,128]{2,1,0:T(8,128)S(1)}, u32[]{:S(2)}, u32[]{:S(2)}) %collective-permute-start.14) | collective-permute-done | bytes 131104 | tf_op jit(solution)/shard_map/ppermute | solution.py:63
  100.3 2.3 collective-permute-done.15
  102.6 1.6 collective-permute-start.16
  105.4 2.3 collective-permute-done.16
  110.1 1.9 collective-permute-done.17
  112.1 8.3 %collective-permute-done.18 = f32[2,256,128]{2,1,0:T(8,128)S(1)} collective-permute-done((f32[2,256,128]{2,1,0:T(8,128)S(1)}, f32[2,256,128]{2,1,0:T(8,128)S(1)}, u32[]{:S(2)}, u32[]{:S(2)}) %collective-permute-start.18) | collective-permute-done | bytes 262176 | tf_op jit(solution)/shard_map/ppermute | solution.py:63
  120.6 8.4 %collective-permute-done.19 = f32[1,256,128]{2,1,0:T(8,128)S(1)} collective-permute-done((f32[1,256,128]{2,1,0:T(8,128)S(1)}, f32[1,256,128]{2,1,0:T(8,128)S(1)}, u32[]{:S(2)}, u32[]{:S(2)}) %collective-permute-start.19) | collective-permute-done | bytes 131104 | tf_op jit(solution)/shard_map/ppermute | solution.py:63
  131.1 2.3 collective-permute-done.20
  133.5 1.7 collective-permute-start.21
  136.2 2.3 collective-permute-done.21
  139.3 10.3 %fusion.35 = f32[2048,128]{1,0:T(8,128)S(1)} fusion(bf16[512,128]{1,0:T(8,128)(2,1)S(1)} %collective-permute-done.21, bf16[2048,1024]{1,0:T(8,128)(2,1)S(1)} %copy-done.3), kind=kOutput, calls=%fused_computation.69 | convolution fusion | flops 268435456 | bytes 3276800 | tf_op jit(solution)/shard_map/dot_general | solution.py:178
  150.5 1.9 collective-permute-done.22
  152.5 8.3 %collective-permute-done.23 = f32[2,256,128]{2,1,0:T(8,128)S(1)} collective-permute-done((f32[2,256,128]{2,1,0:T(8,128)S(1)}, f32[2,256,128]{2,1,0:T(8,128)S(1)}, u32[]{:S(2)}, u32[]{:S(2)}) %collective-permute-start.23) | collective-permute-done | bytes 262176 | tf_op jit(solution)/shard_map/ppermute | solution.py:63
  161.0 8.4 %collective-permute-done.24 = f32[1,256,128]{2,1,0:T(8,128)S(1)} collective-permute-done((f32[1,256,128]{2,1,0:T(8,128)S(1)}, f32[1,256,128]{2,1,0:T(8,128)S(1)}, u32[]{:S(2)}, u32[]{:S(2)}) %collective-permute-start.24) | collective-permute-done | bytes 131104 | tf_op jit(solution)/shard_map/ppermute | solution.py:63
  171.5 2.3 collective-permute-done.25
  173.9 1.7 collective-permute-start.26
  176.6 2.3 collective-permute-done.26
  181.3 1.9 collective-permute-done.27
  183.4 8.3 %collective-permute-done.28 = f32[2,256,128]{2,1,0:T(8,128)S(1)} collective-permute-done((f32[2,256,128]{2,1,0:T(8,128)S(1)}, f32[2,256,128]{2,1,0:T(8,128)S(1)}, u32[]{:S(2)}, u32[]{:S(2)}) %collective-permute-start.28) | collective-permute-done | bytes 262176 | tf_op jit(solution)/shard_map/ppermute | solution.py:63
  192.2 8.0 %collective-permute-done.29 = f32[1,256,128]{2,1,0:T(8,128)S(1)} collective-permute-done((f32[1,256,128]{2,1,0:T(8,128)S(1)}, f32[1,256,128]{2,1,0:T(8,128)S(1)}, u32[]{:S(2)}, u32[]{:S(2)}) %collective-permute-start.29) | collective-permute-done | bytes 131104 | tf_op jit(solution)/shard_map/ppermute | solution.py:63
  202.2 5.5 %collective-permute-done.31 = f32[256,128]{0,1:T(8,128)S(1)} collective-permute-done((f32[256,128]{0,1:T(8,128)S(1)}, f32[256,128]{0,1:T(8,128)S(1)}, u32[]{:S(2)}, u32[]{:S(2)}) %collective-permute-start.31) | collective-permute-done | bytes 131104 | tf_op jit(solution)/shard_map/ppermute | solution.py:28
  207.8 8.4 %collective-permute-done.32 = f32[256,128]{0,1:T(8,128)S(1)} collective-permute-done((f32[256,128]{0,1:T(8,128)S(1)}, f32[256,128]{0,1:T(8,128)S(1)}, u32[]{:S(2)}, u32[]{:S(2)}) %collective-permute-start.32) | collective-permute-done | bytes 131104 | tf_op jit(solution)/shard_map/ppermute | solution.py:28
  217.2 4.6 %collective-permute-done.33 = f32[256,128]{0,1:T(8,128)S(1)} collective-permute-done((f32[256,128]{0,1:T(8,128)S(1)}, f32[256,128]{0,1:T(8,128)S(1)}, u32[]{:S(2)}, u32[]{:S(2)}) %collective-permute-start.33) | collective-permute-done | bytes 131104 | tf_op jit(solution)/shard_map/ppermute | solution.py:28
  221.7 1.7 collective-permute-start.34
  223.4 3.4 %collective-permute-done.34 = f32[256,128]{0,1:T(8,128)S(1)} collective-permute-done((f32[256,128]{0,1:T(8,128)S(1)}, f32[256,128]{0,1:T(8,128)S(1)}, u32[]{:S(2)}, u32[]{:S(2)}) %collective-permute-start.34) | collective-permute-done | bytes 131104 | tf_op jit(solution)/shard_map/ppermute | solution.py:28
  226.9 11.7 %cholesky.16 = f32[128,128]{1,0:T(8,128)S(1)} custom-call(f32[128,128]{1,0:T(8,128)S(1)} %fusion.102), custom_call_target="Cholesky" | custom-call | tf_op jit(solution)/shard_map/jit(cholesky)/cholesky | solution.py:203
  240.0 9.8 %custom-call.10 = f32[1,128,128]{1,2,0:T(8,128)S(1)} custom-call(f32[1,128,128]{2,1,0:T(8,128)S(1)} %fusion.95), custom_call_target="InvertDiagBlocksLowerTriangular" | custom-call | tf_op jit(solution)/shard_map/triangular_solve | solution.py:204
  (183 shorter events, 42.3 us)
Async XLA Ops:
  1.6 30.6 %collective-permute-start = (bf16[256,128]{1,0:T(8,128)(2,1)S(1)}, bf16[256,128]{1,0:T(8,128)(2,1)S(1)}, u32[]{:S(2)}, u32[]{:S(2)}) collective-permute-start(bf16[256,128]{1,0:T(8,128)(2,1)S(1)} %multiply_convert_fusion.4), channel_id=1, source_target_pairs={{0,8},{8,0},{16,24},{24,16},{1,9},{9,1},{17,25},{25,17},{2,10},{10... | collective-permute-start | bytes 196616 | tf_op jit(solution)/shard_map/ppermute | solution.py:114
  4.7 31.0 %collective-permute-start.5 = (bf16[256,128]{1,0:T(8,128)(2,1)}, bf16[256,128]{1,0:T(8,128)(2,1)S(1)}, u32[]{:S(2)}, u32[]{:S(2)}) collective-permute-start(bf16[256,128]{1,0:T(8,128)(2,1)} %param.12), channel_id=1, source_target_pairs={{0,8},{8,0},{16,24},{24,16},{1,9},{9,1},{17,25},{25,17},{2,10},{10... | collective-permute-start | bytes 196616 | tf_op jit(solution)/shard_map/ppermute | solution.py:114
  4.8 29.3 %collective-permute-start.2 = (bf16[1,256,128]{2,1,0:T(8,128)(2,1)}, bf16[1,256,128]{2,1,0:T(8,128)(2,1)S(1)}, u32[]{:S(2)}, u32[]{:S(2)}) collective-permute-start(bf16[1,256,128]{2,1,0:T(8,128)(2,1)} %bitcast.252), channel_id=1, source_target_pairs={{0,4},{1,5},{2,6},{3,7},{4,0},{5,1},{6,2},{7,3},{8,12},{9,13},{10,... | collective-permute-start | bytes 196616 | tf_op jit(solution)/shard_map/ppermute | solution.py:95
  24.0 3.7 %copy-start.5 = (bf16[256,128]{1,0:T(8,128)(2,1)S(1)}, bf16[256,128]{1,0:T(8,128)(2,1)}, u32[]{:S(2)}) copy-start(bf16[256,128]{1,0:T(8,128)(2,1)} %param.12) | copy-start | bytes 196612
  27.7 4.5 %copy-start.10 = (s32[8]{0:T(128)S(1)}, s32[8]{0:T(128)}, u32[]{:S(2)}) copy-start(s32[8]{0:T(128)} %constant.312) | copy-start | bytes 100
  27.7 4.6 %copy-start.6 = (f32[256,128]{1,0:T(8,128)S(1)}, f32[256,128]{1,0:T(8,128)}, u32[]{:S(2)}) copy-start(f32[256,128]{1,0:T(8,128)} %param.11) | copy-start | bytes 393220
  27.7 4.6 %copy-start.7 = (f32[256]{0:T(256)S(1)}, f32[256]{0:T(256)}, u32[]{:S(2)}) copy-start(f32[256]{0:T(256)} %param.10) | copy-start | bytes 3076
  32.3 5.7 %copy-start.4 = (f32[2048,128]{1,0:T(8,128)S(1)}, f32[2048,128]{1,0:T(8,128)}, u32[]{:S(2)}) copy-start(f32[2048,128]{1,0:T(8,128)} %convolution_add_fusion.19) | copy-start | bytes 3145732
  32.4 7.6 %collective-permute-start.1 = (bf16[512,128]{1,0:T(8,128)(2,1)S(1)}, bf16[512,128]{1,0:T(8,128)(2,1)S(1)}, u32[]{:S(2)}, u32[]{:S(2)}) collective-permute-start(bf16[512,128]{1,0:T(8,128)(2,1)S(1)} %pad_maximum_fusion.2), channel_id=1, source_target_pairs={{0,16},{8,24},{16,0},{24,8},{1,17},{9,25},{17,1},{25,9},{2,18},{10... | collective-permute-start | bytes 393224 | tf_op jit(solution)/shard_map/ppermute | solution.py:114
  34.1 6.0 %copy-start.2 = (bf16[2048,1024]{1,0:T(8,128)(2,1)S(1)}, bf16[2048,1024]{1,0:T(8,128)(2,1)}, u32[]{:S(2)}) copy-start(bf16[2048,1024]{1,0:T(8,128)(2,1)} %fusion) | copy-start | bytes 12582916
  34.1 5.8 %collective-permute-start.3 = (bf16[2,256,128]{2,1,0:T(8,128)(2,1)S(1)}, bf16[2,256,128]{2,1,0:T(8,128)(2,1)S(1)}, u32[]{:S(2)}, u32[]{:S(2)}) collective-permute-start(bf16[2,256,128]{2,1,0:T(8,128)(2,1)S(1)} %pad_maximum_fusion.3), channel_id=1, source_target_pairs={{0,2},{1,3},{2,0},{3,1},{4,6},{5,7},{6,4},{7,5},{8,10},{9,11},{10,... | collective-permute-start | bytes 393224 | tf_op jit(solution)/shard_map/ppermute | solution.py:95
  35.8 6.0 %collective-permute-start.6 = (bf16[512,128]{1,0:T(8,128)(2,1)S(1)}, bf16[512,128]{1,0:T(8,128)(2,1)S(1)}, u32[]{:S(2)}, u32[]{:S(2)}) collective-permute-start(bf16[512,128]{1,0:T(8,128)(2,1)S(1)} %pad_maximum_fusion.4), channel_id=1, source_target_pairs={{0,16},{8,24},{16,0},{24,8},{1,17},{9,25},{17,1},{25,9},{2,18},{10... | collective-permute-start | bytes 393224 | tf_op jit(solution)/shard_map/ppermute | solution.py:114
  38.0 3.7 %copy-start.8 = (f32[128]{0:T(128)S(1)}, f32[128]{0:T(128)}, u32[]{:S(2)}) copy-start(f32[128]{0:T(128)} %param.13) | copy-start | bytes 1540
  39.9 2.0 collective-permute-start.4
  42.8 2.2 copy-start
  44.9 13.3 %copy-start.9 = (f32[2]{0:T(128)S(1)}, f32[2]{0:T(128)}, u32[]{:S(2)}) copy-start(f32[2]{0:T(128)} %param.14) | copy-start | bytes 28
  47.0 2.1 collective-permute-start.7
  49.2 8.7 %collective-permute-start.8 = (f32[2,256,128]{2,1,0:T(8,128)S(1)}, f32[2,256,128]{2,1,0:T(8,128)S(1)}, u32[]{:S(2)}, u32[]{:S(2)}) collective-permute-start(f32[2,256,128]{2,1,0:T(8,128)S(1)} %dynamic-slice_bitcast_fusion.9), channel_id=1, source_target_pairs={{0,2},{1,3},{2,0},{3,1},{4,6},{5,7},{6,4},{7,5},{8,10},{9,11},{10,... | collective-permute-start | bytes 786440 | tf_op jit(solution)/shard_map/ppermute | solution.py:63
  57.9 8.7 %collective-permute-start.9 = (f32[1,256,128]{2,1,0:T(8,128)S(1)}, f32[1,256,128]{2,1,0:T(8,128)S(1)}, u32[]{:S(2)}, u32[]{:S(2)}) collective-permute-start(f32[1,256,128]{2,1,0:T(8,128)S(1)} %constant_dynamic-slice_fusion.3), channel_id=1, source_target_pairs={{0,4},{1,5},{2,6},{3,7},{4,0},{5,1},{6,2},{7,3},{8,12},{9,13},{10,... | collective-permute-start | bytes 393224 | tf_op jit(solution)/shard_map/ppermute | solution.py:63
  61.5 11.8 %copy-start.3 = (bf16[2048,1024]{1,0:T(8,128)(2,1)S(1)}, bf16[2048,1024]{1,0:T(8,128)(2,1)}, u32[]{:S(2)}) copy-start(bf16[2048,1024]{1,0:T(8,128)(2,1)} %fusion) | copy-start | bytes 12582916
  66.7 7.0 %copy-start.1 = (bf16[256,8,8,128]{3,1,2,0:T(8,128)(2,1)S(1)}, bf16[256,8,8,128]{3,1,2,0:T(8,128)(2,1)}, u32[]{:S(2)}) copy-start(bf16[256,8,8,128]{3,1,2,0:T(8,128)(2,1)} %copy.43) | copy-start | bytes 12582916
  66.7 5.1 %collective-permute-start.10 = (bf16[256,128]{1,0:T(8,128)(2,1)S(1)}, bf16[256,128]{1,0:T(8,128)(2,1)S(1)}, u32[]{:S(2)}, u32[]{:S(2)}) collective-permute-start(bf16[256,128]{1,0:T(8,128)(2,1)S(1)} %get-tuple-element.10), channel_id=1, source_target_pairs={{0,8},{8,0},{16,24},{24,16},{1,9},{9,1},{17,25},{25,17},{2,10},{10... | collective-permute-start | bytes 196616 | tf_op jit(solution)/shard_map/ppermute | solution.py:114
  71.8 5.0 %collective-permute-start.11 = (bf16[512,128]{1,0:T(8,128)(2,1)S(1)}, bf16[512,128]{1,0:T(8,128)(2,1)S(1)}, u32[]{:S(2)}, u32[]{:S(2)}) collective-permute-start(bf16[512,128]{1,0:T(8,128)(2,1)S(1)} %pad_maximum_fusion.5), channel_id=1, source_target_pairs={{0,16},{8,24},{16,0},{24,8},{1,17},{9,25},{17,1},{25,9},{2,18},{10... | collective-permute-start | bytes 393224 | tf_op jit(solution)/shard_map/ppermute | solution.py:114
  79.1 2.0 collective-permute-start.12
  81.2 8.4 %collective-permute-start.13 = (f32[2,256,128]{2,1,0:T(8,128)S(1)}, f32[2,256,128]{2,1,0:T(8,128)S(1)}, u32[]{:S(2)}, u32[]{:S(2)}) collective-permute-start(f32[2,256,128]{2,1,0:T(8,128)S(1)} %dynamic-slice_bitcast_fusion.8), channel_id=1, source_target_pairs={{0,2},{1,3},{2,0},{3,1},{4,6},{5,7},{6,4},{7,5},{8,10},{9,11},{10,... | collective-permute-start | bytes 786440 | tf_op jit(solution)/shard_map/ppermute | solution.py:63
  89.7 8.5 %collective-permute-start.14 = (f32[1,256,128]{2,1,0:T(8,128)S(1)}, f32[1,256,128]{2,1,0:T(8,128)S(1)}, u32[]{:S(2)}, u32[]{:S(2)}) collective-permute-start(f32[1,256,128]{2,1,0:T(8,128)S(1)} %constant_dynamic-slice_fusion.2), channel_id=1, source_target_pairs={{0,4},{1,5},{2,6},{3,7},{4,0},{5,1},{6,2},{7,3},{8,12},{9,13},{10,... | collective-permute-start | bytes 393224 | tf_op jit(solution)/shard_map/ppermute | solution.py:63
  98.3 4.3 %collective-permute-start.15 = (bf16[256,128]{1,0:T(8,128)(2,1)S(1)}, bf16[256,128]{1,0:T(8,128)(2,1)S(1)}, u32[]{:S(2)}, u32[]{:S(2)}) collective-permute-start(bf16[256,128]{1,0:T(8,128)(2,1)S(1)} %get-tuple-element.8), channel_id=1, source_target_pairs={{0,8},{8,0},{16,24},{24,16},{1,9},{9,1},{17,25},{25,17},{2,10},{10... | collective-permute-start | bytes 196616 | tf_op jit(solution)/shard_map/ppermute | solution.py:114
  102.6 5.0 %collective-permute-start.16 = (bf16[512,128]{1,0:T(8,128)(2,1)S(1)}, bf16[512,128]{1,0:T(8,128)(2,1)S(1)}, u32[]{:S(2)}, u32[]{:S(2)}) collective-permute-start(bf16[512,128]{1,0:T(8,128)(2,1)S(1)} %pad_maximum_fusion.6), channel_id=1, source_target_pairs={{0,16},{8,24},{16,0},{24,8},{1,17},{9,25},{17,1},{25,9},{2,18},{10... | collective-permute-start | bytes 393224 | tf_op jit(solution)/shard_map/ppermute | solution.py:114
  110.0 2.0 collective-permute-start.17
  112.0 8.4 %collective-permute-start.18 = (f32[2,256,128]{2,1,0:T(8,128)S(1)}, f32[2,256,128]{2,1,0:T(8,128)S(1)}, u32[]{:S(2)}, u32[]{:S(2)}) collective-permute-start(f32[2,256,128]{2,1,0:T(8,128)S(1)} %dynamic-slice_bitcast_fusion.7), channel_id=1, source_target_pairs={{0,2},{1,3},{2,0},{3,1},{4,6},{5,7},{6,4},{7,5},{8,10},{9,11},{10,... | collective-permute-start | bytes 786440 | tf_op jit(solution)/shard_map/ppermute | solution.py:63
  120.5 8.5 %collective-permute-start.19 = (f32[1,256,128]{2,1,0:T(8,128)S(1)}, f32[1,256,128]{2,1,0:T(8,128)S(1)}, u32[]{:S(2)}, u32[]{:S(2)}) collective-permute-start(f32[1,256,128]{2,1,0:T(8,128)S(1)} %constant_dynamic-slice_fusion.1), channel_id=1, source_target_pairs={{0,4},{1,5},{2,6},{3,7},{4,0},{5,1},{6,2},{7,3},{8,12},{9,13},{10,... | collective-permute-start | bytes 393224 | tf_op jit(solution)/shard_map/ppermute | solution.py:63
  129.1 4.3 %collective-permute-start.20 = (bf16[256,128]{1,0:T(8,128)(2,1)S(1)}, bf16[256,128]{1,0:T(8,128)(2,1)S(1)}, u32[]{:S(2)}, u32[]{:S(2)}) collective-permute-start(bf16[256,128]{1,0:T(8,128)(2,1)S(1)} %get-tuple-element.6), channel_id=1, source_target_pairs={{0,8},{8,0},{16,24},{24,16},{1,9},{9,1},{17,25},{25,17},{2,10},{10... | collective-permute-start | bytes 196616 | tf_op jit(solution)/shard_map/ppermute | solution.py:114
  133.5 5.0 %collective-permute-start.21 = (bf16[512,128]{1,0:T(8,128)(2,1)S(1)}, bf16[512,128]{1,0:T(8,128)(2,1)S(1)}, u32[]{:S(2)}, u32[]{:S(2)}) collective-permute-start(bf16[512,128]{1,0:T(8,128)(2,1)S(1)} %pad_maximum_fusion.7), channel_id=1, source_target_pairs={{0,16},{8,24},{16,0},{24,8},{1,17},{9,25},{17,1},{25,9},{2,18},{10... | collective-permute-start | bytes 393224 | tf_op jit(solution)/shard_map/ppermute | solution.py:114
  150.4 2.0 collective-permute-start.22
  152.4 8.4 %collective-permute-start.23 = (f32[2,256,128]{2,1,0:T(8,128)S(1)}, f32[2,256,128]{2,1,0:T(8,128)S(1)}, u32[]{:S(2)}, u32[]{:S(2)}) collective-permute-start(f32[2,256,128]{2,1,0:T(8,128)S(1)} %dynamic-slice_bitcast_fusion.6), channel_id=1, source_target_pairs={{0,2},{1,3},{2,0},{3,1},{4,6},{5,7},{6,4},{7,5},{8,10},{9,11},{10,... | collective-permute-start | bytes 786440 | tf_op jit(solution)/shard_map/ppermute | solution.py:63
  160.9 8.5 %collective-permute-start.24 = (f32[1,256,128]{2,1,0:T(8,128)S(1)}, f32[1,256,128]{2,1,0:T(8,128)S(1)}, u32[]{:S(2)}, u32[]{:S(2)}) collective-permute-start(f32[1,256,128]{2,1,0:T(8,128)S(1)} %constant_dynamic-slice_fusion), channel_id=1, source_target_pairs={{0,4},{1,5},{2,6},{3,7},{4,0},{5,1},{6,2},{7,3},{8,12},{9,13},{10,... | collective-permute-start | bytes 393224 | tf_op jit(solution)/shard_map/ppermute | solution.py:63
  169.5 4.3 %collective-permute-start.25 = (bf16[256,128]{1,0:T(8,128)(2,1)S(1)}, bf16[256,128]{1,0:T(8,128)(2,1)S(1)}, u32[]{:S(2)}, u32[]{:S(2)}) collective-permute-start(bf16[256,128]{1,0:T(8,128)(2,1)S(1)} %get-tuple-element.4), channel_id=1, source_target_pairs={{0,8},{8,0},{16,24},{24,16},{1,9},{9,1},{17,25},{25,17},{2,10},{10... | collective-permute-start | bytes 196616 | tf_op jit(solution)/shard_map/ppermute | solution.py:114
  173.9 5.0 %collective-permute-start.26 = (bf16[512,128]{1,0:T(8,128)(2,1)S(1)}, bf16[512,128]{1,0:T(8,128)(2,1)S(1)}, u32[]{:S(2)}, u32[]{:S(2)}) collective-permute-start(bf16[512,128]{1,0:T(8,128)(2,1)S(1)} %pad_maximum_fusion.8), channel_id=1, source_target_pairs={{0,16},{8,24},{16,0},{24,8},{1,17},{9,25},{17,1},{25,9},{2,18},{10... | collective-permute-start | bytes 393224 | tf_op jit(solution)/shard_map/ppermute | solution.py:114
  181.2 2.0 collective-permute-start.27
  183.3 8.4 %collective-permute-start.28 = (f32[2,256,128]{2,1,0:T(8,128)S(1)}, f32[2,256,128]{2,1,0:T(8,128)S(1)}, u32[]{:S(2)}, u32[]{:S(2)}) collective-permute-start(f32[2,256,128]{2,1,0:T(8,128)S(1)} %dynamic-slice_bitcast_fusion.5), channel_id=1, source_target_pairs={{0,2},{1,3},{2,0},{3,1},{4,6},{5,7},{6,4},{7,5},{8,10},{9,11},{10,... | collective-permute-start | bytes 786440 | tf_op jit(solution)/shard_map/ppermute | solution.py:63
  191.8 8.5 %collective-permute-start.29 = (f32[1,256,128]{2,1,0:T(8,128)S(1)}, f32[1,256,128]{2,1,0:T(8,128)S(1)}, u32[]{:S(2)}, u32[]{:S(2)}) collective-permute-start(f32[1,256,128]{2,1,0:T(8,128)S(1)} %constant_dynamic-slice_fusion.4), channel_id=1, source_target_pairs={{0,4},{1,5},{2,6},{3,7},{4,0},{5,1},{6,2},{7,3},{8,12},{9,13},{10,... | collective-permute-start | bytes 393224 | tf_op jit(solution)/shard_map/ppermute | solution.py:63
  200.7 1.4 collective-permute-start.30
  202.1 5.6 %collective-permute-start.31 = (f32[256,128]{0,1:T(8,128)S(1)}, f32[256,128]{0,1:T(8,128)S(1)}, u32[]{:S(2)}, u32[]{:S(2)}) collective-permute-start(f32[256,128]{0,1:T(8,128)S(1)} %fusion.125), channel_id=1, source_target_pairs={{0,2},{1,3},{2,0},{3,1},{4,6},{5,7},{6,4},{7,5},{8,10},{9,11},{10,... | collective-permute-start | bytes 393224 | tf_op jit(solution)/shard_map/ppermute | solution.py:28
  207.8 8.5 %collective-permute-start.32 = (f32[256,128]{0,1:T(8,128)S(1)}, f32[256,128]{0,1:T(8,128)S(1)}, u32[]{:S(2)}, u32[]{:S(2)}) collective-permute-start(f32[256,128]{0,1:T(8,128)S(1)} %add.437), channel_id=1, source_target_pairs={{0,4},{1,5},{2,6},{3,7},{4,0},{5,1},{6,2},{7,3},{8,12},{9,13},{10,... | collective-permute-start | bytes 393224 | tf_op jit(solution)/shard_map/ppermute | solution.py:28
  216.2 5.5 %collective-permute-start.33 = (f32[256,128]{0,1:T(8,128)S(1)}, f32[256,128]{0,1:T(8,128)S(1)}, u32[]{:S(2)}, u32[]{:S(2)}) collective-permute-start(f32[256,128]{0,1:T(8,128)S(1)} %add.438), channel_id=1, source_target_pairs={{0,8},{8,0},{16,24},{24,16},{1,9},{9,1},{17,25},{25,17},{2,10},{10... | collective-permute-start | bytes 393224 | tf_op jit(solution)/shard_map/ppermute | solution.py:28
  221.7 5.0 %collective-permute-start.34 = (f32[256,128]{0,1:T(8,128)S(1)}, f32[256,128]{0,1:T(8,128)S(1)}, u32[]{:S(2)}, u32[]{:S(2)}) collective-permute-start(f32[256,128]{0,1:T(8,128)S(1)} %add.439), channel_id=1, source_target_pairs={{0,16},{8,24},{16,0},{24,8},{1,17},{9,25},{17,1},{25,9},{2,18},{10... | collective-permute-start | bytes 393224 | tf_op jit(solution)/shard_map/ppermute | solution.py:28

commit v10 on v6

--- a/solution.py
+++ b/solution.py
@@ -103,6 +103,24 @@
     return result[jnp.array(order)].reshape(-1, value.shape[1])
 
 
+def split_scatter_sum(kept, sent, axis):
+    size = lax.axis_size(axis)
+    here = lax.axis_index(axis)
+    rows, width = kept.shape[0] // (size // 2), kept.shape[1]
+    blocks = kept.reshape(size // 2, rows, width)
+    blocks = blocks + lax.ppermute(sent.reshape(size // 2, rows, width), axis, [(i, i ^ 1) for i in range(size)])
+    step = 2
+    while step < size:
+        bit = (here // step) % 2
+        paired = blocks.reshape(blocks.shape[0] // 2, 2, rows, width)
+        kept_part = lax.dynamic_index_in_dim(paired, bit, axis=1, keepdims=False)
+        sent_part = lax.dynamic_index_in_dim(paired, 1 - bit, axis=1, keepdims=False)
+        pairs = [(index, index ^ step) for index in range(size)]
+        blocks = kept_part + lax.ppermute(sent_part, axis, pairs)
+        step *= 2
+    return blocks.reshape(rows, width)
+
+
 def local(tiles, tile_cols, degree_scale, start_block, planted, strengths, bounds):
     piece_rows = start_block.shape[0]
     node_count = piece_rows * lax.axis_size("row") * lax.axis_size("col")
@@ -113,21 +131,42 @@
     onehot = (tile_cols[:, :, None] == jnp.arange(n_blocks, dtype=jnp.int32)[None, None, :]).astype(jnp.bfloat16)
     dense = jnp.einsum("rst,rsab->ratb", onehot, tiles, preferred_element_type=jnp.float32)
     dense = dense.reshape(tile_rows * tile_size, n_blocks * tile_size)
+    col_size = lax.axis_size("col")
+    split_rows = col_size % 2 == 0 and col_size & (col_size - 1) == 0
+    if split_rows:
+        col_bit = lax.axis_index("col") % 2
+        halves = jnp.arange(col_size // 2, dtype=jnp.int32) * 2
+        block_perm = jnp.concatenate([halves + col_bit, halves + 1 - col_bit])
+        dense = jnp.take(dense.reshape(col_size, -1, dense.shape[1]), block_perm, axis=0).reshape(dense.shape)
     w_hi, w_lo = split_bf16(dense)
 
     planted_cols = doubling_gather(planted, "row")
     planted_rows = far_first_gather(planted, "col")
+    if split_rows:
+        planted_rows = jnp.take(
+            planted_rows.reshape(col_size, -1, planted_rows.shape[1]), block_perm, axis=0
+        ).reshape(planted_rows.shape)
 
     def operate(vector):
         scaled = (degree_scale[:, None] * vector).astype(jnp.bfloat16)
         gathered = doubling_gather(scaled, "row")
-        product = jnp.dot(w_hi, gathered, preferred_element_type=jnp.float32)
-        product = product + jnp.dot(w_lo, gathered, preferred_element_type=jnp.float32)
         partial = lax.dot_general(
             planted_cols, gathered, (((0,), (0,)), ((), ())), preferred_element_type=jnp.float32
         )
-        product = product + split_dot(planted_rows, weights * partial) / node_count
-        summed = halving_scatter_sum(product, "col")
+        lift = weights * partial
+
+        def rows_product(part):
+            product = jnp.dot(w_hi[part], gathered, preferred_element_type=jnp.float32)
+            product = product + jnp.dot(w_lo[part], gathered, preferred_element_type=jnp.float32)
+            return product + split_dot(planted_rows[part], lift) / node_count
+
+        if split_rows:
+            middle = w_hi.shape[0] // 2
+            sent = rows_product(slice(middle, None))
+            kept = rows_product(slice(0, middle))
+            summed = split_scatter_sum(kept, sent, "col")
+        else:
+            summed = halving_scatter_sum(rows_product(slice(None)), "col")
         return degree_scale[:, None] * summed
 
     center = (bounds[1] + bounds[0]) * 0.5

time: 240 us -> 263 us (1.096)
  local copies, waits for them, and re-layouts: 4.72 us -> 23.2 us
  waiting for transfers between devices: 144 us -> 139 us
  matrix products: 32.4 us -> 37.3 us
  other arithmetic: 31 us -> 34.7 us
    another operation x0 -> x1, local copies, waits for them, and re-layouts: none -> 9.34 us  [local(): dense.reshape(col_size, -1, dense.shape[1])]
    gather x0 -> x2, local copies, waits for them, and re-layouts: none -> 8.42 us  [the longest x1 7.77 us: local(): jnp.take(dense.reshape(col_size, -1, dense.shape[1]), block_perm, axis=0)]
    ppermute x15, waiting for transfers between devices: 87.5 us -> 82.6 us  [the longest x10 78.4 us: split_scatter_sum(): blocks = kept_part + lax.ppermute(sent_part, axis, pairs)]
    dot_general x1, matrix products: 8.2 us -> 11.5 us  [local(): jnp.einsum('rst,rsab->ratb', onehot, tiles, preferred_element_type=jnp.fl...]
    convert_element_type x0 -> x1, other arithmetic: none -> 2.89 us  [split_bf16(): upper = value.astype(jnp.bfloat16)]
    dot_general x10 -> x20, matrix products: 17.2 us -> 17.4 us  [the longest x10 10.2 us: rows_product(): jnp.dot(w_lo[part], gathered, preferred_element_type=jnp.float32)]
  transfers between devices with their start and end apart: 35 -> 35, of which waited for: 29 -> 29; matrix products, arithmetic and copies ran while one was open for 8% -> 18% of each run, Pallas kernels for 0% -> 0%
where the time goes in v10:
time: 263 us; the launch traced here: 262 us
  waiting for transfers between devices  139 us (53%)
  matrix products  37.3 us (14%)
  other arithmetic  34.7 us (13%)
  starting transfers between devices  23.9 us (9%)
  local copies, waits for them, and re-layouts  23.2 us (9%)
  between operations  4.18 us (2%)
    ppermute x10, waiting for transfers between devices, split_scatter_sum(): blocks = kept_part + lax.ppermute(sent_part, axis, pairs)  78.4 us
    ppermute x12, waiting for transfers between devices, doubling_gather(): other = lax.ppermute(result, axis, pairs)  29.7 us
    ppermute x5, waiting for transfers between devices, butterfly_sum(): value = value + lax.ppermute(value, axis, pairs)  23.8 us
    ppermute x12, starting transfers between devices, doubling_gather(): other = lax.ppermute(result, axis, pairs)  13.1 us
    another operation x3, other arithmetic, local(): factor = jnp.linalg.cholesky(gram_matrix)  12.6 us
    dot_general x1, matrix products, local(): jnp.einsum('rst,rsab->ratb', onehot, tiles, preferred_element_type=jnp.fl...  11.5 us
    another operation x2, other arithmetic, local(): lax.linalg.triangular_solve(factor, current, left_side=False, lower=True,...  10.5 us
    dot_general x10, matrix products, rows_product(): jnp.dot(w_lo[part], gathered, preferred_element_type=jnp.float32)  10.2 us
  transfers between devices with their start and end apart: 35, of which 29 were waited for; matrix products, arithmetic and copies ran while one was open for 18% of the time, Pallas kernels for 0%

profile of v10, /device:TPU:0, one launch (start us, length us, event | category | flops | bytes accessed | tf_op | source)
XLA Modules:
  0.0 262.1 jit_solution(2847520476500300809)
XLA Ops:
  0.6 1.0 multiply_convert_fusion.4
  1.6 3.0 %collective-permute-start = (bf16[256,128]{1,0:T(8,128)(2,1)S(1)}, bf16[256,128]{1,0:T(8,128)(2,1)S(1)}, u32[]{:S(2)}, u32[]{:S(2)}) collective-permute-start(bf16[256,128]{1,0:T(8,128)(2,1)S(1)} %multiply_convert_fusion.4), channel_id=1, source_target_pairs={{0,8},{8,0},{16,24},{24,16},{1,9},{9,1},{17,25},{25,17},{2,10},{10... | collective-permute-start | bytes 196616 | tf_op jit(solution)/shard_map/ppermute | solution.py:77
  4.8 3.0 %collective-permute-start.2 = (bf16[1,256,128]{2,1,0:T(8,128)(2,1)}, bf16[1,256,128]{2,1,0:T(8,128)(2,1)S(1)}, u32[]{:S(2)}, u32[]{:S(2)}) collective-permute-start(bf16[1,256,128]{2,1,0:T(8,128)(2,1)} %bitcast.201), channel_id=1, source_target_pairs={{0,4},{1,5},{2,6},{3,7},{4,0},{5,1},{6,2},{7,3},{8,12},{9,13},{10,... | collective-permute-start | bytes 196616 | tf_op jit(solution)/shard_map/ppermute | solution.py:95
  7.9 11.5 %fusion.3 = f32[16,128,8,128]{3,2,1,0:T(8,128)} fusion(bf16[16,16,128,128]{3,2,1,0:T(8,128)(2,1)} %param.8, s32[16,16]{1,0:T(8,128)} %param.9), kind=kOutput, calls=%fused_computation.8 | convolution fusion | flops 67110912 | bytes 16778240 | tf_op jit(solution)/shard_map/rst,rsab->ratb/dot_general | solution.py:132
  19.4 9.3 %reshape_reshape.3 = f32[8,256,1024]{2,1,0:T(8,128)} reshape(f32[16,128,8,128]{3,2,1,0:T(8,128)} %fusion.3) | data formatting | bytes 16777216 | tf_op jit(solution)/shard_map/reshape;reshape | solution.py:140
  28.9 7.8 %gather_fusion = f32[8,256,1024]{2,1,0:T(8,128)} fusion(f32[8,256,1024]{2,1,0:T(8,128)} %reshape_reshape.3, s32[1024]{0:T(1024)S(1)} %pad_clamp_fusion.1), kind=kCustom, calls=%fused_computation | custom fusion | bytes 16777248 | tf_op jit(solution)/shard_map/jit(_take)/gather | solution.py:140
  36.7 5.7 %subtract_convert_fusion = bf16[2048,1024]{1,0:T(8,128)(2,1)} fusion(f32[8,256,1024]{2,1,0:T(8,128)} %gather_fusion, pred[2048]{0:T(1024)(128)(4,1)S(1)} %broadcast_in_dim.46), kind=kLoop, calls=%fused_computation.6 | loop fusion | flops 10485760 | bytes 12584960 | tf_op jit(solution)/shard_map/convert_element_type | solution.py:11
  42.4 1.6 copy-done
  44.1 2.9 %fusion.2 = bf16[2048,1024]{1,0:T(8,128)(2,1)} fusion(f32[8,256,1024]{2,1,0:T(8,128)S(1)} %copy-done, pred[2048]{0:T(1024)(128)(4,1)S(1)} %broadcast_in_dim.46), kind=kLoop, calls=%fused_computation.7 | loop fusion | flops 2097152 | bytes 12584960 | tf_op jit(solution)/shard_map/convert_element_type | solution.py:10
  47.1 1.6 collective-permute-start.1
  48.8 1.6 collective-permute-start.3
  51.0 2.8 %collective-permute-done.3 = bf16[2,256,128]{2,1,0:T(8,128)(2,1)S(1)} collective-permute-done((bf16[2,256,128]{2,1,0:T(8,128)(2,1)S(1)}, bf16[2,256,128]{2,1,0:T(8,128)(2,1)S(1)}, u32[]{:S(2)}, u32[]{:S(2)}) %collective-permute-start.3) | collective-permute-done | bytes 131104 | tf_op jit(solution)/shard_map/ppermute | solution.py:95
  54.0 2.3 fusion.34
  59.4 1.6 copy-done.1
  63.9 1.6 collective-permute-start.8
  65.6 7.0 %collective-permute-done.8 = f32[2,256,128]{2,1,0:T(8,128)S(1)} collective-permute-done((f32[2,256,128]{2,1,0:T(8,128)S(1)}, f32[2,256,128]{2,1,0:T(8,128)S(1)}, u32[]{:S(2)}, u32[]{:S(2)}) %collective-permute-start.8) | collective-permute-done | bytes 262176 | tf_op jit(solution)/shard_map/ppermute | solution.py:119
  76.2 5.1 %collective-permute-done.9 = f32[1,256,128]{2,1,0:T(8,128)S(1)} collective-permute-done((f32[1,256,128]{2,1,0:T(8,128)S(1)}, f32[1,256,128]{2,1,0:T(8,128)S(1)}, u32[]{:S(2)}, u32[]{:S(2)}) %collective-permute-start.9) | collective-permute-done | bytes 131104 | tf_op jit(solution)/shard_map/ppermute | solution.py:119
  81.4 1.6 collective-permute-start.10
  83.0 2.8 %collective-permute-done.10 = bf16[256,128]{1,0:T(8,128)(2,1)S(1)} collective-permute-done((bf16[256,128]{1,0:T(8,128)(2,1)S(1)}, bf16[256,128]{1,0:T(8,128)(2,1)S(1)}, u32[]{:S(2)}, u32[]{:S(2)}) %collective-permute-start.10) | collective-permute-done | bytes 65568 | tf_op jit(solution)/shard_map/ppermute | solution.py:77
  86.2 4.6 %collective-permute-done.11 = bf16[512,128]{1,0:T(8,128)(2,1)S(1)} collective-permute-done((bf16[512,128]{1,0:T(8,128)(2,1)S(1)}, bf16[512,128]{1,0:T(8,128)(2,1)S(1)}, u32[]{:S(2)}, u32[]{:S(2)}) %collective-permute-start.11) | collective-permute-done | bytes 131104 | tf_op jit(solution)/shard_map/ppermute | solution.py:77
  90.9 2.3 fusion.32
  97.1 1.0 collective-permute-done.12
  98.2 8.3 %collective-permute-done.13 = f32[2,256,128]{2,1,0:T(8,128)S(1)} collective-permute-done((f32[2,256,128]{2,1,0:T(8,128)S(1)}, f32[2,256,128]{2,1,0:T(8,128)S(1)}, u32[]{:S(2)}, u32[]{:S(2)}) %collective-permute-start.13) | collective-permute-done | bytes 262176 | tf_op jit(solution)/shard_map/ppermute | solution.py:119
  106.8 8.3 %collective-permute-done.14 = f32[1,256,128]{2,1,0:T(8,128)S(1)} collective-permute-done((f32[1,256,128]{2,1,0:T(8,128)S(1)}, f32[1,256,128]{2,1,0:T(8,128)S(1)}, u32[]{:S(2)}, u32[]{:S(2)}) %collective-permute-start.14) | collective-permute-done | bytes 131104 | tf_op jit(solution)/shard_map/ppermute | solution.py:119
  115.2 1.6 collective-permute-start.15
  116.8 2.8 %collective-permute-done.15 = bf16[256,128]{1,0:T(8,128)(2,1)S(1)} collective-permute-done((bf16[256,128]{1,0:T(8,128)(2,1)S(1)}, bf16[256,128]{1,0:T(8,128)(2,1)S(1)}, u32[]{:S(2)}, u32[]{:S(2)}) %collective-permute-start.15) | collective-permute-done | bytes 65568 | tf_op jit(solution)/shard_map/ppermute | solution.py:77
  120.0 4.7 %collective-permute-done.16 = bf16[512,128]{1,0:T(8,128)(2,1)S(1)} collective-permute-done((bf16[512,128]{1,0:T(8,128)(2,1)S(1)}, bf16[512,128]{1,0:T(8,128)(2,1)S(1)}, u32[]{:S(2)}, u32[]{:S(2)}) %collective-permute-start.16) | collective-permute-done | bytes 131104 | tf_op jit(solution)/shard_map/ppermute | solution.py:77
  128.8 1.0 collective-permute-done.17
  129.9 8.3 %collective-permute-done.18 = f32[2,256,128]{2,1,0:T(8,128)S(1)} collective-permute-done((f32[2,256,128]{2,1,0:T(8,128)S(1)}, f32[2,256,128]{2,1,0:T(8,128)S(1)}, u32[]{:S(2)}, u32[]{:S(2)}) %collective-permute-start.18) | collective-permute-done | bytes 262176 | tf_op jit(solution)/shard_map/ppermute | solution.py:119
  138.6 8.3 %collective-permute-done.19 = f32[1,256,128]{2,1,0:T(8,128)S(1)} collective-permute-done((f32[1,256,128]{2,1,0:T(8,128)S(1)}, f32[1,256,128]{2,1,0:T(8,128)S(1)}, u32[]{:S(2)}, u32[]{:S(2)}) %collective-permute-start.19) | collective-permute-done | bytes 131104 | tf_op jit(solution)/shard_map/ppermute | solution.py:119
  147.1 1.6 collective-permute-start.20
  148.6 2.8 %collective-permute-done.20 = bf16[256,128]{1,0:T(8,128)(2,1)S(1)} collective-permute-done((bf16[256,128]{1,0:T(8,128)(2,1)S(1)}, bf16[256,128]{1,0:T(8,128)(2,1)S(1)}, u32[]{:S(2)}, u32[]{:S(2)}) %collective-permute-start.20) | collective-permute-done | bytes 65568 | tf_op jit(solution)/shard_map/ppermute | solution.py:77
  151.8 4.6 %collective-permute-done.21 = bf16[512,128]{1,0:T(8,128)(2,1)S(1)} collective-permute-done((bf16[512,128]{1,0:T(8,128)(2,1)S(1)}, bf16[512,128]{1,0:T(8,128)(2,1)S(1)}, u32[]{:S(2)}, u32[]{:S(2)}) %collective-permute-start.21) | collective-permute-done | bytes 131104 | tf_op jit(solution)/shard_map/ppermute | solution.py:77
  161.8 8.3 %collective-permute-done.23 = f32[2,256,128]{2,1,0:T(8,128)S(1)} collective-permute-done((f32[2,256,128]{2,1,0:T(8,128)S(1)}, f32[2,256,128]{2,1,0:T(8,128)S(1)}, u32[]{:S(2)}, u32[]{:S(2)}) %collective-permute-start.23) | collective-permute-done | bytes 262176 | tf_op jit(solution)/shard_map/ppermute | solution.py:119
  170.3 8.3 %collective-permute-done.24 = f32[1,256,128]{2,1,0:T(8,128)S(1)} collective-permute-done((f32[1,256,128]{2,1,0:T(8,128)S(1)}, f32[1,256,128]{2,1,0:T(8,128)S(1)}, u32[]{:S(2)}, u32[]{:S(2)}) %collective-permute-start.24) | collective-permute-done | bytes 131104 | tf_op jit(solution)/shard_map/ppermute | solution.py:119
  178.7 1.6 collective-permute-start.25
  180.3 2.8 %collective-permute-done.25 = bf16[256,128]{1,0:T(8,128)(2,1)S(1)} collective-permute-done((bf16[256,128]{1,0:T(8,128)(2,1)S(1)}, bf16[256,128]{1,0:T(8,128)(2,1)S(1)}, u32[]{:S(2)}, u32[]{:S(2)}) %collective-permute-start.25) | collective-permute-done | bytes 65568 | tf_op jit(solution)/shard_map/ppermute | solution.py:77
  183.5 4.7 %collective-permute-done.26 = bf16[512,128]{1,0:T(8,128)(2,1)S(1)} collective-permute-done((bf16[512,128]{1,0:T(8,128)(2,1)S(1)}, bf16[512,128]{1,0:T(8,128)(2,1)S(1)}, u32[]{:S(2)}, u32[]{:S(2)}) %collective-permute-start.26) | collective-permute-done | bytes 131104 | tf_op jit(solution)/shard_map/ppermute | solution.py:77
  193.4 8.3 %collective-permute-done.28 = f32[2,256,128]{2,1,0:T(8,128)S(1)} collective-permute-done((f32[2,256,128]{2,1,0:T(8,128)S(1)}, f32[2,256,128]{2,1,0:T(8,128)S(1)}, u32[]{:S(2)}, u32[]{:S(2)}) %collective-permute-start.28) | collective-permute-done | bytes 262176 | tf_op jit(solution)/shard_map/ppermute | solution.py:119
  202.3 7.9 %collective-permute-done.29 = f32[1,256,128]{2,1,0:T(8,128)S(1)} collective-permute-done((f32[1,256,128]{2,1,0:T(8,128)S(1)}, f32[1,256,128]{2,1,0:T(8,128)S(1)}, u32[]{:S(2)}, u32[]{:S(2)}) %collective-permute-start.29) | collective-permute-done | bytes 131104 | tf_op jit(solution)/shard_map/ppermute | solution.py:119
  210.8 1.3 collective-permute-done.30
  212.3 5.5 %collective-permute-done.31 = f32[256,128]{0,1:T(8,128)S(1)} collective-permute-done((f32[256,128]{0,1:T(8,128)S(1)}, f32[256,128]{0,1:T(8,128)S(1)}, u32[]{:S(2)}, u32[]{:S(2)}) %collective-permute-start.31) | collective-permute-done | bytes 131104 | tf_op jit(solution)/shard_map/ppermute | solution.py:28
  217.9 8.3 %collective-permute-done.32 = f32[256,128]{0,1:T(8,128)S(1)} collective-permute-done((f32[256,128]{0,1:T(8,128)S(1)}, f32[256,128]{0,1:T(8,128)S(1)}, u32[]{:S(2)}, u32[]{:S(2)}) %collective-permute-start.32) | collective-permute-done | bytes 131104 | tf_op jit(solution)/shard_map/ppermute | solution.py:28
  226.3 1.6 collective-permute-start.33
  227.9 3.9 %collective-permute-done.33 = f32[256,128]{0,1:T(8,128)S(1)} collective-permute-done((f32[256,128]{0,1:T(8,128)S(1)}, f32[256,128]{0,1:T(8,128)S(1)}, u32[]{:S(2)}, u32[]{:S(2)}) %collective-permute-start.33) | collective-permute-done | bytes 131104 | tf_op jit(solution)/shard_map/ppermute | solution.py:28
  232.2 4.7 %collective-permute-done.34 = f32[256,128]{0,1:T(8,128)S(1)} collective-permute-done((f32[256,128]{0,1:T(8,128)S(1)}, f32[256,128]{0,1:T(8,128)S(1)}, u32[]{:S(2)}, u32[]{:S(2)}) %collective-permute-start.34) | collective-permute-done | bytes 131104 | tf_op jit(solution)/shard_map/ppermute | solution.py:28
  237.0 11.9 %cholesky.16 = f32[128,128]{1,0:T(8,128)S(1)} custom-call(f32[128,128]{1,0:T(8,128)S(1)} %fusion.80), custom_call_target="Cholesky" | custom-call | tf_op jit(solution)/shard_map/jit(cholesky)/cholesky | solution.py:187
  250.2 9.8 %custom-call.10 = f32[1,128,128]{1,2,0:T(8,128)S(1)} custom-call(f32[1,128,128]{2,1,0:T(8,128)S(1)} %fusion.73), custom_call_target="InvertDiagBlocksLowerTriangular" | custom-call | tf_op jit(solution)/shard_map/triangular_solve | solution.py:188
  (175 shorter events, 34.9 us)
Async XLA Ops:
  1.6 45.4 %collective-permute-start = (bf16[256,128]{1,0:T(8,128)(2,1)S(1)}, bf16[256,128]{1,0:T(8,128)(2,1)S(1)}, u32[]{:S(2)}, u32[]{:S(2)}) collective-permute-start(bf16[256,128]{1,0:T(8,128)(2,1)S(1)} %multiply_convert_fusion.4), channel_id=1, source_target_pairs={{0,8},{8,0},{16,24},{24,16},{1,9},{9,1},{17,25},{25,17},{2,10},{10... | collective-permute-start | bytes 196616 | tf_op jit(solution)/shard_map/ppermute | solution.py:77
  4.7 45.8 %collective-permute-start.5 = (bf16[256,128]{1,0:T(8,128)(2,1)}, bf16[256,128]{1,0:T(8,128)(2,1)S(1)}, u32[]{:S(2)}, u32[]{:S(2)}) collective-permute-start(bf16[256,128]{1,0:T(8,128)(2,1)} %param.12), channel_id=1, source_target_pairs={{0,8},{8,0},{16,24},{24,16},{1,9},{9,1},{17,25},{25,17},{2,10},{10... | collective-permute-start | bytes 196616 | tf_op jit(solution)/shard_map/ppermute | solution.py:77
  4.8 44.0 %collective-permute-start.2 = (bf16[1,256,128]{2,1,0:T(8,128)(2,1)}, bf16[1,256,128]{2,1,0:T(8,128)(2,1)S(1)}, u32[]{:S(2)}, u32[]{:S(2)}) collective-permute-start(bf16[1,256,128]{2,1,0:T(8,128)(2,1)} %bitcast.201), channel_id=1, source_target_pairs={{0,4},{1,5},{2,6},{3,7},{4,0},{5,1},{6,2},{7,3},{8,12},{9,13},{10,... | collective-permute-start | bytes 196616 | tf_op jit(solution)/shard_map/ppermute | solution.py:95
  36.7 7.3 %copy-start = (f32[8,256,1024]{2,1,0:T(8,128)S(1)}, f32[8,256,1024]{2,1,0:T(8,128)}, u32[]{:S(2)}) copy-start(f32[8,256,1024]{2,1,0:T(8,128)} %gather_fusion) | copy-start | bytes 25165828
  44.1 2.9 %copy-start.9 = (s32[8]{0:T(128)S(1)}, s32[8]{0:T(128)}, u32[]{:S(2)}) copy-start(s32[8]{0:T(128)} %constant.320) | copy-start | bytes 100
  44.1 2.9 %copy-start.5 = (f32[256,128]{1,0:T(8,128)S(1)}, f32[256,128]{1,0:T(8,128)}, u32[]{:S(2)}) copy-start(f32[256,128]{1,0:T(8,128)} %param.11) | copy-start | bytes 393220
  44.1 2.9 %copy-start.7 = (f32[256]{0:T(256)S(1)}, f32[256]{0:T(256)}, u32[]{:S(2)}) copy-start(f32[256]{0:T(256)} %param.10) | copy-start | bytes 3076
  44.1 4.7 %copy-start.6 = (bf16[256,128]{1,0:T(8,128)(2,1)S(1)}, bf16[256,128]{1,0:T(8,128)(2,1)}, u32[]{:S(2)}) copy-start(bf16[256,128]{1,0:T(8,128)(2,1)} %param.12) | copy-start | bytes 196612
  47.0 9.4 %copy-start.10 = (f32[128]{0:T(128)S(1)}, f32[128]{0:T(128)}, u32[]{:S(2)}) copy-start(f32[128]{0:T(128)} %param.13) | copy-start | bytes 1540
  47.0 9.7 %copy-start.3 = (bf16[2048,1024]{1,0:T(8,128)(2,1)S(1)}, bf16[2048,1024]{1,0:T(8,128)(2,1)}, u32[]{:S(2)}) copy-start(bf16[2048,1024]{1,0:T(8,128)(2,1)} %subtract_convert_fusion) | copy-start | bytes 12582916
  47.1 6.8 %collective-permute-start.1 = (bf16[512,128]{1,0:T(8,128)(2,1)S(1)}, bf16[512,128]{1,0:T(8,128)(2,1)S(1)}, u32[]{:S(2)}, u32[]{:S(2)}) collective-permute-start(bf16[512,128]{1,0:T(8,128)(2,1)S(1)} %pad_maximum_fusion.8), channel_id=1, source_target_pairs={{0,16},{8,24},{16,0},{24,8},{1,17},{9,25},{17,1},{25,9},{2,18},{10... | collective-permute-start | bytes 393224 | tf_op jit(solution)/shard_map/ppermute | solution.py:77
  48.8 5.0 %collective-permute-start.3 = (bf16[2,256,128]{2,1,0:T(8,128)(2,1)S(1)}, bf16[2,256,128]{2,1,0:T(8,128)(2,1)S(1)}, u32[]{:S(2)}, u32[]{:S(2)}) collective-permute-start(bf16[2,256,128]{2,1,0:T(8,128)(2,1)S(1)} %pad_maximum_fusion.9), channel_id=1, source_target_pairs={{0,2},{1,3},{2,0},{3,1},{4,6},{5,7},{6,4},{7,5},{8,10},{9,11},{10,... | collective-permute-start | bytes 393224 | tf_op jit(solution)/shard_map/ppermute | solution.py:95
  50.5 5.9 %collective-permute-start.6 = (bf16[512,128]{1,0:T(8,128)(2,1)S(1)}, bf16[512,128]{1,0:T(8,128)(2,1)S(1)}, u32[]{:S(2)}, u32[]{:S(2)}) collective-permute-start(bf16[512,128]{1,0:T(8,128)(2,1)S(1)} %pad_maximum_fusion.10), channel_id=1, source_target_pairs={{0,16},{8,24},{16,0},{24,8},{1,17},{9,25},{17,1},{25,9},{2,18},{10... | collective-permute-start | bytes 393224 | tf_op jit(solution)/shard_map/ppermute | solution.py:77
  53.9 3.5 %collective-permute-start.4 = (bf16[4,256,128]{2,1,0:T(8,128)(2,1)S(1)}, bf16[4,256,128]{2,1,0:T(8,128)(2,1)S(1)}, u32[]{:S(2)}, u32[]{:S(2)}) collective-permute-start(bf16[4,256,128]{2,1,0:T(8,128)(2,1)S(1)} %pad_maximum_fusion.2), channel_id=1, source_target_pairs={{0,1},{1,0},{2,3},{3,2},{4,5},{5,4},{6,7},{7,6},{8,9},{9,8},{10,11... | collective-permute-start | bytes 786440 | tf_op jit(solution)/shard_map/ppermute | solution.py:95
  58.8 2.2 copy-start.1
  61.7 2.1 collective-permute-start.7
  62.5 10.5 %copy-start.8 = (f32[2]{0:T(128)S(1)}, f32[2]{0:T(128)}, u32[]{:S(2)}) copy-start(f32[2]{0:T(128)} %param.14) | copy-start | bytes 28
  63.9 8.7 %collective-permute-start.8 = (f32[2,256,128]{2,1,0:T(8,128)S(1)}, f32[2,256,128]{2,1,0:T(8,128)S(1)}, u32[]{:S(2)}, u32[]{:S(2)}) collective-permute-start(f32[2,256,128]{2,1,0:T(8,128)S(1)} %dynamic-slice_bitcast_fusion.4), channel_id=1, source_target_pairs={{0,2},{1,3},{2,0},{3,1},{4,6},{5,7},{6,4},{7,5},{8,10},{9,11},{10,... | collective-permute-start | bytes 786440 | tf_op jit(solution)/shard_map/ppermute | solution.py:119
  72.6 8.7 %collective-permute-start.9 = (f32[1,256,128]{2,1,0:T(8,128)S(1)}, f32[1,256,128]{2,1,0:T(8,128)S(1)}, u32[]{:S(2)}, u32[]{:S(2)}) collective-permute-start(f32[1,256,128]{2,1,0:T(8,128)S(1)} %constant_dynamic-slice_fusion.4), channel_id=1, source_target_pairs={{0,4},{1,5},{2,6},{3,7},{4,0},{5,1},{6,2},{7,3},{8,12},{9,13},{10,... | collective-permute-start | bytes 393224 | tf_op jit(solution)/shard_map/ppermute | solution.py:119
  76.2 17.3 %copy-start.4 = (bf16[2048,1024]{1,0:T(8,128)(2,1)S(1)}, bf16[2048,1024]{1,0:T(8,128)(2,1)}, u32[]{:S(2)}) copy-start(bf16[2048,1024]{1,0:T(8,128)(2,1)} %subtract_convert_fusion) | copy-start | bytes 12582916
  81.4 4.3 %collective-permute-start.10 = (bf16[256,128]{1,0:T(8,128)(2,1)S(1)}, bf16[256,128]{1,0:T(8,128)(2,1)S(1)}, u32[]{:S(2)}, u32[]{:S(2)}) collective-permute-start(bf16[256,128]{1,0:T(8,128)(2,1)S(1)} %get-tuple-element.8), channel_id=1, source_target_pairs={{0,8},{8,0},{16,24},{24,16},{1,9},{9,1},{17,25},{25,17},{2,10},{10... | collective-permute-start | bytes 196616 | tf_op jit(solution)/shard_map/ppermute | solution.py:77
  85.8 5.0 %collective-permute-start.11 = (bf16[512,128]{1,0:T(8,128)(2,1)S(1)}, bf16[512,128]{1,0:T(8,128)(2,1)S(1)}, u32[]{:S(2)}, u32[]{:S(2)}) collective-permute-start(bf16[512,128]{1,0:T(8,128)(2,1)S(1)} %pad_maximum_fusion.11), channel_id=1, source_target_pairs={{0,16},{8,24},{16,0},{24,8},{1,17},{9,25},{17,1},{25,9},{2,18},{10... | collective-permute-start | bytes 393224 | tf_op jit(solution)/shard_map/ppermute | solution.py:77
  93.2 2.2 copy-start.2
  96.1 2.0 collective-permute-start.12
  98.2 8.4 %collective-permute-start.13 = (f32[2,256,128]{2,1,0:T(8,128)S(1)}, f32[2,256,128]{2,1,0:T(8,128)S(1)}, u32[]{:S(2)}, u32[]{:S(2)}) collective-permute-start(f32[2,256,128]{2,1,0:T(8,128)S(1)} %dynamic-slice_bitcast_fusion.3), channel_id=1, source_target_pairs={{0,2},{1,3},{2,0},{3,1},{4,6},{5,7},{6,4},{7,5},{8,10},{9,11},{10,... | collective-permute-start | bytes 786440 | tf_op jit(solution)/shard_map/ppermute | solution.py:119
  106.6 8.5 %collective-permute-start.14 = (f32[1,256,128]{2,1,0:T(8,128)S(1)}, f32[1,256,128]{2,1,0:T(8,128)S(1)}, u32[]{:S(2)}, u32[]{:S(2)}) collective-permute-start(f32[1,256,128]{2,1,0:T(8,128)S(1)} %constant_dynamic-slice_fusion.3), channel_id=1, source_target_pairs={{0,4},{1,5},{2,6},{3,7},{4,0},{5,1},{6,2},{7,3},{8,12},{9,13},{10,... | collective-permute-start | bytes 393224 | tf_op jit(solution)/shard_map/ppermute | solution.py:119
  115.2 4.3 %collective-permute-start.15 = (bf16[256,128]{1,0:T(8,128)(2,1)S(1)}, bf16[256,128]{1,0:T(8,128)(2,1)S(1)}, u32[]{:S(2)}, u32[]{:S(2)}) collective-permute-start(bf16[256,128]{1,0:T(8,128)(2,1)S(1)} %get-tuple-element.6), channel_id=1, source_target_pairs={{0,8},{8,0},{16,24},{24,16},{1,9},{9,1},{17,25},{25,17},{2,10},{10... | collective-permute-start | bytes 196616 | tf_op jit(solution)/shard_map/ppermute | solution.py:77
  119.6 5.0 %collective-permute-start.16 = (bf16[512,128]{1,0:T(8,128)(2,1)S(1)}, bf16[512,128]{1,0:T(8,128)(2,1)S(1)}, u32[]{:S(2)}, u32[]{:S(2)}) collective-permute-start(bf16[512,128]{1,0:T(8,128)(2,1)S(1)} %pad_maximum_fusion.12), channel_id=1, source_target_pairs={{0,16},{8,24},{16,0},{24,8},{1,17},{9,25},{17,1},{25,9},{2,18},{10... | collective-permute-start | bytes 393224 | tf_op jit(solution)/shard_map/ppermute | solution.py:77
  127.7 2.0 collective-permute-start.17
  129.8 8.4 %collective-permute-start.18 = (f32[2,256,128]{2,1,0:T(8,128)S(1)}, f32[2,256,128]{2,1,0:T(8,128)S(1)}, u32[]{:S(2)}, u32[]{:S(2)}) collective-permute-start(f32[2,256,128]{2,1,0:T(8,128)S(1)} %dynamic-slice_bitcast_fusion.2), channel_id=1, source_target_pairs={{0,2},{1,3},{2,0},{3,1},{4,6},{5,7},{6,4},{7,5},{8,10},{9,11},{10,... | collective-permute-start | bytes 786440 | tf_op jit(solution)/shard_map/ppermute | solution.py:119
  138.3 8.7 %collective-permute-start.19 = (f32[1,256,128]{2,1,0:T(8,128)S(1)}, f32[1,256,128]{2,1,0:T(8,128)S(1)}, u32[]{:S(2)}, u32[]{:S(2)}) collective-permute-start(f32[1,256,128]{2,1,0:T(8,128)S(1)} %constant_dynamic-slice_fusion.2), channel_id=1, source_target_pairs={{0,4},{1,5},{2,6},{3,7},{4,0},{5,1},{6,2},{7,3},{8,12},{9,13},{10,... | collective-permute-start | bytes 393224 | tf_op jit(solution)/shard_map/ppermute | solution.py:119
  147.1 4.3 %collective-permute-start.20 = (bf16[256,128]{1,0:T(8,128)(2,1)S(1)}, bf16[256,128]{1,0:T(8,128)(2,1)S(1)}, u32[]{:S(2)}, u32[]{:S(2)}) collective-permute-start(bf16[256,128]{1,0:T(8,128)(2,1)S(1)} %get-tuple-element.4), channel_id=1, source_target_pairs={{0,8},{8,0},{16,24},{24,16},{1,9},{9,1},{17,25},{25,17},{2,10},{10... | collective-permute-start | bytes 196616 | tf_op jit(solution)/shard_map/ppermute | solution.py:77
  151.4 5.0 %collective-permute-start.21 = (bf16[512,128]{1,0:T(8,128)(2,1)S(1)}, bf16[512,128]{1,0:T(8,128)(2,1)S(1)}, u32[]{:S(2)}, u32[]{:S(2)}) collective-permute-start(bf16[512,128]{1,0:T(8,128)(2,1)S(1)} %pad_maximum_fusion.13), channel_id=1, source_target_pairs={{0,16},{8,24},{16,0},{24,8},{1,17},{9,25},{17,1},{25,9},{2,18},{10... | collective-permute-start | bytes 393224 | tf_op jit(solution)/shard_map/ppermute | solution.py:77
  159.6 2.0 collective-permute-start.22
  161.7 8.4 %collective-permute-start.23 = (f32[2,256,128]{2,1,0:T(8,128)S(1)}, f32[2,256,128]{2,1,0:T(8,128)S(1)}, u32[]{:S(2)}, u32[]{:S(2)}) collective-permute-start(f32[2,256,128]{2,1,0:T(8,128)S(1)} %dynamic-slice_bitcast_fusion.1), channel_id=1, source_target_pairs={{0,2},{1,3},{2,0},{3,1},{4,6},{5,7},{6,4},{7,5},{8,10},{9,11},{10,... | collective-permute-start | bytes 786440 | tf_op jit(solution)/shard_map/ppermute | solution.py:119
  170.2 8.5 %collective-permute-start.24 = (f32[1,256,128]{2,1,0:T(8,128)S(1)}, f32[1,256,128]{2,1,0:T(8,128)S(1)}, u32[]{:S(2)}, u32[]{:S(2)}) collective-permute-start(f32[1,256,128]{2,1,0:T(8,128)S(1)} %constant_dynamic-slice_fusion.1), channel_id=1, source_target_pairs={{0,4},{1,5},{2,6},{3,7},{4,0},{5,1},{6,2},{7,3},{8,12},{9,13},{10,... | collective-permute-start | bytes 393224 | tf_op jit(solution)/shard_map/ppermute | solution.py:119
  178.7 4.3 %collective-permute-start.25 = (bf16[256,128]{1,0:T(8,128)(2,1)S(1)}, bf16[256,128]{1,0:T(8,128)(2,1)S(1)}, u32[]{:S(2)}, u32[]{:S(2)}) collective-permute-start(bf16[256,128]{1,0:T(8,128)(2,1)S(1)} %get-tuple-element.2), channel_id=1, source_target_pairs={{0,8},{8,0},{16,24},{24,16},{1,9},{9,1},{17,25},{25,17},{2,10},{10... | collective-permute-start | bytes 196616 | tf_op jit(solution)/shard_map/ppermute | solution.py:77
  183.1 5.0 %collective-permute-start.26 = (bf16[512,128]{1,0:T(8,128)(2,1)S(1)}, bf16[512,128]{1,0:T(8,128)(2,1)S(1)}, u32[]{:S(2)}, u32[]{:S(2)}) collective-permute-start(bf16[512,128]{1,0:T(8,128)(2,1)S(1)} %pad_maximum_fusion.14), channel_id=1, source_target_pairs={{0,16},{8,24},{16,0},{24,8},{1,17},{9,25},{17,1},{25,9},{2,18},{10... | collective-permute-start | bytes 393224 | tf_op jit(solution)/shard_map/ppermute | solution.py:77
  191.3 2.0 collective-permute-start.27
  193.3 8.4 %collective-permute-start.28 = (f32[2,256,128]{2,1,0:T(8,128)S(1)}, f32[2,256,128]{2,1,0:T(8,128)S(1)}, u32[]{:S(2)}, u32[]{:S(2)}) collective-permute-start(f32[2,256,128]{2,1,0:T(8,128)S(1)} %dynamic-slice_bitcast_fusion), channel_id=1, source_target_pairs={{0,2},{1,3},{2,0},{3,1},{4,6},{5,7},{6,4},{7,5},{8,10},{9,11},{10,... | collective-permute-start | bytes 786440 | tf_op jit(solution)/shard_map/ppermute | solution.py:119
  201.8 8.5 %collective-permute-start.29 = (f32[1,256,128]{2,1,0:T(8,128)S(1)}, f32[1,256,128]{2,1,0:T(8,128)S(1)}, u32[]{:S(2)}, u32[]{:S(2)}) collective-permute-start(f32[1,256,128]{2,1,0:T(8,128)S(1)} %constant_dynamic-slice_fusion), channel_id=1, source_target_pairs={{0,4},{1,5},{2,6},{3,7},{4,0},{5,1},{6,2},{7,3},{8,12},{9,13},{10,... | collective-permute-start | bytes 393224 | tf_op jit(solution)/shard_map/ppermute | solution.py:119
  210.7 1.4 collective-permute-start.30
  212.2 5.6 %collective-permute-start.31 = (f32[256,128]{0,1:T(8,128)S(1)}, f32[256,128]{0,1:T(8,128)S(1)}, u32[]{:S(2)}, u32[]{:S(2)}) collective-permute-start(f32[256,128]{0,1:T(8,128)S(1)} %fusion.112), channel_id=1, source_target_pairs={{0,2},{1,3},{2,0},{3,1},{4,6},{5,7},{6,4},{7,5},{8,10},{9,11},{10,... | collective-permute-start | bytes 393224 | tf_op jit(solution)/shard_map/ppermute | solution.py:28
  217.8 8.5 %collective-permute-start.32 = (f32[256,128]{0,1:T(8,128)S(1)}, f32[256,128]{0,1:T(8,128)S(1)}, u32[]{:S(2)}, u32[]{:S(2)}) collective-permute-start(f32[256,128]{0,1:T(8,128)S(1)} %add.358), channel_id=1, source_target_pairs={{0,4},{1,5},{2,6},{3,7},{4,0},{5,1},{6,2},{7,3},{8,12},{9,13},{10,... | collective-permute-start | bytes 393224 | tf_op jit(solution)/shard_map/ppermute | solution.py:28
  226.3 5.5 %collective-permute-start.33 = (f32[256,128]{0,1:T(8,128)S(1)}, f32[256,128]{0,1:T(8,128)S(1)}, u32[]{:S(2)}, u32[]{:S(2)}) collective-permute-start(f32[256,128]{0,1:T(8,128)S(1)} %add.359), channel_id=1, source_target_pairs={{0,8},{8,0},{16,24},{24,16},{1,9},{9,1},{17,25},{25,17},{2,10},{10... | collective-permute-start | bytes 393224 | tf_op jit(solution)/shard_map/ppermute | solution.py:28
  231.8 5.0 %collective-permute-start.34 = (f32[256,128]{0,1:T(8,128)S(1)}, f32[256,128]{0,1:T(8,128)S(1)}, u32[]{:S(2)}, u32[]{:S(2)}) collective-permute-start(f32[256,128]{0,1:T(8,128)S(1)} %add.360), channel_id=1, source_target_pairs={{0,16},{8,24},{16,0},{24,8},{1,17},{9,25},{17,1},{25,9},{2,18},{10... | collective-permute-start | bytes 393224 | tf_op jit(solution)/shard_map/ppermute | solution.py:28

commit v11 on v6

--- a/solution.py
+++ b/solution.py
@@ -99,8 +99,9 @@
         )
         step //= 2
     bits = size.bit_length() - 1
-    order = [int(format(index, f"0{bits}b")[::-1], 2) if bits else 0 for index in range(size)]
-    return result[jnp.array(order)].reshape(-1, value.shape[1])
+    result = result.reshape((2,) * bits + value.shape)
+    result = jnp.transpose(result, tuple(reversed(range(bits))) + (bits, bits + 1))
+    return result.reshape(-1, value.shape[1])
 
 
 def local(tiles, tile_cols, degree_scale, start_block, planted, strengths, bounds):

time: 240 us -> 239 us (level)
  no operation moved by 1% of the time
where the time goes in v11:
time: 239 us
  waiting for transfers between devices  144 us (60%)
  matrix products  32.4 us (14%)
  other arithmetic  31 us (13%)
  starting transfers between devices  23.8 us (10%)
  between operations  4.01 us (2%)
  local copies, waits for them, and re-layouts  3.68 us (2%)
    ppermute x15, waiting for transfers between devices, halving_scatter_sum(): blocks = kept + lax.ppermute(sent, axis, pairs)  87.5 us
    ppermute x12, waiting for transfers between devices, doubling_gather(): other = lax.ppermute(result, axis, pairs)  29.6 us
    ppermute x5, waiting for transfers between devices, butterfly_sum(): value = value + lax.ppermute(value, axis, pairs)  23.8 us
    ppermute x12, starting transfers between devices, doubling_gather(): other = lax.ppermute(result, axis, pairs)  13.1 us
    another operation x3, other arithmetic, local(): factor = jnp.linalg.cholesky(gram_matrix)  12.4 us
    dot_general x5, matrix products, operate(): jnp.dot(w_lo, gathered, preferred_element_type=jnp.float32)  10.9 us
    another operation x2, other arithmetic, local(): lax.linalg.triangular_solve(factor, current, left_side=False, lower=True,...  10.6 us
    dot_general x1, matrix products, local(): jnp.einsum('rst,rsab->ratb', onehot, tiles, preferred_element_type=jnp.fl...  8.2 us
  transfers between devices with their start and end apart: 35, of which 29 were waited for; matrix products, arithmetic and copies ran while one was open for 8% of the time, Pallas kernels for 0%

profile of v11, /device:TPU:0, one launch (start us, length us, event | category | flops | bytes accessed | tf_op | source)
XLA Modules:
  0.0 238.6 jit_solution(16634917071064995736)
XLA Ops:
  1.6 3.0 %collective-permute-start = (bf16[256,128]{1,0:T(8,128)(2,1)S(1)}, bf16[256,128]{1,0:T(8,128)(2,1)S(1)}, u32[]{:S(2)}, u32[]{:S(2)}) collective-permute-start(bf16[256,128]{1,0:T(8,128)(2,1)S(1)} %multiply_convert_fusion.4), channel_id=1, source_target_pairs={{0,8},{8,0},{16,24},{24,16},{1,9},{9,1},{17,25},{25,17},{2,10},{10... | collective-permute-start | bytes 196616 | tf_op jit(solution)/shard_map/ppermute | solution.py:77
  4.8 3.0 %collective-permute-start.2 = (bf16[1,256,128]{2,1,0:T(8,128)(2,1)}, bf16[1,256,128]{2,1,0:T(8,128)(2,1)S(1)}, u32[]{:S(2)}, u32[]{:S(2)}) collective-permute-start(bf16[1,256,128]{2,1,0:T(8,128)(2,1)} %bitcast.186), channel_id=1, source_target_pairs={{0,4},{1,5},{2,6},{3,7},{4,0},{5,1},{6,2},{7,3},{8,12},{9,13},{10,... | collective-permute-start | bytes 196616 | tf_op jit(solution)/shard_map/ppermute | solution.py:95
  7.8 8.2 %fusion.1 = f32[16,8,128,128]{3,1,2,0:T(8,128)S(1)} fusion(bf16[16,16,128,128]{3,2,1,0:T(8,128)(2,1)} %param.7, s32[16,16]{1,0:T(8,128)} %param.8), kind=kOutput, calls=%fused_computation.3 | convolution fusion | flops 67110912 | bytes 16778240 | tf_op jit(solution)/shard_map/rst,rsab->ratb/dot_general | solution.py:115
  16.0 5.3 %fusion = (bf16[2048,1024]{1,0:T(8,128)(2,1)}, bf16[2048,1024]{1,0:T(8,128)(2,1)}) fusion(f32[256,8,8,128]{3,2,1,0:T(8,128)S(1)} %bitcast.164), kind=kLoop, calls=%fused_computation.2 | loop fusion | flops 6291456 | bytes 16777216 | tf_op jit(solution)/shard_map/convert_element_type | solution.py:11
  21.4 1.6 collective-permute-start.1
  23.1 1.6 collective-permute-start.3
  25.3 2.8 %collective-permute-done.3 = bf16[2,256,128]{2,1,0:T(8,128)(2,1)S(1)} collective-permute-done((bf16[2,256,128]{2,1,0:T(8,128)(2,1)S(1)}, bf16[2,256,128]{2,1,0:T(8,128)(2,1)S(1)}, u32[]{:S(2)}, u32[]{:S(2)}) %collective-permute-start.3) | collective-permute-done | bytes 131104 | tf_op jit(solution)/shard_map/ppermute | solution.py:95
  28.3 3.5 %fusion.34 = f32[2048,128]{1,0:T(8,128)S(1)} fusion(bf16[2048,1024]{1,0:T(8,128)(2,1)} %get-tuple-element.10, bf16[512,128]{1,0:T(8,128)(2,1)S(1)} %get-tuple-element.25, bf16[512,128]{1,0:T(8,128)(2,1)S(1)} %get-tuple-element.24), kind=kOutput, calls=%fused_computation.113 | convolution fusion | flops 537395200 | bytes 5505024 | tf_op jit(solution)/shard_map/dot_general | solution.py:126
  34.0 1.3 fusion.12
  35.9 1.5 collective-permute-done.7
  37.6 1.6 collective-permute-start.8
  39.2 7.0 %collective-permute-done.8 = f32[2,256,128]{2,1,0:T(8,128)S(1)} collective-permute-done((f32[2,256,128]{2,1,0:T(8,128)S(1)}, f32[2,256,128]{2,1,0:T(8,128)S(1)}, u32[]{:S(2)}, u32[]{:S(2)}) %collective-permute-start.8) | collective-permute-done | bytes 262176 | tf_op jit(solution)/shard_map/ppermute | solution.py:63
  49.9 5.1 %collective-permute-done.9 = f32[1,256,128]{2,1,0:T(8,128)S(1)} collective-permute-done((f32[1,256,128]{2,1,0:T(8,128)S(1)}, f32[1,256,128]{2,1,0:T(8,128)S(1)}, u32[]{:S(2)}, u32[]{:S(2)}) %collective-permute-start.9) | collective-permute-done | bytes 131104 | tf_op jit(solution)/shard_map/ppermute | solution.py:63
  55.1 1.6 collective-permute-start.10
  56.7 2.8 %collective-permute-done.10 = bf16[256,128]{1,0:T(8,128)(2,1)S(1)} collective-permute-done((bf16[256,128]{1,0:T(8,128)(2,1)S(1)}, bf16[256,128]{1,0:T(8,128)(2,1)S(1)}, u32[]{:S(2)}, u32[]{:S(2)}) %collective-permute-start.10) | collective-permute-done | bytes 65568 | tf_op jit(solution)/shard_map/ppermute | solution.py:77
  59.8 4.7 %collective-permute-done.11 = bf16[512,128]{1,0:T(8,128)(2,1)S(1)} collective-permute-done((bf16[512,128]{1,0:T(8,128)(2,1)S(1)}, bf16[512,128]{1,0:T(8,128)(2,1)S(1)}, u32[]{:S(2)}, u32[]{:S(2)}) %collective-permute-start.11) | collective-permute-done | bytes 131104 | tf_op jit(solution)/shard_map/ppermute | solution.py:77
  64.5 3.4 %fusion.33 = f32[2048,128]{1,0:T(8,128)S(1)} fusion(bf16[2048,1024]{1,0:T(8,128)(2,1)} %get-tuple-element.10, bf16[512,128]{1,0:T(8,128)(2,1)S(1)} %get-tuple-element.21, bf16[512,128]{1,0:T(8,128)(2,1)S(1)} %get-tuple-element.20), kind=kOutput, calls=%fused_computation.112 | convolution fusion | flops 537395200 | bytes 5505024 | tf_op jit(solution)/shard_map/dot_general | solution.py:126
  68.9 1.3 copy-done.1
  71.6 1.9 collective-permute-done.12
  73.7 8.3 %collective-permute-done.13 = f32[2,256,128]{2,1,0:T(8,128)S(1)} collective-permute-done((f32[2,256,128]{2,1,0:T(8,128)S(1)}, f32[2,256,128]{2,1,0:T(8,128)S(1)}, u32[]{:S(2)}, u32[]{:S(2)}) %collective-permute-start.13) | collective-permute-done | bytes 262176 | tf_op jit(solution)/shard_map/ppermute | solution.py:63
  82.2 8.3 %collective-permute-done.14 = f32[1,256,128]{2,1,0:T(8,128)S(1)} collective-permute-done((f32[1,256,128]{2,1,0:T(8,128)S(1)}, f32[1,256,128]{2,1,0:T(8,128)S(1)}, u32[]{:S(2)}, u32[]{:S(2)}) %collective-permute-start.14) | collective-permute-done | bytes 131104 | tf_op jit(solution)/shard_map/ppermute | solution.py:63
  90.6 1.6 collective-permute-start.15
  92.2 2.8 %collective-permute-done.15 = bf16[256,128]{1,0:T(8,128)(2,1)S(1)} collective-permute-done((bf16[256,128]{1,0:T(8,128)(2,1)S(1)}, bf16[256,128]{1,0:T(8,128)(2,1)S(1)}, u32[]{:S(2)}, u32[]{:S(2)}) %collective-permute-start.15) | collective-permute-done | bytes 65568 | tf_op jit(solution)/shard_map/ppermute | solution.py:77
  95.4 4.7 %collective-permute-done.16 = bf16[512,128]{1,0:T(8,128)(2,1)S(1)} collective-permute-done((bf16[512,128]{1,0:T(8,128)(2,1)S(1)}, bf16[512,128]{1,0:T(8,128)(2,1)S(1)}, u32[]{:S(2)}, u32[]{:S(2)}) %collective-permute-start.16) | collective-permute-done | bytes 131104 | tf_op jit(solution)/shard_map/ppermute | solution.py:77
  103.6 1.9 collective-permute-done.17
  105.7 8.3 %collective-permute-done.18 = f32[2,256,128]{2,1,0:T(8,128)S(1)} collective-permute-done((f32[2,256,128]{2,1,0:T(8,128)S(1)}, f32[2,256,128]{2,1,0:T(8,128)S(1)}, u32[]{:S(2)}, u32[]{:S(2)}) %collective-permute-start.18) | collective-permute-done | bytes 262176 | tf_op jit(solution)/shard_map/ppermute | solution.py:63
  114.2 8.3 %collective-permute-done.19 = f32[1,256,128]{2,1,0:T(8,128)S(1)} collective-permute-done((f32[1,256,128]{2,1,0:T(8,128)S(1)}, f32[1,256,128]{2,1,0:T(8,128)S(1)}, u32[]{:S(2)}, u32[]{:S(2)}) %collective-permute-start.19) | collective-permute-done | bytes 131104 | tf_op jit(solution)/shard_map/ppermute | solution.py:63
  122.7 1.6 collective-permute-start.20
  124.2 2.8 %collective-permute-done.20 = bf16[256,128]{1,0:T(8,128)(2,1)S(1)} collective-permute-done((bf16[256,128]{1,0:T(8,128)(2,1)S(1)}, bf16[256,128]{1,0:T(8,128)(2,1)S(1)}, u32[]{:S(2)}, u32[]{:S(2)}) %collective-permute-start.20) | collective-permute-done | bytes 65568 | tf_op jit(solution)/shard_map/ppermute | solution.py:77
  127.4 4.7 %collective-permute-done.21 = bf16[512,128]{1,0:T(8,128)(2,1)S(1)} collective-permute-done((bf16[512,128]{1,0:T(8,128)(2,1)S(1)}, bf16[512,128]{1,0:T(8,128)(2,1)S(1)}, u32[]{:S(2)}, u32[]{:S(2)}) %collective-permute-start.21) | collective-permute-done | bytes 131104 | tf_op jit(solution)/shard_map/ppermute | solution.py:77
  132.1 1.5 fusion.31
  135.9 1.9 collective-permute-done.22
  137.9 8.3 %collective-permute-done.23 = f32[2,256,128]{2,1,0:T(8,128)S(1)} collective-permute-done((f32[2,256,128]{2,1,0:T(8,128)S(1)}, f32[2,256,128]{2,1,0:T(8,128)S(1)}, u32[]{:S(2)}, u32[]{:S(2)}) %collective-permute-start.23) | collective-permute-done | bytes 262176 | tf_op jit(solution)/shard_map/ppermute | solution.py:63
  146.5 8.3 %collective-permute-done.24 = f32[1,256,128]{2,1,0:T(8,128)S(1)} collective-permute-done((f32[1,256,128]{2,1,0:T(8,128)S(1)}, f32[1,256,128]{2,1,0:T(8,128)S(1)}, u32[]{:S(2)}, u32[]{:S(2)}) %collective-permute-start.24) | collective-permute-done | bytes 131104 | tf_op jit(solution)/shard_map/ppermute | solution.py:63
  154.9 1.6 collective-permute-start.25
  156.5 2.8 %collective-permute-done.25 = bf16[256,128]{1,0:T(8,128)(2,1)S(1)} collective-permute-done((bf16[256,128]{1,0:T(8,128)(2,1)S(1)}, bf16[256,128]{1,0:T(8,128)(2,1)S(1)}, u32[]{:S(2)}, u32[]{:S(2)}) %collective-permute-start.25) | collective-permute-done | bytes 65568 | tf_op jit(solution)/shard_map/ppermute | solution.py:77
  159.6 4.7 %collective-permute-done.26 = bf16[512,128]{1,0:T(8,128)(2,1)S(1)} collective-permute-done((bf16[512,128]{1,0:T(8,128)(2,1)S(1)}, bf16[512,128]{1,0:T(8,128)(2,1)S(1)}, u32[]{:S(2)}, u32[]{:S(2)}) %collective-permute-start.26) | collective-permute-done | bytes 131104 | tf_op jit(solution)/shard_map/ppermute | solution.py:77
  167.9 1.9 collective-permute-done.27
  169.9 8.3 %collective-permute-done.28 = f32[2,256,128]{2,1,0:T(8,128)S(1)} collective-permute-done((f32[2,256,128]{2,1,0:T(8,128)S(1)}, f32[2,256,128]{2,1,0:T(8,128)S(1)}, u32[]{:S(2)}, u32[]{:S(2)}) %collective-permute-start.28) | collective-permute-done | bytes 262176 | tf_op jit(solution)/shard_map/ppermute | solution.py:63
  178.8 7.9 %collective-permute-done.29 = f32[1,256,128]{2,1,0:T(8,128)S(1)} collective-permute-done((f32[1,256,128]{2,1,0:T(8,128)S(1)}, f32[1,256,128]{2,1,0:T(8,128)S(1)}, u32[]{:S(2)}, u32[]{:S(2)}) %collective-permute-start.29) | collective-permute-done | bytes 131104 | tf_op jit(solution)/shard_map/ppermute | solution.py:63
  187.3 1.3 collective-permute-done.30
  188.8 5.5 %collective-permute-done.31 = f32[256,128]{0,1:T(8,128)S(1)} collective-permute-done((f32[256,128]{0,1:T(8,128)S(1)}, f32[256,128]{0,1:T(8,128)S(1)}, u32[]{:S(2)}, u32[]{:S(2)}) %collective-permute-start.31) | collective-permute-done | bytes 131104 | tf_op jit(solution)/shard_map/ppermute | solution.py:28
  194.5 8.3 %collective-permute-done.32 = f32[256,128]{0,1:T(8,128)S(1)} collective-permute-done((f32[256,128]{0,1:T(8,128)S(1)}, f32[256,128]{0,1:T(8,128)S(1)}, u32[]{:S(2)}, u32[]{:S(2)}) %collective-permute-start.32) | collective-permute-done | bytes 131104 | tf_op jit(solution)/shard_map/ppermute | solution.py:28
  202.8 1.6 collective-permute-start.33
  204.4 3.9 %collective-permute-done.33 = f32[256,128]{0,1:T(8,128)S(1)} collective-permute-done((f32[256,128]{0,1:T(8,128)S(1)}, f32[256,128]{0,1:T(8,128)S(1)}, u32[]{:S(2)}, u32[]{:S(2)}) %collective-permute-start.33) | collective-permute-done | bytes 131104 | tf_op jit(solution)/shard_map/ppermute | solution.py:28
  208.7 4.7 %collective-permute-done.34 = f32[256,128]{0,1:T(8,128)S(1)} collective-permute-done((f32[256,128]{0,1:T(8,128)S(1)}, f32[256,128]{0,1:T(8,128)S(1)}, u32[]{:S(2)}, u32[]{:S(2)}) %collective-permute-start.34) | collective-permute-done | bytes 131104 | tf_op jit(solution)/shard_map/ppermute | solution.py:28
  213.5 11.7 %cholesky.16 = f32[128,128]{1,0:T(8,128)S(1)} custom-call(f32[128,128]{1,0:T(8,128)S(1)} %fusion.42), custom_call_target="Cholesky" | custom-call | tf_op jit(solution)/shard_map/jit(cholesky)/cholesky | solution.py:149
  226.6 10.0 %custom-call.10 = f32[1,128,128]{1,2,0:T(8,128)S(1)} custom-call(f32[1,128,128]{2,1,0:T(8,128)S(1)} %fusion.35), custom_call_target="InvertDiagBlocksLowerTriangular" | custom-call | tf_op jit(solution)/shard_map/triangular_solve | solution.py:150
  (140 shorter events, 25.9 us)
Async XLA Ops:
  1.6 19.6 %collective-permute-start = (bf16[256,128]{1,0:T(8,128)(2,1)S(1)}, bf16[256,128]{1,0:T(8,128)(2,1)S(1)}, u32[]{:S(2)}, u32[]{:S(2)}) collective-permute-start(bf16[256,128]{1,0:T(8,128)(2,1)S(1)} %multiply_convert_fusion.4), channel_id=1, source_target_pairs={{0,8},{8,0},{16,24},{24,16},{1,9},{9,1},{17,25},{25,17},{2,10},{10... | collective-permute-start | bytes 196616 | tf_op jit(solution)/shard_map/ppermute | solution.py:77
  4.7 20.0 %collective-permute-start.5 = (bf16[256,128]{1,0:T(8,128)(2,1)}, bf16[256,128]{1,0:T(8,128)(2,1)S(1)}, u32[]{:S(2)}, u32[]{:S(2)}) collective-permute-start(bf16[256,128]{1,0:T(8,128)(2,1)} %param.11), channel_id=1, source_target_pairs={{0,8},{8,0},{16,24},{24,16},{1,9},{9,1},{17,25},{25,17},{2,10},{10... | collective-permute-start | bytes 196616 | tf_op jit(solution)/shard_map/ppermute | solution.py:77
  4.8 18.3 %collective-permute-start.2 = (bf16[1,256,128]{2,1,0:T(8,128)(2,1)}, bf16[1,256,128]{2,1,0:T(8,128)(2,1)S(1)}, u32[]{:S(2)}, u32[]{:S(2)}) collective-permute-start(bf16[1,256,128]{2,1,0:T(8,128)(2,1)} %bitcast.186), channel_id=1, source_target_pairs={{0,4},{1,5},{2,6},{3,7},{4,0},{5,1},{6,2},{7,3},{8,12},{9,13},{10,... | collective-permute-start | bytes 196616 | tf_op jit(solution)/shard_map/ppermute | solution.py:95
  16.0 5.3 %copy-start.3 = (f32[256,128]{1,0:T(8,128)S(1)}, f32[256,128]{1,0:T(8,128)}, u32[]{:S(2)}) copy-start(f32[256,128]{1,0:T(8,128)} %param.10) | copy-start | bytes 393220
  16.0 5.3 %copy-start.5 = (f32[256]{0:T(256)S(1)}, f32[256]{0:T(256)}, u32[]{:S(2)}) copy-start(f32[256]{0:T(256)} %param.9) | copy-start | bytes 3076
  16.0 7.0 %copy-start.4 = (bf16[256,128]{1,0:T(8,128)(2,1)S(1)}, bf16[256,128]{1,0:T(8,128)(2,1)}, u32[]{:S(2)}) copy-start(bf16[256,128]{1,0:T(8,128)(2,1)} %param.11) | copy-start | bytes 196612
  21.4 6.8 %collective-permute-start.1 = (bf16[512,128]{1,0:T(8,128)(2,1)S(1)}, bf16[512,128]{1,0:T(8,128)(2,1)S(1)}, u32[]{:S(2)}, u32[]{:S(2)}) collective-permute-start(bf16[512,128]{1,0:T(8,128)(2,1)S(1)} %pad_maximum_fusion.8), channel_id=1, source_target_pairs={{0,16},{8,24},{16,0},{24,8},{1,17},{9,25},{17,1},{25,9},{2,18},{10... | collective-permute-start | bytes 393224 | tf_op jit(solution)/shard_map/ppermute | solution.py:77
  23.1 5.0 %collective-permute-start.3 = (bf16[2,256,128]{2,1,0:T(8,128)(2,1)S(1)}, bf16[2,256,128]{2,1,0:T(8,128)(2,1)S(1)}, u32[]{:S(2)}, u32[]{:S(2)}) collective-permute-start(bf16[2,256,128]{2,1,0:T(8,128)(2,1)S(1)} %pad_maximum_fusion.9), channel_id=1, source_target_pairs={{0,2},{1,3},{2,0},{3,1},{4,6},{5,7},{6,4},{7,5},{8,10},{9,11},{10,... | collective-permute-start | bytes 393224 | tf_op jit(solution)/shard_map/ppermute | solution.py:95
  24.7 7.0 %collective-permute-start.6 = (bf16[512,128]{1,0:T(8,128)(2,1)S(1)}, bf16[512,128]{1,0:T(8,128)(2,1)S(1)}, u32[]{:S(2)}, u32[]{:S(2)}) collective-permute-start(bf16[512,128]{1,0:T(8,128)(2,1)S(1)} %pad_maximum_fusion.10), channel_id=1, source_target_pairs={{0,16},{8,24},{16,0},{24,8},{1,17},{9,25},{17,1},{25,9},{2,18},{10... | collective-permute-start | bytes 393224 | tf_op jit(solution)/shard_map/ppermute | solution.py:77
  28.1 3.7 %copy-start.7 = (f32[128]{0:T(128)S(1)}, f32[128]{0:T(128)}, u32[]{:S(2)}) copy-start(f32[128]{0:T(128)} %param.12) | copy-start | bytes 1540
  28.2 4.0 %collective-permute-start.4 = (bf16[4,256,128]{2,1,0:T(8,128)(2,1)S(1)}, bf16[4,256,128]{2,1,0:T(8,128)(2,1)S(1)}, u32[]{:S(2)}, u32[]{:S(2)}) collective-permute-start(bf16[4,256,128]{2,1,0:T(8,128)(2,1)S(1)} %pad_maximum_fusion.2), channel_id=1, source_target_pairs={{0,1},{1,0},{2,3},{3,2},{4,5},{5,4},{6,7},{7,6},{8,9},{9,8},{10,11... | collective-permute-start | bytes 786440 | tf_op jit(solution)/shard_map/ppermute | solution.py:95
  31.9 2.2 copy-start
  35.3 11.4 %copy-start.6 = (f32[2]{0:T(128)S(1)}, f32[2]{0:T(128)}, u32[]{:S(2)}) copy-start(f32[2]{0:T(128)} %param.13) | copy-start | bytes 28
  35.4 2.1 collective-permute-start.7
  37.6 8.7 %collective-permute-start.8 = (f32[2,256,128]{2,1,0:T(8,128)S(1)}, f32[2,256,128]{2,1,0:T(8,128)S(1)}, u32[]{:S(2)}, u32[]{:S(2)}) collective-permute-start(f32[2,256,128]{2,1,0:T(8,128)S(1)} %dynamic-slice_bitcast_fusion.9), channel_id=1, source_target_pairs={{0,2},{1,3},{2,0},{3,1},{4,6},{5,7},{6,4},{7,5},{8,10},{9,11},{10,... | collective-permute-start | bytes 786440 | tf_op jit(solution)/shard_map/ppermute | solution.py:63
  46.3 8.7 %collective-permute-start.9 = (f32[1,256,128]{2,1,0:T(8,128)S(1)}, f32[1,256,128]{2,1,0:T(8,128)S(1)}, u32[]{:S(2)}, u32[]{:S(2)}) collective-permute-start(f32[1,256,128]{2,1,0:T(8,128)S(1)} %constant_dynamic-slice_fusion.4), channel_id=1, source_target_pairs={{0,4},{1,5},{2,6},{3,7},{4,0},{5,1},{6,2},{7,3},{8,12},{9,13},{10,... | collective-permute-start | bytes 393224 | tf_op jit(solution)/shard_map/ppermute | solution.py:63
  55.1 4.3 %collective-permute-start.10 = (bf16[256,128]{1,0:T(8,128)(2,1)S(1)}, bf16[256,128]{1,0:T(8,128)(2,1)S(1)}, u32[]{:S(2)}, u32[]{:S(2)}) collective-permute-start(bf16[256,128]{1,0:T(8,128)(2,1)S(1)} %get-tuple-element.8), channel_id=1, source_target_pairs={{0,8},{8,0},{16,24},{24,16},{1,9},{9,1},{17,25},{25,17},{2,10},{10... | collective-permute-start | bytes 196616 | tf_op jit(solution)/shard_map/ppermute | solution.py:77
  59.4 5.0 %collective-permute-start.11 = (bf16[512,128]{1,0:T(8,128)(2,1)S(1)}, bf16[512,128]{1,0:T(8,128)(2,1)S(1)}, u32[]{:S(2)}, u32[]{:S(2)}) collective-permute-start(bf16[512,128]{1,0:T(8,128)(2,1)S(1)} %pad_maximum_fusion.11), channel_id=1, source_target_pairs={{0,16},{8,24},{16,0},{24,8},{1,17},{9,25},{17,1},{25,9},{2,18},{10... | collective-permute-start | bytes 393224 | tf_op jit(solution)/shard_map/ppermute | solution.py:77
  68.0 2.2 copy-start.1
  71.5 28.6 %copy-start.2 = (bf16[2048,1024]{1,0:T(8,128)(2,1)S(1)}, bf16[2048,1024]{1,0:T(8,128)(2,1)}, u32[]{:S(2)}) copy-start(bf16[2048,1024]{1,0:T(8,128)(2,1)} %get-tuple-element.10) | copy-start | bytes 12582916
  71.5 2.0 collective-permute-start.12
  73.6 8.4 %collective-permute-start.13 = (f32[2,256,128]{2,1,0:T(8,128)S(1)}, f32[2,256,128]{2,1,0:T(8,128)S(1)}, u32[]{:S(2)}, u32[]{:S(2)}) collective-permute-start(f32[2,256,128]{2,1,0:T(8,128)S(1)} %dynamic-slice_bitcast_fusion.8), channel_id=1, source_target_pairs={{0,2},{1,3},{2,0},{3,1},{4,6},{5,7},{6,4},{7,5},{8,10},{9,11},{10,... | collective-permute-start | bytes 786440 | tf_op jit(solution)/shard_map/ppermute | solution.py:63
  82.1 8.5 %collective-permute-start.14 = (f32[1,256,128]{2,1,0:T(8,128)S(1)}, f32[1,256,128]{2,1,0:T(8,128)S(1)}, u32[]{:S(2)}, u32[]{:S(2)}) collective-permute-start(f32[1,256,128]{2,1,0:T(8,128)S(1)} %constant_dynamic-slice_fusion.3), channel_id=1, source_target_pairs={{0,4},{1,5},{2,6},{3,7},{4,0},{5,1},{6,2},{7,3},{8,12},{9,13},{10,... | collective-permute-start | bytes 393224 | tf_op jit(solution)/shard_map/ppermute | solution.py:63
  90.6 4.3 %collective-permute-start.15 = (bf16[256,128]{1,0:T(8,128)(2,1)S(1)}, bf16[256,128]{1,0:T(8,128)(2,1)S(1)}, u32[]{:S(2)}, u32[]{:S(2)}) collective-permute-start(bf16[256,128]{1,0:T(8,128)(2,1)S(1)} %get-tuple-element.6), channel_id=1, source_target_pairs={{0,8},{8,0},{16,24},{24,16},{1,9},{9,1},{17,25},{25,17},{2,10},{10... | collective-permute-start | bytes 196616 | tf_op jit(solution)/shard_map/ppermute | solution.py:77
  95.0 5.0 %collective-permute-start.16 = (bf16[512,128]{1,0:T(8,128)(2,1)S(1)}, bf16[512,128]{1,0:T(8,128)(2,1)S(1)}, u32[]{:S(2)}, u32[]{:S(2)}) collective-permute-start(bf16[512,128]{1,0:T(8,128)(2,1)S(1)} %pad_maximum_fusion.12), channel_id=1, source_target_pairs={{0,16},{8,24},{16,0},{24,8},{1,17},{9,25},{17,1},{25,9},{2,18},{10... | collective-permute-start | bytes 393224 | tf_op jit(solution)/shard_map/ppermute | solution.py:77
  103.5 2.0 collective-permute-start.17
  105.6 8.4 %collective-permute-start.18 = (f32[2,256,128]{2,1,0:T(8,128)S(1)}, f32[2,256,128]{2,1,0:T(8,128)S(1)}, u32[]{:S(2)}, u32[]{:S(2)}) collective-permute-start(f32[2,256,128]{2,1,0:T(8,128)S(1)} %dynamic-slice_bitcast_fusion.7), channel_id=1, source_target_pairs={{0,2},{1,3},{2,0},{3,1},{4,6},{5,7},{6,4},{7,5},{8,10},{9,11},{10,... | collective-permute-start | bytes 786440 | tf_op jit(solution)/shard_map/ppermute | solution.py:63
  114.1 8.5 %collective-permute-start.19 = (f32[1,256,128]{2,1,0:T(8,128)S(1)}, f32[1,256,128]{2,1,0:T(8,128)S(1)}, u32[]{:S(2)}, u32[]{:S(2)}) collective-permute-start(f32[1,256,128]{2,1,0:T(8,128)S(1)} %constant_dynamic-slice_fusion.2), channel_id=1, source_target_pairs={{0,4},{1,5},{2,6},{3,7},{4,0},{5,1},{6,2},{7,3},{8,12},{9,13},{10,... | collective-permute-start | bytes 393224 | tf_op jit(solution)/shard_map/ppermute | solution.py:63
  122.7 4.3 %collective-permute-start.20 = (bf16[256,128]{1,0:T(8,128)(2,1)S(1)}, bf16[256,128]{1,0:T(8,128)(2,1)S(1)}, u32[]{:S(2)}, u32[]{:S(2)}) collective-permute-start(bf16[256,128]{1,0:T(8,128)(2,1)S(1)} %get-tuple-element.4), channel_id=1, source_target_pairs={{0,8},{8,0},{16,24},{24,16},{1,9},{9,1},{17,25},{25,17},{2,10},{10... | collective-permute-start | bytes 196616 | tf_op jit(solution)/shard_map/ppermute | solution.py:77
  127.0 5.0 %collective-permute-start.21 = (bf16[512,128]{1,0:T(8,128)(2,1)S(1)}, bf16[512,128]{1,0:T(8,128)(2,1)S(1)}, u32[]{:S(2)}, u32[]{:S(2)}) collective-permute-start(bf16[512,128]{1,0:T(8,128)(2,1)S(1)} %pad_maximum_fusion.13), channel_id=1, source_target_pairs={{0,16},{8,24},{16,0},{24,8},{1,17},{9,25},{17,1},{25,9},{2,18},{10... | collective-permute-start | bytes 393224 | tf_op jit(solution)/shard_map/ppermute | solution.py:77
  135.8 2.0 collective-permute-start.22
  137.9 8.4 %collective-permute-start.23 = (f32[2,256,128]{2,1,0:T(8,128)S(1)}, f32[2,256,128]{2,1,0:T(8,128)S(1)}, u32[]{:S(2)}, u32[]{:S(2)}) collective-permute-start(f32[2,256,128]{2,1,0:T(8,128)S(1)} %dynamic-slice_bitcast_fusion.6), channel_id=1, source_target_pairs={{0,2},{1,3},{2,0},{3,1},{4,6},{5,7},{6,4},{7,5},{8,10},{9,11},{10,... | collective-permute-start | bytes 786440 | tf_op jit(solution)/shard_map/ppermute | solution.py:63
  146.3 8.5 %collective-permute-start.24 = (f32[1,256,128]{2,1,0:T(8,128)S(1)}, f32[1,256,128]{2,1,0:T(8,128)S(1)}, u32[]{:S(2)}, u32[]{:S(2)}) collective-permute-start(f32[1,256,128]{2,1,0:T(8,128)S(1)} %constant_dynamic-slice_fusion.1), channel_id=1, source_target_pairs={{0,4},{1,5},{2,6},{3,7},{4,0},{5,1},{6,2},{7,3},{8,12},{9,13},{10,... | collective-permute-start | bytes 393224 | tf_op jit(solution)/shard_map/ppermute | solution.py:63
  154.9 4.3 %collective-permute-start.25 = (bf16[256,128]{1,0:T(8,128)(2,1)S(1)}, bf16[256,128]{1,0:T(8,128)(2,1)S(1)}, u32[]{:S(2)}, u32[]{:S(2)}) collective-permute-start(bf16[256,128]{1,0:T(8,128)(2,1)S(1)} %get-tuple-element.2), channel_id=1, source_target_pairs={{0,8},{8,0},{16,24},{24,16},{1,9},{9,1},{17,25},{25,17},{2,10},{10... | collective-permute-start | bytes 196616 | tf_op jit(solution)/shard_map/ppermute | solution.py:77
  159.3 5.0 %collective-permute-start.26 = (bf16[512,128]{1,0:T(8,128)(2,1)S(1)}, bf16[512,128]{1,0:T(8,128)(2,1)S(1)}, u32[]{:S(2)}, u32[]{:S(2)}) collective-permute-start(bf16[512,128]{1,0:T(8,128)(2,1)S(1)} %pad_maximum_fusion.14), channel_id=1, source_target_pairs={{0,16},{8,24},{16,0},{24,8},{1,17},{9,25},{17,1},{25,9},{2,18},{10... | collective-permute-start | bytes 393224 | tf_op jit(solution)/shard_map/ppermute | solution.py:77
  167.8 2.0 collective-permute-start.27
  169.9 8.4 %collective-permute-start.28 = (f32[2,256,128]{2,1,0:T(8,128)S(1)}, f32[2,256,128]{2,1,0:T(8,128)S(1)}, u32[]{:S(2)}, u32[]{:S(2)}) collective-permute-start(f32[2,256,128]{2,1,0:T(8,128)S(1)} %dynamic-slice_bitcast_fusion.5), channel_id=1, source_target_pairs={{0,2},{1,3},{2,0},{3,1},{4,6},{5,7},{6,4},{7,5},{8,10},{9,11},{10,... | collective-permute-start | bytes 786440 | tf_op jit(solution)/shard_map/ppermute | solution.py:63
  178.3 8.5 %collective-permute-start.29 = (f32[1,256,128]{2,1,0:T(8,128)S(1)}, f32[1,256,128]{2,1,0:T(8,128)S(1)}, u32[]{:S(2)}, u32[]{:S(2)}) collective-permute-start(f32[1,256,128]{2,1,0:T(8,128)S(1)} %constant_dynamic-slice_fusion), channel_id=1, source_target_pairs={{0,4},{1,5},{2,6},{3,7},{4,0},{5,1},{6,2},{7,3},{8,12},{9,13},{10,... | collective-permute-start | bytes 393224 | tf_op jit(solution)/shard_map/ppermute | solution.py:63
  187.3 1.4 collective-permute-start.30
  188.7 5.6 %collective-permute-start.31 = (f32[256,128]{0,1:T(8,128)S(1)}, f32[256,128]{0,1:T(8,128)S(1)}, u32[]{:S(2)}, u32[]{:S(2)}) collective-permute-start(f32[256,128]{0,1:T(8,128)S(1)} %fusion.80), channel_id=1, source_target_pairs={{0,2},{1,3},{2,0},{3,1},{4,6},{5,7},{6,4},{7,5},{8,10},{9,11},{10,... | collective-permute-start | bytes 393224 | tf_op jit(solution)/shard_map/ppermute | solution.py:28
  194.3 8.5 %collective-permute-start.32 = (f32[256,128]{0,1:T(8,128)S(1)}, f32[256,128]{0,1:T(8,128)S(1)}, u32[]{:S(2)}, u32[]{:S(2)}) collective-permute-start(f32[256,128]{0,1:T(8,128)S(1)} %add.261), channel_id=1, source_target_pairs={{0,4},{1,5},{2,6},{3,7},{4,0},{5,1},{6,2},{7,3},{8,12},{9,13},{10,... | collective-permute-start | bytes 393224 | tf_op jit(solution)/shard_map/ppermute | solution.py:28
  202.8 5.5 %collective-permute-start.33 = (f32[256,128]{0,1:T(8,128)S(1)}, f32[256,128]{0,1:T(8,128)S(1)}, u32[]{:S(2)}, u32[]{:S(2)}) collective-permute-start(f32[256,128]{0,1:T(8,128)S(1)} %add.262), channel_id=1, source_target_pairs={{0,8},{8,0},{16,24},{24,16},{1,9},{9,1},{17,25},{25,17},{2,10},{10... | collective-permute-start | bytes 393224 | tf_op jit(solution)/shard_map/ppermute | solution.py:28
  208.3 5.0 %collective-permute-start.34 = (f32[256,128]{0,1:T(8,128)S(1)}, f32[256,128]{0,1:T(8,128)S(1)}, u32[]{:S(2)}, u32[]{:S(2)}) collective-permute-start(f32[256,128]{0,1:T(8,128)S(1)} %add.263), channel_id=1, source_target_pairs={{0,16},{8,24},{16,0},{24,8},{1,17},{9,25},{17,1},{25,9},{2,18},{10... | collective-permute-start | bytes 393224 | tf_op jit(solution)/shard_map/ppermute | solution.py:28

commit v12 on v11

--- a/solution.py
+++ b/solution.py
@@ -115,6 +115,7 @@
     dense = jnp.einsum("rst,rsab->ratb", onehot, tiles, preferred_element_type=jnp.float32)
     dense = dense.reshape(tile_rows * tile_size, n_blocks * tile_size)
     w_hi, w_lo = split_bf16(dense)
+    w_both = jnp.concatenate([w_hi, w_lo], axis=1)
 
     planted_cols = doubling_gather(planted, "row")
     planted_rows = far_first_gather(planted, "col")
@@ -122,8 +123,9 @@
     def operate(vector):
         scaled = (degree_scale[:, None] * vector).astype(jnp.bfloat16)
         gathered = doubling_gather(scaled, "row")
-        product = jnp.dot(w_hi, gathered, preferred_element_type=jnp.float32)
-        product = product + jnp.dot(w_lo, gathered, preferred_element_type=jnp.float32)
+        product = jnp.dot(
+            w_both, jnp.concatenate([gathered, gathered], axis=0), preferred_element_type=jnp.float32
+        )
         partial = lax.dot_general(
             planted_cols, gathered, (((0,), (0,)), ((), ())), preferred_element_type=jnp.float32
         )

time: 239 us -> 244 us (1.021)
  local copies, waits for them, and re-layouts: 3.68 us -> 11.9 us
  matrix products: 32.4 us -> 29.9 us
    unnamed x16 -> x21, local copies, waits for them, and re-layouts: 2.54 us -> 10.8 us
    dot_general x10 -> x5, matrix products: 17.2 us -> 14.5 us  [operate(): jnp.dot(w_both, jnp.concatenate([gathered, gathered], axis=0), preferred_...]
  transfers between devices with their start and end apart: 35 -> 35, of which waited for: 29 -> 30; matrix products, arithmetic and copies ran while one was open for 8% -> 9% of each run, Pallas kernels for 0% -> 0%
where the time goes in v12:
time: 244 us
  waiting for transfers between devices  143 us (59%)
  matrix products  29.9 us (12%)
  other arithmetic  29.3 us (12%)
  starting transfers between devices  25 us (10%)
  local copies, waits for them, and re-layouts  11.9 us (5%)
  between operations  4.12 us (2%)
    ppermute x15, waiting for transfers between devices, halving_scatter_sum(): blocks = kept + lax.ppermute(sent, axis, pairs)  87.9 us
    ppermute x12, waiting for transfers between devices, doubling_gather(): other = lax.ppermute(result, axis, pairs)  29.2 us
    ppermute x5, waiting for transfers between devices, butterfly_sum(): value = value + lax.ppermute(value, axis, pairs)  23.3 us
    ppermute x12, starting transfers between devices, doubling_gather(): other = lax.ppermute(result, axis, pairs)  15 us
    dot_general x5, matrix products, operate(): jnp.dot(w_both, jnp.concatenate([gathered, gathered], axis=0), preferred_...  14.5 us
    another operation x3, other arithmetic, local(): factor = jnp.linalg.cholesky(gram_matrix)  12.4 us
    unnamed x21, local copies, waits for them, and re-layouts  10.8 us
    another operation x2, other arithmetic, local(): lax.linalg.triangular_solve(factor, current, left_side=False, lower=True,...  10.5 us
  transfers between devices with their start and end apart: 35, of which 30 were waited for; matrix products, arithmetic and copies ran while one was open for 9% of the time, Pallas kernels for 0%

profile of v12, /device:TPU:0, one launch (start us, length us, event | category | flops | bytes accessed | tf_op | source)
XLA Modules:
  0.0 243.5 jit_solution(3970673760351244852)
XLA Ops:
  1.6 3.0 %collective-permute-start = (bf16[256,128]{1,0:T(8,128)(2,1)S(1)}, bf16[256,128]{1,0:T(8,128)(2,1)S(1)}, u32[]{:S(2)}, u32[]{:S(2)}) collective-permute-start(bf16[256,128]{1,0:T(8,128)(2,1)S(1)} %multiply_convert_fusion.4), channel_id=1, source_target_pairs={{0,8},{8,0},{16,24},{24,16},{1,9},{9,1},{17,25},{25,17},{2,10},{10... | collective-permute-start | bytes 196616 | tf_op jit(solution)/shard_map/ppermute | solution.py:77
  4.8 3.0 %collective-permute-start.2 = (bf16[1,256,128]{2,1,0:T(8,128)(2,1)}, bf16[1,256,128]{2,1,0:T(8,128)(2,1)S(1)}, u32[]{:S(2)}, u32[]{:S(2)}) collective-permute-start(bf16[1,256,128]{2,1,0:T(8,128)(2,1)} %bitcast.184), channel_id=1, source_target_pairs={{0,4},{1,5},{2,6},{3,7},{4,0},{5,1},{6,2},{7,3},{8,12},{9,13},{10,... | collective-permute-start | bytes 196616 | tf_op jit(solution)/shard_map/ppermute | solution.py:95
  7.8 8.2 %fusion.1 = f32[16,8,128,128]{3,1,2,0:T(8,128)S(1)} fusion(bf16[16,16,128,128]{3,2,1,0:T(8,128)(2,1)} %param.7, s32[16,16]{1,0:T(8,128)} %param.8), kind=kOutput, calls=%fused_computation.4 | convolution fusion | flops 67110912 | bytes 16778240 | tf_op jit(solution)/shard_map/rst,rsab->ratb/dot_general | solution.py:115
  16.0 3.3 %copy-done = f32[16,8,128,128]{3,1,2,0:T(8,128)} copy-done((f32[16,8,128,128]{3,1,2,0:T(8,128)}, f32[16,8,128,128]{3,1,2,0:T(8,128)S(1)}, u32[]{:S(2)}) %copy-start) | copy-done | bytes 8388632
  19.3 3.8 %fusion = bf16[2048,1024]{1,0:T(8,128)(2,1)} fusion(f32[256,8,8,128]{3,2,1,0:T(8,128)S(1)} %bitcast.146), kind=kLoop, calls=%fused_computation.2 | loop fusion | flops 8388608 | bytes 12582912 | tf_op jit(solution)/shard_map/convert_element_type | solution.py:11
  23.1 7.5 %copy.32 = bf16[256,8,8,128]{3,1,2,0:T(8,128)(2,1)} copy(f32[256,8,8,128]{3,2,1,0:T(8,128)} %bitcast.147) | data formatting | bytes 12582912
  30.7 1.6 collective-permute-start.1
  32.4 1.6 collective-permute-start.3
  34.6 2.8 %collective-permute-done.3 = bf16[2,256,128]{2,1,0:T(8,128)(2,1)S(1)} collective-permute-done((bf16[2,256,128]{2,1,0:T(8,128)(2,1)S(1)}, bf16[2,256,128]{2,1,0:T(8,128)(2,1)S(1)}, u32[]{:S(2)}, u32[]{:S(2)}) %collective-permute-start.3) | collective-permute-done | bytes 131104 | tf_op jit(solution)/shard_map/ppermute | solution.py:95
  40.2 2.6 %convolution_add_fusion.9 = f32[2048,128]{1,0:T(8,128)S(1)} fusion(f32[2048,128]{1,0:T(8,128)S(1)} %fusion.7, bf16[512,128]{1,0:T(8,128)(2,1)S(1)} %get-tuple-element.23, bf16[512,128]{1,0:T(8,128)(2,1)S(1)} %get-tuple-element.22, bf16[2048,1024]{1,0:T(8,128)(2,1)S(1)} %copy-done.1, bf16[2048,1024]{1,0:T(8,128)(2,1)S(1)} %bitcast.159), kind=kOutput, calls=%fused_computation.20 | convolution fusion | flops 1092878336 | bytes 10747904 | tf_op jit(solution)/shard_map/dot_general | solution.py:126
  43.0 1.9 collective-permute-done.7
  46.2 7.1 %collective-permute-done.8 = f32[2,256,128]{2,1,0:T(8,128)S(1)} collective-permute-done((f32[2,256,128]{2,1,0:T(8,128)S(1)}, f32[2,256,128]{2,1,0:T(8,128)S(1)}, u32[]{:S(2)}, u32[]{:S(2)}) %collective-permute-start.8) | collective-permute-done | bytes 262176 | tf_op jit(solution)/shard_map/ppermute | solution.py:63
  57.0 4.9 %collective-permute-done.9 = f32[1,256,128]{2,1,0:T(8,128)S(1)} collective-permute-done((f32[1,256,128]{2,1,0:T(8,128)S(1)}, f32[1,256,128]{2,1,0:T(8,128)S(1)}, u32[]{:S(2)}, u32[]{:S(2)}) %collective-permute-start.9) | collective-permute-done | bytes 131104 | tf_op jit(solution)/shard_map/ppermute | solution.py:63
  62.0 1.6 collective-permute-start.10
  63.5 2.8 %collective-permute-done.10 = bf16[256,128]{1,0:T(8,128)(2,1)S(1)} collective-permute-done((bf16[256,128]{1,0:T(8,128)(2,1)S(1)}, bf16[256,128]{1,0:T(8,128)(2,1)S(1)}, u32[]{:S(2)}, u32[]{:S(2)}) %collective-permute-start.10) | collective-permute-done | bytes 65568 | tf_op jit(solution)/shard_map/ppermute | solution.py:77
  67.2 4.2 %collective-permute-done.11 = bf16[512,128]{1,0:T(8,128)(2,1)S(1)} collective-permute-done((bf16[512,128]{1,0:T(8,128)(2,1)S(1)}, bf16[512,128]{1,0:T(8,128)(2,1)S(1)}, u32[]{:S(2)}, u32[]{:S(2)}) %collective-permute-start.11) | collective-permute-done | bytes 131104 | tf_op jit(solution)/shard_map/ppermute | solution.py:77
  72.3 4.8 %convolution_add_fusion.8 = f32[2048,128]{1,0:T(8,128)S(1)} fusion(f32[2048,128]{1,0:T(8,128)S(1)} %fusion.6, bf16[512,128]{1,0:T(8,128)(2,1)S(1)} %get-tuple-element.19, bf16[512,128]{1,0:T(8,128)(2,1)S(1)} %get-tuple-element.18, bf16[2048,1024]{1,0:T(8,128)(2,1)} %fusion, bf16[2048,1024]{1,0:T(8,128)(2,1)} %bitcast.158), kind=kOutput, calls=%fused_computation.19 | convolution fusion | flops 1092878336 | bytes 10747904 | tf_op jit(solution)/shard_map/dot_general | solution.py:126
  77.3 1.9 collective-permute-done.12
  79.3 8.3 %collective-permute-done.13 = f32[2,256,128]{2,1,0:T(8,128)S(1)} collective-permute-done((f32[2,256,128]{2,1,0:T(8,128)S(1)}, f32[2,256,128]{2,1,0:T(8,128)S(1)}, u32[]{:S(2)}, u32[]{:S(2)}) %collective-permute-start.13) | collective-permute-done | bytes 262176 | tf_op jit(solution)/shard_map/ppermute | solution.py:63
  87.8 8.4 %collective-permute-done.14 = f32[1,256,128]{2,1,0:T(8,128)S(1)} collective-permute-done((f32[1,256,128]{2,1,0:T(8,128)S(1)}, f32[1,256,128]{2,1,0:T(8,128)S(1)}, u32[]{:S(2)}, u32[]{:S(2)}) %collective-permute-start.14) | collective-permute-done | bytes 131104 | tf_op jit(solution)/shard_map/ppermute | solution.py:63
  96.3 1.6 collective-permute-start.15
  97.9 2.8 %collective-permute-done.15 = bf16[256,128]{1,0:T(8,128)(2,1)S(1)} collective-permute-done((bf16[256,128]{1,0:T(8,128)(2,1)S(1)}, bf16[256,128]{1,0:T(8,128)(2,1)S(1)}, u32[]{:S(2)}, u32[]{:S(2)}) %collective-permute-start.15) | collective-permute-done | bytes 65568 | tf_op jit(solution)/shard_map/ppermute | solution.py:77
  101.5 4.2 %collective-permute-done.16 = bf16[512,128]{1,0:T(8,128)(2,1)S(1)} collective-permute-done((bf16[512,128]{1,0:T(8,128)(2,1)S(1)}, bf16[512,128]{1,0:T(8,128)(2,1)S(1)}, u32[]{:S(2)}, u32[]{:S(2)}) %collective-permute-start.16) | collective-permute-done | bytes 131104 | tf_op jit(solution)/shard_map/ppermute | solution.py:77
  106.6 2.4 convolution_add_fusion.7
  109.1 1.9 collective-permute-done.17
  111.2 8.3 %collective-permute-done.18 = f32[2,256,128]{2,1,0:T(8,128)S(1)} collective-permute-done((f32[2,256,128]{2,1,0:T(8,128)S(1)}, f32[2,256,128]{2,1,0:T(8,128)S(1)}, u32[]{:S(2)}, u32[]{:S(2)}) %collective-permute-start.18) | collective-permute-done | bytes 262176 | tf_op jit(solution)/shard_map/ppermute | solution.py:63
  119.7 8.4 %collective-permute-done.19 = f32[1,256,128]{2,1,0:T(8,128)S(1)} collective-permute-done((f32[1,256,128]{2,1,0:T(8,128)S(1)}, f32[1,256,128]{2,1,0:T(8,128)S(1)}, u32[]{:S(2)}, u32[]{:S(2)}) %collective-permute-start.19) | collective-permute-done | bytes 131104 | tf_op jit(solution)/shard_map/ppermute | solution.py:63
  128.2 1.6 collective-permute-start.20
  129.7 2.8 %collective-permute-done.20 = bf16[256,128]{1,0:T(8,128)(2,1)S(1)} collective-permute-done((bf16[256,128]{1,0:T(8,128)(2,1)S(1)}, bf16[256,128]{1,0:T(8,128)(2,1)S(1)}, u32[]{:S(2)}, u32[]{:S(2)}) %collective-permute-start.20) | collective-permute-done | bytes 65568 | tf_op jit(solution)/shard_map/ppermute | solution.py:77
  133.4 4.2 %collective-permute-done.21 = bf16[512,128]{1,0:T(8,128)(2,1)S(1)} collective-permute-done((bf16[512,128]{1,0:T(8,128)(2,1)S(1)}, bf16[512,128]{1,0:T(8,128)(2,1)S(1)}, u32[]{:S(2)}, u32[]{:S(2)}) %collective-permute-start.21) | collective-permute-done | bytes 131104 | tf_op jit(solution)/shard_map/ppermute | solution.py:77
  138.5 2.4 convolution_add_fusion.6
  141.0 1.9 collective-permute-done.22
  143.0 8.3 %collective-permute-done.23 = f32[2,256,128]{2,1,0:T(8,128)S(1)} collective-permute-done((f32[2,256,128]{2,1,0:T(8,128)S(1)}, f32[2,256,128]{2,1,0:T(8,128)S(1)}, u32[]{:S(2)}, u32[]{:S(2)}) %collective-permute-start.23) | collective-permute-done | bytes 262176 | tf_op jit(solution)/shard_map/ppermute | solution.py:63
  151.5 8.4 %collective-permute-done.24 = f32[1,256,128]{2,1,0:T(8,128)S(1)} collective-permute-done((f32[1,256,128]{2,1,0:T(8,128)S(1)}, f32[1,256,128]{2,1,0:T(8,128)S(1)}, u32[]{:S(2)}, u32[]{:S(2)}) %collective-permute-start.24) | collective-permute-done | bytes 131104 | tf_op jit(solution)/shard_map/ppermute | solution.py:63
  160.0 1.6 collective-permute-start.25
  161.6 2.8 %collective-permute-done.25 = bf16[256,128]{1,0:T(8,128)(2,1)S(1)} collective-permute-done((bf16[256,128]{1,0:T(8,128)(2,1)S(1)}, bf16[256,128]{1,0:T(8,128)(2,1)S(1)}, u32[]{:S(2)}, u32[]{:S(2)}) %collective-permute-start.25) | collective-permute-done | bytes 65568 | tf_op jit(solution)/shard_map/ppermute | solution.py:77
  165.2 4.2 %collective-permute-done.26 = bf16[512,128]{1,0:T(8,128)(2,1)S(1)} collective-permute-done((bf16[512,128]{1,0:T(8,128)(2,1)S(1)}, bf16[512,128]{1,0:T(8,128)(2,1)S(1)}, u32[]{:S(2)}, u32[]{:S(2)}) %collective-permute-start.26) | collective-permute-done | bytes 131104 | tf_op jit(solution)/shard_map/ppermute | solution.py:77
  170.3 2.4 convolution_add_fusion.5
  172.8 1.9 collective-permute-done.27
  174.8 8.3 %collective-permute-done.28 = f32[2,256,128]{2,1,0:T(8,128)S(1)} collective-permute-done((f32[2,256,128]{2,1,0:T(8,128)S(1)}, f32[2,256,128]{2,1,0:T(8,128)S(1)}, u32[]{:S(2)}, u32[]{:S(2)}) %collective-permute-start.28) | collective-permute-done | bytes 262176 | tf_op jit(solution)/shard_map/ppermute | solution.py:63
  183.7 8.0 %collective-permute-done.29 = f32[1,256,128]{2,1,0:T(8,128)S(1)} collective-permute-done((f32[1,256,128]{2,1,0:T(8,128)S(1)}, f32[1,256,128]{2,1,0:T(8,128)S(1)}, u32[]{:S(2)}, u32[]{:S(2)}) %collective-permute-start.29) | collective-permute-done | bytes 131104 | tf_op jit(solution)/shard_map/ppermute | solution.py:63
  193.9 5.5 %collective-permute-done.31 = f32[256,128]{0,1:T(8,128)S(1)} collective-permute-done((f32[256,128]{0,1:T(8,128)S(1)}, f32[256,128]{0,1:T(8,128)S(1)}, u32[]{:S(2)}, u32[]{:S(2)}) %collective-permute-start.31) | collective-permute-done | bytes 131104 | tf_op jit(solution)/shard_map/ppermute | solution.py:28
  199.5 8.4 %collective-permute-done.32 = f32[256,128]{0,1:T(8,128)S(1)} collective-permute-done((f32[256,128]{0,1:T(8,128)S(1)}, f32[256,128]{0,1:T(8,128)S(1)}, u32[]{:S(2)}, u32[]{:S(2)}) %collective-permute-start.32) | collective-permute-done | bytes 131104 | tf_op jit(solution)/shard_map/ppermute | solution.py:28
  207.9 1.6 collective-permute-start.33
  209.5 3.9 %collective-permute-done.33 = f32[256,128]{0,1:T(8,128)S(1)} collective-permute-done((f32[256,128]{0,1:T(8,128)S(1)}, f32[256,128]{0,1:T(8,128)S(1)}, u32[]{:S(2)}, u32[]{:S(2)}) %collective-permute-start.33) | collective-permute-done | bytes 131104 | tf_op jit(solution)/shard_map/ppermute | solution.py:28
  214.3 4.2 %collective-permute-done.34 = f32[256,128]{0,1:T(8,128)S(1)} collective-permute-done((f32[256,128]{0,1:T(8,128)S(1)}, f32[256,128]{0,1:T(8,128)S(1)}, u32[]{:S(2)}, u32[]{:S(2)}) %collective-permute-start.34) | collective-permute-done | bytes 131104 | tf_op jit(solution)/shard_map/ppermute | solution.py:28
  218.6 11.7 %cholesky.16 = f32[128,128]{1,0:T(8,128)S(1)} custom-call(f32[128,128]{1,0:T(8,128)S(1)} %fusion.82), custom_call_target="Cholesky" | custom-call | tf_op jit(solution)/shard_map/jit(cholesky)/cholesky | solution.py:151
  231.7 9.8 %custom-call.10 = f32[1,128,128]{1,2,0:T(8,128)S(1)} custom-call(f32[1,128,128]{2,1,0:T(8,128)S(1)} %fusion.75), custom_call_target="InvertDiagBlocksLowerTriangular" | custom-call | tf_op jit(solution)/shard_map/triangular_solve | solution.py:152
  (140 shorter events, 23.0 us)
Async XLA Ops:
  1.6 29.0 %collective-permute-start = (bf16[256,128]{1,0:T(8,128)(2,1)S(1)}, bf16[256,128]{1,0:T(8,128)(2,1)S(1)}, u32[]{:S(2)}, u32[]{:S(2)}) collective-permute-start(bf16[256,128]{1,0:T(8,128)(2,1)S(1)} %multiply_convert_fusion.4), channel_id=1, source_target_pairs={{0,8},{8,0},{16,24},{24,16},{1,9},{9,1},{17,25},{25,17},{2,10},{10... | collective-permute-start | bytes 196616 | tf_op jit(solution)/shard_map/ppermute | solution.py:77
  4.7 29.3 %collective-permute-start.5 = (bf16[256,128]{1,0:T(8,128)(2,1)}, bf16[256,128]{1,0:T(8,128)(2,1)S(1)}, u32[]{:S(2)}, u32[]{:S(2)}) collective-permute-start(bf16[256,128]{1,0:T(8,128)(2,1)} %param.11), channel_id=1, source_target_pairs={{0,8},{8,0},{16,24},{24,16},{1,9},{9,1},{17,25},{25,17},{2,10},{10... | collective-permute-start | bytes 196616 | tf_op jit(solution)/shard_map/ppermute | solution.py:77
  4.8 27.6 %collective-permute-start.2 = (bf16[1,256,128]{2,1,0:T(8,128)(2,1)}, bf16[1,256,128]{2,1,0:T(8,128)(2,1)S(1)}, u32[]{:S(2)}, u32[]{:S(2)}) collective-permute-start(bf16[1,256,128]{2,1,0:T(8,128)(2,1)} %bitcast.184), channel_id=1, source_target_pairs={{0,4},{1,5},{2,6},{3,7},{4,0},{5,1},{6,2},{7,3},{8,12},{9,13},{10,... | collective-permute-start | bytes 196616 | tf_op jit(solution)/shard_map/ppermute | solution.py:95
  16.0 3.3 %copy-start = (f32[16,8,128,128]{3,1,2,0:T(8,128)}, f32[16,8,128,128]{3,1,2,0:T(8,128)S(1)}, u32[]{:S(2)}) copy-start(f32[16,8,128,128]{3,1,2,0:T(8,128)S(1)} %fusion.1) | copy-start | bytes 25165828
  23.1 7.6 %copy-start.5 = (f32[256,128]{1,0:T(8,128)S(1)}, f32[256,128]{1,0:T(8,128)}, u32[]{:S(2)}) copy-start(f32[256,128]{1,0:T(8,128)} %param.10) | copy-start | bytes 393220
  23.1 7.6 %copy-start.7 = (f32[256]{0:T(256)S(1)}, f32[256]{0:T(256)}, u32[]{:S(2)}) copy-start(f32[256]{0:T(256)} %param.9) | copy-start | bytes 3076
  23.1 9.3 %copy-start.6 = (bf16[256,128]{1,0:T(8,128)(2,1)S(1)}, bf16[256,128]{1,0:T(8,128)(2,1)}, u32[]{:S(2)}) copy-start(bf16[256,128]{1,0:T(8,128)(2,1)} %param.11) | copy-start | bytes 196612
  23.1 16.1 %copy-start.9 = (f32[128]{0:T(128)S(1)}, f32[128]{0:T(128)}, u32[]{:S(2)}) copy-start(f32[128]{0:T(128)} %param.12) | copy-start | bytes 1540
  30.6 9.6 %copy-start.1 = (bf16[2048,1024]{1,0:T(8,128)(2,1)S(1)}, bf16[2048,1024]{1,0:T(8,128)(2,1)}, u32[]{:S(2)}) copy-start(bf16[2048,1024]{1,0:T(8,128)(2,1)} %fusion) | copy-start | bytes 12582916
  30.6 9.6 %copy-start.3 = (bf16[256,8,8,128]{3,1,2,0:T(8,128)(2,1)S(1)}, bf16[256,8,8,128]{3,1,2,0:T(8,128)(2,1)}, u32[]{:S(2)}) copy-start(bf16[256,8,8,128]{3,1,2,0:T(8,128)(2,1)} %copy.32) | copy-start | bytes 12582916
  30.7 6.8 %collective-permute-start.1 = (bf16[512,128]{1,0:T(8,128)(2,1)S(1)}, bf16[512,128]{1,0:T(8,128)(2,1)S(1)}, u32[]{:S(2)}, u32[]{:S(2)}) collective-permute-start(bf16[512,128]{1,0:T(8,128)(2,1)S(1)} %pad_maximum_fusion.4), channel_id=1, source_target_pairs={{0,16},{8,24},{16,0},{24,8},{1,17},{9,25},{17,1},{25,9},{2,18},{10... | collective-permute-start | bytes 393224 | tf_op jit(solution)/shard_map/ppermute | solution.py:77
  32.4 5.0 %collective-permute-start.3 = (bf16[2,256,128]{2,1,0:T(8,128)(2,1)S(1)}, bf16[2,256,128]{2,1,0:T(8,128)(2,1)S(1)}, u32[]{:S(2)}, u32[]{:S(2)}) collective-permute-start(bf16[2,256,128]{2,1,0:T(8,128)(2,1)S(1)} %pad_maximum_fusion.5), channel_id=1, source_target_pairs={{0,2},{1,3},{2,0},{3,1},{4,6},{5,7},{6,4},{7,5},{8,10},{9,11},{10,... | collective-permute-start | bytes 393224 | tf_op jit(solution)/shard_map/ppermute | solution.py:95
  34.1 5.0 %collective-permute-start.6 = (bf16[512,128]{1,0:T(8,128)(2,1)S(1)}, bf16[512,128]{1,0:T(8,128)(2,1)S(1)}, u32[]{:S(2)}, u32[]{:S(2)}) collective-permute-start(bf16[512,128]{1,0:T(8,128)(2,1)S(1)} %pad_maximum_fusion.6), channel_id=1, source_target_pairs={{0,16},{8,24},{16,0},{24,8},{1,17},{9,25},{17,1},{25,9},{2,18},{10... | collective-permute-start | bytes 393224 | tf_op jit(solution)/shard_map/ppermute | solution.py:77
  37.5 2.0 collective-permute-start.4
  40.2 13.6 %copy-start.8 = (f32[2]{0:T(128)S(1)}, f32[2]{0:T(128)}, u32[]{:S(2)}) copy-start(f32[2]{0:T(128)} %param.13) | copy-start | bytes 28
  42.9 2.0 collective-permute-start.7
  44.9 8.4 %collective-permute-start.8 = (f32[2,256,128]{2,1,0:T(8,128)S(1)}, f32[2,256,128]{2,1,0:T(8,128)S(1)}, u32[]{:S(2)}, u32[]{:S(2)}) collective-permute-start(f32[2,256,128]{2,1,0:T(8,128)S(1)} %dynamic-slice_bitcast_fusion.9), channel_id=1, source_target_pairs={{0,2},{1,3},{2,0},{3,1},{4,6},{5,7},{6,4},{7,5},{8,10},{9,11},{10,... | collective-permute-start | bytes 786440 | tf_op jit(solution)/shard_map/ppermute | solution.py:63
  53.4 8.5 %collective-permute-start.9 = (f32[1,256,128]{2,1,0:T(8,128)S(1)}, f32[1,256,128]{2,1,0:T(8,128)S(1)}, u32[]{:S(2)}, u32[]{:S(2)}) collective-permute-start(f32[1,256,128]{2,1,0:T(8,128)S(1)} %constant_dynamic-slice_fusion.4), channel_id=1, source_target_pairs={{0,4},{1,5},{2,6},{3,7},{4,0},{5,1},{6,2},{7,3},{8,12},{9,13},{10,... | collective-permute-start | bytes 393224 | tf_op jit(solution)/shard_map/ppermute | solution.py:63
  62.0 4.3 %collective-permute-start.10 = (bf16[256,128]{1,0:T(8,128)(2,1)S(1)}, bf16[256,128]{1,0:T(8,128)(2,1)S(1)}, u32[]{:S(2)}, u32[]{:S(2)}) collective-permute-start(bf16[256,128]{1,0:T(8,128)(2,1)S(1)} %get-tuple-element.8), channel_id=1, source_target_pairs={{0,8},{8,0},{16,24},{24,16},{1,9},{9,1},{17,25},{25,17},{2,10},{10... | collective-permute-start | bytes 196616 | tf_op jit(solution)/shard_map/ppermute | solution.py:77
  66.3 5.0 %collective-permute-start.11 = (bf16[512,128]{1,0:T(8,128)(2,1)S(1)}, bf16[512,128]{1,0:T(8,128)(2,1)S(1)}, u32[]{:S(2)}, u32[]{:S(2)}) collective-permute-start(bf16[512,128]{1,0:T(8,128)(2,1)S(1)} %pad_maximum_fusion.7), channel_id=1, source_target_pairs={{0,16},{8,24},{16,0},{24,8},{1,17},{9,25},{17,1},{25,9},{2,18},{10... | collective-permute-start | bytes 393224 | tf_op jit(solution)/shard_map/ppermute | solution.py:77
  77.1 29.5 %copy-start.2 = (bf16[2048,1024]{1,0:T(8,128)(2,1)S(1)}, bf16[2048,1024]{1,0:T(8,128)(2,1)}, u32[]{:S(2)}) copy-start(bf16[2048,1024]{1,0:T(8,128)(2,1)} %fusion) | copy-start | bytes 12582916
  77.1 29.5 %copy-start.4 = (bf16[256,8,8,128]{3,1,2,0:T(8,128)(2,1)S(1)}, bf16[256,8,8,128]{3,1,2,0:T(8,128)(2,1)}, u32[]{:S(2)}) copy-start(bf16[256,8,8,128]{3,1,2,0:T(8,128)(2,1)} %copy.32) | copy-start | bytes 12582916
  77.2 2.0 collective-permute-start.12
  79.3 8.4 %collective-permute-start.13 = (f32[2,256,128]{2,1,0:T(8,128)S(1)}, f32[2,256,128]{2,1,0:T(8,128)S(1)}, u32[]{:S(2)}, u32[]{:S(2)}) collective-permute-start(f32[2,256,128]{2,1,0:T(8,128)S(1)} %dynamic-slice_bitcast_fusion.8), channel_id=1, source_target_pairs={{0,2},{1,3},{2,0},{3,1},{4,6},{5,7},{6,4},{7,5},{8,10},{9,11},{10,... | collective-permute-start | bytes 786440 | tf_op jit(solution)/shard_map/ppermute | solution.py:63
  87.7 8.5 %collective-permute-start.14 = (f32[1,256,128]{2,1,0:T(8,128)S(1)}, f32[1,256,128]{2,1,0:T(8,128)S(1)}, u32[]{:S(2)}, u32[]{:S(2)}) collective-permute-start(f32[1,256,128]{2,1,0:T(8,128)S(1)} %constant_dynamic-slice_fusion.3), channel_id=1, source_target_pairs={{0,4},{1,5},{2,6},{3,7},{4,0},{5,1},{6,2},{7,3},{8,12},{9,13},{10,... | collective-permute-start | bytes 393224 | tf_op jit(solution)/shard_map/ppermute | solution.py:63
  96.3 4.3 %collective-permute-start.15 = (bf16[256,128]{1,0:T(8,128)(2,1)S(1)}, bf16[256,128]{1,0:T(8,128)(2,1)S(1)}, u32[]{:S(2)}, u32[]{:S(2)}) collective-permute-start(bf16[256,128]{1,0:T(8,128)(2,1)S(1)} %get-tuple-element.6), channel_id=1, source_target_pairs={{0,8},{8,0},{16,24},{24,16},{1,9},{9,1},{17,25},{25,17},{2,10},{10... | collective-permute-start | bytes 196616 | tf_op jit(solution)/shard_map/ppermute | solution.py:77
  100.7 5.0 %collective-permute-start.16 = (bf16[512,128]{1,0:T(8,128)(2,1)S(1)}, bf16[512,128]{1,0:T(8,128)(2,1)S(1)}, u32[]{:S(2)}, u32[]{:S(2)}) collective-permute-start(bf16[512,128]{1,0:T(8,128)(2,1)S(1)} %pad_maximum_fusion.8), channel_id=1, source_target_pairs={{0,16},{8,24},{16,0},{24,8},{1,17},{9,25},{17,1},{25,9},{2,18},{10... | collective-permute-start | bytes 393224 | tf_op jit(solution)/shard_map/ppermute | solution.py:77
  109.0 2.0 collective-permute-start.17
  111.1 8.4 %collective-permute-start.18 = (f32[2,256,128]{2,1,0:T(8,128)S(1)}, f32[2,256,128]{2,1,0:T(8,128)S(1)}, u32[]{:S(2)}, u32[]{:S(2)}) collective-permute-start(f32[2,256,128]{2,1,0:T(8,128)S(1)} %dynamic-slice_bitcast_fusion.7), channel_id=1, source_target_pairs={{0,2},{1,3},{2,0},{3,1},{4,6},{5,7},{6,4},{7,5},{8,10},{9,11},{10,... | collective-permute-start | bytes 786440 | tf_op jit(solution)/shard_map/ppermute | solution.py:63
  119.6 8.5 %collective-permute-start.19 = (f32[1,256,128]{2,1,0:T(8,128)S(1)}, f32[1,256,128]{2,1,0:T(8,128)S(1)}, u32[]{:S(2)}, u32[]{:S(2)}) collective-permute-start(f32[1,256,128]{2,1,0:T(8,128)S(1)} %constant_dynamic-slice_fusion.2), channel_id=1, source_target_pairs={{0,4},{1,5},{2,6},{3,7},{4,0},{5,1},{6,2},{7,3},{8,12},{9,13},{10,... | collective-permute-start | bytes 393224 | tf_op jit(solution)/shard_map/ppermute | solution.py:63
  128.2 4.3 %collective-permute-start.20 = (bf16[256,128]{1,0:T(8,128)(2,1)S(1)}, bf16[256,128]{1,0:T(8,128)(2,1)S(1)}, u32[]{:S(2)}, u32[]{:S(2)}) collective-permute-start(bf16[256,128]{1,0:T(8,128)(2,1)S(1)} %get-tuple-element.4), channel_id=1, source_target_pairs={{0,8},{8,0},{16,24},{24,16},{1,9},{9,1},{17,25},{25,17},{2,10},{10... | collective-permute-start | bytes 196616 | tf_op jit(solution)/shard_map/ppermute | solution.py:77
  132.5 5.0 %collective-permute-start.21 = (bf16[512,128]{1,0:T(8,128)(2,1)S(1)}, bf16[512,128]{1,0:T(8,128)(2,1)S(1)}, u32[]{:S(2)}, u32[]{:S(2)}) collective-permute-start(bf16[512,128]{1,0:T(8,128)(2,1)S(1)} %pad_maximum_fusion.9), channel_id=1, source_target_pairs={{0,16},{8,24},{16,0},{24,8},{1,17},{9,25},{17,1},{25,9},{2,18},{10... | collective-permute-start | bytes 393224 | tf_op jit(solution)/shard_map/ppermute | solution.py:77
  140.9 2.0 collective-permute-start.22
  142.9 8.4 %collective-permute-start.23 = (f32[2,256,128]{2,1,0:T(8,128)S(1)}, f32[2,256,128]{2,1,0:T(8,128)S(1)}, u32[]{:S(2)}, u32[]{:S(2)}) collective-permute-start(f32[2,256,128]{2,1,0:T(8,128)S(1)} %dynamic-slice_bitcast_fusion.6), channel_id=1, source_target_pairs={{0,2},{1,3},{2,0},{3,1},{4,6},{5,7},{6,4},{7,5},{8,10},{9,11},{10,... | collective-permute-start | bytes 786440 | tf_op jit(solution)/shard_map/ppermute | solution.py:63
  151.4 8.5 %collective-permute-start.24 = (f32[1,256,128]{2,1,0:T(8,128)S(1)}, f32[1,256,128]{2,1,0:T(8,128)S(1)}, u32[]{:S(2)}, u32[]{:S(2)}) collective-permute-start(f32[1,256,128]{2,1,0:T(8,128)S(1)} %constant_dynamic-slice_fusion.1), channel_id=1, source_target_pairs={{0,4},{1,5},{2,6},{3,7},{4,0},{5,1},{6,2},{7,3},{8,12},{9,13},{10,... | collective-permute-start | bytes 393224 | tf_op jit(solution)/shard_map/ppermute | solution.py:63
  160.0 4.3 %collective-permute-start.25 = (bf16[256,128]{1,0:T(8,128)(2,1)S(1)}, bf16[256,128]{1,0:T(8,128)(2,1)S(1)}, u32[]{:S(2)}, u32[]{:S(2)}) collective-permute-start(bf16[256,128]{1,0:T(8,128)(2,1)S(1)} %get-tuple-element.2), channel_id=1, source_target_pairs={{0,8},{8,0},{16,24},{24,16},{1,9},{9,1},{17,25},{25,17},{2,10},{10... | collective-permute-start | bytes 196616 | tf_op jit(solution)/shard_map/ppermute | solution.py:77
  164.3 5.0 %collective-permute-start.26 = (bf16[512,128]{1,0:T(8,128)(2,1)S(1)}, bf16[512,128]{1,0:T(8,128)(2,1)S(1)}, u32[]{:S(2)}, u32[]{:S(2)}) collective-permute-start(bf16[512,128]{1,0:T(8,128)(2,1)S(1)} %pad_maximum_fusion.10), channel_id=1, source_target_pairs={{0,16},{8,24},{16,0},{24,8},{1,17},{9,25},{17,1},{25,9},{2,18},{10... | collective-permute-start | bytes 393224 | tf_op jit(solution)/shard_map/ppermute | solution.py:77
  172.7 2.0 collective-permute-start.27
  174.8 8.4 %collective-permute-start.28 = (f32[2,256,128]{2,1,0:T(8,128)S(1)}, f32[2,256,128]{2,1,0:T(8,128)S(1)}, u32[]{:S(2)}, u32[]{:S(2)}) collective-permute-start(f32[2,256,128]{2,1,0:T(8,128)S(1)} %dynamic-slice_bitcast_fusion.5), channel_id=1, source_target_pairs={{0,2},{1,3},{2,0},{3,1},{4,6},{5,7},{6,4},{7,5},{8,10},{9,11},{10,... | collective-permute-start | bytes 786440 | tf_op jit(solution)/shard_map/ppermute | solution.py:63
  183.2 8.5 %collective-permute-start.29 = (f32[1,256,128]{2,1,0:T(8,128)S(1)}, f32[1,256,128]{2,1,0:T(8,128)S(1)}, u32[]{:S(2)}, u32[]{:S(2)}) collective-permute-start(f32[1,256,128]{2,1,0:T(8,128)S(1)} %constant_dynamic-slice_fusion), channel_id=1, source_target_pairs={{0,4},{1,5},{2,6},{3,7},{4,0},{5,1},{6,2},{7,3},{8,12},{9,13},{10,... | collective-permute-start | bytes 393224 | tf_op jit(solution)/shard_map/ppermute | solution.py:63
  192.4 1.4 collective-permute-start.30
  193.8 5.6 %collective-permute-start.31 = (f32[256,128]{0,1:T(8,128)S(1)}, f32[256,128]{0,1:T(8,128)S(1)}, u32[]{:S(2)}, u32[]{:S(2)}) collective-permute-start(f32[256,128]{0,1:T(8,128)S(1)} %fusion.115), channel_id=1, source_target_pairs={{0,2},{1,3},{2,0},{3,1},{4,6},{5,7},{6,4},{7,5},{8,10},{9,11},{10,... | collective-permute-start | bytes 393224 | tf_op jit(solution)/shard_map/ppermute | solution.py:28
  199.5 8.5 %collective-permute-start.32 = (f32[256,128]{0,1:T(8,128)S(1)}, f32[256,128]{0,1:T(8,128)S(1)}, u32[]{:S(2)}, u32[]{:S(2)}) collective-permute-start(f32[256,128]{0,1:T(8,128)S(1)} %add.241), channel_id=1, source_target_pairs={{0,4},{1,5},{2,6},{3,7},{4,0},{5,1},{6,2},{7,3},{8,12},{9,13},{10,... | collective-permute-start | bytes 393224 | tf_op jit(solution)/shard_map/ppermute | solution.py:28
  207.9 5.5 %collective-permute-start.33 = (f32[256,128]{0,1:T(8,128)S(1)}, f32[256,128]{0,1:T(8,128)S(1)}, u32[]{:S(2)}, u32[]{:S(2)}) collective-permute-start(f32[256,128]{0,1:T(8,128)S(1)} %add.242), channel_id=1, source_target_pairs={{0,8},{8,0},{16,24},{24,16},{1,9},{9,1},{17,25},{25,17},{2,10},{10... | collective-permute-start | bytes 393224 | tf_op jit(solution)/shard_map/ppermute | solution.py:28
  213.4 5.0 %collective-permute-start.34 = (f32[256,128]{0,1:T(8,128)S(1)}, f32[256,128]{0,1:T(8,128)S(1)}, u32[]{:S(2)}, u32[]{:S(2)}) collective-permute-start(f32[256,128]{0,1:T(8,128)S(1)} %add.243), channel_id=1, source_target_pairs={{0,16},{8,24},{16,0},{24,8},{1,17},{9,25},{17,1},{25,9},{2,18},{10... | collective-permute-start | bytes 393224 | tf_op jit(solution)/shard_map/ppermute | solution.py:28

commit v13 on v11

--- a/solution.py
+++ b/solution.py
@@ -127,7 +127,7 @@
         partial = lax.dot_general(
             planted_cols, gathered, (((0,), (0,)), ((), ())), preferred_element_type=jnp.float32
         )
-        product = product + split_dot(planted_rows, weights * partial) / node_count
+        product = product + split_dot(planted_rows, weights * partial / node_count)
         summed = halving_scatter_sum(product, "col")
         return degree_scale[:, None] * summed
 

time: 239 us -> 239 us (level)
  no operation moved by 1% of the time
where the time goes in v13:
time: 239 us
  waiting for transfers between devices  144 us (60%)
  matrix products  32.7 us (14%)
  other arithmetic  31 us (13%)
  starting transfers between devices  23.8 us (10%)
  between operations  3.99 us (2%)
  local copies, waits for them, and re-layouts  3.58 us (1%)
    ppermute x15, waiting for transfers between devices, halving_scatter_sum(): blocks = kept + lax.ppermute(sent, axis, pairs)  87.5 us
    ppermute x12, waiting for transfers between devices, doubling_gather(): other = lax.ppermute(result, axis, pairs)  29.7 us
    ppermute x5, waiting for transfers between devices, butterfly_sum(): value = value + lax.ppermute(value, axis, pairs)  23.8 us
    ppermute x12, starting transfers between devices, doubling_gather(): other = lax.ppermute(result, axis, pairs)  13.1 us
    another operation x3, other arithmetic, local(): factor = jnp.linalg.cholesky(gram_matrix)  12.4 us
    dot_general x5, matrix products, operate(): jnp.dot(w_lo, gathered, preferred_element_type=jnp.float32)  10.9 us
    another operation x2, other arithmetic, local(): lax.linalg.triangular_solve(factor, current, left_side=False, lower=True,...  10.6 us
    dot_general x1, matrix products, local(): jnp.einsum('rst,rsab->ratb', onehot, tiles, preferred_element_type=jnp.fl...  8.2 us
  transfers between devices with their start and end apart: 35, of which 29 were waited for; matrix products, arithmetic and copies ran while one was open for 8% of the time, Pallas kernels for 0%

profile of v13, /device:TPU:0, one launch (start us, length us, event | category | flops | bytes accessed | tf_op | source)
XLA Modules:
  0.0 238.7 jit_solution(7340109510138828966)
XLA Ops:
  1.6 3.0 %collective-permute-start = (bf16[256,128]{1,0:T(8,128)(2,1)S(1)}, bf16[256,128]{1,0:T(8,128)(2,1)S(1)}, u32[]{:S(2)}, u32[]{:S(2)}) collective-permute-start(bf16[256,128]{1,0:T(8,128)(2,1)S(1)} %multiply_convert_fusion.4), channel_id=1, source_target_pairs={{0,8},{8,0},{16,24},{24,16},{1,9},{9,1},{17,25},{25,17},{2,10},{10... | collective-permute-start | bytes 196616 | tf_op jit(solution)/shard_map/ppermute | solution.py:77
  4.8 3.0 %collective-permute-start.2 = (bf16[1,256,128]{2,1,0:T(8,128)(2,1)}, bf16[1,256,128]{2,1,0:T(8,128)(2,1)S(1)}, u32[]{:S(2)}, u32[]{:S(2)}) collective-permute-start(bf16[1,256,128]{2,1,0:T(8,128)(2,1)} %bitcast.186), channel_id=1, source_target_pairs={{0,4},{1,5},{2,6},{3,7},{4,0},{5,1},{6,2},{7,3},{8,12},{9,13},{10,... | collective-permute-start | bytes 196616 | tf_op jit(solution)/shard_map/ppermute | solution.py:95
  7.8 8.2 %fusion.1 = f32[16,8,128,128]{3,1,2,0:T(8,128)S(1)} fusion(bf16[16,16,128,128]{3,2,1,0:T(8,128)(2,1)} %param.7, s32[16,16]{1,0:T(8,128)} %param.8), kind=kOutput, calls=%fused_computation.3 | convolution fusion | flops 67110912 | bytes 16778240 | tf_op jit(solution)/shard_map/rst,rsab->ratb/dot_general | solution.py:115
  16.0 5.3 %fusion = (bf16[2048,1024]{1,0:T(8,128)(2,1)}, bf16[2048,1024]{1,0:T(8,128)(2,1)}) fusion(f32[256,8,8,128]{3,2,1,0:T(8,128)S(1)} %bitcast.164), kind=kLoop, calls=%fused_computation.2 | loop fusion | flops 6291456 | bytes 16777216 | tf_op jit(solution)/shard_map/convert_element_type | solution.py:11
  21.4 1.6 collective-permute-start.1
  23.1 1.6 collective-permute-start.3
  25.3 2.8 %collective-permute-done.3 = bf16[2,256,128]{2,1,0:T(8,128)(2,1)S(1)} collective-permute-done((bf16[2,256,128]{2,1,0:T(8,128)(2,1)S(1)}, bf16[2,256,128]{2,1,0:T(8,128)(2,1)S(1)}, u32[]{:S(2)}, u32[]{:S(2)}) %collective-permute-start.3) | collective-permute-done | bytes 131104 | tf_op jit(solution)/shard_map/ppermute | solution.py:95
  28.3 3.5 %fusion.34 = f32[2048,128]{1,0:T(8,128)S(1)} fusion(bf16[2048,1024]{1,0:T(8,128)(2,1)} %get-tuple-element.10, bf16[512,128]{1,0:T(8,128)(2,1)S(1)} %get-tuple-element.25, bf16[512,128]{1,0:T(8,128)(2,1)S(1)} %get-tuple-element.24), kind=kOutput, calls=%fused_computation.113 | convolution fusion | flops 537395200 | bytes 5505024 | tf_op jit(solution)/shard_map/dot_general | solution.py:126
  34.0 1.3 fusion.7
  35.9 1.5 collective-permute-done.7
  37.6 1.6 collective-permute-start.8
  39.2 7.0 %collective-permute-done.8 = f32[2,256,128]{2,1,0:T(8,128)S(1)} collective-permute-done((f32[2,256,128]{2,1,0:T(8,128)S(1)}, f32[2,256,128]{2,1,0:T(8,128)S(1)}, u32[]{:S(2)}, u32[]{:S(2)}) %collective-permute-start.8) | collective-permute-done | bytes 262176 | tf_op jit(solution)/shard_map/ppermute | solution.py:63
  49.9 5.1 %collective-permute-done.9 = f32[1,256,128]{2,1,0:T(8,128)S(1)} collective-permute-done((f32[1,256,128]{2,1,0:T(8,128)S(1)}, f32[1,256,128]{2,1,0:T(8,128)S(1)}, u32[]{:S(2)}, u32[]{:S(2)}) %collective-permute-start.9) | collective-permute-done | bytes 131104 | tf_op jit(solution)/shard_map/ppermute | solution.py:63
  55.1 1.6 collective-permute-start.10
  56.7 2.8 %collective-permute-done.10 = bf16[256,128]{1,0:T(8,128)(2,1)S(1)} collective-permute-done((bf16[256,128]{1,0:T(8,128)(2,1)S(1)}, bf16[256,128]{1,0:T(8,128)(2,1)S(1)}, u32[]{:S(2)}, u32[]{:S(2)}) %collective-permute-start.10) | collective-permute-done | bytes 65568 | tf_op jit(solution)/shard_map/ppermute | solution.py:77
  59.8 4.7 %collective-permute-done.11 = bf16[512,128]{1,0:T(8,128)(2,1)S(1)} collective-permute-done((bf16[512,128]{1,0:T(8,128)(2,1)S(1)}, bf16[512,128]{1,0:T(8,128)(2,1)S(1)}, u32[]{:S(2)}, u32[]{:S(2)}) %collective-permute-start.11) | collective-permute-done | bytes 131104 | tf_op jit(solution)/shard_map/ppermute | solution.py:77
  64.5 3.4 %fusion.33 = f32[2048,128]{1,0:T(8,128)S(1)} fusion(bf16[2048,1024]{1,0:T(8,128)(2,1)} %get-tuple-element.10, bf16[512,128]{1,0:T(8,128)(2,1)S(1)} %get-tuple-element.21, bf16[512,128]{1,0:T(8,128)(2,1)S(1)} %get-tuple-element.20), kind=kOutput, calls=%fused_computation.112 | convolution fusion | flops 537395200 | bytes 5505024 | tf_op jit(solution)/shard_map/dot_general | solution.py:126
  68.9 1.3 copy-done.1
  71.6 1.9 collective-permute-done.12
  73.7 8.3 %collective-permute-done.13 = f32[2,256,128]{2,1,0:T(8,128)S(1)} collective-permute-done((f32[2,256,128]{2,1,0:T(8,128)S(1)}, f32[2,256,128]{2,1,0:T(8,128)S(1)}, u32[]{:S(2)}, u32[]{:S(2)}) %collective-permute-start.13) | collective-permute-done | bytes 262176 | tf_op jit(solution)/shard_map/ppermute | solution.py:63
  82.2 8.3 %collective-permute-done.14 = f32[1,256,128]{2,1,0:T(8,128)S(1)} collective-permute-done((f32[1,256,128]{2,1,0:T(8,128)S(1)}, f32[1,256,128]{2,1,0:T(8,128)S(1)}, u32[]{:S(2)}, u32[]{:S(2)}) %collective-permute-start.14) | collective-permute-done | bytes 131104 | tf_op jit(solution)/shard_map/ppermute | solution.py:63
  90.6 1.6 collective-permute-start.15
  92.2 2.8 %collective-permute-done.15 = bf16[256,128]{1,0:T(8,128)(2,1)S(1)} collective-permute-done((bf16[256,128]{1,0:T(8,128)(2,1)S(1)}, bf16[256,128]{1,0:T(8,128)(2,1)S(1)}, u32[]{:S(2)}, u32[]{:S(2)}) %collective-permute-start.15) | collective-permute-done | bytes 65568 | tf_op jit(solution)/shard_map/ppermute | solution.py:77
  95.4 4.7 %collective-permute-done.16 = bf16[512,128]{1,0:T(8,128)(2,1)S(1)} collective-permute-done((bf16[512,128]{1,0:T(8,128)(2,1)S(1)}, bf16[512,128]{1,0:T(8,128)(2,1)S(1)}, u32[]{:S(2)}, u32[]{:S(2)}) %collective-permute-start.16) | collective-permute-done | bytes 131104 | tf_op jit(solution)/shard_map/ppermute | solution.py:77
  103.7 1.9 collective-permute-done.17
  105.7 8.3 %collective-permute-done.18 = f32[2,256,128]{2,1,0:T(8,128)S(1)} collective-permute-done((f32[2,256,128]{2,1,0:T(8,128)S(1)}, f32[2,256,128]{2,1,0:T(8,128)S(1)}, u32[]{:S(2)}, u32[]{:S(2)}) %collective-permute-start.18) | collective-permute-done | bytes 262176 | tf_op jit(solution)/shard_map/ppermute | solution.py:63
  114.3 8.3 %collective-permute-done.19 = f32[1,256,128]{2,1,0:T(8,128)S(1)} collective-permute-done((f32[1,256,128]{2,1,0:T(8,128)S(1)}, f32[1,256,128]{2,1,0:T(8,128)S(1)}, u32[]{:S(2)}, u32[]{:S(2)}) %collective-permute-start.19) | collective-permute-done | bytes 131104 | tf_op jit(solution)/shard_map/ppermute | solution.py:63
  122.7 1.6 collective-permute-start.20
  124.3 2.8 %collective-permute-done.20 = bf16[256,128]{1,0:T(8,128)(2,1)S(1)} collective-permute-done((bf16[256,128]{1,0:T(8,128)(2,1)S(1)}, bf16[256,128]{1,0:T(8,128)(2,1)S(1)}, u32[]{:S(2)}, u32[]{:S(2)}) %collective-permute-start.20) | collective-permute-done | bytes 65568 | tf_op jit(solution)/shard_map/ppermute | solution.py:77
  127.4 4.7 %collective-permute-done.21 = bf16[512,128]{1,0:T(8,128)(2,1)S(1)} collective-permute-done((bf16[512,128]{1,0:T(8,128)(2,1)S(1)}, bf16[512,128]{1,0:T(8,128)(2,1)S(1)}, u32[]{:S(2)}, u32[]{:S(2)}) %collective-permute-start.21) | collective-permute-done | bytes 131104 | tf_op jit(solution)/shard_map/ppermute | solution.py:77
  132.2 1.5 fusion.31
  136.0 1.9 collective-permute-done.22
  138.0 8.3 %collective-permute-done.23 = f32[2,256,128]{2,1,0:T(8,128)S(1)} collective-permute-done((f32[2,256,128]{2,1,0:T(8,128)S(1)}, f32[2,256,128]{2,1,0:T(8,128)S(1)}, u32[]{:S(2)}, u32[]{:S(2)}) %collective-permute-start.23) | collective-permute-done | bytes 262176 | tf_op jit(solution)/shard_map/ppermute | solution.py:63
  146.6 8.3 %collective-permute-done.24 = f32[1,256,128]{2,1,0:T(8,128)S(1)} collective-permute-done((f32[1,256,128]{2,1,0:T(8,128)S(1)}, f32[1,256,128]{2,1,0:T(8,128)S(1)}, u32[]{:S(2)}, u32[]{:S(2)}) %collective-permute-start.24) | collective-permute-done | bytes 131104 | tf_op jit(solution)/shard_map/ppermute | solution.py:63
  155.0 1.6 collective-permute-start.25
  156.6 2.8 %collective-permute-done.25 = bf16[256,128]{1,0:T(8,128)(2,1)S(1)} collective-permute-done((bf16[256,128]{1,0:T(8,128)(2,1)S(1)}, bf16[256,128]{1,0:T(8,128)(2,1)S(1)}, u32[]{:S(2)}, u32[]{:S(2)}) %collective-permute-start.25) | collective-permute-done | bytes 65568 | tf_op jit(solution)/shard_map/ppermute | solution.py:77
  159.7 4.7 %collective-permute-done.26 = bf16[512,128]{1,0:T(8,128)(2,1)S(1)} collective-permute-done((bf16[512,128]{1,0:T(8,128)(2,1)S(1)}, bf16[512,128]{1,0:T(8,128)(2,1)S(1)}, u32[]{:S(2)}, u32[]{:S(2)}) %collective-permute-start.26) | collective-permute-done | bytes 131104 | tf_op jit(solution)/shard_map/ppermute | solution.py:77
  168.0 1.9 collective-permute-done.27
  170.1 8.3 %collective-permute-done.28 = f32[2,256,128]{2,1,0:T(8,128)S(1)} collective-permute-done((f32[2,256,128]{2,1,0:T(8,128)S(1)}, f32[2,256,128]{2,1,0:T(8,128)S(1)}, u32[]{:S(2)}, u32[]{:S(2)}) %collective-permute-start.28) | collective-permute-done | bytes 262176 | tf_op jit(solution)/shard_map/ppermute | solution.py:63
  179.0 7.9 %collective-permute-done.29 = f32[1,256,128]{2,1,0:T(8,128)S(1)} collective-permute-done((f32[1,256,128]{2,1,0:T(8,128)S(1)}, f32[1,256,128]{2,1,0:T(8,128)S(1)}, u32[]{:S(2)}, u32[]{:S(2)}) %collective-permute-start.29) | collective-permute-done | bytes 131104 | tf_op jit(solution)/shard_map/ppermute | solution.py:63
  187.5 1.3 collective-permute-done.30
  188.9 5.5 %collective-permute-done.31 = f32[256,128]{0,1:T(8,128)S(1)} collective-permute-done((f32[256,128]{0,1:T(8,128)S(1)}, f32[256,128]{0,1:T(8,128)S(1)}, u32[]{:S(2)}, u32[]{:S(2)}) %collective-permute-start.31) | collective-permute-done | bytes 131104 | tf_op jit(solution)/shard_map/ppermute | solution.py:28
  194.6 8.3 %collective-permute-done.32 = f32[256,128]{0,1:T(8,128)S(1)} collective-permute-done((f32[256,128]{0,1:T(8,128)S(1)}, f32[256,128]{0,1:T(8,128)S(1)}, u32[]{:S(2)}, u32[]{:S(2)}) %collective-permute-start.32) | collective-permute-done | bytes 131104 | tf_op jit(solution)/shard_map/ppermute | solution.py:28
  203.0 1.6 collective-permute-start.33
  204.6 3.9 %collective-permute-done.33 = f32[256,128]{0,1:T(8,128)S(1)} collective-permute-done((f32[256,128]{0,1:T(8,128)S(1)}, f32[256,128]{0,1:T(8,128)S(1)}, u32[]{:S(2)}, u32[]{:S(2)}) %collective-permute-start.33) | collective-permute-done | bytes 131104 | tf_op jit(solution)/shard_map/ppermute | solution.py:28
  208.8 4.7 %collective-permute-done.34 = f32[256,128]{0,1:T(8,128)S(1)} collective-permute-done((f32[256,128]{0,1:T(8,128)S(1)}, f32[256,128]{0,1:T(8,128)S(1)}, u32[]{:S(2)}, u32[]{:S(2)}) %collective-permute-start.34) | collective-permute-done | bytes 131104 | tf_op jit(solution)/shard_map/ppermute | solution.py:28
  213.7 11.7 %cholesky.16 = f32[128,128]{1,0:T(8,128)S(1)} custom-call(f32[128,128]{1,0:T(8,128)S(1)} %fusion.42), custom_call_target="Cholesky" | custom-call | tf_op jit(solution)/shard_map/jit(cholesky)/cholesky | solution.py:149
  226.7 9.9 %custom-call.10 = f32[1,128,128]{1,2,0:T(8,128)S(1)} custom-call(f32[1,128,128]{2,1,0:T(8,128)S(1)} %fusion.35), custom_call_target="InvertDiagBlocksLowerTriangular" | custom-call | tf_op jit(solution)/shard_map/triangular_solve | solution.py:150
  (140 shorter events, 26.1 us)
Async XLA Ops:
  1.6 19.6 %collective-permute-start = (bf16[256,128]{1,0:T(8,128)(2,1)S(1)}, bf16[256,128]{1,0:T(8,128)(2,1)S(1)}, u32[]{:S(2)}, u32[]{:S(2)}) collective-permute-start(bf16[256,128]{1,0:T(8,128)(2,1)S(1)} %multiply_convert_fusion.4), channel_id=1, source_target_pairs={{0,8},{8,0},{16,24},{24,16},{1,9},{9,1},{17,25},{25,17},{2,10},{10... | collective-permute-start | bytes 196616 | tf_op jit(solution)/shard_map/ppermute | solution.py:77
  4.7 20.0 %collective-permute-start.5 = (bf16[256,128]{1,0:T(8,128)(2,1)}, bf16[256,128]{1,0:T(8,128)(2,1)S(1)}, u32[]{:S(2)}, u32[]{:S(2)}) collective-permute-start(bf16[256,128]{1,0:T(8,128)(2,1)} %param.11), channel_id=1, source_target_pairs={{0,8},{8,0},{16,24},{24,16},{1,9},{9,1},{17,25},{25,17},{2,10},{10... | collective-permute-start | bytes 196616 | tf_op jit(solution)/shard_map/ppermute | solution.py:77
  4.8 18.3 %collective-permute-start.2 = (bf16[1,256,128]{2,1,0:T(8,128)(2,1)}, bf16[1,256,128]{2,1,0:T(8,128)(2,1)S(1)}, u32[]{:S(2)}, u32[]{:S(2)}) collective-permute-start(bf16[1,256,128]{2,1,0:T(8,128)(2,1)} %bitcast.186), channel_id=1, source_target_pairs={{0,4},{1,5},{2,6},{3,7},{4,0},{5,1},{6,2},{7,3},{8,12},{9,13},{10,... | collective-permute-start | bytes 196616 | tf_op jit(solution)/shard_map/ppermute | solution.py:95
  16.0 5.3 %copy-start.3 = (f32[256,128]{1,0:T(8,128)S(1)}, f32[256,128]{1,0:T(8,128)}, u32[]{:S(2)}) copy-start(f32[256,128]{1,0:T(8,128)} %param.10) | copy-start | bytes 393220
  16.0 5.3 %copy-start.5 = (f32[256]{0:T(256)S(1)}, f32[256]{0:T(256)}, u32[]{:S(2)}) copy-start(f32[256]{0:T(256)} %param.9) | copy-start | bytes 3076
  16.0 7.0 %copy-start.4 = (bf16[256,128]{1,0:T(8,128)(2,1)S(1)}, bf16[256,128]{1,0:T(8,128)(2,1)}, u32[]{:S(2)}) copy-start(bf16[256,128]{1,0:T(8,128)(2,1)} %param.11) | copy-start | bytes 196612
  21.4 6.8 %collective-permute-start.1 = (bf16[512,128]{1,0:T(8,128)(2,1)S(1)}, bf16[512,128]{1,0:T(8,128)(2,1)S(1)}, u32[]{:S(2)}, u32[]{:S(2)}) collective-permute-start(bf16[512,128]{1,0:T(8,128)(2,1)S(1)} %pad_maximum_fusion.8), channel_id=1, source_target_pairs={{0,16},{8,24},{16,0},{24,8},{1,17},{9,25},{17,1},{25,9},{2,18},{10... | collective-permute-start | bytes 393224 | tf_op jit(solution)/shard_map/ppermute | solution.py:77
  23.1 5.0 %collective-permute-start.3 = (bf16[2,256,128]{2,1,0:T(8,128)(2,1)S(1)}, bf16[2,256,128]{2,1,0:T(8,128)(2,1)S(1)}, u32[]{:S(2)}, u32[]{:S(2)}) collective-permute-start(bf16[2,256,128]{2,1,0:T(8,128)(2,1)S(1)} %pad_maximum_fusion.9), channel_id=1, source_target_pairs={{0,2},{1,3},{2,0},{3,1},{4,6},{5,7},{6,4},{7,5},{8,10},{9,11},{10,... | collective-permute-start | bytes 393224 | tf_op jit(solution)/shard_map/ppermute | solution.py:95
  24.7 7.0 %collective-permute-start.6 = (bf16[512,128]{1,0:T(8,128)(2,1)S(1)}, bf16[512,128]{1,0:T(8,128)(2,1)S(1)}, u32[]{:S(2)}, u32[]{:S(2)}) collective-permute-start(bf16[512,128]{1,0:T(8,128)(2,1)S(1)} %pad_maximum_fusion.10), channel_id=1, source_target_pairs={{0,16},{8,24},{16,0},{24,8},{1,17},{9,25},{17,1},{25,9},{2,18},{10... | collective-permute-start | bytes 393224 | tf_op jit(solution)/shard_map/ppermute | solution.py:77
  28.1 3.7 %copy-start.7 = (f32[128]{0:T(128)S(1)}, f32[128]{0:T(128)}, u32[]{:S(2)}) copy-start(f32[128]{0:T(128)} %param.12) | copy-start | bytes 1540
  28.2 4.0 %collective-permute-start.4 = (bf16[4,256,128]{2,1,0:T(8,128)(2,1)S(1)}, bf16[4,256,128]{2,1,0:T(8,128)(2,1)S(1)}, u32[]{:S(2)}, u32[]{:S(2)}) collective-permute-start(bf16[4,256,128]{2,1,0:T(8,128)(2,1)S(1)} %pad_maximum_fusion.2), channel_id=1, source_target_pairs={{0,1},{1,0},{2,3},{3,2},{4,5},{5,4},{6,7},{7,6},{8,9},{9,8},{10,11... | collective-permute-start | bytes 786440 | tf_op jit(solution)/shard_map/ppermute | solution.py:95
  31.9 2.2 copy-start
  35.3 11.4 %copy-start.6 = (f32[2]{0:T(128)S(1)}, f32[2]{0:T(128)}, u32[]{:S(2)}) copy-start(f32[2]{0:T(128)} %param.13) | copy-start | bytes 28
  35.4 2.1 collective-permute-start.7
  37.6 8.7 %collective-permute-start.8 = (f32[2,256,128]{2,1,0:T(8,128)S(1)}, f32[2,256,128]{2,1,0:T(8,128)S(1)}, u32[]{:S(2)}, u32[]{:S(2)}) collective-permute-start(f32[2,256,128]{2,1,0:T(8,128)S(1)} %dynamic-slice_bitcast_fusion.9), channel_id=1, source_target_pairs={{0,2},{1,3},{2,0},{3,1},{4,6},{5,7},{6,4},{7,5},{8,10},{9,11},{10,... | collective-permute-start | bytes 786440 | tf_op jit(solution)/shard_map/ppermute | solution.py:63
  46.3 8.7 %collective-permute-start.9 = (f32[1,256,128]{2,1,0:T(8,128)S(1)}, f32[1,256,128]{2,1,0:T(8,128)S(1)}, u32[]{:S(2)}, u32[]{:S(2)}) collective-permute-start(f32[1,256,128]{2,1,0:T(8,128)S(1)} %constant_dynamic-slice_fusion.4), channel_id=1, source_target_pairs={{0,4},{1,5},{2,6},{3,7},{4,0},{5,1},{6,2},{7,3},{8,12},{9,13},{10,... | collective-permute-start | bytes 393224 | tf_op jit(solution)/shard_map/ppermute | solution.py:63
  55.1 4.3 %collective-permute-start.10 = (bf16[256,128]{1,0:T(8,128)(2,1)S(1)}, bf16[256,128]{1,0:T(8,128)(2,1)S(1)}, u32[]{:S(2)}, u32[]{:S(2)}) collective-permute-start(bf16[256,128]{1,0:T(8,128)(2,1)S(1)} %get-tuple-element.8), channel_id=1, source_target_pairs={{0,8},{8,0},{16,24},{24,16},{1,9},{9,1},{17,25},{25,17},{2,10},{10... | collective-permute-start | bytes 196616 | tf_op jit(solution)/shard_map/ppermute | solution.py:77
  59.4 5.0 %collective-permute-start.11 = (bf16[512,128]{1,0:T(8,128)(2,1)S(1)}, bf16[512,128]{1,0:T(8,128)(2,1)S(1)}, u32[]{:S(2)}, u32[]{:S(2)}) collective-permute-start(bf16[512,128]{1,0:T(8,128)(2,1)S(1)} %pad_maximum_fusion.11), channel_id=1, source_target_pairs={{0,16},{8,24},{16,0},{24,8},{1,17},{9,25},{17,1},{25,9},{2,18},{10... | collective-permute-start | bytes 393224 | tf_op jit(solution)/shard_map/ppermute | solution.py:77
  68.0 2.2 copy-start.1
  71.5 28.6 %copy-start.2 = (bf16[2048,1024]{1,0:T(8,128)(2,1)S(1)}, bf16[2048,1024]{1,0:T(8,128)(2,1)}, u32[]{:S(2)}) copy-start(bf16[2048,1024]{1,0:T(8,128)(2,1)} %get-tuple-element.10) | copy-start | bytes 12582916
  71.5 2.0 collective-permute-start.12
  73.6 8.4 %collective-permute-start.13 = (f32[2,256,128]{2,1,0:T(8,128)S(1)}, f32[2,256,128]{2,1,0:T(8,128)S(1)}, u32[]{:S(2)}, u32[]{:S(2)}) collective-permute-start(f32[2,256,128]{2,1,0:T(8,128)S(1)} %dynamic-slice_bitcast_fusion.8), channel_id=1, source_target_pairs={{0,2},{1,3},{2,0},{3,1},{4,6},{5,7},{6,4},{7,5},{8,10},{9,11},{10,... | collective-permute-start | bytes 786440 | tf_op jit(solution)/shard_map/ppermute | solution.py:63
  82.1 8.5 %collective-permute-start.14 = (f32[1,256,128]{2,1,0:T(8,128)S(1)}, f32[1,256,128]{2,1,0:T(8,128)S(1)}, u32[]{:S(2)}, u32[]{:S(2)}) collective-permute-start(f32[1,256,128]{2,1,0:T(8,128)S(1)} %constant_dynamic-slice_fusion.3), channel_id=1, source_target_pairs={{0,4},{1,5},{2,6},{3,7},{4,0},{5,1},{6,2},{7,3},{8,12},{9,13},{10,... | collective-permute-start | bytes 393224 | tf_op jit(solution)/shard_map/ppermute | solution.py:63
  90.6 4.3 %collective-permute-start.15 = (bf16[256,128]{1,0:T(8,128)(2,1)S(1)}, bf16[256,128]{1,0:T(8,128)(2,1)S(1)}, u32[]{:S(2)}, u32[]{:S(2)}) collective-permute-start(bf16[256,128]{1,0:T(8,128)(2,1)S(1)} %get-tuple-element.6), channel_id=1, source_target_pairs={{0,8},{8,0},{16,24},{24,16},{1,9},{9,1},{17,25},{25,17},{2,10},{10... | collective-permute-start | bytes 196616 | tf_op jit(solution)/shard_map/ppermute | solution.py:77
  95.0 5.0 %collective-permute-start.16 = (bf16[512,128]{1,0:T(8,128)(2,1)S(1)}, bf16[512,128]{1,0:T(8,128)(2,1)S(1)}, u32[]{:S(2)}, u32[]{:S(2)}) collective-permute-start(bf16[512,128]{1,0:T(8,128)(2,1)S(1)} %pad_maximum_fusion.12), channel_id=1, source_target_pairs={{0,16},{8,24},{16,0},{24,8},{1,17},{9,25},{17,1},{25,9},{2,18},{10... | collective-permute-start | bytes 393224 | tf_op jit(solution)/shard_map/ppermute | solution.py:77
  103.6 2.0 collective-permute-start.17
  105.7 8.4 %collective-permute-start.18 = (f32[2,256,128]{2,1,0:T(8,128)S(1)}, f32[2,256,128]{2,1,0:T(8,128)S(1)}, u32[]{:S(2)}, u32[]{:S(2)}) collective-permute-start(f32[2,256,128]{2,1,0:T(8,128)S(1)} %dynamic-slice_bitcast_fusion.7), channel_id=1, source_target_pairs={{0,2},{1,3},{2,0},{3,1},{4,6},{5,7},{6,4},{7,5},{8,10},{9,11},{10,... | collective-permute-start | bytes 786440 | tf_op jit(solution)/shard_map/ppermute | solution.py:63
  114.1 8.5 %collective-permute-start.19 = (f32[1,256,128]{2,1,0:T(8,128)S(1)}, f32[1,256,128]{2,1,0:T(8,128)S(1)}, u32[]{:S(2)}, u32[]{:S(2)}) collective-permute-start(f32[1,256,128]{2,1,0:T(8,128)S(1)} %constant_dynamic-slice_fusion.2), channel_id=1, source_target_pairs={{0,4},{1,5},{2,6},{3,7},{4,0},{5,1},{6,2},{7,3},{8,12},{9,13},{10,... | collective-permute-start | bytes 393224 | tf_op jit(solution)/shard_map/ppermute | solution.py:63
  122.7 4.3 %collective-permute-start.20 = (bf16[256,128]{1,0:T(8,128)(2,1)S(1)}, bf16[256,128]{1,0:T(8,128)(2,1)S(1)}, u32[]{:S(2)}, u32[]{:S(2)}) collective-permute-start(bf16[256,128]{1,0:T(8,128)(2,1)S(1)} %get-tuple-element.4), channel_id=1, source_target_pairs={{0,8},{8,0},{16,24},{24,16},{1,9},{9,1},{17,25},{25,17},{2,10},{10... | collective-permute-start | bytes 196616 | tf_op jit(solution)/shard_map/ppermute | solution.py:77
  127.1 5.0 %collective-permute-start.21 = (bf16[512,128]{1,0:T(8,128)(2,1)S(1)}, bf16[512,128]{1,0:T(8,128)(2,1)S(1)}, u32[]{:S(2)}, u32[]{:S(2)}) collective-permute-start(bf16[512,128]{1,0:T(8,128)(2,1)S(1)} %pad_maximum_fusion.13), channel_id=1, source_target_pairs={{0,16},{8,24},{16,0},{24,8},{1,17},{9,25},{17,1},{25,9},{2,18},{10... | collective-permute-start | bytes 393224 | tf_op jit(solution)/shard_map/ppermute | solution.py:77
  135.9 2.0 collective-permute-start.22
  137.9 8.4 %collective-permute-start.23 = (f32[2,256,128]{2,1,0:T(8,128)S(1)}, f32[2,256,128]{2,1,0:T(8,128)S(1)}, u32[]{:S(2)}, u32[]{:S(2)}) collective-permute-start(f32[2,256,128]{2,1,0:T(8,128)S(1)} %dynamic-slice_bitcast_fusion.6), channel_id=1, source_target_pairs={{0,2},{1,3},{2,0},{3,1},{4,6},{5,7},{6,4},{7,5},{8,10},{9,11},{10,... | collective-permute-start | bytes 786440 | tf_op jit(solution)/shard_map/ppermute | solution.py:63
  146.4 8.5 %collective-permute-start.24 = (f32[1,256,128]{2,1,0:T(8,128)S(1)}, f32[1,256,128]{2,1,0:T(8,128)S(1)}, u32[]{:S(2)}, u32[]{:S(2)}) collective-permute-start(f32[1,256,128]{2,1,0:T(8,128)S(1)} %constant_dynamic-slice_fusion.1), channel_id=1, source_target_pairs={{0,4},{1,5},{2,6},{3,7},{4,0},{5,1},{6,2},{7,3},{8,12},{9,13},{10,... | collective-permute-start | bytes 393224 | tf_op jit(solution)/shard_map/ppermute | solution.py:63
  155.0 4.3 %collective-permute-start.25 = (bf16[256,128]{1,0:T(8,128)(2,1)S(1)}, bf16[256,128]{1,0:T(8,128)(2,1)S(1)}, u32[]{:S(2)}, u32[]{:S(2)}) collective-permute-start(bf16[256,128]{1,0:T(8,128)(2,1)S(1)} %get-tuple-element.2), channel_id=1, source_target_pairs={{0,8},{8,0},{16,24},{24,16},{1,9},{9,1},{17,25},{25,17},{2,10},{10... | collective-permute-start | bytes 196616 | tf_op jit(solution)/shard_map/ppermute | solution.py:77
  159.4 5.0 %collective-permute-start.26 = (bf16[512,128]{1,0:T(8,128)(2,1)S(1)}, bf16[512,128]{1,0:T(8,128)(2,1)S(1)}, u32[]{:S(2)}, u32[]{:S(2)}) collective-permute-start(bf16[512,128]{1,0:T(8,128)(2,1)S(1)} %pad_maximum_fusion.14), channel_id=1, source_target_pairs={{0,16},{8,24},{16,0},{24,8},{1,17},{9,25},{17,1},{25,9},{2,18},{10... | collective-permute-start | bytes 393224 | tf_op jit(solution)/shard_map/ppermute | solution.py:77
  167.9 2.0 collective-permute-start.27
  170.0 8.4 %collective-permute-start.28 = (f32[2,256,128]{2,1,0:T(8,128)S(1)}, f32[2,256,128]{2,1,0:T(8,128)S(1)}, u32[]{:S(2)}, u32[]{:S(2)}) collective-permute-start(f32[2,256,128]{2,1,0:T(8,128)S(1)} %dynamic-slice_bitcast_fusion.5), channel_id=1, source_target_pairs={{0,2},{1,3},{2,0},{3,1},{4,6},{5,7},{6,4},{7,5},{8,10},{9,11},{10,... | collective-permute-start | bytes 786440 | tf_op jit(solution)/shard_map/ppermute | solution.py:63
  178.5 8.5 %collective-permute-start.29 = (f32[1,256,128]{2,1,0:T(8,128)S(1)}, f32[1,256,128]{2,1,0:T(8,128)S(1)}, u32[]{:S(2)}, u32[]{:S(2)}) collective-permute-start(f32[1,256,128]{2,1,0:T(8,128)S(1)} %constant_dynamic-slice_fusion), channel_id=1, source_target_pairs={{0,4},{1,5},{2,6},{3,7},{4,0},{5,1},{6,2},{7,3},{8,12},{9,13},{10,... | collective-permute-start | bytes 393224 | tf_op jit(solution)/shard_map/ppermute | solution.py:63
  187.4 1.4 collective-permute-start.30
  188.8 5.6 %collective-permute-start.31 = (f32[256,128]{0,1:T(8,128)S(1)}, f32[256,128]{0,1:T(8,128)S(1)}, u32[]{:S(2)}, u32[]{:S(2)}) collective-permute-start(f32[256,128]{0,1:T(8,128)S(1)} %fusion.80), channel_id=1, source_target_pairs={{0,2},{1,3},{2,0},{3,1},{4,6},{5,7},{6,4},{7,5},{8,10},{9,11},{10,... | collective-permute-start | bytes 393224 | tf_op jit(solution)/shard_map/ppermute | solution.py:28
  194.5 8.5 %collective-permute-start.32 = (f32[256,128]{0,1:T(8,128)S(1)}, f32[256,128]{0,1:T(8,128)S(1)}, u32[]{:S(2)}, u32[]{:S(2)}) collective-permute-start(f32[256,128]{0,1:T(8,128)S(1)} %add.261), channel_id=1, source_target_pairs={{0,4},{1,5},{2,6},{3,7},{4,0},{5,1},{6,2},{7,3},{8,12},{9,13},{10,... | collective-permute-start | bytes 393224 | tf_op jit(solution)/shard_map/ppermute | solution.py:28
  203.0 5.5 %collective-permute-start.33 = (f32[256,128]{0,1:T(8,128)S(1)}, f32[256,128]{0,1:T(8,128)S(1)}, u32[]{:S(2)}, u32[]{:S(2)}) collective-permute-start(f32[256,128]{0,1:T(8,128)S(1)} %add.262), channel_id=1, source_target_pairs={{0,8},{8,0},{16,24},{24,16},{1,9},{9,1},{17,25},{25,17},{2,10},{10... | collective-permute-start | bytes 393224 | tf_op jit(solution)/shard_map/ppermute | solution.py:28
  208.5 5.0 %collective-permute-start.34 = (f32[256,128]{0,1:T(8,128)S(1)}, f32[256,128]{0,1:T(8,128)S(1)}, u32[]{:S(2)}, u32[]{:S(2)}) collective-permute-start(f32[256,128]{0,1:T(8,128)S(1)} %add.263), channel_id=1, source_target_pairs={{0,16},{8,24},{16,0},{24,8},{1,17},{9,25},{17,1},{25,9},{2,18},{10... | collective-permute-start | bytes 393224 | tf_op jit(solution)/shard_map/ppermute | solution.py:28

commit v14 on v13

--- a/solution.py
+++ b/solution.py
@@ -139,11 +139,10 @@
         applied = operate(current)
         following = 2.0 * (applied - center * current) / half_width - previous
         previous, current = (current, following)
-    local_gram = jnp.dot(current.T, current, precision=lax.Precision.HIGHEST)
     applied = operate(current)
-    local_rayleigh = jnp.dot(current.T, applied, precision=lax.Precision.HIGHEST)
-    totals = all_sum(jnp.concatenate([local_gram, local_rayleigh], axis=0))
-    gram_total, rayleigh_total = totals[: local_gram.shape[0]], totals[local_gram.shape[0] :]
+    both = jnp.dot(current.T, jnp.concatenate([current, applied], axis=1), precision=lax.Precision.HIGHEST)
+    totals = all_sum(both)
+    gram_total, rayleigh_total = totals[:, : current.shape[1]], totals[:, current.shape[1] :]
     gram_matrix = gram_total / node_count
     rayleigh = rayleigh_total / node_count
     factor = jnp.linalg.cholesky(gram_matrix)

time: 239 us -> 239 us (level)
  no operation moved by 1% of the time
where the time goes in v14:
time: 239 us
  waiting for transfers between devices  144 us (60%)
  matrix products  32.5 us (14%)
  other arithmetic  30.9 us (13%)
  starting transfers between devices  23.8 us (10%)
  between operations  3.98 us (2%)
  local copies, waits for them, and re-layouts  3.58 us (1%)
    ppermute x15, waiting for transfers between devices, halving_scatter_sum(): blocks = kept + lax.ppermute(sent, axis, pairs)  87.8 us
    ppermute x12, waiting for transfers between devices, doubling_gather(): other = lax.ppermute(result, axis, pairs)  29.6 us
    ppermute x5, waiting for transfers between devices, butterfly_sum(): value = value + lax.ppermute(value, axis, pairs)  23.7 us
    ppermute x12, starting transfers between devices, doubling_gather(): other = lax.ppermute(result, axis, pairs)  13.1 us
    another operation x3, other arithmetic, local(): factor = jnp.linalg.cholesky(gram_matrix)  12.4 us
    dot_general x5, matrix products, operate(): jnp.dot(w_lo, gathered, preferred_element_type=jnp.float32)  10.9 us
    another operation x2, other arithmetic, local(): lax.linalg.triangular_solve(factor, current, left_side=False, lower=True,...  10.5 us
    dot_general x1, matrix products, local(): jnp.einsum('rst,rsab->ratb', onehot, tiles, preferred_element_type=jnp.fl...  8.2 us
  transfers between devices with their start and end apart: 35, of which 29 were waited for; matrix products, arithmetic and copies ran while one was open for 8% of the time, Pallas kernels for 0%

profile of v14, /device:TPU:0, one launch (start us, length us, event | category | flops | bytes accessed | tf_op | source)
XLA Modules:
  0.0 238.8 jit_solution(4327579809363437539)
XLA Ops:
  1.6 3.0 %collective-permute-start = (bf16[256,128]{1,0:T(8,128)(2,1)S(1)}, bf16[256,128]{1,0:T(8,128)(2,1)S(1)}, u32[]{:S(2)}, u32[]{:S(2)}) collective-permute-start(bf16[256,128]{1,0:T(8,128)(2,1)S(1)} %multiply_convert_fusion.4), channel_id=1, source_target_pairs={{0,8},{8,0},{16,24},{24,16},{1,9},{9,1},{17,25},{25,17},{2,10},{10... | collective-permute-start | bytes 196616 | tf_op jit(solution)/shard_map/ppermute | solution.py:77
  4.8 3.0 %collective-permute-start.2 = (bf16[1,256,128]{2,1,0:T(8,128)(2,1)}, bf16[1,256,128]{2,1,0:T(8,128)(2,1)S(1)}, u32[]{:S(2)}, u32[]{:S(2)}) collective-permute-start(bf16[1,256,128]{2,1,0:T(8,128)(2,1)} %bitcast.183), channel_id=1, source_target_pairs={{0,4},{1,5},{2,6},{3,7},{4,0},{5,1},{6,2},{7,3},{8,12},{9,13},{10,... | collective-permute-start | bytes 196616 | tf_op jit(solution)/shard_map/ppermute | solution.py:95
  7.8 8.2 %fusion.1 = f32[16,8,128,128]{3,1,2,0:T(8,128)S(1)} fusion(bf16[16,16,128,128]{3,2,1,0:T(8,128)(2,1)} %param.7, s32[16,16]{1,0:T(8,128)} %param.8), kind=kOutput, calls=%fused_computation.3 | convolution fusion | flops 67110912 | bytes 16778240 | tf_op jit(solution)/shard_map/rst,rsab->ratb/dot_general | solution.py:115
  16.0 5.3 %fusion = (bf16[2048,1024]{1,0:T(8,128)(2,1)}, bf16[2048,1024]{1,0:T(8,128)(2,1)}) fusion(f32[256,8,8,128]{3,2,1,0:T(8,128)S(1)} %bitcast.161), kind=kLoop, calls=%fused_computation.2 | loop fusion | flops 6291456 | bytes 16777216 | tf_op jit(solution)/shard_map/convert_element_type | solution.py:11
  21.4 1.6 collective-permute-start.1
  23.1 1.6 collective-permute-start.3
  25.3 2.8 %collective-permute-done.3 = bf16[2,256,128]{2,1,0:T(8,128)(2,1)S(1)} collective-permute-done((bf16[2,256,128]{2,1,0:T(8,128)(2,1)S(1)}, bf16[2,256,128]{2,1,0:T(8,128)(2,1)S(1)}, u32[]{:S(2)}, u32[]{:S(2)}) %collective-permute-start.3) | collective-permute-done | bytes 131104 | tf_op jit(solution)/shard_map/ppermute | solution.py:95
  28.3 3.5 %fusion.35 = f32[2048,128]{1,0:T(8,128)S(1)} fusion(bf16[2048,1024]{1,0:T(8,128)(2,1)} %get-tuple-element.10, bf16[512,128]{1,0:T(8,128)(2,1)S(1)} %get-tuple-element.25, bf16[512,128]{1,0:T(8,128)(2,1)S(1)} %get-tuple-element.24), kind=kOutput, calls=%fused_computation.113 | convolution fusion | flops 537395200 | bytes 5505024 | tf_op jit(solution)/shard_map/dot_general | solution.py:126
  34.0 1.3 fusion.7
  35.9 1.5 collective-permute-done.7
  37.6 1.6 collective-permute-start.8
  39.2 7.0 %collective-permute-done.8 = f32[2,256,128]{2,1,0:T(8,128)S(1)} collective-permute-done((f32[2,256,128]{2,1,0:T(8,128)S(1)}, f32[2,256,128]{2,1,0:T(8,128)S(1)}, u32[]{:S(2)}, u32[]{:S(2)}) %collective-permute-start.8) | collective-permute-done | bytes 262176 | tf_op jit(solution)/shard_map/ppermute | solution.py:63
  49.9 5.1 %collective-permute-done.9 = f32[1,256,128]{2,1,0:T(8,128)S(1)} collective-permute-done((f32[1,256,128]{2,1,0:T(8,128)S(1)}, f32[1,256,128]{2,1,0:T(8,128)S(1)}, u32[]{:S(2)}, u32[]{:S(2)}) %collective-permute-start.9) | collective-permute-done | bytes 131104 | tf_op jit(solution)/shard_map/ppermute | solution.py:63
  55.1 1.6 collective-permute-start.10
  56.7 2.8 %collective-permute-done.10 = bf16[256,128]{1,0:T(8,128)(2,1)S(1)} collective-permute-done((bf16[256,128]{1,0:T(8,128)(2,1)S(1)}, bf16[256,128]{1,0:T(8,128)(2,1)S(1)}, u32[]{:S(2)}, u32[]{:S(2)}) %collective-permute-start.10) | collective-permute-done | bytes 65568 | tf_op jit(solution)/shard_map/ppermute | solution.py:77
  59.8 4.7 %collective-permute-done.11 = bf16[512,128]{1,0:T(8,128)(2,1)S(1)} collective-permute-done((bf16[512,128]{1,0:T(8,128)(2,1)S(1)}, bf16[512,128]{1,0:T(8,128)(2,1)S(1)}, u32[]{:S(2)}, u32[]{:S(2)}) %collective-permute-start.11) | collective-permute-done | bytes 131104 | tf_op jit(solution)/shard_map/ppermute | solution.py:77
  64.5 3.4 %fusion.34 = f32[2048,128]{1,0:T(8,128)S(1)} fusion(bf16[2048,1024]{1,0:T(8,128)(2,1)} %get-tuple-element.10, bf16[512,128]{1,0:T(8,128)(2,1)S(1)} %get-tuple-element.21, bf16[512,128]{1,0:T(8,128)(2,1)S(1)} %get-tuple-element.20), kind=kOutput, calls=%fused_computation.112 | convolution fusion | flops 537395200 | bytes 5505024 | tf_op jit(solution)/shard_map/dot_general | solution.py:126
  68.9 1.3 copy-done.1
  71.6 1.9 collective-permute-done.12
  73.7 8.3 %collective-permute-done.13 = f32[2,256,128]{2,1,0:T(8,128)S(1)} collective-permute-done((f32[2,256,128]{2,1,0:T(8,128)S(1)}, f32[2,256,128]{2,1,0:T(8,128)S(1)}, u32[]{:S(2)}, u32[]{:S(2)}) %collective-permute-start.13) | collective-permute-done | bytes 262176 | tf_op jit(solution)/shard_map/ppermute | solution.py:63
  82.2 8.3 %collective-permute-done.14 = f32[1,256,128]{2,1,0:T(8,128)S(1)} collective-permute-done((f32[1,256,128]{2,1,0:T(8,128)S(1)}, f32[1,256,128]{2,1,0:T(8,128)S(1)}, u32[]{:S(2)}, u32[]{:S(2)}) %collective-permute-start.14) | collective-permute-done | bytes 131104 | tf_op jit(solution)/shard_map/ppermute | solution.py:63
  90.6 1.6 collective-permute-start.15
  92.2 2.8 %collective-permute-done.15 = bf16[256,128]{1,0:T(8,128)(2,1)S(1)} collective-permute-done((bf16[256,128]{1,0:T(8,128)(2,1)S(1)}, bf16[256,128]{1,0:T(8,128)(2,1)S(1)}, u32[]{:S(2)}, u32[]{:S(2)}) %collective-permute-start.15) | collective-permute-done | bytes 65568 | tf_op jit(solution)/shard_map/ppermute | solution.py:77
  95.4 4.7 %collective-permute-done.16 = bf16[512,128]{1,0:T(8,128)(2,1)S(1)} collective-permute-done((bf16[512,128]{1,0:T(8,128)(2,1)S(1)}, bf16[512,128]{1,0:T(8,128)(2,1)S(1)}, u32[]{:S(2)}, u32[]{:S(2)}) %collective-permute-start.16) | collective-permute-done | bytes 131104 | tf_op jit(solution)/shard_map/ppermute | solution.py:77
  103.7 1.9 collective-permute-done.17
  105.7 8.3 %collective-permute-done.18 = f32[2,256,128]{2,1,0:T(8,128)S(1)} collective-permute-done((f32[2,256,128]{2,1,0:T(8,128)S(1)}, f32[2,256,128]{2,1,0:T(8,128)S(1)}, u32[]{:S(2)}, u32[]{:S(2)}) %collective-permute-start.18) | collective-permute-done | bytes 262176 | tf_op jit(solution)/shard_map/ppermute | solution.py:63
  114.3 8.3 %collective-permute-done.19 = f32[1,256,128]{2,1,0:T(8,128)S(1)} collective-permute-done((f32[1,256,128]{2,1,0:T(8,128)S(1)}, f32[1,256,128]{2,1,0:T(8,128)S(1)}, u32[]{:S(2)}, u32[]{:S(2)}) %collective-permute-start.19) | collective-permute-done | bytes 131104 | tf_op jit(solution)/shard_map/ppermute | solution.py:63
  122.7 1.6 collective-permute-start.20
  124.3 2.8 %collective-permute-done.20 = bf16[256,128]{1,0:T(8,128)(2,1)S(1)} collective-permute-done((bf16[256,128]{1,0:T(8,128)(2,1)S(1)}, bf16[256,128]{1,0:T(8,128)(2,1)S(1)}, u32[]{:S(2)}, u32[]{:S(2)}) %collective-permute-start.20) | collective-permute-done | bytes 65568 | tf_op jit(solution)/shard_map/ppermute | solution.py:77
  127.4 4.7 %collective-permute-done.21 = bf16[512,128]{1,0:T(8,128)(2,1)S(1)} collective-permute-done((bf16[512,128]{1,0:T(8,128)(2,1)S(1)}, bf16[512,128]{1,0:T(8,128)(2,1)S(1)}, u32[]{:S(2)}, u32[]{:S(2)}) %collective-permute-start.21) | collective-permute-done | bytes 131104 | tf_op jit(solution)/shard_map/ppermute | solution.py:77
  132.2 1.5 fusion.32
  136.0 1.9 collective-permute-done.22
  138.0 8.3 %collective-permute-done.23 = f32[2,256,128]{2,1,0:T(8,128)S(1)} collective-permute-done((f32[2,256,128]{2,1,0:T(8,128)S(1)}, f32[2,256,128]{2,1,0:T(8,128)S(1)}, u32[]{:S(2)}, u32[]{:S(2)}) %collective-permute-start.23) | collective-permute-done | bytes 262176 | tf_op jit(solution)/shard_map/ppermute | solution.py:63
  146.6 8.3 %collective-permute-done.24 = f32[1,256,128]{2,1,0:T(8,128)S(1)} collective-permute-done((f32[1,256,128]{2,1,0:T(8,128)S(1)}, f32[1,256,128]{2,1,0:T(8,128)S(1)}, u32[]{:S(2)}, u32[]{:S(2)}) %collective-permute-start.24) | collective-permute-done | bytes 131104 | tf_op jit(solution)/shard_map/ppermute | solution.py:63
  155.0 1.6 collective-permute-start.25
  156.6 2.8 %collective-permute-done.25 = bf16[256,128]{1,0:T(8,128)(2,1)S(1)} collective-permute-done((bf16[256,128]{1,0:T(8,128)(2,1)S(1)}, bf16[256,128]{1,0:T(8,128)(2,1)S(1)}, u32[]{:S(2)}, u32[]{:S(2)}) %collective-permute-start.25) | collective-permute-done | bytes 65568 | tf_op jit(solution)/shard_map/ppermute | solution.py:77
  159.7 4.7 %collective-permute-done.26 = bf16[512,128]{1,0:T(8,128)(2,1)S(1)} collective-permute-done((bf16[512,128]{1,0:T(8,128)(2,1)S(1)}, bf16[512,128]{1,0:T(8,128)(2,1)S(1)}, u32[]{:S(2)}, u32[]{:S(2)}) %collective-permute-start.26) | collective-permute-done | bytes 131104 | tf_op jit(solution)/shard_map/ppermute | solution.py:77
  168.0 1.9 collective-permute-done.27
  170.1 8.3 %collective-permute-done.28 = f32[2,256,128]{2,1,0:T(8,128)S(1)} collective-permute-done((f32[2,256,128]{2,1,0:T(8,128)S(1)}, f32[2,256,128]{2,1,0:T(8,128)S(1)}, u32[]{:S(2)}, u32[]{:S(2)}) %collective-permute-start.28) | collective-permute-done | bytes 262176 | tf_op jit(solution)/shard_map/ppermute | solution.py:63
  178.6 8.3 %collective-permute-done.29 = f32[1,256,128]{2,1,0:T(8,128)S(1)} collective-permute-done((f32[1,256,128]{2,1,0:T(8,128)S(1)}, f32[1,256,128]{2,1,0:T(8,128)S(1)}, u32[]{:S(2)}, u32[]{:S(2)}) %collective-permute-start.29) | collective-permute-done | bytes 131104 | tf_op jit(solution)/shard_map/ppermute | solution.py:63
  187.7 1.3 collective-permute-done.30
  189.2 5.5 %collective-permute-done.31 = f32[128,256]{0,1:T(8,128)S(1)} collective-permute-done((f32[128,256]{0,1:T(8,128)S(1)}, f32[128,256]{0,1:T(8,128)S(1)}, u32[]{:S(2)}, u32[]{:S(2)}) %collective-permute-start.31) | collective-permute-done | bytes 131104 | tf_op jit(solution)/shard_map/ppermute | solution.py:28
  194.9 8.3 %collective-permute-done.32 = f32[128,256]{0,1:T(8,128)S(1)} collective-permute-done((f32[128,256]{0,1:T(8,128)S(1)}, f32[128,256]{0,1:T(8,128)S(1)}, u32[]{:S(2)}, u32[]{:S(2)}) %collective-permute-start.32) | collective-permute-done | bytes 131104 | tf_op jit(solution)/shard_map/ppermute | solution.py:28
  203.2 1.6 collective-permute-start.33
  204.8 3.9 %collective-permute-done.33 = f32[128,256]{0,1:T(8,128)S(1)} collective-permute-done((f32[128,256]{0,1:T(8,128)S(1)}, f32[128,256]{0,1:T(8,128)S(1)}, u32[]{:S(2)}, u32[]{:S(2)}) %collective-permute-start.33) | collective-permute-done | bytes 131104 | tf_op jit(solution)/shard_map/ppermute | solution.py:28
  209.1 4.7 %collective-permute-done.34 = f32[128,256]{0,1:T(8,128)S(1)} collective-permute-done((f32[128,256]{0,1:T(8,128)S(1)}, f32[128,256]{0,1:T(8,128)S(1)}, u32[]{:S(2)}, u32[]{:S(2)}) %collective-permute-start.34) | collective-permute-done | bytes 131104 | tf_op jit(solution)/shard_map/ppermute | solution.py:28
  213.9 11.7 %cholesky.16 = f32[128,128]{1,0:T(8,128)S(1)} custom-call(f32[128,128]{1,0:T(8,128)S(1)} %fusion.43), custom_call_target="Cholesky" | custom-call | tf_op jit(solution)/shard_map/jit(cholesky)/cholesky | solution.py:148
  226.9 9.8 %custom-call.10 = f32[1,128,128]{1,2,0:T(8,128)S(1)} custom-call(f32[1,128,128]{2,1,0:T(8,128)S(1)} %fusion.36), custom_call_target="InvertDiagBlocksLowerTriangular" | custom-call | tf_op jit(solution)/shard_map/triangular_solve | solution.py:149
  (139 shorter events, 26.1 us)
Async XLA Ops:
  1.6 19.6 %collective-permute-start = (bf16[256,128]{1,0:T(8,128)(2,1)S(1)}, bf16[256,128]{1,0:T(8,128)(2,1)S(1)}, u32[]{:S(2)}, u32[]{:S(2)}) collective-permute-start(bf16[256,128]{1,0:T(8,128)(2,1)S(1)} %multiply_convert_fusion.4), channel_id=1, source_target_pairs={{0,8},{8,0},{16,24},{24,16},{1,9},{9,1},{17,25},{25,17},{2,10},{10... | collective-permute-start | bytes 196616 | tf_op jit(solution)/shard_map/ppermute | solution.py:77
  4.7 20.0 %collective-permute-start.5 = (bf16[256,128]{1,0:T(8,128)(2,1)}, bf16[256,128]{1,0:T(8,128)(2,1)S(1)}, u32[]{:S(2)}, u32[]{:S(2)}) collective-permute-start(bf16[256,128]{1,0:T(8,128)(2,1)} %param.11), channel_id=1, source_target_pairs={{0,8},{8,0},{16,24},{24,16},{1,9},{9,1},{17,25},{25,17},{2,10},{10... | collective-permute-start | bytes 196616 | tf_op jit(solution)/shard_map/ppermute | solution.py:77
  4.8 18.3 %collective-permute-start.2 = (bf16[1,256,128]{2,1,0:T(8,128)(2,1)}, bf16[1,256,128]{2,1,0:T(8,128)(2,1)S(1)}, u32[]{:S(2)}, u32[]{:S(2)}) collective-permute-start(bf16[1,256,128]{2,1,0:T(8,128)(2,1)} %bitcast.183), channel_id=1, source_target_pairs={{0,4},{1,5},{2,6},{3,7},{4,0},{5,1},{6,2},{7,3},{8,12},{9,13},{10,... | collective-permute-start | bytes 196616 | tf_op jit(solution)/shard_map/ppermute | solution.py:95
  16.0 5.3 %copy-start.3 = (f32[256,128]{1,0:T(8,128)S(1)}, f32[256,128]{1,0:T(8,128)}, u32[]{:S(2)}) copy-start(f32[256,128]{1,0:T(8,128)} %param.10) | copy-start | bytes 393220
  16.0 5.3 %copy-start.5 = (f32[256]{0:T(256)S(1)}, f32[256]{0:T(256)}, u32[]{:S(2)}) copy-start(f32[256]{0:T(256)} %param.9) | copy-start | bytes 3076
  16.0 7.0 %copy-start.4 = (bf16[256,128]{1,0:T(8,128)(2,1)S(1)}, bf16[256,128]{1,0:T(8,128)(2,1)}, u32[]{:S(2)}) copy-start(bf16[256,128]{1,0:T(8,128)(2,1)} %param.11) | copy-start | bytes 196612
  21.4 6.8 %collective-permute-start.1 = (bf16[512,128]{1,0:T(8,128)(2,1)S(1)}, bf16[512,128]{1,0:T(8,128)(2,1)S(1)}, u32[]{:S(2)}, u32[]{:S(2)}) collective-permute-start(bf16[512,128]{1,0:T(8,128)(2,1)S(1)} %pad_maximum_fusion.8), channel_id=1, source_target_pairs={{0,16},{8,24},{16,0},{24,8},{1,17},{9,25},{17,1},{25,9},{2,18},{10... | collective-permute-start | bytes 393224 | tf_op jit(solution)/shard_map/ppermute | solution.py:77
  23.1 5.0 %collective-permute-start.3 = (bf16[2,256,128]{2,1,0:T(8,128)(2,1)S(1)}, bf16[2,256,128]{2,1,0:T(8,128)(2,1)S(1)}, u32[]{:S(2)}, u32[]{:S(2)}) collective-permute-start(bf16[2,256,128]{2,1,0:T(8,128)(2,1)S(1)} %pad_maximum_fusion.9), channel_id=1, source_target_pairs={{0,2},{1,3},{2,0},{3,1},{4,6},{5,7},{6,4},{7,5},{8,10},{9,11},{10,... | collective-permute-start | bytes 393224 | tf_op jit(solution)/shard_map/ppermute | solution.py:95
  24.7 7.0 %collective-permute-start.6 = (bf16[512,128]{1,0:T(8,128)(2,1)S(1)}, bf16[512,128]{1,0:T(8,128)(2,1)S(1)}, u32[]{:S(2)}, u32[]{:S(2)}) collective-permute-start(bf16[512,128]{1,0:T(8,128)(2,1)S(1)} %pad_maximum_fusion.10), channel_id=1, source_target_pairs={{0,16},{8,24},{16,0},{24,8},{1,17},{9,25},{17,1},{25,9},{2,18},{10... | collective-permute-start | bytes 393224 | tf_op jit(solution)/shard_map/ppermute | solution.py:77
  28.1 3.7 %copy-start.7 = (f32[128]{0:T(128)S(1)}, f32[128]{0:T(128)}, u32[]{:S(2)}) copy-start(f32[128]{0:T(128)} %param.12) | copy-start | bytes 1540
  28.2 4.0 %collective-permute-start.4 = (bf16[4,256,128]{2,1,0:T(8,128)(2,1)S(1)}, bf16[4,256,128]{2,1,0:T(8,128)(2,1)S(1)}, u32[]{:S(2)}, u32[]{:S(2)}) collective-permute-start(bf16[4,256,128]{2,1,0:T(8,128)(2,1)S(1)} %pad_maximum_fusion.2), channel_id=1, source_target_pairs={{0,1},{1,0},{2,3},{3,2},{4,5},{5,4},{6,7},{7,6},{8,9},{9,8},{10,11... | collective-permute-start | bytes 786440 | tf_op jit(solution)/shard_map/ppermute | solution.py:95
  31.9 2.2 copy-start
  35.3 11.4 %copy-start.6 = (f32[2]{0:T(128)S(1)}, f32[2]{0:T(128)}, u32[]{:S(2)}) copy-start(f32[2]{0:T(128)} %param.13) | copy-start | bytes 28
  35.4 2.1 collective-permute-start.7
  37.6 8.7 %collective-permute-start.8 = (f32[2,256,128]{2,1,0:T(8,128)S(1)}, f32[2,256,128]{2,1,0:T(8,128)S(1)}, u32[]{:S(2)}, u32[]{:S(2)}) collective-permute-start(f32[2,256,128]{2,1,0:T(8,128)S(1)} %dynamic-slice_bitcast_fusion.9), channel_id=1, source_target_pairs={{0,2},{1,3},{2,0},{3,1},{4,6},{5,7},{6,4},{7,5},{8,10},{9,11},{10,... | collective-permute-start | bytes 786440 | tf_op jit(solution)/shard_map/ppermute | solution.py:63
  46.3 8.7 %collective-permute-start.9 = (f32[1,256,128]{2,1,0:T(8,128)S(1)}, f32[1,256,128]{2,1,0:T(8,128)S(1)}, u32[]{:S(2)}, u32[]{:S(2)}) collective-permute-start(f32[1,256,128]{2,1,0:T(8,128)S(1)} %constant_dynamic-slice_fusion.4), channel_id=1, source_target_pairs={{0,4},{1,5},{2,6},{3,7},{4,0},{5,1},{6,2},{7,3},{8,12},{9,13},{10,... | collective-permute-start | bytes 393224 | tf_op jit(solution)/shard_map/ppermute | solution.py:63
  55.1 4.3 %collective-permute-start.10 = (bf16[256,128]{1,0:T(8,128)(2,1)S(1)}, bf16[256,128]{1,0:T(8,128)(2,1)S(1)}, u32[]{:S(2)}, u32[]{:S(2)}) collective-permute-start(bf16[256,128]{1,0:T(8,128)(2,1)S(1)} %get-tuple-element.8), channel_id=1, source_target_pairs={{0,8},{8,0},{16,24},{24,16},{1,9},{9,1},{17,25},{25,17},{2,10},{10... | collective-permute-start | bytes 196616 | tf_op jit(solution)/shard_map/ppermute | solution.py:77
  59.4 5.0 %collective-permute-start.11 = (bf16[512,128]{1,0:T(8,128)(2,1)S(1)}, bf16[512,128]{1,0:T(8,128)(2,1)S(1)}, u32[]{:S(2)}, u32[]{:S(2)}) collective-permute-start(bf16[512,128]{1,0:T(8,128)(2,1)S(1)} %pad_maximum_fusion.11), channel_id=1, source_target_pairs={{0,16},{8,24},{16,0},{24,8},{1,17},{9,25},{17,1},{25,9},{2,18},{10... | collective-permute-start | bytes 393224 | tf_op jit(solution)/shard_map/ppermute | solution.py:77
  68.0 2.2 copy-start.1
  71.5 28.6 %copy-start.2 = (bf16[2048,1024]{1,0:T(8,128)(2,1)S(1)}, bf16[2048,1024]{1,0:T(8,128)(2,1)}, u32[]{:S(2)}) copy-start(bf16[2048,1024]{1,0:T(8,128)(2,1)} %get-tuple-element.10) | copy-start | bytes 12582916
  71.5 2.0 collective-permute-start.12
  73.6 8.4 %collective-permute-start.13 = (f32[2,256,128]{2,1,0:T(8,128)S(1)}, f32[2,256,128]{2,1,0:T(8,128)S(1)}, u32[]{:S(2)}, u32[]{:S(2)}) collective-permute-start(f32[2,256,128]{2,1,0:T(8,128)S(1)} %dynamic-slice_bitcast_fusion.8), channel_id=1, source_target_pairs={{0,2},{1,3},{2,0},{3,1},{4,6},{5,7},{6,4},{7,5},{8,10},{9,11},{10,... | collective-permute-start | bytes 786440 | tf_op jit(solution)/shard_map/ppermute | solution.py:63
  82.1 8.5 %collective-permute-start.14 = (f32[1,256,128]{2,1,0:T(8,128)S(1)}, f32[1,256,128]{2,1,0:T(8,128)S(1)}, u32[]{:S(2)}, u32[]{:S(2)}) collective-permute-start(f32[1,256,128]{2,1,0:T(8,128)S(1)} %constant_dynamic-slice_fusion.3), channel_id=1, source_target_pairs={{0,4},{1,5},{2,6},{3,7},{4,0},{5,1},{6,2},{7,3},{8,12},{9,13},{10,... | collective-permute-start | bytes 393224 | tf_op jit(solution)/shard_map/ppermute | solution.py:63
  90.6 4.3 %collective-permute-start.15 = (bf16[256,128]{1,0:T(8,128)(2,1)S(1)}, bf16[256,128]{1,0:T(8,128)(2,1)S(1)}, u32[]{:S(2)}, u32[]{:S(2)}) collective-permute-start(bf16[256,128]{1,0:T(8,128)(2,1)S(1)} %get-tuple-element.6), channel_id=1, source_target_pairs={{0,8},{8,0},{16,24},{24,16},{1,9},{9,1},{17,25},{25,17},{2,10},{10... | collective-permute-start | bytes 196616 | tf_op jit(solution)/shard_map/ppermute | solution.py:77
  95.0 5.0 %collective-permute-start.16 = (bf16[512,128]{1,0:T(8,128)(2,1)S(1)}, bf16[512,128]{1,0:T(8,128)(2,1)S(1)}, u32[]{:S(2)}, u32[]{:S(2)}) collective-permute-start(bf16[512,128]{1,0:T(8,128)(2,1)S(1)} %pad_maximum_fusion.12), channel_id=1, source_target_pairs={{0,16},{8,24},{16,0},{24,8},{1,17},{9,25},{17,1},{25,9},{2,18},{10... | collective-permute-start | bytes 393224 | tf_op jit(solution)/shard_map/ppermute | solution.py:77
  103.6 2.0 collective-permute-start.17
  105.7 8.4 %collective-permute-start.18 = (f32[2,256,128]{2,1,0:T(8,128)S(1)}, f32[2,256,128]{2,1,0:T(8,128)S(1)}, u32[]{:S(2)}, u32[]{:S(2)}) collective-permute-start(f32[2,256,128]{2,1,0:T(8,128)S(1)} %dynamic-slice_bitcast_fusion.7), channel_id=1, source_target_pairs={{0,2},{1,3},{2,0},{3,1},{4,6},{5,7},{6,4},{7,5},{8,10},{9,11},{10,... | collective-permute-start | bytes 786440 | tf_op jit(solution)/shard_map/ppermute | solution.py:63
  114.1 8.5 %collective-permute-start.19 = (f32[1,256,128]{2,1,0:T(8,128)S(1)}, f32[1,256,128]{2,1,0:T(8,128)S(1)}, u32[]{:S(2)}, u32[]{:S(2)}) collective-permute-start(f32[1,256,128]{2,1,0:T(8,128)S(1)} %constant_dynamic-slice_fusion.2), channel_id=1, source_target_pairs={{0,4},{1,5},{2,6},{3,7},{4,0},{5,1},{6,2},{7,3},{8,12},{9,13},{10,... | collective-permute-start | bytes 393224 | tf_op jit(solution)/shard_map/ppermute | solution.py:63
  122.7 4.3 %collective-permute-start.20 = (bf16[256,128]{1,0:T(8,128)(2,1)S(1)}, bf16[256,128]{1,0:T(8,128)(2,1)S(1)}, u32[]{:S(2)}, u32[]{:S(2)}) collective-permute-start(bf16[256,128]{1,0:T(8,128)(2,1)S(1)} %get-tuple-element.4), channel_id=1, source_target_pairs={{0,8},{8,0},{16,24},{24,16},{1,9},{9,1},{17,25},{25,17},{2,10},{10... | collective-permute-start | bytes 196616 | tf_op jit(solution)/shard_map/ppermute | solution.py:77
  127.1 5.0 %collective-permute-start.21 = (bf16[512,128]{1,0:T(8,128)(2,1)S(1)}, bf16[512,128]{1,0:T(8,128)(2,1)S(1)}, u32[]{:S(2)}, u32[]{:S(2)}) collective-permute-start(bf16[512,128]{1,0:T(8,128)(2,1)S(1)} %pad_maximum_fusion.13), channel_id=1, source_target_pairs={{0,16},{8,24},{16,0},{24,8},{1,17},{9,25},{17,1},{25,9},{2,18},{10... | collective-permute-start | bytes 393224 | tf_op jit(solution)/shard_map/ppermute | solution.py:77
  135.9 2.0 collective-permute-start.22
  137.9 8.4 %collective-permute-start.23 = (f32[2,256,128]{2,1,0:T(8,128)S(1)}, f32[2,256,128]{2,1,0:T(8,128)S(1)}, u32[]{:S(2)}, u32[]{:S(2)}) collective-permute-start(f32[2,256,128]{2,1,0:T(8,128)S(1)} %dynamic-slice_bitcast_fusion.6), channel_id=1, source_target_pairs={{0,2},{1,3},{2,0},{3,1},{4,6},{5,7},{6,4},{7,5},{8,10},{9,11},{10,... | collective-permute-start | bytes 786440 | tf_op jit(solution)/shard_map/ppermute | solution.py:63
  146.4 8.5 %collective-permute-start.24 = (f32[1,256,128]{2,1,0:T(8,128)S(1)}, f32[1,256,128]{2,1,0:T(8,128)S(1)}, u32[]{:S(2)}, u32[]{:S(2)}) collective-permute-start(f32[1,256,128]{2,1,0:T(8,128)S(1)} %constant_dynamic-slice_fusion.1), channel_id=1, source_target_pairs={{0,4},{1,5},{2,6},{3,7},{4,0},{5,1},{6,2},{7,3},{8,12},{9,13},{10,... | collective-permute-start | bytes 393224 | tf_op jit(solution)/shard_map/ppermute | solution.py:63
  155.0 4.3 %collective-permute-start.25 = (bf16[256,128]{1,0:T(8,128)(2,1)S(1)}, bf16[256,128]{1,0:T(8,128)(2,1)S(1)}, u32[]{:S(2)}, u32[]{:S(2)}) collective-permute-start(bf16[256,128]{1,0:T(8,128)(2,1)S(1)} %get-tuple-element.2), channel_id=1, source_target_pairs={{0,8},{8,0},{16,24},{24,16},{1,9},{9,1},{17,25},{25,17},{2,10},{10... | collective-permute-start | bytes 196616 | tf_op jit(solution)/shard_map/ppermute | solution.py:77
  159.4 5.0 %collective-permute-start.26 = (bf16[512,128]{1,0:T(8,128)(2,1)S(1)}, bf16[512,128]{1,0:T(8,128)(2,1)S(1)}, u32[]{:S(2)}, u32[]{:S(2)}) collective-permute-start(bf16[512,128]{1,0:T(8,128)(2,1)S(1)} %pad_maximum_fusion.14), channel_id=1, source_target_pairs={{0,16},{8,24},{16,0},{24,8},{1,17},{9,25},{17,1},{25,9},{2,18},{10... | collective-permute-start | bytes 393224 | tf_op jit(solution)/shard_map/ppermute | solution.py:77
  167.9 2.0 collective-permute-start.27
  170.0 8.4 %collective-permute-start.28 = (f32[2,256,128]{2,1,0:T(8,128)S(1)}, f32[2,256,128]{2,1,0:T(8,128)S(1)}, u32[]{:S(2)}, u32[]{:S(2)}) collective-permute-start(f32[2,256,128]{2,1,0:T(8,128)S(1)} %dynamic-slice_bitcast_fusion.5), channel_id=1, source_target_pairs={{0,2},{1,3},{2,0},{3,1},{4,6},{5,7},{6,4},{7,5},{8,10},{9,11},{10,... | collective-permute-start | bytes 786440 | tf_op jit(solution)/shard_map/ppermute | solution.py:63
  178.5 8.5 %collective-permute-start.29 = (f32[1,256,128]{2,1,0:T(8,128)S(1)}, f32[1,256,128]{2,1,0:T(8,128)S(1)}, u32[]{:S(2)}, u32[]{:S(2)}) collective-permute-start(f32[1,256,128]{2,1,0:T(8,128)S(1)} %constant_dynamic-slice_fusion), channel_id=1, source_target_pairs={{0,4},{1,5},{2,6},{3,7},{4,0},{5,1},{6,2},{7,3},{8,12},{9,13},{10,... | collective-permute-start | bytes 393224 | tf_op jit(solution)/shard_map/ppermute | solution.py:63
  187.6 1.4 collective-permute-start.30
  189.1 5.6 %collective-permute-start.31 = (f32[128,256]{0,1:T(8,128)S(1)}, f32[128,256]{0,1:T(8,128)S(1)}, u32[]{:S(2)}, u32[]{:S(2)}) collective-permute-start(f32[128,256]{0,1:T(8,128)S(1)} %add.260), channel_id=1, source_target_pairs={{0,2},{1,3},{2,0},{3,1},{4,6},{5,7},{6,4},{7,5},{8,10},{9,11},{10,... | collective-permute-start | bytes 393224 | tf_op jit(solution)/shard_map/ppermute | solution.py:28
  194.7 8.5 %collective-permute-start.32 = (f32[128,256]{0,1:T(8,128)S(1)}, f32[128,256]{0,1:T(8,128)S(1)}, u32[]{:S(2)}, u32[]{:S(2)}) collective-permute-start(f32[128,256]{0,1:T(8,128)S(1)} %add.261), channel_id=1, source_target_pairs={{0,4},{1,5},{2,6},{3,7},{4,0},{5,1},{6,2},{7,3},{8,12},{9,13},{10,... | collective-permute-start | bytes 393224 | tf_op jit(solution)/shard_map/ppermute | solution.py:28
  203.2 5.5 %collective-permute-start.33 = (f32[128,256]{0,1:T(8,128)S(1)}, f32[128,256]{0,1:T(8,128)S(1)}, u32[]{:S(2)}, u32[]{:S(2)}) collective-permute-start(f32[128,256]{0,1:T(8,128)S(1)} %add.262), channel_id=1, source_target_pairs={{0,8},{8,0},{16,24},{24,16},{1,9},{9,1},{17,25},{25,17},{2,10},{10... | collective-permute-start | bytes 393224 | tf_op jit(solution)/shard_map/ppermute | solution.py:28
  208.7 5.0 %collective-permute-start.34 = (f32[128,256]{0,1:T(8,128)S(1)}, f32[128,256]{0,1:T(8,128)S(1)}, u32[]{:S(2)}, u32[]{:S(2)}) collective-permute-start(f32[128,256]{0,1:T(8,128)S(1)} %add.263), channel_id=1, source_target_pairs={{0,16},{8,24},{16,0},{24,8},{1,17},{9,25},{17,1},{25,9},{2,18},{10... | collective-permute-start | bytes 393224 | tf_op jit(solution)/shard_map/ppermute | solution.py:28
